TPU v7x, 32 devices: a whole 2x2x4 slice. The times are simulated.
32 devices in a mesh: parts: 2 (over x), chan: 8 (over z, y), tm: 2 (over core).
Axes of the slice: x: 2, y: 2, z: 4, core: 2. Of those that a mesh axis runs over, the one named last changes fastest.
Arguments:
- records: bfloat16 [8192, 6144], P(('chan', 'tm'), 'parts'), parts along dimension 1, may hold values from -500 to 500
- fir_taps: float32 [32], replicated, may hold values from -1 to 1
- channel_map: int32 [6144], P('parts'), parts along dimension 0, may hold values from 0 to 3071, each once
- source_owner: int32 [4], P('parts'), parts along dimension 0, may hold values from 0 to 7
- source_offset: int32 [4], P('parts'), parts along dimension 0, may hold values from 0 to 368
Outputs:
- correlations: float32 [2, 16, 6144, 512], P(None, None, ('parts', 'chan'), 'tm'), parts along dimension 2
There are 2 independent parts, one for each index of `parts`. A program takes and returns all parts, laid end to end along the dimension named above; an argument that names none is the same for every part. Nothing has to cross between parts.
All inputs are finite; a program needn't handle non-finite values.
Results may differ from a plain program's by a relative error of at most 0.014.
Values may be sent and summed in bfloat16 or wider, within the bound.
No kernel may reach another device: no remote copies, remote signals or barrier semaphores. Data moves between devices by JAX's collectives and lax.ppermute only.
A program may use at most 128 MiB of HBM per device.

v0:
```python
import math

import jax
import jax.numpy as jnp
from jax import lax
from jax.sharding import PartitionSpec as P

SRC = 16
STEPS = 2
LAGS = 512
TAPS = 32
STRIDE = 8
HALF_BAND = 32

two_pi = 2.0 * math.pi
epsilon = 1e-06


def split_bf16(x, parts):
    pieces = []
    rest = x
    for _ in range(parts):
        piece = rest.astype(jnp.bfloat16)
        pieces.append(piece)
        rest = rest - piece.astype(jnp.float32)
    return pieces


def decimation_matrix(fir_taps, out_rows, in_rows):
    rows = jnp.arange(out_rows, dtype=jnp.int32)[:, None]
    cols = jnp.arange(in_rows, dtype=jnp.int32)[None, :]
    tap = cols - rows * STRIDE
    inside = (tap >= 0) & (tap < TAPS)
    picked = jnp.take(fir_taps, jnp.clip(tap, 0, TAPS - 1), mode="clip")
    return jnp.where(inside, picked, 0.0)


def dft_table(samples, bins):
    inner = 32
    outer = samples // inner
    frequency = jnp.arange(bins, dtype=jnp.int32)[None, :]
    low = jnp.arange(inner, dtype=jnp.int32)[:, None]
    high = jnp.arange(outer, dtype=jnp.int32)[:, None] * inner
    scale = two_pi / samples
    low_angle = ((low * frequency) % samples).astype(jnp.float32) * scale
    high_angle = ((high * frequency) % samples).astype(jnp.float32) * scale
    cl, sl = jnp.cos(low_angle)[None], jnp.sin(low_angle)[None]
    ch, sh = jnp.cos(high_angle)[:, None], jnp.sin(high_angle)[:, None]
    cosine = (ch * cl - sh * sl).reshape(samples, bins)
    sine = (sh * cl + ch * sl).reshape(samples, bins)
    return jnp.concatenate([cosine, -sine], axis=1)


def band_matrix(bins):
    g = jnp.arange(bins, dtype=jnp.int32)
    near = jnp.abs(g[:, None] - g[None, :]) <= HALF_BAND
    return near.astype(jnp.bfloat16)


def lag_kernel(samples, first_lag, lag_count):
    bin_count = samples // 2
    frequency = jnp.arange(bin_count, dtype=jnp.int32)
    shifts = first_lag + jnp.arange(lag_count, dtype=jnp.int32) - LAGS // 2
    phases = jnp.mod(frequency[:, None] * shifts[None, :], samples)
    angles = phases.astype(jnp.float32) * (two_pi / samples)
    return jnp.concatenate([jnp.cos(angles), -jnp.sin(angles)], axis=0).astype(jnp.bfloat16)


def whiten_series(series):
    samples = series.shape[0]
    bins = samples // 2
    table = dft_table(samples, bins)
    hi, lo = split_bf16(table, 2)
    dims = (((0,), (0,)), ((), ()))
    both = lax.dot_general(
        series, jnp.concatenate([hi, lo], axis=1), dims, preferred_element_type=jnp.float32
    )
    spectrum = both[:, : 2 * bins] + both[:, 2 * bins :]
    real_part = spectrum[:, :bins]
    imag_part = spectrum[:, bins:]
    powers = real_part * real_part + imag_part * imag_part
    pieces = split_bf16(powers, 3)
    band = band_matrix(bins)
    window = jnp.dot(
        jnp.concatenate(pieces, axis=1),
        jnp.concatenate([band] * 3, axis=0),
        preferred_element_type=jnp.float32,
    )
    window_span = 2 * HALF_BAND + 1
    factor = 1.0 / jnp.sqrt(window / window_span + epsilon)
    return jnp.concatenate([real_part * factor, imag_part * factor], axis=1).astype(jnp.bfloat16)


def local(records, fir_taps, channel_map, source_owner, source_offset):
    n_chan = lax.axis_size("chan")
    n_tm = lax.axis_size("tm")
    n_dev = n_chan * n_tm
    raw_rows, channels = records.shape
    block = channels // n_chan
    out_rows = raw_rows // STRIDE
    halo_rows = TAPS - STRIDE
    samples = out_rows * n_dev

    shift = [(b, b - 1) for b in range(1, n_dev)]
    halo = lax.ppermute(records[:halo_rows], ("chan", "tm"), perm=shift)

    taps_matrix = decimation_matrix(fir_taps, out_rows, raw_rows + halo_rows)
    parts = split_bf16(taps_matrix, 3)
    stacked = jnp.concatenate(parts, axis=0)
    main = jnp.dot(stacked[:, :raw_rows], records, preferred_element_type=jnp.float32)
    tail = jnp.dot(stacked[:, raw_rows:], halo, preferred_element_type=jnp.float32)
    summed = main + tail
    decimated = (
        summed[:out_rows] + summed[out_rows : 2 * out_rows] + summed[2 * out_rows :]
    ).astype(jnp.bfloat16)

    first_rows = source_owner * block + source_offset
    picked = (first_rows[:, None] + jnp.arange(SRC, dtype=jnp.int32)[None, :]).reshape(-1)
    source_raw = jnp.take(channel_map, picked, mode="clip")
    block_raw = channel_map.reshape(n_chan, 1, block)
    block_raw = jnp.broadcast_to(block_raw, (n_chan, n_tm, block)).reshape(n_dev, block)
    index = jnp.concatenate(
        [block_raw, jnp.broadcast_to(source_raw[None], (n_dev, source_raw.shape[0]))], axis=1
    )
    width = index.shape[1]
    columns = jnp.take(decimated, index.reshape(-1), axis=1, mode="clip")
    series = lax.all_to_all(columns, ("chan", "tm"), 1, 0, tiled=True)

    white = whiten_series(series)
    receivers = white[:block]
    sources = white[block:].astype(jnp.float32)
    bins = samples // 2
    real_src = sources[:, :bins][:, :, None]
    imag_src = sources[:, bins:][:, :, None]

    lag_share = LAGS // n_tm
    kernel = lag_kernel(samples, lax.axis_index("tm") * lag_share, lag_share).astype(jnp.float32)
    cosine = kernel[:bins][None]
    sine = kernel[bins:][None]
    mixed = jnp.concatenate(
        [real_src * cosine + imag_src * sine, imag_src * cosine - real_src * sine], axis=1
    ).astype(jnp.bfloat16)
    factor = 1.0 / math.sqrt(bins)
    result = jnp.einsum("jf,sfl->sjl", receivers, mixed, preferred_element_type=jnp.float32) * factor
    return result.reshape(STEPS, SRC, block, lag_share)


def solution(mesh):
    return jax.shard_map(
        local,
        mesh=mesh,
        in_specs=(P(("chan", "tm"), "parts"), P(), P("parts"), P("parts"), P("parts")),
        out_specs=P(None, None, ("parts", "chan"), "tm"),
        check_vma=False,
    )
```

profile of v0, /device:TPU:0, one launch (start us, length us, event | category | flops | bytes accessed | tf_op | source)
XLA Modules:
  0.0 285.0 jit_solution(17625998810458868693)
XLA Ops:
  0.0 0.0 copy-start
  0.0 0.9 slice.50
  0.9 1.3 collective-permute-start
  2.3 0.3 fusion.66
  2.5 0.1 subtract_clamp_fusion
  2.6 0.2 reshape.195
  2.8 0.0 copy-done
  2.8 0.0 copy-start.3
  2.9 0.0 copy-start.4
  2.9 0.0 copy-start.2
  2.9 190.3 %gather_fusion = f32[34304]{0:T(1024)S(1)} fusion(f32[32]{0:T(128)S(1)} %copy-done, s32[34816]{0:T(1024)S(1)} %pad_clamp_fusion), kind=kCustom, calls=%fused_computation | custom fusion | bytes 411648 | tf_op jit(solution)/shard_map/jit(_take)/gather | solution.py:34
  193.1 0.1 reshape.194
  193.3 0.1 fusion.75
  193.4 0.1 fusion.48
  193.5 0.0 copy-done.3
  193.5 0.0 copy-done.4
  193.6 0.1 iota_add_fusion
  193.6 0.1 reshape.203
  193.7 0.0 copy-done.2
  193.7 0.7 gather_fusion.1
  194.5 0.1 reshape.211
  194.6 2.7 fusion.42
  197.3 0.1 abs_compare_fusion
  197.5 0.0 collective-permute-done
  197.5 0.4 convolution_add_fusion
  197.9 0.1 fusion.34
  198.1 0.4 copy.8
  198.4 12.5 %gather_fusion.2 = bf16[6656,64]{1,0:T(8,128)(2,1)S(1)} fusion(bf16[64,3072]{0,1:T(8,128)(2,1)S(1)} %copy.8, s32[7168]{0:T(1024)S(1)} %pad_clamp_fusion.1), kind=kCustom, calls=%fused_computation.2 | custom fusion | bytes 1730560 | tf_op jit(solution)/shard_map/jit(_take)/gather | solution.py:126
  211.0 1.6 copy.9
  212.6 8.2 %all-to-all-start = ((bf16[64,16,416]{2,0,1:T(8,128)(2,1)}), bf16[64,16,416]{2,0,1:T(8,128)(2,1)}, u32[]{:S(2)}, u32[]{:S(2)}) async-start(bf16[64,16,416]{2,0,1:T(8,128)(2,1)} %copy.9), calls=%async_computation | async-start | bytes 2097152 | tf_op jit(solution)/shard_map/all_to_all | solution.py:127
  220.8 2.5 cosine_convert_fusion
  223.3 0.1 maximum_convert_fusion
  223.4 0.3 fusion.69
  223.7 0.6 multiply_subtract_fusion
  224.3 0.5 subtract_convert_fusion.1
  224.9 1.6 fusion.10
  226.5 0.1 fusion.77
  226.5 17.2 %all-to-all-done = bf16[64,16,416]{2,0,1:T(8,128)(2,1)} async-done(((bf16[64,16,416]{2,0,1:T(8,128)(2,1)}), bf16[64,16,416]{2,0,1:T(8,128)(2,1)}, u32[]{:S(2)}, u32[]{:S(2)}) %all-to-all-start) | async-done | bytes 852000 | tf_op jit(solution)/shard_map/all_to_all | solution.py:127
  243.8 3.9 %fusion.4 = f32[416,2048]{1,0:T(8,128)S(1)} fusion(bf16[1024,416]{1,0:T(8,128)(2,1)} %bitcast.3, bf16[1024,1024]{1,0:T(8,128)(2,1)S(1)} %subtract_convert_fusion.1, bf16[1024,1024]{1,0:T(8,128)(2,1)} %fusion.10), kind=kOutput, calls=%fused_computation.11 | convolution fusion | flops 1753219072 | bytes 8454144 | tf_op jit(solution)/shard_map/dot_general | solution.py:75
  247.7 0.4 slice_add_fusion
  248.0 0.3 fusion.76
  248.3 0.9 multiply_convert_fusion.1
  249.3 7.9 %add_convert_fusion = (bf16[32,512,256]{1,2,0:T(8,128)(2,1)}, bf16[32,512,256]{1,2,0:T(8,128)(2,1)}) fusion(f32[512,256]{0,1:T(8,128)S(1)} %get-tuple-element.13, f32[32,512]{1,0:T(8,128)S(1)} %get-tuple-element.19, f32[512,256]{0,1:T(8,128)S(1)} %get-tuple-element.12, f32[32,512]{1,0:T(8,128)S(1)} %get-tuple-element.18), kind=kLoop, calls=%fused_computation.8 | loop fusion | flops 33554432 | bytes 17956864 | tf_op jit(solution)/shard_map/convert.1
  257.1 15.3 %broadcast_multiply_fusion = f32[32,256,384]{2,1,0:T(8,128)} fusion(bf16[32,512,256]{1,2,0:T(8,128)(2,1)} %get-tuple-element.11, bf16[32,512,256]{1,2,0:T(8,128)(2,1)} %get-tuple-element.10, bf16[416,512]{1,0:T(8,128)(2,1)S(1)} %get-tuple-element.6, bf16[416,512]{1,0:T(8,128)(2,1)S(1)} %get-tuple-element.5), kind=kOutput, calls=%fused_computation.9 | convolution fusion | flops 6480723968 | bytes 30212096 | tf_op jit(solution)/shard_map/jf,sfl->sjl/dot_general | solution.py:144
  272.4 0.0 copy-start.1
  272.4 12.6 %copy.10 = f32[2,16,384,256]{3,2,1,0:T(8,128)} copy(f32[2,16,384,256]{2,3,1,0:T(8,128)} %bitcast.23) | data formatting | bytes 25165824 | tf_op jit(solution)/shard_map/reshape | solution.py:145
  285.0 0.0 copy-done.1
  (15 shorter events, 0.2 us)
Async XLA Ops:
  0.0 2.8 copy-start
  0.9 196.5 %collective-permute-start = (bf16[24,3072]{1,0:T(8,128)(2,1)S(1)}, bf16[24,3072]{1,0:T(8,128)(2,1)S(1)}, u32[]{:S(2)}, u32[]{:S(2)}) collective-permute-start(bf16[24,3072]{1,0:T(8,128)(2,1)S(1)} %slice.50), channel_id=1, source_target_pairs={{1,0},{2,1},{3,2},{4,3},{5,4},{6,5},{7,6},{8,7},{9,8},{10,9},{11,1... | collective-permute-start | bytes 442376 | tf_op jit(solution)/shard_map/ppermute | solution.py:105
  2.8 190.7 %copy-start.3 = (s32[2]{0:T(128)S(1)}, s32[2]{0:T(128)}, u32[]{:S(2)}) copy-start(s32[2]{0:T(128)} %param.9) | copy-start | bytes 28
  2.9 190.7 %copy-start.4 = (s32[2]{0:T(128)S(1)}, s32[2]{0:T(128)}, u32[]{:S(2)}) copy-start(s32[2]{0:T(128)} %param.8) | copy-start | bytes 28
  2.9 190.9 %copy-start.2 = (s32[3072]{0:T(1024)S(1)}, s32[3072]{0:T(1024)}, u32[]{:S(2)}) copy-start(s32[3072]{0:T(1024)} %param.7) | copy-start | bytes 36868
  212.6 31.2 %all-to-all-start = ((bf16[64,16,416]{2,0,1:T(8,128)(2,1)}), bf16[64,16,416]{2,0,1:T(8,128)(2,1)}, u32[]{:S(2)}, u32[]{:S(2)}) async-start(bf16[64,16,416]{2,0,1:T(8,128)(2,1)} %copy.9), calls=%async_computation | async-start | bytes 2097152 | tf_op jit(solution)/shard_map/all_to_all | solution.py:127
  272.4 12.6 %copy-start.1 = (f32[32]{0:T(128)S(1)}, f32[32]{0:T(128)}, u32[]{:S(2)}) copy-start(f32[32]{0:T(128)} %param.6) | copy-start | bytes 388
where the time goes:
time: 287 us; the launch traced here: 285 us
  local copies, waits for them, and re-layouts  220 us (77%)
  matrix products  23.3 us (8%)
  waiting for transfers between devices  17.2 us (6%)
  other arithmetic  15.1 us (5%)
  starting transfers between devices  9.47 us (3%)
    gather x2, local copies, waits for them, and re-layouts, decimation_matrix(): picked = jnp.take(fir_taps, jnp.clip(tap, 0, TAPS - 1), mode='clip')  190 us
    all_to_all x1, waiting for transfers between devices, local(): series = lax.all_to_all(columns, ('chan', 'tm'), 1, 0, tiled=True)  17.2 us
    dot_general x1, matrix products, local(): jnp.einsum('jf,sfl->sjl', receivers, mixed, preferred_element_type=jnp.fl...  15.3 us
    reshape x1, local copies, waits for them, and re-layouts, local(): return result.reshape(STEPS, SRC, block, lag_share)  12.6 us
    gather x1, local copies, waits for them, and re-layouts, local(): columns = jnp.take(decimated, index.reshape(-1), axis=1, mode='clip')  12.5 us
    another operation x2, other arithmetic  10.3 us
    all_to_all x1, starting transfers between devices, local(): series = lax.all_to_all(columns, ('chan', 'tm'), 1, 0, tiled=True)  8.18 us
  transfers between devices with their start and end apart: 2, of which 1 were waited for; matrix products, arithmetic and copies ran while one was open for 70% of the time, Pallas kernels for 0%

commit v1 on v0

--- a/solution.py
+++ b/solution.py
@@ -1,8 +1,11 @@
+import functools
 import math
 
 import jax
 import jax.numpy as jnp
 from jax import lax
+from jax.experimental import pallas as pl
+from jax.experimental.pallas import tpu as pltpu
 from jax.sharding import PartitionSpec as P
 
 SRC = 16
@@ -27,12 +30,14 @@
 
 
 def decimation_matrix(fir_taps, out_rows, in_rows):
-    rows = jnp.arange(out_rows, dtype=jnp.int32)[:, None]
-    cols = jnp.arange(in_rows, dtype=jnp.int32)[None, :]
-    tap = cols - rows * STRIDE
-    inside = (tap >= 0) & (tap < TAPS)
-    picked = jnp.take(fir_taps, jnp.clip(tap, 0, TAPS - 1), mode="clip")
-    return jnp.where(inside, picked, 0.0)
+    rows = jnp.arange(out_rows, dtype=jnp.int32)[:, None, None]
+    groups = jnp.arange(in_rows // STRIDE, dtype=jnp.int32)[None, :, None]
+    lead = groups - rows
+    matrix = jnp.zeros((out_rows, in_rows // STRIDE, STRIDE), jnp.float32)
+    for lead_index in range(TAPS // STRIDE):
+        taps = fir_taps[lead_index * STRIDE : (lead_index + 1) * STRIDE][None, None, :]
+        matrix = matrix + jnp.where(lead == lead_index, taps, 0.0)
+    return matrix.reshape(out_rows, in_rows)
 
 
 def dft_table(samples, bins):
@@ -91,6 +96,47 @@
     return jnp.concatenate([real_part * factor, imag_part * factor], axis=1).astype(jnp.bfloat16)
 
 
+def correlate_kernel(factor, bins, white_ref, src_ref, cos_ref, sin_ref, out_ref):
+    step = pl.program_id(0)
+    row = src_ref[pl.ds(step, 1), :]
+    real_src = row[:, :bins]
+    imag_src = row[:, bins:]
+    cosine = cos_ref[...]
+    sine = sin_ref[...]
+    top = (cosine * real_src + sine * imag_src).astype(jnp.bfloat16)
+    bottom = (cosine * imag_src - sine * real_src).astype(jnp.bfloat16)
+    nt = (((1,), (1,)), ((), ()))
+    total = lax.dot_general(white_ref[:, :bins], top, nt, preferred_element_type=jnp.float32)
+    total = total + lax.dot_general(
+        white_ref[:, bins:], bottom, nt, preferred_element_type=jnp.float32
+    )
+    out_ref[0] = total * factor
+
+
+def correlate(receivers, sources, cosine_t, sine_t):
+    block, width = receivers.shape
+    bins = width // 2
+    count = sources.shape[0]
+    lags = cosine_t.shape[0]
+    factor = 1.0 / math.sqrt(bins)
+    flops = 2 * count * block * width * lags + 6 * count * bins * lags
+    moved = 2 * block * width + 4 * count * width + 8 * lags * bins + 4 * count * block * lags
+    return pl.pallas_call(
+        functools.partial(correlate_kernel, factor, bins),
+        out_shape=jax.ShapeDtypeStruct((count, block, lags), jnp.float32),
+        grid=(count,),
+        in_specs=[
+            pl.BlockSpec((block, width), lambda s: (0, 0)),
+            pl.BlockSpec((count, width), lambda s: (0, 0)),
+            pl.BlockSpec((lags, bins), lambda s: (0, 0)),
+            pl.BlockSpec((lags, bins), lambda s: (0, 0)),
+        ],
+        out_specs=pl.BlockSpec((1, block, lags), lambda s: (s, 0, 0)),
+        compiler_params=pltpu.CompilerParams(dimension_semantics=("arbitrary",)),
+        cost_estimate=pl.CostEstimate(flops=flops, bytes_accessed=moved, transcendentals=0),
+    )(receivers, sources, cosine_t, sine_t)
+
+
 def local(records, fir_taps, channel_map, source_owner, source_offset):
     n_chan = lax.axis_size("chan")
     n_tm = lax.axis_size("tm")
@@ -130,18 +176,11 @@
     receivers = white[:block]
     sources = white[block:].astype(jnp.float32)
     bins = samples // 2
-    real_src = sources[:, :bins][:, :, None]
-    imag_src = sources[:, bins:][:, :, None]
-
     lag_share = LAGS // n_tm
     kernel = lag_kernel(samples, lax.axis_index("tm") * lag_share, lag_share).astype(jnp.float32)
-    cosine = kernel[:bins][None]
-    sine = kernel[bins:][None]
-    mixed = jnp.concatenate(
-        [real_src * cosine + imag_src * sine, imag_src * cosine - real_src * sine], axis=1
-    ).astype(jnp.bfloat16)
-    factor = 1.0 / math.sqrt(bins)
-    result = jnp.einsum("jf,sfl->sjl", receivers, mixed, preferred_element_type=jnp.float32) * factor
+    cosine_t = kernel[:bins].T
+    sine_t = kernel[bins:].T
+    result = correlate(receivers, sources, cosine_t, sine_t)
     return result.reshape(STEPS, SRC, block, lag_share)
 
 

time: 287 us -> 85.5 us (0.30)
  local copies, waits for them, and re-layouts: 220 us -> 20 us
  Pallas kernels: 0 us -> 20.5 us
  matrix products: 23.3 us -> 7.8 us
  other arithmetic: 15.1 us -> 9.8 us
    gather x2 -> x0, local copies, waits for them, and re-layouts: 190 us -> none  [decimation_matrix(): picked = jnp.take(fir_taps, jnp.clip(tap, 0, TAPS - 1), mode='clip')]
    pallas_call x0 -> x1, Pallas kernels: none -> 20.5 us  [correlate(): pl.pallas_call(functools.partial(correlate_kernel, factor, bins), out_sha...]
    dot_general x1 -> x0, matrix products: 15.3 us -> none  [local(): jnp.einsum('jf,sfl->sjl', receivers, mixed, preferred_element_type=jnp.fl...]
    reshape x1 -> x0, local copies, waits for them, and re-layouts: 12.6 us -> none  [local(): return result.reshape(STEPS, SRC, block, lag_share)]
    another operation x2 -> x1, other arithmetic: 10.3 us -> 2.47 us
  transfers between devices with their start and end apart: 2 -> 2, of which waited for: 1 -> 1; matrix products, arithmetic and copies ran while one was open for 70% -> 18% of each run, Pallas kernels for 0% -> 0%
where the time goes in v1:
time: 85.5 us; the launch traced here: 84 us
  Pallas kernels  20.5 us (24%)
  local copies, waits for them, and re-layouts  20 us (23%)
  waiting for transfers between devices  16.1 us (19%)
  other arithmetic  9.8 us (11%)
  starting transfers between devices  9.41 us (11%)
  matrix products  7.8 us (9%)
    pallas_call x1, Pallas kernels, correlate(): pl.pallas_call(functools.partial(correlate_kernel, factor, bins), out_sha...  20.5 us
    all_to_all x1, waiting for transfers between devices, local(): series = lax.all_to_all(columns, ('chan', 'tm'), 1, 0, tiled=True)  16.1 us
    gather x1, local copies, waits for them, and re-layouts, local(): columns = jnp.take(decimated, index.reshape(-1), axis=1, mode='clip')  12.5 us
    all_to_all x1, starting transfers between devices, local(): series = lax.all_to_all(columns, ('chan', 'tm'), 1, 0, tiled=True)  8.12 us
    dot_general x1, matrix products, whiten_series(): lax.dot_general(series, jnp.concatenate([hi, lo], axis=1), dims, preferre...  3.59 us
    convert_element_type x4, other arithmetic, split_bf16(): piece = rest.astype(jnp.bfloat16)  2.76 us
    dot_general x1, matrix products, local(): jnp.dot(stacked[:, :raw_rows], records, preferred_element_type=jnp.float32)  2.71 us
    another operation x1, other arithmetic  2.47 us
  transfers between devices with their start and end apart: 2, of which 1 were waited for; matrix products, arithmetic and copies ran while one was open for 18% of the time, Pallas kernels for 0%

profile of v1, /device:TPU:0, one launch (start us, length us, event | category | flops | bytes accessed | tf_op | source)
XLA Modules:
  0.0 84.0 jit_solution(927490023826316685)
XLA Ops:
  0.0 0.9 %slice.60 = bf16[24,3072]{1,0:T(8,128)(2,1)S(1)} slice(bf16[512,3072]{1,0:T(8,128)(2,1)} %param.5), slice={[0:24], [0:3072]} | slice | bytes 294912 | tf_op jit(solution)/shard_map/slice | solution.py:151
  0.9 1.3 %collective-permute-start = (bf16[24,3072]{1,0:T(8,128)(2,1)S(1)}, bf16[24,3072]{1,0:T(8,128)(2,1)S(1)}, u32[]{:S(2)}, u32[]{:S(2)}) collective-permute-start(bf16[24,3072]{1,0:T(8,128)(2,1)S(1)} %slice.60), channel_id=1, source_target_pairs={{1,0},{2,1},{3,2},{4,3},{5,4},{6,5},{7,6},{8,7},{9,8},{10,9},{11,1... | collective-permute-start | bytes 442376 | tf_op jit(solution)/shard_map/ppermute | solution.py:151
  2.3 0.3 fusion.55
  2.6 0.7 multiply_add_fusion.1
  3.2 0.1 iota_add_fusion
  3.3 0.1 reshape.216
  3.4 0.9 %fusion.71 = (f32[8]{0:T(128)S(1)}, f32[8]{0:T(128)S(1)}, f32[8]{0:T(128)S(1)}, f32[8]{0:T(128)S(1)}) fusion(f32[32]{0:T(128)} %param.6), kind=kLoop, calls=%fused_computation.108 | loop fusion | bytes 256 | tf_op jit(solution)/shard_map/slice | solution.py:38
  4.3 0.7 broadcast_in_dim.136
  5.0 1.4 %gather_fusion = s32[32]{0:T(128)S(1)} fusion(s32[3072]{0:T(1024)} %param.7, s32[1024]{0:T(1024)S(1)} %pad_clamp_fusion.1), kind=kCustom, calls=%fused_computation | custom fusion | bytes 384 | tf_op jit(solution)/shard_map/jit(_take)/gather | solution.py:165
  6.5 0.1 reshape.224
  6.6 0.1 broadcast_in_dim.118
  6.7 0.1 broadcast_in_dim.124
  6.8 0.1 broadcast_in_dim.134
  6.9 0.1 broadcast_in_dim.129
  7.0 0.4 subtract_convert_fusion.2
  7.3 0.1 pad_maximum_fusion.1
  7.5 2.7 %fusion.35 = f32[192,3072]{1,0:T(8,128)S(1)} fusion(bf16[512,3072]{1,0:T(8,128)(2,1)} %param.5, bf16[192,536]{0,1:T(8,128)(2,1)S(1)} %pad_maximum_fusion.1), kind=kOutput, calls=%fused_computation.59 | convolution fusion | flops 603979776 | bytes 5767168 | tf_op jit(solution)/shard_map/dot_general | solution.py:156
  10.2 0.1 abs_compare_fusion
  10.3 0.0 collective-permute-done
  10.4 0.6 convolution_add_fusion
  10.9 0.1 fusion.26
  11.0 0.4 copy.7
  11.4 12.5 %gather_fusion.1 = bf16[6656,64]{1,0:T(8,128)(2,1)S(1)} fusion(bf16[64,3072]{0,1:T(8,128)(2,1)S(1)} %copy.7, s32[7168]{0:T(1024)S(1)} %pad_clamp_fusion), kind=kCustom, calls=%fused_computation.1 | custom fusion | bytes 1730560 | tf_op jit(solution)/shard_map/jit(_take)/gather | solution.py:172
  23.9 1.6 %copy.8 = bf16[64,16,416]{2,0,1:T(8,128)(2,1)} copy(bf16[64,16,416]{0,2,1:T(8,128)(2,1)S(1)} %bitcast.68) | data formatting | bytes 1703936 | tf_op jit(solution)/shard_map/all_to_all | solution.py:173
  25.5 8.1 %all-to-all-start = ((bf16[64,16,416]{2,0,1:T(8,128)(2,1)}), bf16[64,16,416]{2,0,1:T(8,128)(2,1)S(1)}, u32[]{:S(2)}, u32[]{:S(2)}) async-start(bf16[64,16,416]{2,0,1:T(8,128)(2,1)} %copy.8), calls=%async_computation | async-start | bytes 2097152 | tf_op jit(solution)/shard_map/all_to_all | solution.py:173
  33.7 2.5 %cosine_convert_fusion = (bf16[512,256]{0,1:T(8,128)(2,1)S(1)}, bf16[512,256]{0,1:T(8,128)(2,1)S(1)}) fusion(s32[256]{0:T(256)S(1)} %add_add_fusion), kind=kLoop, calls=%fused_computation.50 | loop fusion | flops 2228224 | bytes 525312 | tf_op jit(solution)/shard_map/convert.1
  36.1 0.1 maximum_convert_fusion
  36.3 0.3 fusion.58
  36.6 0.6 multiply_subtract_fusion
  37.2 0.6 subtract_convert_fusion
  37.8 1.6 %fusion.4 = bf16[1024,1024]{1,0:T(8,128)(2,1)} fusion(f32[1024,512]{1,0:T(8,128)S(1)} %bitcast.67, f32[1024,512]{1,0:T(8,128)S(1)} %bitcast.65), kind=kLoop, calls=%fused_computation.9 | loop fusion | flops 4194304 | bytes 6291456 | tf_op jit(solution)/shard_map/convert_element_type | solution.py:26
  39.4 1.1 %slice_bitcast_fusion = (f32[256,512]{1,0:T(8,128)}, f32[256,512]{1,0:T(8,128)}) fusion(f32[1024,256]{0,1:T(8,128)S(1)} %maximum_convert_fusion), kind=kLoop, calls=%fused_computation.46 | loop fusion | bytes 2097152 | tf_op jit(solution)/shard_map/transpose | solution.py:182
  40.5 16.1 %all-to-all-done = bf16[64,16,416]{2,0,1:T(8,128)(2,1)S(1)} async-done(((bf16[64,16,416]{2,0,1:T(8,128)(2,1)}), bf16[64,16,416]{2,0,1:T(8,128)(2,1)S(1)}, u32[]{:S(2)}, u32[]{:S(2)}) %all-to-all-start) | async-done | bytes 852000 | tf_op jit(solution)/shard_map/all_to_all | solution.py:173
  56.6 3.6 %fusion = f32[416,2048]{1,0:T(8,128)S(1)} fusion(bf16[1024,416]{1,0:T(8,128)(2,1)S(1)} %bitcast.69, bf16[1024,1024]{1,0:T(8,128)(2,1)S(1)} %subtract_convert_fusion, bf16[1024,1024]{1,0:T(8,128)(2,1)} %fusion.4), kind=kOutput, calls=%fused_computation.3 | convolution fusion | flops 1753219072 | bytes 8454144 | tf_op jit(solution)/shard_map/dot_general | solution.py:80
  60.2 0.4 slice_add_fusion
  60.6 0.3 fusion.68
  60.8 0.9 %multiply_convert_fusion = (bf16[416,512]{1,0:T(8,128)(2,1)S(1)}, bf16[416,512]{1,0:T(8,128)(2,1)S(1)}) fusion(f32[416,1024]{1,0:T(8,128)S(1)} %slice_add_fusion, pred[512,512]{1,0:T(32,128)(4,1)S(1)} %abs_compare_fusion, bf16[416,512]{1,0:T(8,128)(2,1)S(1)} %get-tuple-element.12, bf16[416,512]{1,0:T(8,128)(2,1)S(1)} %get-tuple-element.11, ...), kind=kOutput, calls=%fused_computation.30 | convolution fusion | flops 660996096 | bytes 4096000 | tf_op jit(solution)/shard_map/dot_general | solution.py:89
  61.8 0.7 fusion.44.src_ref
  62.4 1.0 %fusion.25.white_ref = bf16[384,1024]{1,0:T(8,128)(2,1)} fusion(bf16[416,512]{1,0:T(8,128)(2,1)S(1)} %get-tuple-element.9, bf16[416,512]{1,0:T(8,128)(2,1)S(1)} %get-tuple-element.8), kind=kLoop, calls=%fused_computation.35 | loop fusion | flops 1572864 | bytes 1638400 | tf_op jit(solution)/shard_map/concatenate | solution.py:96
  63.4 20.5 %shard_map.55 = f32[32,384,256]{2,1,0:T(8,128)} custom-call(bf16[384,1024]{1,0:T(8,128)(2,1)} %fusion.25.white_ref, f32[32,1024]{1,0:T(8,128)} %fusion.44.src_ref, f32[256,512]{1,0:T(8,128)} %get-tuple-element.14.cos_ref, f32[256,512]{1,0:T(8,128)} %get-tuple-element.13.sin_ref), custom_call_target="tpu_custom_call" | custom-call | flops 6467616768 | bytes 14548992 | tf_op jit(solution)/shard_map/pallas_call | solution.py:124
  (14 shorter events, 0.1 us)
Async XLA Ops:
  0.9 9.4 %collective-permute-start = (bf16[24,3072]{1,0:T(8,128)(2,1)S(1)}, bf16[24,3072]{1,0:T(8,128)(2,1)S(1)}, u32[]{:S(2)}, u32[]{:S(2)}) collective-permute-start(bf16[24,3072]{1,0:T(8,128)(2,1)S(1)} %slice.60), channel_id=1, source_target_pairs={{1,0},{2,1},{3,2},{4,3},{5,4},{6,5},{7,6},{8,7},{9,8},{10,9},{11,1... | collective-permute-start | bytes 442376 | tf_op jit(solution)/shard_map/ppermute | solution.py:151
  25.5 31.1 %all-to-all-start = ((bf16[64,16,416]{2,0,1:T(8,128)(2,1)}), bf16[64,16,416]{2,0,1:T(8,128)(2,1)S(1)}, u32[]{:S(2)}, u32[]{:S(2)}) async-start(bf16[64,16,416]{2,0,1:T(8,128)(2,1)} %copy.8), calls=%async_computation | async-start | bytes 2097152 | tf_op jit(solution)/shard_map/all_to_all | solution.py:173

commit v2 on v1

--- a/solution.py
+++ b/solution.py
@@ -72,14 +72,11 @@
 
 
 def whiten_series(series):
-    samples = series.shape[0]
+    samples = series.shape[1]
     bins = samples // 2
     table = dft_table(samples, bins)
     hi, lo = split_bf16(table, 2)
-    dims = (((0,), (0,)), ((), ()))
-    both = lax.dot_general(
-        series, jnp.concatenate([hi, lo], axis=1), dims, preferred_element_type=jnp.float32
-    )
+    both = jnp.dot(series, jnp.concatenate([hi, lo], axis=1), preferred_element_type=jnp.float32)
     spectrum = both[:, : 2 * bins] + both[:, 2 * bins :]
     real_part = spectrum[:, :bins]
     imag_part = spectrum[:, bins:]
@@ -96,56 +93,64 @@
     return jnp.concatenate([real_part * factor, imag_part * factor], axis=1).astype(jnp.bfloat16)
 
 
-def correlate_kernel(factor, bins, white_ref, src_ref, cos_ref, sin_ref, out_ref):
-    step = pl.program_id(0)
-    row = src_ref[pl.ds(step, 1), :]
-    real_src = row[:, :bins]
-    imag_src = row[:, bins:]
+def correlate_kernel(factor, bins, group, white_ref, src_ref, cos_ref, sin_ref, out_ref):
     cosine = cos_ref[...]
     sine = sin_ref[...]
-    top = (cosine * real_src + sine * imag_src).astype(jnp.bfloat16)
-    bottom = (cosine * imag_src - sine * real_src).astype(jnp.bfloat16)
-    nt = (((1,), (1,)), ((), ()))
-    total = lax.dot_general(white_ref[:, :bins], top, nt, preferred_element_type=jnp.float32)
-    total = total + lax.dot_general(
-        white_ref[:, bins:], bottom, nt, preferred_element_type=jnp.float32
-    )
-    out_ref[0] = total * factor
-
-
-def correlate(receivers, sources, cosine_t, sine_t):
+    for k in range(group):
+        real_src = src_ref[0, :bins, k : k + 1]
+        imag_src = src_ref[0, bins:, k : k + 1]
+        top = (cosine * real_src + sine * imag_src).astype(jnp.bfloat16)
+        bottom = (cosine * imag_src - sine * real_src).astype(jnp.bfloat16)
+        total = jnp.dot(white_ref[:, :bins], top, preferred_element_type=jnp.float32)
+        total = total + jnp.dot(white_ref[:, bins:], bottom, preferred_element_type=jnp.float32)
+        out_ref[k] = total * factor
+
+
+def correlate(receivers, sources, cosine, sine):
     block, width = receivers.shape
     bins = width // 2
     count = sources.shape[0]
-    lags = cosine_t.shape[0]
+    lags = cosine.shape[1]
+    group = 8
+    grouped = sources.reshape(count // group, group, width).transpose(0, 2, 1)
     factor = 1.0 / math.sqrt(bins)
     flops = 2 * count * block * width * lags + 6 * count * bins * lags
     moved = 2 * block * width + 4 * count * width + 8 * lags * bins + 4 * count * block * lags
     return pl.pallas_call(
-        functools.partial(correlate_kernel, factor, bins),
+        functools.partial(correlate_kernel, factor, bins, group),
         out_shape=jax.ShapeDtypeStruct((count, block, lags), jnp.float32),
-        grid=(count,),
+        grid=(count // group,),
         in_specs=[
             pl.BlockSpec((block, width), lambda s: (0, 0)),
-            pl.BlockSpec((count, width), lambda s: (0, 0)),
-            pl.BlockSpec((lags, bins), lambda s: (0, 0)),
-            pl.BlockSpec((lags, bins), lambda s: (0, 0)),
+            pl.BlockSpec((1, width, group), lambda s: (s, 0, 0)),
+            pl.BlockSpec((bins, lags), lambda s: (0, 0)),
+            pl.BlockSpec((bins, lags), lambda s: (0, 0)),
         ],
-        out_specs=pl.BlockSpec((1, block, lags), lambda s: (s, 0, 0)),
+        out_specs=pl.BlockSpec((group, block, lags), lambda s: (s, 0, 0)),
         compiler_params=pltpu.CompilerParams(dimension_semantics=("arbitrary",)),
         cost_estimate=pl.CostEstimate(flops=flops, bytes_accessed=moved, transcendentals=0),
-    )(receivers, sources, cosine_t, sine_t)
+    )(receivers, grouped, cosine, sine)
+
+
+def swap_tm(x):
+    other = lax.ppermute(x, "tm", perm=[(0, 1), (1, 0)])
+    first = lax.axis_index("tm") == 0
+    return jnp.where(first, x, other), jnp.where(first, other, x)
 
 
 def local(records, fir_taps, channel_map, source_owner, source_offset):
     n_chan = lax.axis_size("chan")
     n_tm = lax.axis_size("tm")
+    assert n_tm == 2
     n_dev = n_chan * n_tm
     raw_rows, channels = records.shape
     block = channels // n_chan
+    half = block // n_tm
     out_rows = raw_rows // STRIDE
     halo_rows = TAPS - STRIDE
     samples = out_rows * n_dev
+    bins = samples // 2
+    tm = lax.axis_index("tm")
 
     shift = [(b, b - 1) for b in range(1, n_dev)]
     halo = lax.ppermute(records[:halo_rows], ("chan", "tm"), perm=shift)
@@ -153,34 +158,37 @@
     taps_matrix = decimation_matrix(fir_taps, out_rows, raw_rows + halo_rows)
     parts = split_bf16(taps_matrix, 3)
     stacked = jnp.concatenate(parts, axis=0)
-    main = jnp.dot(stacked[:, :raw_rows], records, preferred_element_type=jnp.float32)
-    tail = jnp.dot(stacked[:, raw_rows:], halo, preferred_element_type=jnp.float32)
+    dims = (((0,), (1,)), ((), ()))
+    main = lax.dot_general(records, stacked[:, :raw_rows], dims, preferred_element_type=jnp.float32)
+    tail = lax.dot_general(halo, stacked[:, raw_rows:], dims, preferred_element_type=jnp.float32)
     summed = main + tail
     decimated = (
-        summed[:out_rows] + summed[out_rows : 2 * out_rows] + summed[2 * out_rows :]
+        summed[:, :out_rows] + summed[:, out_rows : 2 * out_rows] + summed[:, 2 * out_rows :]
     ).astype(jnp.bfloat16)
 
+    first, second = swap_tm(decimated)
+    paired = jnp.concatenate([first, second], axis=1)
+
     first_rows = source_owner * block + source_offset
-    picked = (first_rows[:, None] + jnp.arange(SRC, dtype=jnp.int32)[None, :]).reshape(-1)
-    source_raw = jnp.take(channel_map, picked, mode="clip")
-    block_raw = channel_map.reshape(n_chan, 1, block)
-    block_raw = jnp.broadcast_to(block_raw, (n_chan, n_tm, block)).reshape(n_dev, block)
+    own_first = lax.dynamic_index_in_dim(first_rows, tm, keepdims=False)
+    source_raw = jnp.take(channel_map, own_first + jnp.arange(SRC, dtype=jnp.int32), mode="clip")
+    halves = channel_map.reshape(n_chan, n_tm, half)
+    half_raw = lax.dynamic_index_in_dim(halves, tm, axis=1, keepdims=False)
     index = jnp.concatenate(
-        [block_raw, jnp.broadcast_to(source_raw[None], (n_dev, source_raw.shape[0]))], axis=1
+        [half_raw, jnp.broadcast_to(source_raw[None], (n_chan, SRC))], axis=1
     )
     width = index.shape[1]
-    columns = jnp.take(decimated, index.reshape(-1), axis=1, mode="clip")
-    series = lax.all_to_all(columns, ("chan", "tm"), 1, 0, tiled=True)
+    rows = jnp.take(paired, index.reshape(-1), axis=0, mode="clip").reshape(n_chan, width, -1)
+    series = lax.all_to_all(rows, "chan", 0, 2, tiled=True).reshape(width, samples)
 
     white = whiten_series(series)
-    receivers = white[:block]
-    sources = white[block:].astype(jnp.float32)
-    bins = samples // 2
+    low, high = swap_tm(white)
+    receivers = jnp.concatenate([low[:half], high[:half]], axis=0)
+    sources = jnp.concatenate([low[half:], high[half:]], axis=0).astype(jnp.float32)
+
     lag_share = LAGS // n_tm
-    kernel = lag_kernel(samples, lax.axis_index("tm") * lag_share, lag_share).astype(jnp.float32)
-    cosine_t = kernel[:bins].T
-    sine_t = kernel[bins:].T
-    result = correlate(receivers, sources, cosine_t, sine_t)
+    kernel = lag_kernel(samples, tm * lag_share, lag_share).astype(jnp.float32)
+    result = correlate(receivers, sources, kernel[:bins], kernel[bins:])
     return result.reshape(STEPS, SRC, block, lag_share)
 
 

time: 85.5 us -> 65.9 us (0.77); the launches traced: 84 us -> 65.4 us
  Pallas kernels: 20.5 us -> 14.3 us
  local copies, waits for them, and re-layouts: 20 us -> 13.9 us
  waiting for transfers between devices: 16.1 us -> 10.3 us
  matrix products: 7.8 us -> 6.51 us
    gather x2, local copies, waits for them, and re-layouts: 13.9 us -> 5.95 us  [the longest x1 4.58 us: local(): jnp.take(paired, index.reshape(-1), axis=0, mode='clip')]
    pallas_call x1, Pallas kernels: 20.5 us -> 14.3 us  [correlate(): pl.pallas_call(functools.partial(correlate_kernel, factor, bins, group),...]
    all_to_all x1, waiting for transfers between devices: 16.1 us -> 10.1 us  [local(): lax.all_to_all(rows, 'chan', 0, 2, tiled=True).reshape(width, samples)]
    all_to_all x1, local copies, waits for them, and re-layouts: 1.59 us -> 0.11 us  [local(): lax.all_to_all(rows, 'chan', 0, 2, tiled=True).reshape(width, samples)]
    ppermute x0 -> x2, starting transfers between devices: none -> 1.26 us  [swap_tm(): other = lax.ppermute(x, 'tm', perm=[(0, 1), (1, 0)])]
    slice x0 -> x5, local copies, waits for them, and re-layouts: none -> 1.11 us  [the longest x1 1.04 us: local(): result = correlate(receivers, sources, kernel[:bins], kernel[bins:])]
    concatenate x1 -> x3, other arithmetic: 0.01 us -> 1.01 us  [the longest x1 0.94 us: local(): receivers = jnp.concatenate([low[:half], high[:half]], axis=0)]
    concatenate x1, other arithmetic: 1.01 us -> 0.04 us  [whiten_series(): jnp.concatenate([real_part * factor, imag_part * factor], axis=1)]
  transfers between devices with their start and end apart: 2 -> 4, of which waited for: 1 -> 2; matrix products, arithmetic and copies ran while one was open for 18% -> 25% of each run, Pallas kernels for 0% -> 0%
where the time goes in v2:
time: 65.9 us; the launch traced here: 65.4 us
  Pallas kernels  14.3 us (22%)
  local copies, waits for them, and re-layouts  13.9 us (21%)
  waiting for transfers between devices  10.3 us (16%)
  other arithmetic  10.1 us (15%)
  starting transfers between devices  9.85 us (15%)
  matrix products  6.51 us (10%)
    pallas_call x1, Pallas kernels, correlate(): pl.pallas_call(functools.partial(correlate_kernel, factor, bins, group),...  14.3 us
    all_to_all x1, waiting for transfers between devices, local(): lax.all_to_all(rows, 'chan', 0, 2, tiled=True).reshape(width, samples)  10.1 us
    all_to_all x1, starting transfers between devices, local(): lax.all_to_all(rows, 'chan', 0, 2, tiled=True).reshape(width, samples)  7.3 us
    gather x1, local copies, waits for them, and re-layouts, local(): jnp.take(paired, index.reshape(-1), axis=0, mode='clip')  4.58 us
    dot_general x1, matrix products, local(): lax.dot_general(records, stacked[:, :raw_rows], dims, preferred_element_t...  2.71 us
    dot_general x1, matrix products, whiten_series(): jnp.dot(series, jnp.concatenate([hi, lo], axis=1), preferred_element_type...  2.64 us
    convert_element_type x4, other arithmetic, split_bf16(): piece = rest.astype(jnp.bfloat16)  2.63 us
    another operation x1, other arithmetic  2.23 us
  transfers between devices with their start and end apart: 4, of which 2 were waited for; matrix products, arithmetic and copies ran while one was open for 25% of the time, Pallas kernels for 0%

profile of v2, /device:TPU:0, one launch (start us, length us, event | category | flops | bytes accessed | tf_op | source)
XLA Modules:
  0.0 65.4 jit_solution(17522102985448923682)
XLA Ops:
  0.0 0.9 %slice.66 = bf16[24,3072]{1,0:T(8,128)(2,1)S(1)} slice(bf16[512,3072]{1,0:T(8,128)(2,1)} %param.5), slice={[0:24], [0:3072]} | slice | bytes 294912 | tf_op jit(solution)/shard_map/slice | solution.py:156
  0.9 1.3 %collective-permute-start = (bf16[24,3072]{1,0:T(8,128)(2,1)S(1)}, bf16[24,3072]{1,0:T(8,128)(2,1)S(1)}, u32[]{:S(2)}, u32[]{:S(2)}) collective-permute-start(bf16[24,3072]{1,0:T(8,128)(2,1)S(1)} %slice.66), channel_id=1, source_target_pairs={{1,0},{2,1},{3,2},{4,3},{5,4},{6,5},{7,6},{8,7},{9,8},{10,9},{11,1... | collective-permute-start | bytes 442376 | tf_op jit(solution)/shard_map/ppermute | solution.py:156
  2.3 0.7 %multiply_add_fusion.1 = s32[2]{0:T(128)S(1)} fusion(s32[2]{0:T(128)} %param.9, s32[2]{0:T(128)} %param.8), kind=kLoop, calls=%fused_computation.108 | loop fusion | flops 4 | bytes 24 | tf_op jit(solution)/shard_map/add | solution.py:172
  3.0 0.6 dynamic_slice.9
  3.5 0.6 add_bitcast_fusion
  4.2 0.9 %fusion.74 = (f32[8]{0:T(128)S(1)}, f32[8]{0:T(128)S(1)}, f32[8]{0:T(128)S(1)}, f32[8]{0:T(128)S(1)}) fusion(f32[32]{0:T(128)} %param.6), kind=kLoop, calls=%fused_computation.116 | loop fusion | bytes 256 | tf_op jit(solution)/shard_map/slice | solution.py:38
  5.1 0.8 %reshape.200 = s32[8,2,192]{2,1,0:T(2,128)S(1)} reshape(s32[3072]{0:T(1024)} %param.7) | data formatting | bytes 24576 | tf_op jit(solution)/shard_map/reshape | solution.py:175
  5.9 1.4 %gather_fusion = s32[16]{0:T(128)S(1)} fusion(s32[3072]{0:T(1024)} %param.7, s32[1024]{0:T(1024)S(1)} %pad_clamp_fusion.1), kind=kCustom, calls=%fused_computation | custom fusion | bytes 192 | tf_op jit(solution)/shard_map/jit(_take)/gather | solution.py:174
  7.2 0.1 pad.19.clone
  7.4 0.1 reshape.215
  7.5 0.1 broadcast_in_dim.109
  7.6 0.1 broadcast_in_dim.115
  7.7 0.1 broadcast_in_dim.125
  7.8 0.1 broadcast_in_dim.120
  7.8 0.4 subtract_convert_fusion.2
  8.2 0.1 pad_maximum_fusion.4
  8.4 2.7 %fusion.37 = f32[192,3072]{1,0:T(8,128)S(1)} fusion(bf16[512,3072]{1,0:T(8,128)(2,1)} %param.5, bf16[192,536]{0,1:T(8,128)(2,1)S(1)} %pad_maximum_fusion.4), kind=kOutput, calls=%fused_computation.64 | convolution fusion | flops 603979776 | bytes 5767168 | tf_op jit(solution)/shard_map/dot_general | solution.py:162
  11.1 0.3 fusion.57
  11.4 0.6 fusion.4
  12.0 0.1 fusion.21
  12.1 1.2 %collective-permute-start.1 = (bf16[3072,64]{0,1:T(8,128)(2,1)S(1)}, bf16[3072,64]{0,1:T(8,128)(2,1)S(1)}, u32[]{:S(2)}, u32[]{:S(2)}) collective-permute-start(bf16[3072,64]{0,1:T(8,128)(2,1)S(1)} %fusion.21), channel_id=1, source_target_pairs={{0,1},{1,0},{2,3},{3,2},{4,5},{5,4},{6,7},{7,6},{8,9},{9,8},{10,11... | collective-permute-start | bytes 1179656 | tf_op jit(solution)/shard_map/ppermute | solution.py:136
  13.3 0.8 %abs_compare_fusion = pred[512,512]{1,0:T(32,128)(4,1)} fusion(), kind=kLoop, calls=%fused_computation.22 | loop fusion | flops 786432 | bytes 262144 | tf_op jit(solution)/shard_map/le | solution.py:61
  14.1 0.3 fusion.60
  14.4 0.2 collective-permute-done.1
  14.6 0.2 broadcast_select_fusion.3
  14.8 0.1 pad_maximum_fusion.1
  14.9 0.4 copy.10
  15.2 4.6 %gather_fusion.1 = bf16[1664,128]{1,0:T(8,128)(2,1)} fusion(bf16[3072,128]{1,0:T(8,128)(2,1)S(1)} %copy.10, s32[2048]{0:T(1024)S(1)} %pad_clamp_fusion), kind=kCustom, calls=%fused_computation.1 | custom fusion | bytes 858624 | tf_op jit(solution)/shard_map/jit(_take)/gather | solution.py:181
  19.8 7.3 %all-to-all-start = ((bf16[8,208,128]{2,1,0:T(8,128)(2,1)}), bf16[8,208,128]{2,1,0:T(8,128)(2,1)S(1)}, u32[]{:S(2)}, u32[]{:S(2)}) async-start(bf16[8,208,128]{2,1,0:T(8,128)(2,1)} %bitcast.7), calls=%async_computation | async-start | bytes 851968 | tf_op jit(solution)/shard_map/all_to_all | solution.py:182
  27.1 0.6 multiply_subtract_fusion
  27.7 0.6 subtract_convert_fusion
  28.3 1.6 %fusion.5 = bf16[1024,1024]{1,0:T(8,128)(2,1)} fusion(f32[1024,512]{1,0:T(8,128)S(1)} %bitcast.79, f32[1024,512]{1,0:T(8,128)S(1)} %bitcast.77), kind=kLoop, calls=%fused_computation.10 | loop fusion | flops 4194304 | bytes 6291456 | tf_op jit(solution)/shard_map/convert_element_type | solution.py:26
  29.9 10.1 %all-to-all-done = bf16[8,208,128]{2,1,0:T(8,128)(2,1)S(1)} async-done(((bf16[8,208,128]{2,1,0:T(8,128)(2,1)}), bf16[8,208,128]{2,1,0:T(8,128)(2,1)S(1)}, u32[]{:S(2)}, u32[]{:S(2)}) %all-to-all-start) | async-done | bytes 426016 | tf_op jit(solution)/shard_map/all_to_all | solution.py:182
  40.0 0.1 copy.11
  40.1 2.6 %fusion = f32[208,2048]{1,0:T(8,128)S(1)} fusion(bf16[1024,1024]{1,0:T(8,128)(2,1)S(1)} %subtract_convert_fusion, bf16[1024,1024]{1,0:T(8,128)(2,1)} %fusion.5, bf16[26,8,8,128]{3,2,1,0:T(8,128)(2,1)S(1)} %bitcast.82), kind=kOutput, calls=%fused_computation.3 | convolution fusion | flops 880803840 | bytes 6324224 | tf_op jit(solution)/shard_map/dot_general | solution.py:79
  42.8 0.1 slice_add_fusion
  42.9 0.1 fusion.70
  43.0 0.7 %copy-done = pred[512,512]{1,0:T(32,128)(4,1)S(1)} copy-done((pred[512,512]{1,0:T(32,128)(4,1)S(1)}, pred[512,512]{1,0:T(32,128)(4,1)}, u32[]{:S(2)}) %copy-start) | copy-done | bytes 262168
  43.7 0.6 multiply_convert_fusion.1
  44.4 0.1 collective-permute-start.2
  44.5 2.2 %cosine_convert_fusion = (bf16[512,256]{1,0:T(8,128)(2,1)S(1)}, bf16[512,256]{1,0:T(8,128)(2,1)S(1)}) fusion(s32[256]{0:T(256)S(1)} %add_add_fusion), kind=kLoop, calls=%fused_computation.42 | loop fusion | flops 2228224 | bytes 525312 | tf_op jit(solution)/shard_map/convert.3
  46.7 0.1 maximum_convert_fusion
  46.8 1.0 %fusion.73 = (f32[512,256]{1,0:T(8,128)}, f32[512,256]{1,0:T(8,128)}) fusion(f32[1024,256]{1,0:T(8,128)S(1)} %maximum_convert_fusion), kind=kLoop, calls=%fused_computation.115 | loop fusion | bytes 2097152 | tf_op jit(solution)/shard_map/slice | solution.py:191
  47.8 0.0 collective-permute-done.2
  47.8 0.2 broadcast_select_fusion.1
  48.2 1.9 %copy.12 = f32[4,8,1024]{1,2,0:T(8,128)} copy(f32[4,8,1024]{2,1,0:T(8,128)S(1)} %fusion.46) | data formatting | bytes 262144 | tf_op jit(solution)/shard_map/transpose | solution.py:115
  50.1 0.9 %pad_maximum_fusion.2.white_ref = bf16[384,1024]{1,0:T(8,128)(2,1)} fusion(bf16[192,1024]{1,0:T(8,128)(2,1)S(1)} %slice.93, bf16[192,1024]{1,0:T(8,128)(2,1)S(1)} %slice.92), kind=kLoop, calls=%fused_computation.28 | loop fusion | flops 1572864 | bytes 1572864 | tf_op jit(solution)/shard_map/concatenate | solution.py:186
  51.0 14.3 %shard_map.55 = f32[32,384,256]{2,1,0:T(8,128)} custom-call(bf16[384,1024]{1,0:T(8,128)(2,1)} %pad_maximum_fusion.2.white_ref, f32[4,1024,8]{2,1,0:T(8,128)} %bitcast.80, f32[512,256]{1,0:T(8,128)} %get-tuple-element.11.cos_ref, f32[512,256]{1,0:T(8,128)} %get-tuple-element.10.sin_ref), custom_call_target="tpu_custom_call" | custom-call | flops 6467616768 | bytes 14548992 | tf_op jit(solution)/shard_map/pallas_call | solution.py:119
  (21 shorter events, 0.2 us)
Async XLA Ops:
  0.9 10.4 %collective-permute-start = (bf16[24,3072]{1,0:T(8,128)(2,1)S(1)}, bf16[24,3072]{1,0:T(8,128)(2,1)S(1)}, u32[]{:S(2)}, u32[]{:S(2)}) collective-permute-start(bf16[24,3072]{1,0:T(8,128)(2,1)S(1)} %slice.66), channel_id=1, source_target_pairs={{1,0},{2,1},{3,2},{4,3},{5,4},{6,5},{7,6},{8,7},{9,8},{10,9},{11,1... | collective-permute-start | bytes 442376 | tf_op jit(solution)/shard_map/ppermute | solution.py:156
  12.1 2.5 %collective-permute-start.1 = (bf16[3072,64]{0,1:T(8,128)(2,1)S(1)}, bf16[3072,64]{0,1:T(8,128)(2,1)S(1)}, u32[]{:S(2)}, u32[]{:S(2)}) collective-permute-start(bf16[3072,64]{0,1:T(8,128)(2,1)S(1)} %fusion.21), channel_id=1, source_target_pairs={{0,1},{1,0},{2,3},{3,2},{4,5},{5,4},{6,7},{7,6},{8,9},{9,8},{10,11... | collective-permute-start | bytes 1179656 | tf_op jit(solution)/shard_map/ppermute | solution.py:136
  19.8 20.2 %all-to-all-start = ((bf16[8,208,128]{2,1,0:T(8,128)(2,1)}), bf16[8,208,128]{2,1,0:T(8,128)(2,1)S(1)}, u32[]{:S(2)}, u32[]{:S(2)}) async-start(bf16[8,208,128]{2,1,0:T(8,128)(2,1)} %bitcast.7), calls=%async_computation | async-start | bytes 851968 | tf_op jit(solution)/shard_map/all_to_all | solution.py:182
  42.8 1.0 %copy-start = (pred[512,512]{1,0:T(32,128)(4,1)S(1)}, pred[512,512]{1,0:T(32,128)(4,1)}, u32[]{:S(2)}) copy-start(pred[512,512]{1,0:T(32,128)(4,1)} %abs_compare_fusion) | copy-start | bytes 786436
  44.4 3.4 %collective-permute-start.2 = (bf16[208,1024]{1,0:T(8,128)(2,1)S(1)}, bf16[208,1024]{1,0:T(8,128)(2,1)S(1)}, u32[]{:S(2)}, u32[]{:S(2)}) collective-permute-start(bf16[208,1024]{1,0:T(8,128)(2,1)S(1)} %pad_maximum_fusion.3), channel_id=1, source_target_pairs={{0,1},{1,0},{2,3},{3,2},{4,5},{5,4},{6,7},{7,6},{8,9},{9,8},{10,11... | collective-permute-start | bytes 1277960 | tf_op jit(solution)/shard_map/ppermute | solution.py:136

commit v3 on v2

--- a/solution.py
+++ b/solution.py
@@ -40,12 +40,12 @@
     return matrix.reshape(out_rows, in_rows)
 
 
-def dft_table(samples, bins):
+def dft_table(samples, bins, time_index):
     inner = 32
     outer = samples // inner
     frequency = jnp.arange(bins, dtype=jnp.int32)[None, :]
     low = jnp.arange(inner, dtype=jnp.int32)[:, None]
-    high = jnp.arange(outer, dtype=jnp.int32)[:, None] * inner
+    high = time_index.reshape(outer, inner)[:, :1]
     scale = two_pi / samples
     low_angle = ((low * frequency) % samples).astype(jnp.float32) * scale
     high_angle = ((high * frequency) % samples).astype(jnp.float32) * scale
@@ -71,10 +71,10 @@
     return jnp.concatenate([jnp.cos(angles), -jnp.sin(angles)], axis=0).astype(jnp.bfloat16)
 
 
-def whiten_series(series):
+def whiten_series(series, time_index):
     samples = series.shape[1]
     bins = samples // 2
-    table = dft_table(samples, bins)
+    table = dft_table(samples, bins, time_index)
     hi, lo = split_bf16(table, 2)
     both = jnp.dot(series, jnp.concatenate([hi, lo], axis=1), preferred_element_type=jnp.float32)
     spectrum = both[:, : 2 * bins] + both[:, 2 * bins :]
@@ -96,9 +96,16 @@
 def correlate_kernel(factor, bins, group, white_ref, src_ref, cos_ref, sin_ref, out_ref):
     cosine = cos_ref[...]
     sine = sin_ref[...]
+    count = src_ref.shape[1]
+    lags = cosine.shape[1]
+    lanes = 128
+    which = lax.broadcasted_iota(jnp.int32, (count, lanes), 0)
     for k in range(group):
-        real_src = src_ref[0, :bins, k : k + 1]
-        imag_src = src_ref[0, bins:, k : k + 1]
+        pick = (which == pl.program_id(0) * group + k).astype(jnp.bfloat16)
+        real_src = jnp.dot(src_ref[:bins, :], pick, preferred_element_type=jnp.float32)
+        imag_src = jnp.dot(src_ref[bins:, :], pick, preferred_element_type=jnp.float32)
+        real_src = jnp.concatenate([real_src] * (lags // lanes), axis=1)
+        imag_src = jnp.concatenate([imag_src] * (lags // lanes), axis=1)
         top = (cosine * real_src + sine * imag_src).astype(jnp.bfloat16)
         bottom = (cosine * imag_src - sine * real_src).astype(jnp.bfloat16)
         total = jnp.dot(white_ref[:, :bins], top, preferred_element_type=jnp.float32)
@@ -112,24 +119,24 @@
     count = sources.shape[0]
     lags = cosine.shape[1]
     group = 8
-    grouped = sources.reshape(count // group, group, width).transpose(0, 2, 1)
+    columns = sources.T
     factor = 1.0 / math.sqrt(bins)
     flops = 2 * count * block * width * lags + 6 * count * bins * lags
-    moved = 2 * block * width + 4 * count * width + 8 * lags * bins + 4 * count * block * lags
+    moved = 2 * block * width + 2 * count * width + 8 * lags * bins + 4 * count * block * lags
     return pl.pallas_call(
         functools.partial(correlate_kernel, factor, bins, group),
         out_shape=jax.ShapeDtypeStruct((count, block, lags), jnp.float32),
         grid=(count // group,),
         in_specs=[
             pl.BlockSpec((block, width), lambda s: (0, 0)),
-            pl.BlockSpec((1, width, group), lambda s: (s, 0, 0)),
+            pl.BlockSpec((width, count), lambda s: (0, 0)),
             pl.BlockSpec((bins, lags), lambda s: (0, 0)),
             pl.BlockSpec((bins, lags), lambda s: (0, 0)),
         ],
         out_specs=pl.BlockSpec((group, block, lags), lambda s: (s, 0, 0)),
         compiler_params=pltpu.CompilerParams(dimension_semantics=("arbitrary",)),
         cost_estimate=pl.CostEstimate(flops=flops, bytes_accessed=moved, transcendentals=0),
-    )(receivers, grouped, cosine, sine)
+    )(receivers, columns, cosine, sine)
 
 
 def swap_tm(x):
@@ -171,7 +178,7 @@
 
     first_rows = source_owner * block + source_offset
     own_first = lax.dynamic_index_in_dim(first_rows, tm, keepdims=False)
-    source_raw = jnp.take(channel_map, own_first + jnp.arange(SRC, dtype=jnp.int32), mode="clip")
+    source_raw = lax.dynamic_slice_in_dim(channel_map, own_first, SRC)
     halves = channel_map.reshape(n_chan, n_tm, half)
     half_raw = lax.dynamic_index_in_dim(halves, tm, axis=1, keepdims=False)
     index = jnp.concatenate(
@@ -179,12 +186,21 @@
     )
     width = index.shape[1]
     rows = jnp.take(paired, index.reshape(-1), axis=0, mode="clip").reshape(n_chan, width, -1)
-    series = lax.all_to_all(rows, "chan", 0, 2, tiled=True).reshape(width, samples)
-
-    white = whiten_series(series)
+    chip = lax.axis_index("chan")
+    arrived = [lax.dynamic_index_in_dim(rows, chip, keepdims=False)]
+    for k in range(1, n_chan):
+        outgoing = lax.dynamic_index_in_dim(rows, (chip + k) % n_chan, keepdims=False)
+        perm = [(c, (c + k) % n_chan) for c in range(n_chan)]
+        arrived.append(lax.ppermute(outgoing, "chan", perm=perm))
+    series = jnp.concatenate(arrived, axis=1)
+    chunk = 2 * out_rows
+    origin = (chip - jnp.arange(n_chan, dtype=jnp.int32)) % n_chan
+    time_index = (origin[:, None] * chunk + jnp.arange(chunk, dtype=jnp.int32)[None, :]).reshape(-1)
+
+    white = whiten_series(series, time_index)
     low, high = swap_tm(white)
     receivers = jnp.concatenate([low[:half], high[:half]], axis=0)
-    sources = jnp.concatenate([low[half:], high[half:]], axis=0).astype(jnp.float32)
+    sources = jnp.concatenate([low[half:], high[half:]], axis=0)
 
     lag_share = LAGS // n_tm
     kernel = lag_kernel(samples, tm * lag_share, lag_share).astype(jnp.float32)

time: 65.9 us -> 78.9 us (1.20)
  starting transfers between devices: 9.85 us -> 14.2 us
  matrix products: 6.51 us -> 9.59 us
  other arithmetic: 10.1 us -> 12.4 us
  between operations: 0.34 us -> 2.39 us
  local copies, waits for them, and re-layouts: 13.9 us -> 12 us
  Pallas kernels: 14.3 us -> 16 us
  waiting for transfers between devices: 10.3 us -> 11.8 us
    ppermute x0 -> x7, waiting for transfers between devices: none -> 11.8 us  [local(): arrived.append(lax.ppermute(outgoing, 'chan', perm=perm))]
    ppermute x0 -> x7, starting transfers between devices: none -> 11.7 us  [local(): arrived.append(lax.ppermute(outgoing, 'chan', perm=perm))]
    all_to_all x1 -> x0, waiting for transfers between devices: 10.1 us -> none  [local(): lax.all_to_all(rows, 'chan', 0, 2, tiled=True).reshape(width, samples)]
    all_to_all x1 -> x0, starting transfers between devices: 7.3 us -> none  [local(): lax.all_to_all(rows, 'chan', 0, 2, tiled=True).reshape(width, samples)]
    transpose x1 -> x0, local copies, waits for them, and re-layouts: 1.95 us -> none  [correlate(): grouped = sources.reshape(count // group, group, width).transpose(0, 2, 1)]
    dot_general x1, matrix products: 0.57 us -> 2.24 us  [local(): lax.dot_general(halo, stacked[:, raw_rows:], dims, preferred_element_type...]
    pallas_call x1, Pallas kernels: 14.3 us -> 16 us  [correlate(): pl.pallas_call(functools.partial(correlate_kernel, factor, bins, group),...]
    dot_general x1, matrix products: 2.71 us -> 4.12 us  [local(): lax.dot_general(records, stacked[:, :raw_rows], dims, preferred_element_t...]
  transfers between devices with their start and end apart: 4 -> 10, of which waited for: 2 -> 2; matrix products, arithmetic and copies ran while one was open for 25% -> 25% of each run, Pallas kernels for 0% -> 0%
where the time goes in v3:
time: 78.9 us; the launch traced here: 78.4 us
  Pallas kernels  16 us (20%)
  starting transfers between devices  14.2 us (18%)
  other arithmetic  12.4 us (16%)
  local copies, waits for them, and re-layouts  12 us (15%)
  waiting for transfers between devices  11.8 us (15%)
  matrix products  9.59 us (12%)
  between operations  2.39 us (3%)
    pallas_call x1, Pallas kernels, correlate(): pl.pallas_call(functools.partial(correlate_kernel, factor, bins, group),...  16 us
    ppermute x7, waiting for transfers between devices, local(): arrived.append(lax.ppermute(outgoing, 'chan', perm=perm))  11.8 us
    ppermute x7, starting transfers between devices, local(): arrived.append(lax.ppermute(outgoing, 'chan', perm=perm))  11.7 us
    dot_general x1, matrix products, local(): lax.dot_general(records, stacked[:, :raw_rows], dims, preferred_element_t...  4.12 us
    convert_element_type x4, other arithmetic, split_bf16(): piece = rest.astype(jnp.bfloat16)  3.98 us
    gather x1, local copies, waits for them, and re-layouts, local(): jnp.take(paired, index.reshape(-1), axis=0, mode='clip')  3.88 us
    dot_general x1, matrix products, whiten_series(): jnp.dot(series, jnp.concatenate([hi, lo], axis=1), preferred_element_type...  2.65 us
    dot_general x1, matrix products, local(): lax.dot_general(halo, stacked[:, raw_rows:], dims, preferred_element_type...  2.24 us
  transfers between devices with their start and end apart: 10, of which 2 were waited for; matrix products, arithmetic and copies ran while one was open for 25% of the time, Pallas kernels for 0%

profile of v3, /device:TPU:0, one launch (start us, length us, event | category | flops | bytes accessed | tf_op | source)
XLA Modules:
  0.0 78.4 jit_solution(457080372098862796)
XLA Ops:
  0.0 0.9 %slice.69 = bf16[24,3072]{1,0:T(8,128)(2,1)S(1)} slice(bf16[512,3072]{1,0:T(8,128)(2,1)} %param.5), slice={[0:24], [0:3072]} | slice | bytes 294912 | tf_op jit(solution)/shard_map/slice | solution.py:163
  0.9 1.3 %collective-permute-start = (bf16[24,3072]{1,0:T(8,128)(2,1)S(1)}, bf16[24,3072]{1,0:T(8,128)(2,1)S(1)}, u32[]{:S(2)}, u32[]{:S(2)}) collective-permute-start(bf16[24,3072]{1,0:T(8,128)(2,1)S(1)} %slice.69), channel_id=1, source_target_pairs={{1,0},{2,1},{3,2},{4,3},{5,4},{6,5},{7,6},{8,7},{9,8},{10,9},{11,1... | collective-permute-start | bytes 442376 | tf_op jit(solution)/shard_map/ppermute | solution.py:163
  2.3 0.3 fusion.54
  2.6 0.7 multiply_add_fusion.2
  3.3 0.6 dynamic_slice.37
  5.1 0.8 %reshape.202 = s32[8,2,192]{2,1,0:T(2,128)S(1)} reshape(s32[3072]{0:T(1024)} %param.7) | data formatting | bytes 24576 | tf_op jit(solution)/shard_map/reshape | solution.py:182
  6.6 0.8 dynamic_slice.38
  7.4 0.1 pad.19.clone
  7.4 0.9 %fusion.74 = (f32[8]{0:T(128)S(1)}, f32[8]{0:T(128)S(1)}, f32[8]{0:T(128)S(1)}, f32[8]{0:T(128)S(1)}) fusion(f32[32]{0:T(128)} %param.6), kind=kLoop, calls=%fused_computation.132 | loop fusion | bytes 256 | tf_op jit(solution)/shard_map/slice | solution.py:38
  8.4 0.1 add.243
  8.5 0.1 reshape.207
  8.6 0.1 broadcast_in_dim.108
  8.7 0.1 broadcast_in_dim.114
  8.8 0.1 broadcast_in_dim.124
  8.9 0.1 broadcast_in_dim.119
  9.0 0.2 fusion.58
  9.2 0.3 fusion.57
  9.5 0.4 subtract_convert_fusion.2
  9.9 0.1 pad_maximum_fusion.4
  10.1 4.1 %fusion.35 = f32[192,3072]{1,0:T(8,128)} fusion(bf16[512,3072]{1,0:T(8,128)(2,1)} %param.5, bf16[192,536]{0,1:T(8,128)(2,1)S(1)} %pad_maximum_fusion.4), kind=kOutput, calls=%fused_computation.61 | convolution fusion | flops 603979776 | bytes 5767168 | tf_op jit(solution)/shard_map/dot_general | solution.py:169
  14.2 1.9 %multiply_subtract_fusion = (f32[32,32,512]{2,1,0:T(8,128)S(1)}, f32[32,32,512]{2,1,0:T(8,128)}) fusion(f32[32,512]{1,0:T(8,128)S(1)} %get-tuple-element.40, f32[32,512]{1,0:T(8,128)S(1)} %get-tuple-element.31, f32[32,512]{1,0:T(8,128)S(1)} %get-tuple-element.41, f32[32,512]{1,0:T(8,128)S(1)} %get-tuple-element.30), kind=kLoop, calls=%fused_computation.17 | loop fusion | flops 3670016 | bytes 4456448 | tf_op jit(solution)/shard_map/sub | solution.py:54
  16.1 0.8 %abs_compare_fusion = pred[512,512]{1,0:T(32,128)(4,1)} fusion(), kind=kLoop, calls=%fused_computation.21 | loop fusion | flops 786432 | bytes 262144 | tf_op jit(solution)/shard_map/le | solution.py:61
  17.0 2.2 %fusion.4 = f32[3072,192]{0,1:T(8,128)S(1)} fusion(f32[192,3072]{1,0:T(8,128)} %fusion.35, bf16[24,3072]{1,0:T(8,128)(2,1)S(1)} %collective-permute-done, bf16[64,536]{0,1:T(8,128)(2,1)S(1)} %get-tuple-element.5, bf16[64,536]{0,1:T(8,128)(2,1)S(1)} %get-tuple-element.6, bf16[64,536]{0,1:T(8,128)(2,1)S(1)} %get-tuple-element.7), kind=kOutput, calls=%fused_computation.8 | convolution fusion | flops 28929024 | bytes 5071872 | tf_op jit(solution)/shard_map/dot_general | solution.py:170
  19.2 0.1 fusion.21
  19.3 1.2 %collective-permute-start.1 = (bf16[3072,64]{0,1:T(8,128)(2,1)S(1)}, bf16[3072,64]{0,1:T(8,128)(2,1)S(1)}, u32[]{:S(2)}, u32[]{:S(2)}) collective-permute-start(bf16[3072,64]{0,1:T(8,128)(2,1)S(1)} %fusion.21), channel_id=1, source_target_pairs={{0,1},{1,0},{2,3},{3,2},{4,5},{5,4},{6,7},{7,6},{8,9},{9,8},{10,11... | collective-permute-start | bytes 1179656 | tf_op jit(solution)/shard_map/ppermute | solution.py:143
  20.5 0.3 copy-done
  20.8 1.9 %subtract_convert_fusion = bf16[1024,1024]{1,0:T(8,128)(2,1)} fusion(f32[1024,512]{1,0:T(8,128)S(1)} %bitcast.81, f32[1024,512]{1,0:T(8,128)S(1)} %bitcast.79), kind=kLoop, calls=%fused_computation.6 | loop fusion | flops 5242880 | bytes 6291456 | tf_op jit(solution)/shard_map/convert_element_type | solution.py:26
  22.7 1.6 %fusion.5 = bf16[1024,1024]{1,0:T(8,128)(2,1)} fusion(f32[1024,512]{1,0:T(8,128)S(1)} %bitcast.82, f32[1024,512]{1,0:T(8,128)S(1)} %bitcast.80), kind=kLoop, calls=%fused_computation.9 | loop fusion | flops 4194304 | bytes 6291456 | tf_op jit(solution)/shard_map/convert_element_type | solution.py:26
  24.3 0.2 broadcast_select_fusion.3
  24.6 0.4 copy.21
  24.9 3.9 %gather_fusion = bf16[1664,128]{1,0:T(8,128)(2,1)S(1)} fusion(bf16[3072,128]{1,0:T(8,128)(2,1)S(1)} %copy.21, s32[2048]{0:T(1024)S(1)} %pad_clamp_fusion), kind=kCustom, calls=%fused_computation | custom fusion | bytes 858624 | tf_op jit(solution)/shard_map/jit(_take)/gather | solution.py:188
  28.9 3.6 %collective-permute-start.2 = (bf16[208,128]{1,0:T(8,128)(2,1)S(1)}, bf16[208,128]{1,0:T(8,128)(2,1)S(1)}, u32[]{:S(2)}, u32[]{:S(2)}) collective-permute-start(bf16[208,128]{1,0:T(8,128)(2,1)S(1)} %get-tuple-element.25), channel_id=1, source_target_pairs={{0,2},{2,4},{4,6},{6,8},{8,10},{10,12},{12,14},{14,0},{1,3},{3,5},... | collective-permute-start | bytes 159752 | tf_op jit(solution)/shard_map/ppermute | solution.py:194
  32.5 3.1 %collective-permute-start.8 = (bf16[208,128]{1,0:T(8,128)(2,1)S(1)}, bf16[208,128]{1,0:T(8,128)(2,1)S(1)}, u32[]{:S(2)}, u32[]{:S(2)}) collective-permute-start(bf16[208,128]{1,0:T(8,128)(2,1)S(1)} %get-tuple-element.19), channel_id=1, source_target_pairs={{0,14},{2,0},{4,2},{6,4},{8,6},{10,8},{12,10},{14,12},{1,15},{3,1}... | collective-permute-start | bytes 159752 | tf_op jit(solution)/shard_map/ppermute | solution.py:194
  35.6 2.8 %collective-permute-start.7 = (bf16[208,128]{1,0:T(8,128)(2,1)S(1)}, bf16[208,128]{1,0:T(8,128)(2,1)S(1)}, u32[]{:S(2)}, u32[]{:S(2)}) collective-permute-start(bf16[208,128]{1,0:T(8,128)(2,1)S(1)} %get-tuple-element.20), channel_id=1, source_target_pairs={{0,12},{2,14},{4,0},{6,2},{8,4},{10,6},{12,8},{14,10},{1,13},{3,15... | collective-permute-start | bytes 159752 | tf_op jit(solution)/shard_map/ppermute | solution.py:194
  38.4 2.1 %collective-permute-start.5 = (bf16[208,128]{1,0:T(8,128)(2,1)S(1)}, bf16[208,128]{1,0:T(8,128)(2,1)S(1)}, u32[]{:S(2)}, u32[]{:S(2)}) collective-permute-start(bf16[208,128]{1,0:T(8,128)(2,1)S(1)} %get-tuple-element.22), channel_id=1, source_target_pairs={{0,8},{2,10},{4,12},{6,14},{8,0},{10,2},{12,4},{14,6},{1,9},{3,11}... | collective-permute-start | bytes 159752 | tf_op jit(solution)/shard_map/ppermute | solution.py:194
  40.6 5.9 %collective-permute-done.3 = bf16[208,128]{1,0:T(8,128)(2,1)S(1)} collective-permute-done((bf16[208,128]{1,0:T(8,128)(2,1)S(1)}, bf16[208,128]{1,0:T(8,128)(2,1)S(1)}, u32[]{:S(2)}, u32[]{:S(2)}) %collective-permute-start.3) | collective-permute-done | bytes 53280 | tf_op jit(solution)/shard_map/ppermute | solution.py:194
  46.5 5.9 %collective-permute-done.4 = bf16[208,128]{1,0:T(8,128)(2,1)S(1)} collective-permute-done((bf16[208,128]{1,0:T(8,128)(2,1)S(1)}, bf16[208,128]{1,0:T(8,128)(2,1)S(1)}, u32[]{:S(2)}, u32[]{:S(2)}) %collective-permute-start.4) | collective-permute-done | bytes 53280 | tf_op jit(solution)/shard_map/ppermute | solution.py:194
  52.6 2.6 %fusion = f32[208,2048]{1,0:T(8,128)S(1)} fusion(bf16[208,1024]{1,0:T(8,128)(2,1)S(1)} %constant_dynamic-update-slice_fusion, bf16[1024,1024]{1,0:T(8,128)(2,1)S(1)} %copy-done.1, bf16[1024,1024]{1,0:T(8,128)(2,1)} %fusion.5), kind=kOutput, calls=%fused_computation.2 | convolution fusion | flops 880803840 | bytes 6324224 | tf_op jit(solution)/shard_map/dot_general | solution.py:79
  55.3 0.1 slice_add_fusion
  55.4 0.1 fusion.70
  55.5 0.7 copy-done.2
  56.2 0.6 multiply_convert_fusion.1
  56.9 2.2 %cosine_convert_fusion = (bf16[512,256]{1,0:T(8,128)(2,1)S(1)}, bf16[512,256]{1,0:T(8,128)(2,1)S(1)}) fusion(s32[256]{0:T(256)S(1)} %add_add_fusion), kind=kLoop, calls=%fused_computation.41 | loop fusion | flops 2228224 | bytes 525312 | tf_op jit(solution)/shard_map/convert.1
  59.3 1.1 %fusion.73 = (f32[512,256]{1,0:T(8,128)}, f32[512,256]{1,0:T(8,128)}) fusion(f32[1024,256]{1,0:T(8,128)S(1)} %maximum_convert_fusion), kind=kLoop, calls=%fused_computation.131 | loop fusion | bytes 2097152 | tf_op jit(solution)/shard_map/slice | solution.py:207
  60.4 0.2 broadcast_select_fusion.1
  60.7 0.8 %copy.22 = bf16[32,1024]{0,1:T(8,128)(2,1)} copy(bf16[32,1024]{1,0:T(8,128)(2,1)S(1)} %pad_maximum_fusion.5) | data formatting | bytes 131072 | tf_op jit(solution)/shard_map/concatenate | solution.py:203
  61.5 0.9 %pad_maximum_fusion.2.white_ref = bf16[384,1024]{1,0:T(8,128)(2,1)} fusion(bf16[192,1024]{1,0:T(8,128)(2,1)S(1)} %slice.96, bf16[192,1024]{1,0:T(8,128)(2,1)S(1)} %slice.95), kind=kLoop, calls=%fused_computation.27 | loop fusion | flops 1572864 | bytes 1572864 | tf_op jit(solution)/shard_map/concatenate | solution.py:202
  62.4 16.0 %shard_map.55 = f32[32,384,256]{2,1,0:T(8,128)} custom-call(bf16[384,1024]{1,0:T(8,128)(2,1)} %pad_maximum_fusion.2.white_ref, bf16[1024,32]{1,0:T(8,128)(2,1)} %bitcast.85, f32[512,256]{1,0:T(8,128)} %get-tuple-element.11.cos_ref, f32[512,256]{1,0:T(8,128)} %get-tuple-element.10.sin_ref), custom_call_target="tpu_custom_call" | custom-call | flops 6467616768 | bytes 14483456 | tf_op jit(solution)/shard_map/pallas_call | solution.py:126
  (48 shorter events, 0.7 us)
Async XLA Ops:
  0.9 16.0 %collective-permute-start = (bf16[24,3072]{1,0:T(8,128)(2,1)S(1)}, bf16[24,3072]{1,0:T(8,128)(2,1)S(1)}, u32[]{:S(2)}, u32[]{:S(2)}) collective-permute-start(bf16[24,3072]{1,0:T(8,128)(2,1)S(1)} %slice.69), channel_id=1, source_target_pairs={{1,0},{2,1},{3,2},{4,3},{5,4},{6,5},{7,6},{8,7},{9,8},{10,9},{11,1... | collective-permute-start | bytes 442376 | tf_op jit(solution)/shard_map/ppermute | solution.py:163
  19.2 1.6 %copy-start = (f32[32,32,512]{2,1,0:T(8,128)S(1)}, f32[32,32,512]{2,1,0:T(8,128)}, u32[]{:S(2)}) copy-start(f32[32,32,512]{2,1,0:T(8,128)} %get-tuple-element.27) | copy-start | bytes 6291460
  19.3 5.0 %collective-permute-start.1 = (bf16[3072,64]{0,1:T(8,128)(2,1)S(1)}, bf16[3072,64]{0,1:T(8,128)(2,1)S(1)}, u32[]{:S(2)}, u32[]{:S(2)}) collective-permute-start(bf16[3072,64]{0,1:T(8,128)(2,1)S(1)} %fusion.21), channel_id=1, source_target_pairs={{0,1},{1,0},{2,3},{3,2},{4,5},{5,4},{6,7},{7,6},{8,9},{9,8},{10,11... | collective-permute-start | bytes 1179656 | tf_op jit(solution)/shard_map/ppermute | solution.py:143
  24.9 27.7 %copy-start.1 = (bf16[1024,1024]{1,0:T(8,128)(2,1)S(1)}, bf16[1024,1024]{1,0:T(8,128)(2,1)}, u32[]{:S(2)}) copy-start(bf16[1024,1024]{1,0:T(8,128)(2,1)} %subtract_convert_fusion) | copy-start | bytes 6291460
  28.9 11.7 %collective-permute-start.2 = (bf16[208,128]{1,0:T(8,128)(2,1)S(1)}, bf16[208,128]{1,0:T(8,128)(2,1)S(1)}, u32[]{:S(2)}, u32[]{:S(2)}) collective-permute-start(bf16[208,128]{1,0:T(8,128)(2,1)S(1)} %get-tuple-element.25), channel_id=1, source_target_pairs={{0,2},{2,4},{4,6},{6,8},{8,10},{10,12},{12,14},{14,0},{1,3},{3,5},... | collective-permute-start | bytes 159752 | tf_op jit(solution)/shard_map/ppermute | solution.py:194
  32.5 20.0 %collective-permute-start.8 = (bf16[208,128]{1,0:T(8,128)(2,1)S(1)}, bf16[208,128]{1,0:T(8,128)(2,1)S(1)}, u32[]{:S(2)}, u32[]{:S(2)}) collective-permute-start(bf16[208,128]{1,0:T(8,128)(2,1)S(1)} %get-tuple-element.19), channel_id=1, source_target_pairs={{0,14},{2,0},{4,2},{6,4},{8,6},{10,8},{12,10},{14,12},{1,15},{3,1}... | collective-permute-start | bytes 159752 | tf_op jit(solution)/shard_map/ppermute | solution.py:194
  35.6 16.9 %collective-permute-start.7 = (bf16[208,128]{1,0:T(8,128)(2,1)S(1)}, bf16[208,128]{1,0:T(8,128)(2,1)S(1)}, u32[]{:S(2)}, u32[]{:S(2)}) collective-permute-start(bf16[208,128]{1,0:T(8,128)(2,1)S(1)} %get-tuple-element.20), channel_id=1, source_target_pairs={{0,12},{2,14},{4,0},{6,2},{8,4},{10,6},{12,8},{14,10},{1,13},{3,15... | collective-permute-start | bytes 159752 | tf_op jit(solution)/shard_map/ppermute | solution.py:194
  38.4 14.1 %collective-permute-start.6 = (bf16[208,128]{1,0:T(8,128)(2,1)S(1)}, bf16[208,128]{1,0:T(8,128)(2,1)S(1)}, u32[]{:S(2)}, u32[]{:S(2)}) collective-permute-start(bf16[208,128]{1,0:T(8,128)(2,1)S(1)} %get-tuple-element.21), channel_id=1, source_target_pairs={{0,10},{2,12},{4,14},{6,0},{8,2},{10,4},{12,6},{14,8},{1,11},{3,13... | collective-permute-start | bytes 159752 | tf_op jit(solution)/shard_map/ppermute | solution.py:194
  38.4 14.0 %collective-permute-start.5 = (bf16[208,128]{1,0:T(8,128)(2,1)S(1)}, bf16[208,128]{1,0:T(8,128)(2,1)S(1)}, u32[]{:S(2)}, u32[]{:S(2)}) collective-permute-start(bf16[208,128]{1,0:T(8,128)(2,1)S(1)} %get-tuple-element.22), channel_id=1, source_target_pairs={{0,8},{2,10},{4,12},{6,14},{8,0},{10,2},{12,4},{14,6},{1,9},{3,11}... | collective-permute-start | bytes 159752 | tf_op jit(solution)/shard_map/ppermute | solution.py:194
  40.6 5.9 %collective-permute-start.3 = (bf16[208,128]{1,0:T(8,128)(2,1)S(1)}, bf16[208,128]{1,0:T(8,128)(2,1)S(1)}, u32[]{:S(2)}, u32[]{:S(2)}) collective-permute-start(bf16[208,128]{1,0:T(8,128)(2,1)S(1)} %get-tuple-element.24), channel_id=1, source_target_pairs={{0,4},{2,6},{4,8},{6,10},{8,12},{10,14},{12,0},{14,2},{1,5},{3,7},... | collective-permute-start | bytes 159752 | tf_op jit(solution)/shard_map/ppermute | solution.py:194
  46.5 5.9 %collective-permute-start.4 = (bf16[208,128]{1,0:T(8,128)(2,1)S(1)}, bf16[208,128]{1,0:T(8,128)(2,1)S(1)}, u32[]{:S(2)}, u32[]{:S(2)}) collective-permute-start(bf16[208,128]{1,0:T(8,128)(2,1)S(1)} %get-tuple-element.23), channel_id=1, source_target_pairs={{0,6},{2,8},{4,10},{6,12},{8,14},{10,0},{12,2},{14,4},{1,7},{3,9},... | collective-permute-start | bytes 159752 | tf_op jit(solution)/shard_map/ppermute | solution.py:194
  55.3 1.0 %copy-start.2 = (pred[512,512]{1,0:T(32,128)(4,1)S(1)}, pred[512,512]{1,0:T(32,128)(4,1)}, u32[]{:S(2)}) copy-start(pred[512,512]{1,0:T(32,128)(4,1)} %abs_compare_fusion) | copy-start | bytes 786436
  56.9 3.5 %collective-permute-start.9 = (bf16[208,1024]{1,0:T(8,128)(2,1)S(1)}, bf16[208,1024]{1,0:T(8,128)(2,1)S(1)}, u32[]{:S(2)}, u32[]{:S(2)}) collective-permute-start(bf16[208,1024]{1,0:T(8,128)(2,1)S(1)} %pad_maximum_fusion.3), channel_id=1, source_target_pairs={{0,1},{1,0},{2,3},{3,2},{4,5},{5,4},{6,7},{7,6},{8,9},{9,8},{10,11... | collective-permute-start | bytes 1277960 | tf_op jit(solution)/shard_map/ppermute | solution.py:143

commit v4 on v2

--- a/solution.py
+++ b/solution.py
@@ -40,12 +40,12 @@
     return matrix.reshape(out_rows, in_rows)
 
 
-def dft_table(samples, bins):
+def dft_table(samples, bins, time_index):
     inner = 32
     outer = samples // inner
     frequency = jnp.arange(bins, dtype=jnp.int32)[None, :]
     low = jnp.arange(inner, dtype=jnp.int32)[:, None]
-    high = jnp.arange(outer, dtype=jnp.int32)[:, None] * inner
+    high = time_index.reshape(outer, inner)[:, :1]
     scale = two_pi / samples
     low_angle = ((low * frequency) % samples).astype(jnp.float32) * scale
     high_angle = ((high * frequency) % samples).astype(jnp.float32) * scale
@@ -71,10 +71,10 @@
     return jnp.concatenate([jnp.cos(angles), -jnp.sin(angles)], axis=0).astype(jnp.bfloat16)
 
 
-def whiten_series(series):
+def whiten_series(series, time_index):
     samples = series.shape[1]
     bins = samples // 2
-    table = dft_table(samples, bins)
+    table = dft_table(samples, bins, time_index)
     hi, lo = split_bf16(table, 2)
     both = jnp.dot(series, jnp.concatenate([hi, lo], axis=1), preferred_element_type=jnp.float32)
     spectrum = both[:, : 2 * bins] + both[:, 2 * bins :]
@@ -93,43 +93,43 @@
     return jnp.concatenate([real_part * factor, imag_part * factor], axis=1).astype(jnp.bfloat16)
 
 
-def correlate_kernel(factor, bins, group, white_ref, src_ref, cos_ref, sin_ref, out_ref):
-    cosine = cos_ref[...]
-    sine = sin_ref[...]
+def correlate_kernel(factor, bins, group, white_ref, src_ref, lag_ref, out_ref):
+    real_rcv = white_ref[:, :bins]
+    imag_rcv = white_ref[:, bins:]
+    lag = lag_ref[...]
     for k in range(group):
-        real_src = src_ref[0, :bins, k : k + 1]
-        imag_src = src_ref[0, bins:, k : k + 1]
-        top = (cosine * real_src + sine * imag_src).astype(jnp.bfloat16)
-        bottom = (cosine * imag_src - sine * real_src).astype(jnp.bfloat16)
-        total = jnp.dot(white_ref[:, :bins], top, preferred_element_type=jnp.float32)
-        total = total + jnp.dot(white_ref[:, bins:], bottom, preferred_element_type=jnp.float32)
-        out_ref[k] = total * factor
-
-
-def correlate(receivers, sources, cosine, sine):
+        row = src_ref[pl.ds(pl.program_id(0) * group + k, 1), :]
+        real_src = row[:, :bins]
+        imag_src = row[:, bins:]
+        cross = jnp.concatenate(
+            [real_src * real_rcv + imag_src * imag_rcv, imag_src * real_rcv - real_src * imag_rcv],
+            axis=1,
+        ).astype(jnp.bfloat16)
+        out_ref[k] = jnp.dot(cross, lag, preferred_element_type=jnp.float32) * factor
+
+
+def correlate(receivers, sources, lag):
     block, width = receivers.shape
     bins = width // 2
     count = sources.shape[0]
-    lags = cosine.shape[1]
+    lags = lag.shape[1]
     group = 8
-    grouped = sources.reshape(count // group, group, width).transpose(0, 2, 1)
     factor = 1.0 / math.sqrt(bins)
-    flops = 2 * count * block * width * lags + 6 * count * bins * lags
-    moved = 2 * block * width + 4 * count * width + 8 * lags * bins + 4 * count * block * lags
+    flops = 2 * count * block * width * lags + 6 * count * block * bins
+    moved = 4 * block * width + 4 * count * width + 2 * lags * width + 4 * count * block * lags
     return pl.pallas_call(
         functools.partial(correlate_kernel, factor, bins, group),
         out_shape=jax.ShapeDtypeStruct((count, block, lags), jnp.float32),
         grid=(count // group,),
         in_specs=[
             pl.BlockSpec((block, width), lambda s: (0, 0)),
-            pl.BlockSpec((1, width, group), lambda s: (s, 0, 0)),
-            pl.BlockSpec((bins, lags), lambda s: (0, 0)),
-            pl.BlockSpec((bins, lags), lambda s: (0, 0)),
+            pl.BlockSpec((count, width), lambda s: (0, 0)),
+            pl.BlockSpec((width, lags), lambda s: (0, 0)),
         ],
         out_specs=pl.BlockSpec((group, block, lags), lambda s: (s, 0, 0)),
         compiler_params=pltpu.CompilerParams(dimension_semantics=("arbitrary",)),
         cost_estimate=pl.CostEstimate(flops=flops, bytes_accessed=moved, transcendentals=0),
-    )(receivers, grouped, cosine, sine)
+    )(receivers, sources, lag)
 
 
 def swap_tm(x):
@@ -171,7 +171,7 @@
 
     first_rows = source_owner * block + source_offset
     own_first = lax.dynamic_index_in_dim(first_rows, tm, keepdims=False)
-    source_raw = jnp.take(channel_map, own_first + jnp.arange(SRC, dtype=jnp.int32), mode="clip")
+    source_raw = lax.dynamic_slice_in_dim(channel_map, own_first, SRC)
     halves = channel_map.reshape(n_chan, n_tm, half)
     half_raw = lax.dynamic_index_in_dim(halves, tm, axis=1, keepdims=False)
     index = jnp.concatenate(
@@ -180,15 +180,16 @@
     width = index.shape[1]
     rows = jnp.take(paired, index.reshape(-1), axis=0, mode="clip").reshape(n_chan, width, -1)
     series = lax.all_to_all(rows, "chan", 0, 2, tiled=True).reshape(width, samples)
-
-    white = whiten_series(series)
+    time_index = jnp.arange(samples, dtype=jnp.int32)
+
+    white = whiten_series(series, time_index)
     low, high = swap_tm(white)
-    receivers = jnp.concatenate([low[:half], high[:half]], axis=0)
+    receivers = jnp.concatenate([low[:half], high[:half]], axis=0).astype(jnp.float32)
     sources = jnp.concatenate([low[half:], high[half:]], axis=0).astype(jnp.float32)
 
     lag_share = LAGS // n_tm
-    kernel = lag_kernel(samples, tm * lag_share, lag_share).astype(jnp.float32)
-    result = correlate(receivers, sources, kernel[:bins], kernel[bins:])
+    kernel = lag_kernel(samples, tm * lag_share, lag_share)
+    result = correlate(receivers, sources, kernel)
     return result.reshape(STEPS, SRC, block, lag_share)
 
 

time: 65.9 us -> 63.8 us (0.968)
  local copies, waits for them, and re-layouts: 13.9 us -> 9.58 us
  Pallas kernels: 14.3 us -> 10.7 us
  matrix products: 6.51 us -> 9.59 us
  between operations: 0.34 us -> 2.25 us
    pallas_call x1, Pallas kernels: 14.3 us -> 10.7 us  [correlate(): pl.pallas_call(functools.partial(correlate_kernel, factor, bins, group),...]
    transpose x1 -> x0, local copies, waits for them, and re-layouts: 1.95 us -> none  [correlate(): grouped = sources.reshape(count // group, group, width).transpose(0, 2, 1)]
    convert_element_type x1 -> x2, other arithmetic: 0.07 us -> 2.02 us  [the longest x1 1.35 us: local(): jnp.concatenate([low[:half], high[:half]], axis=0).astype(jnp.float32)]
    dot_general x1, matrix products: 0.57 us -> 2.24 us  [local(): lax.dot_general(halo, stacked[:, raw_rows:], dims, preferred_element_type...]
    dot_general x1, matrix products: 2.71 us -> 4.11 us  [local(): lax.dot_general(records, stacked[:, :raw_rows], dims, preferred_element_t...]
    gather x1 -> x0, local copies, waits for them, and re-layouts: 1.37 us -> none  [local(): jnp.take(channel_map, own_first + jnp.arange(SRC, dtype=jnp.int32), mode=...]
    slice x3 -> x2, local copies, waits for them, and re-layouts: 1.1 us -> 0.05 us  [the longest x1 0.03 us: local(): high[:half]]
    dynamic_slice x0 -> x1, local copies, waits for them, and re-layouts: none -> 0.78 us  [local(): source_raw = lax.dynamic_slice_in_dim(channel_map, own_first, SRC)]
  transfers between devices with their start and end apart: 4 -> 4, of which waited for: 2 -> 2; matrix products, arithmetic and copies ran while one was open for 25% -> 24% of each run, Pallas kernels for 0% -> 0%
where the time goes in v4:
time: 63.8 us; the launch traced here: 63.3 us
  other arithmetic  10.7 us (17%)
  waiting for transfers between devices  10.7 us (17%)
  Pallas kernels  10.7 us (17%)
  starting transfers between devices  9.85 us (15%)
  matrix products  9.59 us (15%)
  local copies, waits for them, and re-layouts  9.58 us (15%)
  between operations  2.25 us (4%)
    pallas_call x1, Pallas kernels, correlate(): pl.pallas_call(functools.partial(correlate_kernel, factor, bins, group),...  10.7 us
    all_to_all x1, waiting for transfers between devices, local(): lax.all_to_all(rows, 'chan', 0, 2, tiled=True).reshape(width, samples)  9.85 us
    all_to_all x1, starting transfers between devices, local(): lax.all_to_all(rows, 'chan', 0, 2, tiled=True).reshape(width, samples)  7.31 us
    gather x1, local copies, waits for them, and re-layouts, local(): jnp.take(paired, index.reshape(-1), axis=0, mode='clip')  4.57 us
    dot_general x1, matrix products, local(): lax.dot_general(records, stacked[:, :raw_rows], dims, preferred_element_t...  4.11 us
    dot_general x1, matrix products, whiten_series(): jnp.dot(series, jnp.concatenate([hi, lo], axis=1), preferred_element_type...  2.64 us
    convert_element_type x4, other arithmetic, split_bf16(): piece = rest.astype(jnp.bfloat16)  2.63 us
    dot_general x1, matrix products, local(): lax.dot_general(halo, stacked[:, raw_rows:], dims, preferred_element_type...  2.24 us
  transfers between devices with their start and end apart: 4, of which 2 were waited for; matrix products, arithmetic and copies ran while one was open for 24% of the time, Pallas kernels for 0%

profile of v4, /device:TPU:0, one launch (start us, length us, event | category | flops | bytes accessed | tf_op | source)
XLA Modules:
  0.0 63.3 jit_solution(1934936387321579071)
XLA Ops:
  0.0 0.9 %slice.65 = bf16[24,3072]{1,0:T(8,128)(2,1)S(1)} slice(bf16[512,3072]{1,0:T(8,128)(2,1)} %param.5), slice={[0:24], [0:3072]} | slice | bytes 294912 | tf_op jit(solution)/shard_map/slice | solution.py:156
  0.9 1.3 %collective-permute-start = (bf16[24,3072]{1,0:T(8,128)(2,1)S(1)}, bf16[24,3072]{1,0:T(8,128)(2,1)S(1)}, u32[]{:S(2)}, u32[]{:S(2)}) collective-permute-start(bf16[24,3072]{1,0:T(8,128)(2,1)S(1)} %slice.65), channel_id=1, source_target_pairs={{1,0},{2,1},{3,2},{4,3},{5,4},{6,5},{7,6},{8,7},{9,8},{10,9},{11,1... | collective-permute-start | bytes 442376 | tf_op jit(solution)/shard_map/ppermute | solution.py:156
  2.3 0.7 %multiply_add_fusion.1 = s32[2]{0:T(128)S(1)} fusion(s32[2]{0:T(128)} %param.9, s32[2]{0:T(128)} %param.8), kind=kLoop, calls=%fused_computation.106 | loop fusion | flops 4 | bytes 24 | tf_op jit(solution)/shard_map/add | solution.py:172
  3.0 0.6 dynamic_slice.12
  4.8 0.8 %reshape.197 = s32[8,2,192]{2,1,0:T(2,128)S(1)} reshape(s32[3072]{0:T(1024)} %param.7) | data formatting | bytes 24576 | tf_op jit(solution)/shard_map/reshape | solution.py:175
  6.3 0.8 %dynamic_slice.13 = s32[16]{0:T(128)S(1)} dynamic-slice(s32[3072]{0:T(1024)} %param.7, s32[]{:T(128)S(6)} %select_n.94), dynamic_slice_sizes={16} | dynamic-slice | bytes 132 | tf_op jit(solution)/shard_map/dynamic_slice | solution.py:174
  7.1 0.1 pad.19.clone
  7.1 0.9 %fusion.73 = (f32[8]{0:T(128)S(1)}, f32[8]{0:T(128)S(1)}, f32[8]{0:T(128)S(1)}, f32[8]{0:T(128)S(1)}) fusion(f32[32]{0:T(128)} %param.6), kind=kLoop, calls=%fused_computation.113 | loop fusion | bytes 256 | tf_op jit(solution)/shard_map/slice | solution.py:38
  8.1 0.1 broadcast_in_dim.106
  8.2 0.1 broadcast_in_dim.112
  8.3 0.1 broadcast_in_dim.122
  8.4 0.1 broadcast_in_dim.117
  8.4 0.4 subtract_convert_fusion.2
  8.8 0.1 pad_maximum_fusion.4
  9.0 4.1 %fusion.37 = f32[192,3072]{1,0:T(8,128)} fusion(bf16[512,3072]{1,0:T(8,128)(2,1)} %param.5, bf16[192,536]{0,1:T(8,128)(2,1)S(1)} %pad_maximum_fusion.4), kind=kOutput, calls=%fused_computation.63 | convolution fusion | flops 603979776 | bytes 5767168 | tf_op jit(solution)/shard_map/dot_general | solution.py:162
  13.1 0.1 reshape.206
  13.2 0.0 collective-permute-done
  13.2 2.2 %fusion.4 = f32[3072,192]{0,1:T(8,128)S(1)} fusion(f32[192,3072]{1,0:T(8,128)} %fusion.37, bf16[24,3072]{1,0:T(8,128)(2,1)S(1)} %collective-permute-done, bf16[64,536]{0,1:T(8,128)(2,1)S(1)} %get-tuple-element.5, bf16[64,536]{0,1:T(8,128)(2,1)S(1)} %get-tuple-element.6, bf16[64,536]{0,1:T(8,128)(2,1)S(1)} %get-tuple-element.7), kind=kOutput, calls=%fused_computation.8 | convolution fusion | flops 28929024 | bytes 5071872 | tf_op jit(solution)/shard_map/dot_general | solution.py:163
  15.4 0.1 fusion.21
  15.5 1.2 %collective-permute-start.1 = (bf16[3072,64]{0,1:T(8,128)(2,1)S(1)}, bf16[3072,64]{0,1:T(8,128)(2,1)S(1)}, u32[]{:S(2)}, u32[]{:S(2)}) collective-permute-start(bf16[3072,64]{0,1:T(8,128)(2,1)S(1)} %fusion.21), channel_id=1, source_target_pairs={{0,1},{1,0},{2,3},{3,2},{4,5},{5,4},{6,7},{7,6},{8,9},{9,8},{10,11... | collective-permute-start | bytes 1179656 | tf_op jit(solution)/shard_map/ppermute | solution.py:136
  16.7 0.1 abs_compare_fusion
  16.9 0.3 fusion.59
  17.2 0.9 %collective-permute-done.1 = bf16[3072,64]{0,1:T(8,128)(2,1)S(1)} collective-permute-done((bf16[3072,64]{0,1:T(8,128)(2,1)S(1)}, bf16[3072,64]{0,1:T(8,128)(2,1)S(1)}, u32[]{:S(2)}, u32[]{:S(2)}) %collective-permute-start.1) | collective-permute-done | bytes 393248 | tf_op jit(solution)/shard_map/ppermute | solution.py:136
  18.1 0.2 broadcast_select_fusion.3
  18.3 0.1 pad_maximum_fusion.1
  18.3 0.4 copy.9
  18.7 4.6 %gather_fusion = bf16[1664,128]{1,0:T(8,128)(2,1)} fusion(bf16[3072,128]{1,0:T(8,128)(2,1)S(1)} %copy.9, s32[2048]{0:T(1024)S(1)} %pad_clamp_fusion), kind=kCustom, calls=%fused_computation | custom fusion | bytes 858624 | tf_op jit(solution)/shard_map/jit(_take)/gather | solution.py:181
  23.3 7.3 %all-to-all-start = ((bf16[8,208,128]{2,1,0:T(8,128)(2,1)}), bf16[8,208,128]{2,1,0:T(8,128)(2,1)S(1)}, u32[]{:S(2)}, u32[]{:S(2)}) async-start(bf16[8,208,128]{2,1,0:T(8,128)(2,1)} %bitcast.6), calls=%async_computation | async-start | bytes 851968 | tf_op jit(solution)/shard_map/all_to_all | solution.py:182
  30.6 0.3 fusion.56
  30.9 0.6 multiply_subtract_fusion
  31.5 0.6 subtract_convert_fusion
  32.1 1.6 %fusion.5 = bf16[1024,1024]{1,0:T(8,128)(2,1)} fusion(f32[1024,512]{1,0:T(8,128)S(1)} %bitcast.73, f32[1024,512]{1,0:T(8,128)S(1)} %bitcast.71), kind=kLoop, calls=%fused_computation.9 | loop fusion | flops 4194304 | bytes 6291456 | tf_op jit(solution)/shard_map/convert_element_type | solution.py:26
  33.6 9.8 %all-to-all-done = bf16[8,208,128]{2,1,0:T(8,128)(2,1)S(1)} async-done(((bf16[8,208,128]{2,1,0:T(8,128)(2,1)}), bf16[8,208,128]{2,1,0:T(8,128)(2,1)S(1)}, u32[]{:S(2)}, u32[]{:S(2)}) %all-to-all-start) | async-done | bytes 426016 | tf_op jit(solution)/shard_map/all_to_all | solution.py:182
  43.5 0.1 copy.10
  43.6 2.6 %fusion = f32[208,2048]{1,0:T(8,128)S(1)} fusion(bf16[1024,1024]{1,0:T(8,128)(2,1)S(1)} %subtract_convert_fusion, bf16[1024,1024]{1,0:T(8,128)(2,1)} %fusion.5, bf16[26,8,8,128]{3,2,1,0:T(8,128)(2,1)S(1)} %bitcast.75), kind=kOutput, calls=%fused_computation.2 | convolution fusion | flops 880803840 | bytes 6324224 | tf_op jit(solution)/shard_map/dot_general | solution.py:79
  46.3 0.1 slice_add_fusion
  46.4 0.1 fusion.70
  46.5 0.6 multiply_convert_fusion.1
  47.1 0.1 collective-permute-start.2
  47.2 2.2 %cosine_convert_fusion = (bf16[512,256]{1,0:T(8,128)(2,1)S(1)}, bf16[512,256]{1,0:T(8,128)(2,1)S(1)}) fusion(s32[256]{0:T(256)S(1)} %add_add_fusion), kind=kLoop, calls=%fused_computation.41 | loop fusion | flops 2228224 | bytes 525312 | tf_op jit(solution)/shard_map/convert.1
  49.5 0.9 %pad_maximum_fusion.2.lag_ref = bf16[1024,256]{1,0:T(8,128)(2,1)} fusion(bf16[512,256]{1,0:T(8,128)(2,1)S(1)} %get-tuple-element.20, bf16[512,256]{1,0:T(8,128)(2,1)S(1)} %get-tuple-element.19), kind=kLoop, calls=%fused_computation.39 | loop fusion | flops 1048576 | bytes 1048576 | tf_op jit(solution)/shard_map/concatenate | solution.py:71
  50.3 0.0 collective-permute-done.2
  50.3 0.2 broadcast_select_fusion.1
  50.6 0.7 %maximum_convert_fusion.1.src_ref = f32[32,1024]{1,0:T(8,128)} fusion(bf16[16,1024]{1,0:T(8,128)(2,1)S(1)} %slice.91, bf16[16,1024]{1,0:T(8,128)(2,1)S(1)} %slice.90), kind=kLoop, calls=%fused_computation.78 | loop fusion | flops 131072 | bytes 196608 | tf_op jit(solution)/shard_map/convert_element_type | solution.py:188
  51.3 1.4 %maximum_convert_fusion.white_ref = f32[384,1024]{1,0:T(8,128)} fusion(bf16[192,1024]{1,0:T(8,128)(2,1)S(1)} %slice.89, bf16[192,1024]{1,0:T(8,128)(2,1)S(1)} %slice.88), kind=kLoop, calls=%fused_computation.27 | loop fusion | flops 1572864 | bytes 2359296 | tf_op jit(solution)/shard_map/convert_element_type | solution.py:187
  52.6 10.7 %shard_map.55 = f32[32,384,256]{2,1,0:T(8,128)} custom-call(f32[384,1024]{1,0:T(8,128)} %maximum_convert_fusion.white_ref, f32[32,1024]{1,0:T(8,128)} %maximum_convert_fusion.1.src_ref, bf16[1024,256]{1,0:T(8,128)(2,1)} %pad_maximum_fusion.2.lag_ref), custom_call_target="tpu_custom_call" | custom-call | flops 6480199680 | bytes 14811136 | tf_op jit(solution)/shard_map/pallas_call | solution.py:120
  (17 shorter events, 0.2 us)
Async XLA Ops:
  0.9 12.3 %collective-permute-start = (bf16[24,3072]{1,0:T(8,128)(2,1)S(1)}, bf16[24,3072]{1,0:T(8,128)(2,1)S(1)}, u32[]{:S(2)}, u32[]{:S(2)}) collective-permute-start(bf16[24,3072]{1,0:T(8,128)(2,1)S(1)} %slice.65), channel_id=1, source_target_pairs={{1,0},{2,1},{3,2},{4,3},{5,4},{6,5},{7,6},{8,7},{9,8},{10,9},{11,1... | collective-permute-start | bytes 442376 | tf_op jit(solution)/shard_map/ppermute | solution.py:156
  15.5 2.5 %collective-permute-start.1 = (bf16[3072,64]{0,1:T(8,128)(2,1)S(1)}, bf16[3072,64]{0,1:T(8,128)(2,1)S(1)}, u32[]{:S(2)}, u32[]{:S(2)}) collective-permute-start(bf16[3072,64]{0,1:T(8,128)(2,1)S(1)} %fusion.21), channel_id=1, source_target_pairs={{0,1},{1,0},{2,3},{3,2},{4,5},{5,4},{6,7},{7,6},{8,9},{9,8},{10,11... | collective-permute-start | bytes 1179656 | tf_op jit(solution)/shard_map/ppermute | solution.py:136
  23.3 20.2 %all-to-all-start = ((bf16[8,208,128]{2,1,0:T(8,128)(2,1)}), bf16[8,208,128]{2,1,0:T(8,128)(2,1)S(1)}, u32[]{:S(2)}, u32[]{:S(2)}) async-start(bf16[8,208,128]{2,1,0:T(8,128)(2,1)} %bitcast.6), calls=%async_computation | async-start | bytes 851968 | tf_op jit(solution)/shard_map/all_to_all | solution.py:182
  47.1 3.2 %collective-permute-start.2 = (bf16[208,1024]{1,0:T(8,128)(2,1)S(1)}, bf16[208,1024]{1,0:T(8,128)(2,1)S(1)}, u32[]{:S(2)}, u32[]{:S(2)}) collective-permute-start(bf16[208,1024]{1,0:T(8,128)(2,1)S(1)} %pad_maximum_fusion.3), channel_id=1, source_target_pairs={{0,1},{1,0},{2,3},{3,2},{4,5},{5,4},{6,7},{7,6},{8,9},{9,8},{10,11... | collective-permute-start | bytes 1277960 | tf_op jit(solution)/shard_map/ppermute | solution.py:136

commit v5 on v4

--- a/solution.py
+++ b/solution.py
@@ -30,13 +30,12 @@
 
 
 def decimation_matrix(fir_taps, out_rows, in_rows):
-    rows = jnp.arange(out_rows, dtype=jnp.int32)[:, None, None]
-    groups = jnp.arange(in_rows // STRIDE, dtype=jnp.int32)[None, :, None]
-    lead = groups - rows
-    matrix = jnp.zeros((out_rows, in_rows // STRIDE, STRIDE), jnp.float32)
-    for lead_index in range(TAPS // STRIDE):
-        taps = fir_taps[lead_index * STRIDE : (lead_index + 1) * STRIDE][None, None, :]
-        matrix = matrix + jnp.where(lead == lead_index, taps, 0.0)
+    leads = TAPS // STRIDE
+    rows = jnp.arange(out_rows, dtype=jnp.int32)[:, None, None, None]
+    groups = jnp.arange(in_rows // STRIDE, dtype=jnp.int32)[None, :, None, None]
+    lead = jnp.arange(leads, dtype=jnp.int32)[None, None, :, None]
+    taps = fir_taps.reshape(1, 1, leads, STRIDE)
+    matrix = jnp.where(groups - rows == lead, taps, 0.0).sum(axis=2)
     return matrix.reshape(out_rows, in_rows)
 
 
@@ -71,10 +70,9 @@
     return jnp.concatenate([jnp.cos(angles), -jnp.sin(angles)], axis=0).astype(jnp.bfloat16)
 
 
-def whiten_series(series, time_index):
+def whiten_series(series, table):
     samples = series.shape[1]
     bins = samples // 2
-    table = dft_table(samples, bins, time_index)
     hi, lo = split_bf16(table, 2)
     both = jnp.dot(series, jnp.concatenate([hi, lo], axis=1), preferred_element_type=jnp.float32)
     spectrum = both[:, : 2 * bins] + both[:, 2 * bins :]
@@ -93,43 +91,53 @@
     return jnp.concatenate([real_part * factor, imag_part * factor], axis=1).astype(jnp.bfloat16)
 
 
-def correlate_kernel(factor, bins, group, white_ref, src_ref, lag_ref, out_ref):
-    real_rcv = white_ref[:, :bins]
-    imag_rcv = white_ref[:, bins:]
+def correlate_kernel(factor, bins, group, half, low_ref, high_ref, lag_ref, out_ref):
+    step = pl.program_id(0)
     lag = lag_ref[...]
+    receivers = [low_ref[:half, :].astype(jnp.float32), high_ref[:half, :].astype(jnp.float32)]
+    every = jnp.concatenate([low_ref[half:, :], high_ref[half:, :]], axis=0).astype(jnp.float32)
+    picked = every[:group]
+    for g in range(1, every.shape[0] // group):
+        picked = jnp.where(step == g, every[g * group : (g + 1) * group], picked)
     for k in range(group):
-        row = src_ref[pl.ds(pl.program_id(0) * group + k, 1), :]
+        row = picked[k : k + 1]
         real_src = row[:, :bins]
         imag_src = row[:, bins:]
-        cross = jnp.concatenate(
-            [real_src * real_rcv + imag_src * imag_rcv, imag_src * real_rcv - real_src * imag_rcv],
-            axis=1,
-        ).astype(jnp.bfloat16)
-        out_ref[k] = jnp.dot(cross, lag, preferred_element_type=jnp.float32) * factor
-
-
-def correlate(receivers, sources, lag):
-    block, width = receivers.shape
+        for part, rcv in enumerate(receivers):
+            real_rcv = rcv[:, :bins]
+            imag_rcv = rcv[:, bins:]
+            cross = jnp.concatenate(
+                [real_src * real_rcv + imag_src * imag_rcv, imag_src * real_rcv - real_src * imag_rcv],
+                axis=1,
+            ).astype(jnp.bfloat16)
+            out_ref[k, part * half : (part + 1) * half, :] = (
+                jnp.dot(cross, lag, preferred_element_type=jnp.float32) * factor
+            )
+
+
+def correlate(low, high, half, lag):
+    rows, width = low.shape
     bins = width // 2
-    count = sources.shape[0]
+    count = 2 * (rows - half)
+    block = 2 * half
     lags = lag.shape[1]
     group = 8
     factor = 1.0 / math.sqrt(bins)
     flops = 2 * count * block * width * lags + 6 * count * block * bins
-    moved = 4 * block * width + 4 * count * width + 2 * lags * width + 4 * count * block * lags
+    moved = 4 * rows * width + 2 * lags * width + 4 * count * block * lags
     return pl.pallas_call(
-        functools.partial(correlate_kernel, factor, bins, group),
+        functools.partial(correlate_kernel, factor, bins, group, half),
         out_shape=jax.ShapeDtypeStruct((count, block, lags), jnp.float32),
         grid=(count // group,),
         in_specs=[
-            pl.BlockSpec((block, width), lambda s: (0, 0)),
-            pl.BlockSpec((count, width), lambda s: (0, 0)),
+            pl.BlockSpec((rows, width), lambda s: (0, 0)),
+            pl.BlockSpec((rows, width), lambda s: (0, 0)),
             pl.BlockSpec((width, lags), lambda s: (0, 0)),
         ],
         out_specs=pl.BlockSpec((group, block, lags), lambda s: (s, 0, 0)),
         compiler_params=pltpu.CompilerParams(dimension_semantics=("arbitrary",)),
         cost_estimate=pl.CostEstimate(flops=flops, bytes_accessed=moved, transcendentals=0),
-    )(receivers, sources, lag)
+    )(low, high, lag)
 
 
 def swap_tm(x):
@@ -156,40 +164,33 @@
     halo = lax.ppermute(records[:halo_rows], ("chan", "tm"), perm=shift)
 
     taps_matrix = decimation_matrix(fir_taps, out_rows, raw_rows + halo_rows)
-    parts = split_bf16(taps_matrix, 3)
-    stacked = jnp.concatenate(parts, axis=0)
-    dims = (((0,), (1,)), ((), ()))
-    main = lax.dot_general(records, stacked[:, :raw_rows], dims, preferred_element_type=jnp.float32)
-    tail = lax.dot_general(halo, stacked[:, raw_rows:], dims, preferred_element_type=jnp.float32)
+    stacked = jnp.concatenate(split_bf16(taps_matrix, 2), axis=0)
+    main = jnp.dot(stacked[:, :raw_rows], records, preferred_element_type=jnp.float32)
+    tail = jnp.dot(stacked[:, raw_rows:], halo, preferred_element_type=jnp.float32)
     summed = main + tail
-    decimated = (
-        summed[:, :out_rows] + summed[:, out_rows : 2 * out_rows] + summed[:, 2 * out_rows :]
-    ).astype(jnp.bfloat16)
+    decimated = (summed[:out_rows] + summed[out_rows:]).astype(jnp.bfloat16).T
 
     first, second = swap_tm(decimated)
     paired = jnp.concatenate([first, second], axis=1)
 
-    first_rows = source_owner * block + source_offset
-    own_first = lax.dynamic_index_in_dim(first_rows, tm, keepdims=False)
-    source_raw = lax.dynamic_slice_in_dim(channel_map, own_first, SRC)
-    halves = channel_map.reshape(n_chan, n_tm, half)
-    half_raw = lax.dynamic_index_in_dim(halves, tm, axis=1, keepdims=False)
+    owner = lax.dynamic_index_in_dim(source_owner, tm, keepdims=False)
+    offset = lax.dynamic_index_in_dim(source_offset, tm, keepdims=False)
+    source_raw = lax.dynamic_slice_in_dim(channel_map, owner * block + offset, SRC)
+    half_raw = lax.dynamic_slice(channel_map.reshape(n_chan, block), (0, tm * half), (n_chan, half))
     index = jnp.concatenate(
         [half_raw, jnp.broadcast_to(source_raw[None], (n_chan, SRC))], axis=1
     )
     width = index.shape[1]
     rows = jnp.take(paired, index.reshape(-1), axis=0, mode="clip").reshape(n_chan, width, -1)
     series = lax.all_to_all(rows, "chan", 0, 2, tiled=True).reshape(width, samples)
-    time_index = jnp.arange(samples, dtype=jnp.int32)
-
-    white = whiten_series(series, time_index)
+    table = dft_table(samples, bins, jnp.arange(samples, dtype=jnp.int32))
+    lag_share = LAGS // n_tm
+    first_lag = (tm * lag_share - LAGS // 2) % samples
+    lag = lax.dynamic_slice_in_dim(table, first_lag, lag_share).T.astype(jnp.bfloat16)
+
+    white = whiten_series(series, table)
     low, high = swap_tm(white)
-    receivers = jnp.concatenate([low[:half], high[:half]], axis=0).astype(jnp.float32)
-    sources = jnp.concatenate([low[half:], high[half:]], axis=0).astype(jnp.float32)
-
-    lag_share = LAGS // n_tm
-    kernel = lag_kernel(samples, tm * lag_share, lag_share)
-    result = correlate(receivers, sources, kernel)
+    result = correlate(low, high, half, lag)
     return result.reshape(STEPS, SRC, block, lag_share)
 
 

time: 63.8 us -> 60.8 us (0.953)
  waiting for transfers between devices: 10.7 us -> 0.74 us
  local copies, waits for them, and re-layouts: 9.58 us -> 15.9 us
  other arithmetic: 10.7 us -> 12.8 us
  matrix products: 9.59 us -> 8.25 us
  between operations: 2.25 us -> 1.4 us
  starting transfers between devices: 9.85 us -> 10.5 us
    all_to_all x1, waiting for transfers between devices: 9.85 us -> 0.02 us  [local(): lax.all_to_all(rows, 'chan', 0, 2, tiled=True).reshape(width, samples)]
    neg x0 -> x1, local copies, waits for them, and re-layouts: none -> 2.89 us  [dft_table(): return jnp.concatenate([cosine, -sine], axis=1)]
    convert_element_type x4, other arithmetic: 2.63 us -> 5.45 us  [split_bf16(): piece = rest.astype(jnp.bfloat16)]
    dot_general x2, matrix products: 6.35 us -> 3.95 us  [the longest x1 2.57 us: local(): jnp.dot(stacked[:, :raw_rows], records, preferred_element_type=jnp.float32)]
    another operation x1 -> x0, other arithmetic: 2.23 us -> none
    sub x1, other arithmetic: 0.61 us -> 2.63 us  [dft_table(): cosine = (ch * cl - sh * sl).reshape(samples, bins)]
    dynamic_slice x3 -> x4, local copies, waits for them, and re-layouts: 1.37 us -> 3.33 us  [the longest x1 1.24 us: local(): offset = lax.dynamic_index_in_dim(source_offset, tm, keepdims=False)]
    sub x0 -> x1, local copies, waits for them, and re-layouts: none -> 1.92 us  [dft_table(): cosine = (ch * cl - sh * sl).reshape(samples, bins)]
  transfers between devices with their start and end apart: 4 -> 4, of which waited for: 2 -> 1; matrix products, arithmetic and copies ran while one was open for 24% -> 39% of each run, Pallas kernels for 0% -> 0%
where the time goes in v5:
time: 60.8 us; the launch traced here: 60.1 us
  local copies, waits for them, and re-layouts  15.9 us (26%)
  other arithmetic  12.8 us (21%)
  starting transfers between devices  10.5 us (17%)
  Pallas kernels  10.5 us (17%)
  matrix products  8.25 us (14%)
  between operations  1.4 us (2%)
  waiting for transfers between devices  0.74 us (1%)
    pallas_call x1, Pallas kernels, correlate(): pl.pallas_call(functools.partial(correlate_kernel, factor, bins, group, h...  10.5 us
    all_to_all x1, starting transfers between devices, local(): lax.all_to_all(rows, 'chan', 0, 2, tiled=True).reshape(width, samples)  7.92 us
    convert_element_type x4, other arithmetic, split_bf16(): piece = rest.astype(jnp.bfloat16)  5.45 us
    gather x1, local copies, waits for them, and re-layouts, local(): jnp.take(paired, index.reshape(-1), axis=0, mode='clip')  4.56 us
    dot_general x1, matrix products, whiten_series(): jnp.dot(series, jnp.concatenate([hi, lo], axis=1), preferred_element_type...  3.7 us
    neg x1, local copies, waits for them, and re-layouts, dft_table(): return jnp.concatenate([cosine, -sine], axis=1)  2.89 us
    sub x1, other arithmetic, dft_table(): cosine = (ch * cl - sh * sl).reshape(samples, bins)  2.63 us
    dot_general x1, matrix products, local(): jnp.dot(stacked[:, :raw_rows], records, preferred_element_type=jnp.float32)  2.57 us
  transfers between devices with their start and end apart: 4, of which 1 were waited for; matrix products, arithmetic and copies ran while one was open for 39% of the time, Pallas kernels for 0%

profile of v5, /device:TPU:0, one launch (start us, length us, event | category | flops | bytes accessed | tf_op | source)
XLA Modules:
  0.0 60.1 jit_solution(15915736566001999464)
XLA Ops:
  0.0 0.9 %slice.34 = bf16[24,3072]{1,0:T(8,128)(2,1)S(1)} slice(bf16[512,3072]{1,0:T(8,128)(2,1)} %param.5), slice={[0:24], [0:3072]} | slice | bytes 294912 | tf_op jit(solution)/shard_map/slice | solution.py:164
  0.9 1.3 %collective-permute-start = (bf16[24,3072]{1,0:T(8,128)(2,1)S(1)}, bf16[24,3072]{1,0:T(8,128)(2,1)}, u32[]{:S(2)}, u32[]{:S(2)}) collective-permute-start(bf16[24,3072]{1,0:T(8,128)(2,1)S(1)} %slice.34), channel_id=1, source_target_pairs={{1,0},{2,1},{3,2},{4,3},{5,4},{6,5},{7,6},{8,7},{9,8},{10,9},{11,1... | collective-permute-start | bytes 442376 | tf_op jit(solution)/shard_map/ppermute | solution.py:164
  2.2 1.2 %dynamic_slice.18 = s32[1]{0:T(128)} dynamic-slice(s32[2]{0:T(128)} %param.9, s32[]{:T(128)S(6)} %select_n.83), dynamic_slice_sizes={1} | dynamic-slice | bytes 12 | tf_op jit(solution)/shard_map/jit(dynamic_index_in_dim)/dynamic_slice | solution.py:177
  3.5 1.2 %dynamic_slice.17 = s32[1]{0:T(128)} dynamic-slice(s32[2]{0:T(128)} %param.8, s32[]{:T(128)S(6)} %select_n.83), dynamic_slice_sizes={1} | dynamic-slice | bytes 12 | tf_op jit(solution)/shard_map/jit(dynamic_index_in_dim)/dynamic_slice | solution.py:176
  5.9 0.7 %reshape.160 = s32[8,384]{1,0:T(8,128)S(1)} reshape(s32[3072]{0:T(1024)} %param.7) | data formatting | bytes 24576 | tf_op jit(solution)/shard_map/reshape | solution.py:179
  6.7 0.8 %dynamic_slice.19 = s32[16]{0:T(128)S(1)} dynamic-slice(s32[3072]{0:T(1024)} %param.7, s32[]{:T(128)S(6)} %select_n.84), dynamic_slice_sizes={16} | dynamic-slice | bytes 132 | tf_op jit(solution)/shard_map/dynamic_slice | solution.py:178
  7.4 0.1 pad.13.clone
  7.5 0.7 %broadcast_in_dim.29 = f32[4,8]{1,0:T(4,128)S(1)} reshape(f32[32]{0:T(128)} %param.6) | data formatting | bytes 256 | tf_op jit(solution)/shard_map/jit(_where)/broadcast_in_dim | solution.py:38
  8.3 0.2 select_reduce_fusion
  8.5 0.2 copy.15
  8.8 0.1 constant_dynamic-slice_fusion
  8.8 2.6 %fusion.35 = f32[128,3072]{1,0:T(8,128)S(1)} fusion(bf16[512,3072]{1,0:T(8,128)(2,1)} %param.5, bf16[64,536]{0,1:T(8,128)(2,1)S(1)} %get-tuple-element.6, bf16[64,536]{0,1:T(8,128)(2,1)S(1)} %get-tuple-element.5), kind=kOutput, calls=%fused_computation.56 | convolution fusion | flops 402915328 | bytes 4855808 | tf_op jit(solution)/shard_map/dot_general | solution.py:168
  11.4 0.1 reshape.169
  11.5 0.0 collective-permute-done
  11.6 1.4 %convolution_add_fusion = f32[128,3072]{1,0:T(8,128)S(1)} fusion(f32[128,3072]{1,0:T(8,128)S(1)} %fusion.35, bf16[24,3072]{1,0:T(8,128)(2,1)} %collective-permute-done, bf16[64,536]{0,1:T(8,128)(2,1)S(1)} %get-tuple-element.5, bf16[64,536]{0,1:T(8,128)(2,1)S(1)} %get-tuple-element.6), kind=kOutput, calls=%fused_computation.9 | convolution fusion | flops 19279872 | bytes 3430400 | tf_op jit(solution)/shard_map/dot_general | solution.py:169
  12.9 0.1 fusion.31
  13.0 1.2 %collective-permute-start.1 = (bf16[3072,64]{0,1:T(8,128)(2,1)S(1)}, bf16[3072,64]{0,1:T(8,128)(2,1)S(1)}, u32[]{:S(2)}, u32[]{:S(2)}) collective-permute-start(bf16[3072,64]{0,1:T(8,128)(2,1)S(1)} %fusion.31), channel_id=1, source_target_pairs={{0,1},{1,0},{2,3},{3,2},{4,5},{5,4},{6,7},{7,6},{8,9},{9,8},{10,11... | collective-permute-start | bytes 1179656 | tf_op jit(solution)/shard_map/ppermute | solution.py:144
  14.2 0.3 fusion.49
  14.5 0.3 fusion.52
  14.8 0.7 %collective-permute-done.1 = bf16[3072,64]{0,1:T(8,128)(2,1)S(1)} collective-permute-done((bf16[3072,64]{0,1:T(8,128)(2,1)S(1)}, bf16[3072,64]{0,1:T(8,128)(2,1)S(1)}, u32[]{:S(2)}, u32[]{:S(2)}) %collective-permute-start.1) | collective-permute-done | bytes 393248 | tf_op jit(solution)/shard_map/ppermute | solution.py:144
  15.6 0.1 broadcast_select_fusion.3
  15.7 0.1 pad_maximum_fusion.1
  15.7 0.4 copy.16
  16.1 4.6 %gather_fusion = bf16[1664,128]{1,0:T(8,128)(2,1)} fusion(bf16[3072,128]{1,0:T(8,128)(2,1)S(1)} %copy.16, s32[2048]{0:T(1024)S(1)} %pad_clamp_fusion), kind=kCustom, calls=%fused_computation | custom fusion | bytes 858624 | tf_op jit(solution)/shard_map/jit(_take)/gather | solution.py:184
  20.7 7.9 %all-to-all-start = ((bf16[8,208,128]{2,1,0:T(8,128)(2,1)}), bf16[8,208,128]{2,1,0:T(8,128)(2,1)S(1)}, u32[]{:S(2)}, u32[]{:S(2)}) async-start(bf16[8,208,128]{2,1,0:T(8,128)(2,1)} %bitcast.3), calls=%async_computation | async-start | bytes 851968 | tf_op jit(solution)/shard_map/all_to_all | solution.py:185
  28.6 2.6 %multiply_subtract_fusion = (f32[32,32,512]{2,1,0:T(8,128)}, f32[32,32,512]{2,1,0:T(8,128)}) fusion(f32[32,512]{1,0:T(8,128)S(1)} %get-tuple-element.20, f32[32,512]{1,0:T(8,128)S(1)} %get-tuple-element.19, f32[32,512]{1,0:T(8,128)S(1)} %get-tuple-element.21, f32[32,512]{1,0:T(8,128)S(1)} %get-tuple-element.18), kind=kLoop, calls=%fused_computation.18 | loop fusion | flops 3670016 | bytes 4456448 | tf_op jit(solution)/shard_map/sub | solution.py:53
  31.2 1.9 %copy.18 = f32[1024,512]{0,1:T(8,128)S(1)} copy(f32[1024,512]{1,0:T(8,128)} %bitcast.30) | data formatting | bytes 4194304 | tf_op jit(solution)/shard_map/sub | solution.py:53
  33.2 2.9 %copy.19 = f32[1024,512]{0,1:T(8,128)} copy(f32[1024,512]{1,0:T(8,128)} %bitcast.29) | data formatting | bytes 4194304 | tf_op jit(solution)/shard_map/neg | solution.py:55
  36.0 0.1 abs_compare_fusion
  36.2 0.0 copy-start
  36.2 3.6 %subtract_convert_fusion = bf16[1024,1024]{0,1:T(8,128)(2,1)} fusion(f32[1024,512]{0,1:T(8,128)} %copy.19, f32[1024,512]{0,1:T(8,128)S(1)} %copy.18), kind=kLoop, calls=%fused_computation.8 | loop fusion | flops 5242880 | bytes 6291456 | tf_op jit(solution)/shard_map/convert_element_type | solution.py:26
  39.8 0.0 copy-done
  39.8 1.7 %fusion.4 = bf16[1024,1024]{0,1:T(8,128)(2,1)} fusion(f32[1024,512]{0,1:T(8,128)S(1)} %copy-done, f32[1024,512]{0,1:T(8,128)S(1)} %copy.18), kind=kLoop, calls=%fused_computation.10 | loop fusion | flops 4194304 | bytes 6291456 | tf_op jit(solution)/shard_map/convert_element_type | solution.py:26
  41.5 0.0 all-to-all-done
  41.5 0.1 copy.17
  41.6 3.7 %fusion = f32[208,2048]{1,0:T(8,128)S(1)} fusion(bf16[1024,1024]{0,1:T(8,128)(2,1)} %subtract_convert_fusion, bf16[1024,1024]{0,1:T(8,128)(2,1)} %fusion.4, bf16[26,8,8,128]{3,2,1,0:T(8,128)(2,1)S(1)} %bitcast.32), kind=kOutput, calls=%fused_computation.4 | convolution fusion | flops 880803840 | bytes 6324224 | tf_op jit(solution)/shard_map/dot_general | solution.py:77
  45.3 0.1 slice_add_fusion
  45.4 0.1 fusion.60
  45.6 0.6 multiply_convert_fusion.1
  46.2 0.1 collective-permute-start.2
  46.3 2.1 %fusion.28.lag_ref = bf16[1024,256]{1,0:T(8,128)(2,1)} fusion(s32[]{:T(128)S(6)} %select_n.90, f32[1024,512]{0,1:T(8,128)} %copy.19, f32[1024,512]{0,1:T(8,128)S(1)} %copy.18), kind=kLoop, calls=%fused_computation.35 | loop fusion | flops 1048576 | bytes 4718596 | tf_op jit(solution)/shard_map/convert_element_type | solution.py:189
  48.5 0.0 collective-permute-done.2
  48.5 1.1 %broadcast_select_fusion = (bf16[208,1024]{1,0:T(8,128)(2,1)}, bf16[208,1024]{1,0:T(8,128)(2,1)}) fusion(bf16[208,1024]{1,0:T(8,128)(2,1)S(1)} %collective-permute-done.2, pred[]{:T(512)S(6)} %eq.27, bf16[208,512]{1,0:T(8,128)(2,1)S(1)} %get-tuple-element.8, bf16[208,512]{1,0:T(8,128)(2,1)S(1)} %get-tuple-element.7), kind=kLoop, calls=%fused_computation.44 | loop fusion | flops 1277952 | bytes 1703937 | tf_op jit(solution)/shard_map/jit(_where)/select_n | solution.py:146
  49.6 10.5 %shard_map.55 = f32[32,384,256]{2,1,0:T(8,128)} custom-call(bf16[208,1024]{1,0:T(8,128)(2,1)} %get-tuple-element.10.low_ref, bf16[208,1024]{1,0:T(8,128)(2,1)} %get-tuple-element.9.high_ref, bf16[1024,256]{1,0:T(8,128)(2,1)} %fusion.28.lag_ref), custom_call_target="tpu_custom_call" | custom-call | flops 6480199680 | bytes 13959168 | tf_op jit(solution)/shard_map/pallas_call | solution.py:128
  (7 shorter events, 0.2 us)
Async XLA Ops:
  0.9 10.6 %collective-permute-start = (bf16[24,3072]{1,0:T(8,128)(2,1)S(1)}, bf16[24,3072]{1,0:T(8,128)(2,1)}, u32[]{:S(2)}, u32[]{:S(2)}) collective-permute-start(bf16[24,3072]{1,0:T(8,128)(2,1)S(1)} %slice.34), channel_id=1, source_target_pairs={{1,0},{2,1},{3,2},{4,3},{5,4},{6,5},{7,6},{8,7},{9,8},{10,9},{11,1... | collective-permute-start | bytes 442376 | tf_op jit(solution)/shard_map/ppermute | solution.py:164
  13.0 2.5 %collective-permute-start.1 = (bf16[3072,64]{0,1:T(8,128)(2,1)S(1)}, bf16[3072,64]{0,1:T(8,128)(2,1)S(1)}, u32[]{:S(2)}, u32[]{:S(2)}) collective-permute-start(bf16[3072,64]{0,1:T(8,128)(2,1)S(1)} %fusion.31), channel_id=1, source_target_pairs={{0,1},{1,0},{2,3},{3,2},{4,5},{5,4},{6,7},{7,6},{8,9},{9,8},{10,11... | collective-permute-start | bytes 1179656 | tf_op jit(solution)/shard_map/ppermute | solution.py:144
  20.7 20.8 %all-to-all-start = ((bf16[8,208,128]{2,1,0:T(8,128)(2,1)}), bf16[8,208,128]{2,1,0:T(8,128)(2,1)S(1)}, u32[]{:S(2)}, u32[]{:S(2)}) async-start(bf16[8,208,128]{2,1,0:T(8,128)(2,1)} %bitcast.3), calls=%async_computation | async-start | bytes 851968 | tf_op jit(solution)/shard_map/all_to_all | solution.py:185
  36.2 3.7 %copy-start = (f32[1024,512]{0,1:T(8,128)S(1)}, f32[1024,512]{0,1:T(8,128)}, u32[]{:S(2)}) copy-start(f32[1024,512]{0,1:T(8,128)} %copy.19) | copy-start | bytes 6291460
  46.2 2.2 %collective-permute-start.2 = (bf16[208,1024]{1,0:T(8,128)(2,1)S(1)}, bf16[208,1024]{1,0:T(8,128)(2,1)S(1)}, u32[]{:S(2)}, u32[]{:S(2)}) collective-permute-start(bf16[208,1024]{1,0:T(8,128)(2,1)S(1)} %pad_maximum_fusion.2), channel_id=1, source_target_pairs={{0,1},{1,0},{2,3},{3,2},{4,5},{5,4},{6,7},{7,6},{8,9},{9,8},{10,11... | collective-permute-start | bytes 1277960 | tf_op jit(solution)/shard_map/ppermute | solution.py:144

commit v6 on v5

--- a/solution.py
+++ b/solution.py
@@ -63,11 +63,18 @@
 
 def lag_kernel(samples, first_lag, lag_count):
     bin_count = samples // 2
-    frequency = jnp.arange(bin_count, dtype=jnp.int32)
-    shifts = first_lag + jnp.arange(lag_count, dtype=jnp.int32) - LAGS // 2
-    phases = jnp.mod(frequency[:, None] * shifts[None, :], samples)
-    angles = phases.astype(jnp.float32) * (two_pi / samples)
-    return jnp.concatenate([jnp.cos(angles), -jnp.sin(angles)], axis=0).astype(jnp.bfloat16)
+    inner = 32
+    frequency = jnp.arange(bin_count, dtype=jnp.int32)[:, None]
+    low = jnp.arange(inner, dtype=jnp.int32)[None, :]
+    high = first_lag - LAGS // 2 + jnp.arange(lag_count // inner, dtype=jnp.int32)[None, :] * inner
+    scale = two_pi / samples
+    low_angle = jnp.mod(frequency * low, samples).astype(jnp.float32) * scale
+    high_angle = jnp.mod(frequency * high, samples).astype(jnp.float32) * scale
+    cl, sl = jnp.cos(low_angle)[:, None, :], jnp.sin(low_angle)[:, None, :]
+    ch, sh = jnp.cos(high_angle)[:, :, None], jnp.sin(high_angle)[:, :, None]
+    cosine = (ch * cl - sh * sl).reshape(bin_count, lag_count)
+    sine = (sh * cl + ch * sl).reshape(bin_count, lag_count)
+    return jnp.concatenate([cosine, -sine], axis=0).astype(jnp.bfloat16)
 
 
 def whiten_series(series, table):
@@ -91,11 +98,19 @@
     return jnp.concatenate([real_part * factor, imag_part * factor], axis=1).astype(jnp.bfloat16)
 
 
-def correlate_kernel(factor, bins, group, half, low_ref, high_ref, lag_ref, out_ref):
+def correlate_kernel(factor, bins, group, half, mine_ref, other_ref, lag_ref, out_ref):
     step = pl.program_id(0)
+    first = lax.axis_index("tm") == 0
     lag = lag_ref[...]
-    receivers = [low_ref[:half, :].astype(jnp.float32), high_ref[:half, :].astype(jnp.float32)]
-    every = jnp.concatenate([low_ref[half:, :], high_ref[half:, :]], axis=0).astype(jnp.float32)
+    receivers = [mine_ref[:half, :].astype(jnp.float32), other_ref[:half, :].astype(jnp.float32)]
+    places = [jnp.where(first, 0, half), jnp.where(first, half, 0)]
+    mine_src = mine_ref[half:, :]
+    other_src = other_ref[half:, :]
+    every = jnp.where(
+        first,
+        jnp.concatenate([mine_src, other_src], axis=0),
+        jnp.concatenate([other_src, mine_src], axis=0),
+    ).astype(jnp.float32)
     picked = every[:group]
     for g in range(1, every.shape[0] // group):
         picked = jnp.where(step == g, every[g * group : (g + 1) * group], picked)
@@ -110,7 +125,7 @@
                 [real_src * real_rcv + imag_src * imag_rcv, imag_src * real_rcv - real_src * imag_rcv],
                 axis=1,
             ).astype(jnp.bfloat16)
-            out_ref[k, part * half : (part + 1) * half, :] = (
+            out_ref[k, pl.ds(pl.multiple_of(places[part], 8), half), :] = (
                 jnp.dot(cross, lag, preferred_element_type=jnp.float32) * factor
             )
 
@@ -185,12 +200,11 @@
     series = lax.all_to_all(rows, "chan", 0, 2, tiled=True).reshape(width, samples)
     table = dft_table(samples, bins, jnp.arange(samples, dtype=jnp.int32))
     lag_share = LAGS // n_tm
-    first_lag = (tm * lag_share - LAGS // 2) % samples
-    lag = lax.dynamic_slice_in_dim(table, first_lag, lag_share).T.astype(jnp.bfloat16)
+    lag = lag_kernel(samples, tm * lag_share, lag_share)
 
     white = whiten_series(series, table)
-    low, high = swap_tm(white)
-    result = correlate(low, high, half, lag)
+    other = lax.ppermute(white, "tm", perm=[(0, 1), (1, 0)])
+    result = correlate(white, other, half, lag)
     return result.reshape(STEPS, SRC, block, lag_share)
 
 

time: 60.8 us -> 61.9 us (1.018)
  waiting for transfers between devices: 0.74 us -> 7.24 us
  other arithmetic: 12.8 us -> 11.1 us
  local copies, waits for them, and re-layouts: 15.9 us -> 14.4 us
  matrix products: 8.25 us -> 6.91 us
  starting transfers between devices: 10.5 us -> 9.85 us
    all_to_all x1, waiting for transfers between devices: 0.02 us -> 7.02 us  [local(): lax.all_to_all(rows, 'chan', 0, 2, tiled=True).reshape(width, samples)]
    neg x1, local copies, waits for them, and re-layouts: 2.89 us -> 0.13 us  [lag_kernel(): return jnp.concatenate([cosine, -sine], axis=0).astype(jnp.bfloat16)]
    convert_element_type x1 -> x0, other arithmetic: 2.11 us -> none  [local(): lax.dynamic_slice_in_dim(table, first_lag, lag_share).T.astype(jnp.bfloat16)]
    unnamed x2 -> x10, local copies, waits for them, and re-layouts: 0.01 us -> 1.95 us
    sub x1, local copies, waits for them, and re-layouts: 1.92 us -> 0.13 us  [lag_kernel(): cosine = (ch * cl - sh * sl).reshape(bin_count, lag_count)]
    concatenate x1, local copies, waits for them, and re-layouts: 0.37 us -> 1.5 us  [local(): paired = jnp.concatenate([first, second], axis=1)]
    select_n x2 -> x1, other arithmetic: 1.23 us -> 0.14 us  [swap_tm(): return (jnp.where(first, x, other), jnp.where(first, other, x))]
    dot_general x1, matrix products: 1.38 us -> 0.47 us  [local(): jnp.dot(stacked[:, raw_rows:], halo, preferred_element_type=jnp.float32)]
  transfers between devices with their start and end apart: 4 -> 4, of which waited for: 1 -> 2; matrix products, arithmetic and copies ran while one was open for 39% -> 29% of each run, Pallas kernels for 0% -> 0%
where the time goes in v6:
time: 61.9 us; the launch traced here: 61.5 us
  local copies, waits for them, and re-layouts  14.4 us (23%)
  other arithmetic  11.1 us (18%)
  Pallas kernels  10.5 us (17%)
  starting transfers between devices  9.85 us (16%)
  waiting for transfers between devices  7.24 us (12%)
  matrix products  6.91 us (11%)
  between operations  1.43 us (2%)
    pallas_call x1, Pallas kernels, correlate(): pl.pallas_call(functools.partial(correlate_kernel, factor, bins, group, h...  10.5 us
    all_to_all x1, starting transfers between devices, local(): lax.all_to_all(rows, 'chan', 0, 2, tiled=True).reshape(width, samples)  7.29 us
    all_to_all x1, waiting for transfers between devices, local(): lax.all_to_all(rows, 'chan', 0, 2, tiled=True).reshape(width, samples)  7.02 us
    convert_element_type x4, other arithmetic, split_bf16(): piece = rest.astype(jnp.bfloat16)  5.41 us
    gather x1, local copies, waits for them, and re-layouts, local(): jnp.take(paired, index.reshape(-1), axis=0, mode='clip')  4.57 us
    dot_general x1, matrix products, whiten_series(): jnp.dot(series, jnp.concatenate([hi, lo], axis=1), preferred_element_type...  3.27 us
    dot_general x1, matrix products, local(): jnp.dot(stacked[:, :raw_rows], records, preferred_element_type=jnp.float32)  2.57 us
    unnamed x10, local copies, waits for them, and re-layouts  1.95 us
  transfers between devices with their start and end apart: 4, of which 2 were waited for; matrix products, arithmetic and copies ran while one was open for 29% of the time, Pallas kernels for 0%

profile of v6, /device:TPU:0, one launch (start us, length us, event | category | flops | bytes accessed | tf_op | source)
XLA Modules:
  0.0 61.5 jit_solution(4420583611641562729)
XLA Ops:
  0.0 0.9 %slice.34 = bf16[24,3072]{1,0:T(8,128)(2,1)S(1)} slice(bf16[512,3072]{1,0:T(8,128)(2,1)} %param.5), slice={[0:24], [0:3072]} | slice | bytes 294912 | tf_op jit(solution)/shard_map/slice | solution.py:179
  0.9 1.3 %collective-permute-start = (bf16[24,3072]{1,0:T(8,128)(2,1)S(1)}, bf16[24,3072]{1,0:T(8,128)(2,1)S(1)}, u32[]{:S(2)}, u32[]{:S(2)}) collective-permute-start(bf16[24,3072]{1,0:T(8,128)(2,1)S(1)} %slice.34), channel_id=1, source_target_pairs={{1,0},{2,1},{3,2},{4,3},{5,4},{6,5},{7,6},{8,7},{9,8},{10,9},{11,1... | collective-permute-start | bytes 442376 | tf_op jit(solution)/shard_map/ppermute | solution.py:179
  2.3 1.2 %dynamic_slice.15 = s32[1]{0:T(128)} dynamic-slice(s32[2]{0:T(128)} %param.9, s32[]{:T(128)S(6)} %select_n.93), dynamic_slice_sizes={1} | dynamic-slice | bytes 12 | tf_op jit(solution)/shard_map/jit(dynamic_index_in_dim)/dynamic_slice | solution.py:192
  3.5 1.2 %dynamic_slice.14 = s32[1]{0:T(128)} dynamic-slice(s32[2]{0:T(128)} %param.8, s32[]{:T(128)S(6)} %select_n.93), dynamic_slice_sizes={1} | dynamic-slice | bytes 12 | tf_op jit(solution)/shard_map/jit(dynamic_index_in_dim)/dynamic_slice | solution.py:191
  5.9 0.7 %reshape.271 = s32[8,384]{1,0:T(8,128)S(1)} reshape(s32[3072]{0:T(1024)} %param.7) | data formatting | bytes 24576 | tf_op jit(solution)/shard_map/reshape | solution.py:194
  6.6 0.8 %dynamic_slice.16 = s32[16]{0:T(128)S(1)} dynamic-slice(s32[3072]{0:T(1024)} %param.7, s32[]{:T(128)S(6)} %select_n.94), dynamic_slice_sizes={16} | dynamic-slice | bytes 132 | tf_op jit(solution)/shard_map/dynamic_slice | solution.py:193
  7.4 0.1 pad.15.clone
  7.5 0.7 %broadcast_in_dim.29 = f32[4,8]{1,0:T(4,128)S(1)} reshape(f32[32]{0:T(128)} %param.6) | data formatting | bytes 256 | tf_op jit(solution)/shard_map/jit(_where)/broadcast_in_dim | solution.py:38
  8.2 0.3 fusion.57
  8.6 0.2 select_reduce_fusion
  8.8 0.2 copy.15
  9.1 0.1 constant_dynamic-slice_fusion
  9.1 2.6 %fusion.32 = f32[128,3072]{1,0:T(8,128)S(1)} fusion(bf16[512,3072]{1,0:T(8,128)(2,1)} %param.5, bf16[64,536]{0,1:T(8,128)(2,1)S(1)} %get-tuple-element.6, bf16[64,536]{0,1:T(8,128)(2,1)S(1)} %get-tuple-element.5), kind=kOutput, calls=%fused_computation.52 | convolution fusion | flops 402915328 | bytes 4855808 | tf_op jit(solution)/shard_map/dot_general | solution.py:183
  11.7 0.1 reshape.280
  11.8 0.3 fusion.54
  12.1 0.0 collective-permute-done
  12.1 0.5 convolution_add_fusion
  12.6 1.2 %copy-done.1 = f32[128,3072]{1,0:T(8,128)} copy-done((f32[128,3072]{1,0:T(8,128)}, f32[128,3072]{1,0:T(8,128)S(1)}, u32[]{:S(2)}) %copy-start.1) | copy-done | bytes 1572888
  13.8 0.1 fusion.28
  13.8 1.2 %collective-permute-start.1 = (bf16[3072,64]{0,1:T(8,128)(2,1)S(1)}, bf16[3072,64]{0,1:T(8,128)(2,1)S(1)}, u32[]{:S(2)}, u32[]{:S(2)}) collective-permute-start(bf16[3072,64]{0,1:T(8,128)(2,1)S(1)} %fusion.28), channel_id=1, source_target_pairs={{0,1},{1,0},{2,3},{3,2},{4,5},{5,4},{6,7},{7,6},{8,9},{9,8},{10,11... | collective-permute-start | bytes 1179656 | tf_op jit(solution)/shard_map/ppermute | solution.py:159
  15.0 1.9 %multiply_subtract_fusion = (f32[32,32,512]{2,1,0:T(8,128)S(1)}, f32[32,32,512]{2,1,0:T(8,128)}) fusion(f32[32,512]{1,0:T(8,128)S(1)} %get-tuple-element.22, f32[32,512]{1,0:T(8,128)S(1)} %get-tuple-element.21, f32[32,512]{1,0:T(8,128)S(1)} %get-tuple-element.23, f32[32,512]{1,0:T(8,128)S(1)} %get-tuple-element.20), kind=kLoop, calls=%fused_computation.16 | loop fusion | flops 3670016 | bytes 4456448 | tf_op jit(solution)/shard_map/sub | solution.py:53
  17.0 0.0 collective-permute-done.1
  17.0 0.0 copy-done.2
  17.0 0.1 broadcast_select_fusion.1
  17.1 1.0 %pad_maximum_fusion.1 = bf16[3072,128]{0,1:T(8,128)(2,1)} fusion(bf16[3072,64]{0,1:T(8,128)(2,1)S(1)} %get-tuple-element.13, bf16[3072,64]{0,1:T(8,128)(2,1)S(1)} %get-tuple-element.12), kind=kLoop, calls=%fused_computation.25 | loop fusion | flops 1572864 | bytes 1572864 | tf_op jit(solution)/shard_map/concatenate | solution.py:189
  18.1 1.5 %copy.16 = bf16[3072,128]{1,0:T(8,128)(2,1)S(1)} copy(bf16[3072,128]{0,1:T(8,128)(2,1)} %pad_maximum_fusion.1) | data formatting | bytes 1572864 | tf_op jit(solution)/shard_map/concatenate | solution.py:189
  19.6 4.6 %gather_fusion = bf16[1664,128]{1,0:T(8,128)(2,1)} fusion(bf16[3072,128]{1,0:T(8,128)(2,1)S(1)} %copy.16, s32[2048]{0:T(1024)S(1)} %pad_clamp_fusion), kind=kCustom, calls=%fused_computation | custom fusion | bytes 858624 | tf_op jit(solution)/shard_map/jit(_take)/gather | solution.py:199
  24.2 7.3 %all-to-all-start = ((bf16[8,208,128]{2,1,0:T(8,128)(2,1)}), bf16[8,208,128]{2,1,0:T(8,128)(2,1)S(1)}, u32[]{:S(2)}, u32[]{:S(2)}) async-start(bf16[8,208,128]{2,1,0:T(8,128)(2,1)} %bitcast.3), calls=%async_computation | async-start | bytes 851968 | tf_op jit(solution)/shard_map/all_to_all | solution.py:200
  31.5 0.1 abs_compare_fusion
  31.6 0.0 copy-start
  31.6 3.7 %subtract_convert_fusion = bf16[1024,1024]{1,0:T(8,128)(2,1)} fusion(f32[1024,512]{1,0:T(8,128)} %bitcast.31, f32[1024,512]{1,0:T(8,128)S(1)} %bitcast.29), kind=kLoop, calls=%fused_computation.6 | loop fusion | flops 5242880 | bytes 6291456 | tf_op jit(solution)/shard_map/convert_element_type | solution.py:26
  35.3 1.6 %fusion.4 = bf16[1024,1024]{1,0:T(8,128)(2,1)} fusion(f32[1024,512]{1,0:T(8,128)S(1)} %bitcast.32, f32[1024,512]{1,0:T(8,128)S(1)} %bitcast.30), kind=kLoop, calls=%fused_computation.8 | loop fusion | flops 4194304 | bytes 6291456 | tf_op jit(solution)/shard_map/convert_element_type | solution.py:26
  36.9 0.2 fusion.65
  37.0 7.0 %all-to-all-done = bf16[8,208,128]{2,1,0:T(8,128)(2,1)S(1)} async-done(((bf16[8,208,128]{2,1,0:T(8,128)(2,1)}), bf16[8,208,128]{2,1,0:T(8,128)(2,1)S(1)}, u32[]{:S(2)}, u32[]{:S(2)}) %all-to-all-start) | async-done | bytes 426016 | tf_op jit(solution)/shard_map/all_to_all | solution.py:200
  44.0 0.1 copy.17
  44.1 3.3 %fusion = f32[208,2048]{1,0:T(8,128)S(1)} fusion(bf16[1024,1024]{1,0:T(8,128)(2,1)} %subtract_convert_fusion, bf16[1024,1024]{1,0:T(8,128)(2,1)} %fusion.4, bf16[26,8,8,128]{3,2,1,0:T(8,128)(2,1)S(1)} %bitcast.36), kind=kOutput, calls=%fused_computation.2 | convolution fusion | flops 880803840 | bytes 6324224 | tf_op jit(solution)/shard_map/dot_general | solution.py:84
  47.4 0.1 slice_add_fusion
  47.5 0.1 fusion.73
  47.7 0.6 multiply_convert_fusion.1
  48.3 0.1 collective-permute-start.2
  48.4 0.3 fusion.52
  48.7 0.1 subtract_convert_fusion.1
  48.8 0.1 copy.18
  49.0 0.1 copy.19
  49.1 0.8 %pad_maximum_fusion.2.lag_ref = bf16[1024,256]{1,0:T(8,128)(2,1)} fusion(bf16[512,256]{1,0:T(8,128)(2,1)S(1)} %copy.19, bf16[512,256]{1,0:T(8,128)(2,1)S(1)} %copy.18), kind=kLoop, calls=%fused_computation.31 | loop fusion | flops 1048576 | bytes 1048576 | tf_op jit(solution)/shard_map/concatenate | solution.py:77
  49.9 0.2 collective-permute-done.2.other_ref
  50.2 0.8 %copy-done.4 = bf16[208,1024]{1,0:T(8,128)(2,1)} copy-done((bf16[208,1024]{1,0:T(8,128)(2,1)}, bf16[208,1024]{1,0:T(8,128)(2,1)S(1)}, u32[]{:S(2)}) %copy-start.4) | copy-done | bytes 426008
  50.9 10.5 %shard_map.55 = f32[32,384,256]{2,1,0:T(8,128)} custom-call(bf16[208,1024]{1,0:T(8,128)(2,1)} %copy-done.3, bf16[208,1024]{1,0:T(8,128)(2,1)} %copy-done.4, bf16[1024,256]{1,0:T(8,128)(2,1)} %pad_maximum_fusion.2.lag_ref), custom_call_target="tpu_custom_call" | custom-call | flops 6480199680 | bytes 13959168 | tf_op jit(solution)/shard_map/pallas_call | solution.py:143
  (14 shorter events, 0.2 us)
Async XLA Ops:
  0.9 11.2 %collective-permute-start = (bf16[24,3072]{1,0:T(8,128)(2,1)S(1)}, bf16[24,3072]{1,0:T(8,128)(2,1)S(1)}, u32[]{:S(2)}, u32[]{:S(2)}) collective-permute-start(bf16[24,3072]{1,0:T(8,128)(2,1)S(1)} %slice.34), channel_id=1, source_target_pairs={{1,0},{2,1},{3,2},{4,3},{5,4},{6,5},{7,6},{8,7},{9,8},{10,9},{11,1... | collective-permute-start | bytes 442376 | tf_op jit(solution)/shard_map/ppermute | solution.py:179
  12.6 1.2 %copy-start.1 = (f32[128,3072]{1,0:T(8,128)}, f32[128,3072]{1,0:T(8,128)S(1)}, u32[]{:S(2)}) copy-start(f32[128,3072]{1,0:T(8,128)S(1)} %convolution_add_fusion) | copy-start | bytes 4718596
  13.8 3.1 %collective-permute-start.1 = (bf16[3072,64]{0,1:T(8,128)(2,1)S(1)}, bf16[3072,64]{0,1:T(8,128)(2,1)S(1)}, u32[]{:S(2)}, u32[]{:S(2)}) collective-permute-start(bf16[3072,64]{0,1:T(8,128)(2,1)S(1)} %fusion.28), channel_id=1, source_target_pairs={{0,1},{1,0},{2,3},{3,2},{4,5},{5,4},{6,7},{7,6},{8,9},{9,8},{10,11... | collective-permute-start | bytes 1179656 | tf_op jit(solution)/shard_map/ppermute | solution.py:159
  15.0 1.9 %copy-start.2 = (f32[128,3072]{1,0:T(8,128)S(1)}, f32[128,3072]{1,0:T(8,128)}, u32[]{:S(2)}) copy-start(f32[128,3072]{1,0:T(8,128)} %copy-done.1) | copy-start | bytes 4718596
  24.2 19.9 %all-to-all-start = ((bf16[8,208,128]{2,1,0:T(8,128)(2,1)}), bf16[8,208,128]{2,1,0:T(8,128)(2,1)S(1)}, u32[]{:S(2)}, u32[]{:S(2)}) async-start(bf16[8,208,128]{2,1,0:T(8,128)(2,1)} %bitcast.3), calls=%async_computation | async-start | bytes 851968 | tf_op jit(solution)/shard_map/all_to_all | solution.py:200
  31.6 3.7 %copy-start = (f32[32,32,512]{2,1,0:T(8,128)S(1)}, f32[32,32,512]{2,1,0:T(8,128)}, u32[]{:S(2)}) copy-start(f32[32,32,512]{2,1,0:T(8,128)} %get-tuple-element.15) | copy-start | bytes 6291460
  48.3 1.8 %copy-start.3 = (bf16[208,1024]{1,0:T(8,128)(2,1)}, bf16[208,1024]{1,0:T(8,128)(2,1)S(1)}, u32[]{:S(2)}) copy-start(bf16[208,1024]{1,0:T(8,128)(2,1)S(1)} %pad_maximum_fusion.3.mine_ref) | copy-start | bytes 1277956
  48.3 1.8 %collective-permute-start.2 = (bf16[208,1024]{1,0:T(8,128)(2,1)S(1)}, bf16[208,1024]{1,0:T(8,128)(2,1)S(1)}, u32[]{:S(2)}, u32[]{:S(2)}) collective-permute-start(bf16[208,1024]{1,0:T(8,128)(2,1)S(1)} %pad_maximum_fusion.3.mine_ref), channel_id=1, source_target_pairs={{0,1},{1,0},{2,3},{3,2},{4,5},{5,4},{6,7},{7,6},{8,9},{9,8},{10,11... | collective-permute-start | bytes 1277960 | tf_op jit(solution)/shard_map/ppermute | solution.py:206
  50.2 0.8 %copy-start.4 = (bf16[208,1024]{1,0:T(8,128)(2,1)}, bf16[208,1024]{1,0:T(8,128)(2,1)S(1)}, u32[]{:S(2)}) copy-start(bf16[208,1024]{1,0:T(8,128)(2,1)S(1)} %collective-permute-done.2.other_ref) | copy-start | bytes 1277956

commit v7 on v6

--- a/solution.py
+++ b/solution.py
@@ -102,7 +102,7 @@
     step = pl.program_id(0)
     first = lax.axis_index("tm") == 0
     lag = lag_ref[...]
-    receivers = [mine_ref[:half, :].astype(jnp.float32), other_ref[:half, :].astype(jnp.float32)]
+    receivers = [mine_ref[:half, :], other_ref[:half, :]]
     places = [jnp.where(first, 0, half), jnp.where(first, half, 0)]
     mine_src = mine_ref[half:, :]
     other_src = other_ref[half:, :]
@@ -110,7 +110,7 @@
         first,
         jnp.concatenate([mine_src, other_src], axis=0),
         jnp.concatenate([other_src, mine_src], axis=0),
-    ).astype(jnp.float32)
+    )
     picked = every[:group]
     for g in range(1, every.shape[0] // group):
         picked = jnp.where(step == g, every[g * group : (g + 1) * group], picked)
@@ -124,7 +124,7 @@
             cross = jnp.concatenate(
                 [real_src * real_rcv + imag_src * imag_rcv, imag_src * real_rcv - real_src * imag_rcv],
                 axis=1,
-            ).astype(jnp.bfloat16)
+            )
             out_ref[k, pl.ds(pl.multiple_of(places[part], 8), half), :] = (
                 jnp.dot(cross, lag, preferred_element_type=jnp.float32) * factor
             )

time: 61.9 us -> 61.7 us (level)
  no operation moved by 1% of the time
where the time goes in v7:
time: 61.7 us; the launch traced here: 61.2 us
  local copies, waits for them, and re-layouts  14.4 us (23%)
  other arithmetic  11.1 us (18%)
  Pallas kernels  10.3 us (17%)
  starting transfers between devices  9.85 us (16%)
  waiting for transfers between devices  7.25 us (12%)
  matrix products  6.91 us (11%)
  between operations  1.43 us (2%)
    pallas_call x1, Pallas kernels, correlate(): pl.pallas_call(functools.partial(correlate_kernel, factor, bins, group, h...  10.3 us
    all_to_all x1, starting transfers between devices, local(): lax.all_to_all(rows, 'chan', 0, 2, tiled=True).reshape(width, samples)  7.29 us
    all_to_all x1, waiting for transfers between devices, local(): lax.all_to_all(rows, 'chan', 0, 2, tiled=True).reshape(width, samples)  7.02 us
    convert_element_type x4, other arithmetic, split_bf16(): piece = rest.astype(jnp.bfloat16)  5.41 us
    gather x1, local copies, waits for them, and re-layouts, local(): jnp.take(paired, index.reshape(-1), axis=0, mode='clip')  4.57 us
    dot_general x1, matrix products, whiten_series(): jnp.dot(series, jnp.concatenate([hi, lo], axis=1), preferred_element_type...  3.27 us
    dot_general x1, matrix products, local(): jnp.dot(stacked[:, :raw_rows], records, preferred_element_type=jnp.float32)  2.57 us
    unnamed x10, local copies, waits for them, and re-layouts  1.95 us
  transfers between devices with their start and end apart: 4, of which 2 were waited for; matrix products, arithmetic and copies ran while one was open for 29% of the time, Pallas kernels for 0%

profile of v7, /device:TPU:0, one launch (start us, length us, event | category | flops | bytes accessed | tf_op | source)
XLA Modules:
  0.0 61.2 jit_solution(16054057296384050977)
XLA Ops:
  0.0 0.9 %slice.34 = bf16[24,3072]{1,0:T(8,128)(2,1)S(1)} slice(bf16[512,3072]{1,0:T(8,128)(2,1)} %param.5), slice={[0:24], [0:3072]} | slice | bytes 294912 | tf_op jit(solution)/shard_map/slice | solution.py:179
  0.9 1.3 %collective-permute-start = (bf16[24,3072]{1,0:T(8,128)(2,1)S(1)}, bf16[24,3072]{1,0:T(8,128)(2,1)S(1)}, u32[]{:S(2)}, u32[]{:S(2)}) collective-permute-start(bf16[24,3072]{1,0:T(8,128)(2,1)S(1)} %slice.34), channel_id=1, source_target_pairs={{1,0},{2,1},{3,2},{4,3},{5,4},{6,5},{7,6},{8,7},{9,8},{10,9},{11,1... | collective-permute-start | bytes 442376 | tf_op jit(solution)/shard_map/ppermute | solution.py:179
  2.3 1.2 %dynamic_slice.15 = s32[1]{0:T(128)} dynamic-slice(s32[2]{0:T(128)} %param.9, s32[]{:T(128)S(6)} %select_n.93), dynamic_slice_sizes={1} | dynamic-slice | bytes 12 | tf_op jit(solution)/shard_map/jit(dynamic_index_in_dim)/dynamic_slice | solution.py:192
  3.5 1.2 %dynamic_slice.14 = s32[1]{0:T(128)} dynamic-slice(s32[2]{0:T(128)} %param.8, s32[]{:T(128)S(6)} %select_n.93), dynamic_slice_sizes={1} | dynamic-slice | bytes 12 | tf_op jit(solution)/shard_map/jit(dynamic_index_in_dim)/dynamic_slice | solution.py:191
  5.9 0.7 %reshape.271 = s32[8,384]{1,0:T(8,128)S(1)} reshape(s32[3072]{0:T(1024)} %param.7) | data formatting | bytes 24576 | tf_op jit(solution)/shard_map/reshape | solution.py:194
  6.6 0.8 %dynamic_slice.16 = s32[16]{0:T(128)S(1)} dynamic-slice(s32[3072]{0:T(1024)} %param.7, s32[]{:T(128)S(6)} %select_n.94), dynamic_slice_sizes={16} | dynamic-slice | bytes 132 | tf_op jit(solution)/shard_map/dynamic_slice | solution.py:193
  7.4 0.1 pad.15.clone
  7.5 0.7 %broadcast_in_dim.29 = f32[4,8]{1,0:T(4,128)S(1)} reshape(f32[32]{0:T(128)} %param.6) | data formatting | bytes 256 | tf_op jit(solution)/shard_map/jit(_where)/broadcast_in_dim | solution.py:38
  8.2 0.3 fusion.57
  8.6 0.2 select_reduce_fusion
  8.8 0.2 copy.15
  9.1 0.1 constant_dynamic-slice_fusion
  9.2 2.6 %fusion.32 = f32[128,3072]{1,0:T(8,128)S(1)} fusion(bf16[512,3072]{1,0:T(8,128)(2,1)} %param.5, bf16[64,536]{0,1:T(8,128)(2,1)S(1)} %get-tuple-element.6, bf16[64,536]{0,1:T(8,128)(2,1)S(1)} %get-tuple-element.5), kind=kOutput, calls=%fused_computation.52 | convolution fusion | flops 402915328 | bytes 4855808 | tf_op jit(solution)/shard_map/dot_general | solution.py:183
  11.8 0.1 reshape.280
  11.8 0.3 fusion.54
  12.1 0.0 collective-permute-done
  12.1 0.5 convolution_add_fusion
  12.6 1.2 %copy-done.1 = f32[128,3072]{1,0:T(8,128)} copy-done((f32[128,3072]{1,0:T(8,128)}, f32[128,3072]{1,0:T(8,128)S(1)}, u32[]{:S(2)}) %copy-start.1) | copy-done | bytes 1572888
  13.8 0.1 fusion.28
  13.9 1.2 %collective-permute-start.1 = (bf16[3072,64]{0,1:T(8,128)(2,1)S(1)}, bf16[3072,64]{0,1:T(8,128)(2,1)S(1)}, u32[]{:S(2)}, u32[]{:S(2)}) collective-permute-start(bf16[3072,64]{0,1:T(8,128)(2,1)S(1)} %fusion.28), channel_id=1, source_target_pairs={{0,1},{1,0},{2,3},{3,2},{4,5},{5,4},{6,7},{7,6},{8,9},{9,8},{10,11... | collective-permute-start | bytes 1179656 | tf_op jit(solution)/shard_map/ppermute | solution.py:159
  15.1 1.9 %multiply_subtract_fusion = (f32[32,32,512]{2,1,0:T(8,128)S(1)}, f32[32,32,512]{2,1,0:T(8,128)}) fusion(f32[32,512]{1,0:T(8,128)S(1)} %get-tuple-element.22, f32[32,512]{1,0:T(8,128)S(1)} %get-tuple-element.21, f32[32,512]{1,0:T(8,128)S(1)} %get-tuple-element.23, f32[32,512]{1,0:T(8,128)S(1)} %get-tuple-element.20), kind=kLoop, calls=%fused_computation.16 | loop fusion | flops 3670016 | bytes 4456448 | tf_op jit(solution)/shard_map/sub | solution.py:53
  17.0 0.0 collective-permute-done.1
  17.0 0.0 copy-done.2
  17.0 0.1 broadcast_select_fusion.1
  17.1 1.0 %pad_maximum_fusion.1 = bf16[3072,128]{0,1:T(8,128)(2,1)} fusion(bf16[3072,64]{0,1:T(8,128)(2,1)S(1)} %get-tuple-element.13, bf16[3072,64]{0,1:T(8,128)(2,1)S(1)} %get-tuple-element.12), kind=kLoop, calls=%fused_computation.25 | loop fusion | flops 1572864 | bytes 1572864 | tf_op jit(solution)/shard_map/concatenate | solution.py:189
  18.1 1.5 %copy.16 = bf16[3072,128]{1,0:T(8,128)(2,1)S(1)} copy(bf16[3072,128]{0,1:T(8,128)(2,1)} %pad_maximum_fusion.1) | data formatting | bytes 1572864 | tf_op jit(solution)/shard_map/concatenate | solution.py:189
  19.6 4.6 %gather_fusion = bf16[1664,128]{1,0:T(8,128)(2,1)} fusion(bf16[3072,128]{1,0:T(8,128)(2,1)S(1)} %copy.16, s32[2048]{0:T(1024)S(1)} %pad_clamp_fusion), kind=kCustom, calls=%fused_computation | custom fusion | bytes 858624 | tf_op jit(solution)/shard_map/jit(_take)/gather | solution.py:199
  24.2 7.3 %all-to-all-start = ((bf16[8,208,128]{2,1,0:T(8,128)(2,1)}), bf16[8,208,128]{2,1,0:T(8,128)(2,1)S(1)}, u32[]{:S(2)}, u32[]{:S(2)}) async-start(bf16[8,208,128]{2,1,0:T(8,128)(2,1)} %bitcast.3), calls=%async_computation | async-start | bytes 851968 | tf_op jit(solution)/shard_map/all_to_all | solution.py:200
  31.5 0.1 abs_compare_fusion
  31.6 0.0 copy-start
  31.6 3.7 %subtract_convert_fusion = bf16[1024,1024]{1,0:T(8,128)(2,1)} fusion(f32[1024,512]{1,0:T(8,128)} %bitcast.31, f32[1024,512]{1,0:T(8,128)S(1)} %bitcast.29), kind=kLoop, calls=%fused_computation.6 | loop fusion | flops 5242880 | bytes 6291456 | tf_op jit(solution)/shard_map/convert_element_type | solution.py:26
  35.3 1.6 %fusion.4 = bf16[1024,1024]{1,0:T(8,128)(2,1)} fusion(f32[1024,512]{1,0:T(8,128)S(1)} %bitcast.32, f32[1024,512]{1,0:T(8,128)S(1)} %bitcast.30), kind=kLoop, calls=%fused_computation.8 | loop fusion | flops 4194304 | bytes 6291456 | tf_op jit(solution)/shard_map/convert_element_type | solution.py:26
  36.9 0.2 fusion.65
  37.0 7.0 %all-to-all-done = bf16[8,208,128]{2,1,0:T(8,128)(2,1)S(1)} async-done(((bf16[8,208,128]{2,1,0:T(8,128)(2,1)}), bf16[8,208,128]{2,1,0:T(8,128)(2,1)S(1)}, u32[]{:S(2)}, u32[]{:S(2)}) %all-to-all-start) | async-done | bytes 426016 | tf_op jit(solution)/shard_map/all_to_all | solution.py:200
  44.0 0.1 copy.17
  44.2 3.3 %fusion = f32[208,2048]{1,0:T(8,128)S(1)} fusion(bf16[1024,1024]{1,0:T(8,128)(2,1)} %subtract_convert_fusion, bf16[1024,1024]{1,0:T(8,128)(2,1)} %fusion.4, bf16[26,8,8,128]{3,2,1,0:T(8,128)(2,1)S(1)} %bitcast.36), kind=kOutput, calls=%fused_computation.2 | convolution fusion | flops 880803840 | bytes 6324224 | tf_op jit(solution)/shard_map/dot_general | solution.py:84
  47.4 0.1 slice_add_fusion
  47.5 0.1 fusion.73
  47.7 0.6 multiply_convert_fusion.1
  48.3 0.1 collective-permute-start.2
  48.4 0.3 fusion.52
  48.7 0.1 subtract_convert_fusion.1
  48.8 0.1 copy.18
  49.0 0.1 copy.19
  49.1 0.8 %pad_maximum_fusion.2.lag_ref = bf16[1024,256]{1,0:T(8,128)(2,1)} fusion(bf16[512,256]{1,0:T(8,128)(2,1)S(1)} %copy.19, bf16[512,256]{1,0:T(8,128)(2,1)S(1)} %copy.18), kind=kLoop, calls=%fused_computation.31 | loop fusion | flops 1048576 | bytes 1048576 | tf_op jit(solution)/shard_map/concatenate | solution.py:77
  50.0 0.2 collective-permute-done.2.other_ref
  50.2 0.8 %copy-done.4 = bf16[208,1024]{1,0:T(8,128)(2,1)} copy-done((bf16[208,1024]{1,0:T(8,128)(2,1)}, bf16[208,1024]{1,0:T(8,128)(2,1)S(1)}, u32[]{:S(2)}) %copy-start.4) | copy-done | bytes 426008
  50.9 10.3 %shard_map.55 = f32[32,384,256]{2,1,0:T(8,128)} custom-call(bf16[208,1024]{1,0:T(8,128)(2,1)} %copy-done.3, bf16[208,1024]{1,0:T(8,128)(2,1)} %copy-done.4, bf16[1024,256]{1,0:T(8,128)(2,1)} %pad_maximum_fusion.2.lag_ref), custom_call_target="tpu_custom_call" | custom-call | flops 6480199680 | bytes 13959168 | tf_op jit(solution)/shard_map/pallas_call | solution.py:143
  (14 shorter events, 0.2 us)
Async XLA Ops:
  0.9 11.2 %collective-permute-start = (bf16[24,3072]{1,0:T(8,128)(2,1)S(1)}, bf16[24,3072]{1,0:T(8,128)(2,1)S(1)}, u32[]{:S(2)}, u32[]{:S(2)}) collective-permute-start(bf16[24,3072]{1,0:T(8,128)(2,1)S(1)} %slice.34), channel_id=1, source_target_pairs={{1,0},{2,1},{3,2},{4,3},{5,4},{6,5},{7,6},{8,7},{9,8},{10,9},{11,1... | collective-permute-start | bytes 442376 | tf_op jit(solution)/shard_map/ppermute | solution.py:179
  12.6 1.2 %copy-start.1 = (f32[128,3072]{1,0:T(8,128)}, f32[128,3072]{1,0:T(8,128)S(1)}, u32[]{:S(2)}) copy-start(f32[128,3072]{1,0:T(8,128)S(1)} %convolution_add_fusion) | copy-start | bytes 4718596
  13.9 3.1 %collective-permute-start.1 = (bf16[3072,64]{0,1:T(8,128)(2,1)S(1)}, bf16[3072,64]{0,1:T(8,128)(2,1)S(1)}, u32[]{:S(2)}, u32[]{:S(2)}) collective-permute-start(bf16[3072,64]{0,1:T(8,128)(2,1)S(1)} %fusion.28), channel_id=1, source_target_pairs={{0,1},{1,0},{2,3},{3,2},{4,5},{5,4},{6,7},{7,6},{8,9},{9,8},{10,11... | collective-permute-start | bytes 1179656 | tf_op jit(solution)/shard_map/ppermute | solution.py:159
  15.1 1.9 %copy-start.2 = (f32[128,3072]{1,0:T(8,128)S(1)}, f32[128,3072]{1,0:T(8,128)}, u32[]{:S(2)}) copy-start(f32[128,3072]{1,0:T(8,128)} %copy-done.1) | copy-start | bytes 4718596
  24.2 19.9 %all-to-all-start = ((bf16[8,208,128]{2,1,0:T(8,128)(2,1)}), bf16[8,208,128]{2,1,0:T(8,128)(2,1)S(1)}, u32[]{:S(2)}, u32[]{:S(2)}) async-start(bf16[8,208,128]{2,1,0:T(8,128)(2,1)} %bitcast.3), calls=%async_computation | async-start | bytes 851968 | tf_op jit(solution)/shard_map/all_to_all | solution.py:200
  31.6 3.7 %copy-start = (f32[32,32,512]{2,1,0:T(8,128)S(1)}, f32[32,32,512]{2,1,0:T(8,128)}, u32[]{:S(2)}) copy-start(f32[32,32,512]{2,1,0:T(8,128)} %get-tuple-element.15) | copy-start | bytes 6291460
  48.3 1.8 %copy-start.3 = (bf16[208,1024]{1,0:T(8,128)(2,1)}, bf16[208,1024]{1,0:T(8,128)(2,1)S(1)}, u32[]{:S(2)}) copy-start(bf16[208,1024]{1,0:T(8,128)(2,1)S(1)} %pad_maximum_fusion.3.mine_ref) | copy-start | bytes 1277956
  48.3 1.8 %collective-permute-start.2 = (bf16[208,1024]{1,0:T(8,128)(2,1)S(1)}, bf16[208,1024]{1,0:T(8,128)(2,1)S(1)}, u32[]{:S(2)}, u32[]{:S(2)}) collective-permute-start(bf16[208,1024]{1,0:T(8,128)(2,1)S(1)} %pad_maximum_fusion.3.mine_ref), channel_id=1, source_target_pairs={{0,1},{1,0},{2,3},{3,2},{4,5},{5,4},{6,7},{7,6},{8,9},{9,8},{10,11... | collective-permute-start | bytes 1277960 | tf_op jit(solution)/shard_map/ppermute | solution.py:206
  50.2 0.8 %copy-start.4 = (bf16[208,1024]{1,0:T(8,128)(2,1)}, bf16[208,1024]{1,0:T(8,128)(2,1)S(1)}, u32[]{:S(2)}) copy-start(bf16[208,1024]{1,0:T(8,128)(2,1)S(1)} %collective-permute-done.2.other_ref) | copy-start | bytes 1277956

commit v8 on v6

--- a/solution.py
+++ b/solution.py
@@ -30,13 +30,10 @@
 
 
 def decimation_matrix(fir_taps, out_rows, in_rows):
-    leads = TAPS // STRIDE
-    rows = jnp.arange(out_rows, dtype=jnp.int32)[:, None, None, None]
-    groups = jnp.arange(in_rows // STRIDE, dtype=jnp.int32)[None, :, None, None]
-    lead = jnp.arange(leads, dtype=jnp.int32)[None, None, :, None]
-    taps = fir_taps.reshape(1, 1, leads, STRIDE)
-    matrix = jnp.where(groups - rows == lead, taps, 0.0).sum(axis=2)
-    return matrix.reshape(out_rows, in_rows)
+    rows = jnp.arange(out_rows, dtype=jnp.int32)[:, None, None]
+    cols = jnp.arange(in_rows, dtype=jnp.int32)[None, :, None]
+    tap = jnp.arange(TAPS, dtype=jnp.int32)[None, None, :]
+    return jnp.where(cols - STRIDE * rows == tap, fir_taps[None, None, :], 0.0).sum(axis=2)
 
 
 def dft_table(samples, bins, time_index):
@@ -183,14 +180,14 @@
     main = jnp.dot(stacked[:, :raw_rows], records, preferred_element_type=jnp.float32)
     tail = jnp.dot(stacked[:, raw_rows:], halo, preferred_element_type=jnp.float32)
     summed = main + tail
-    decimated = (summed[:out_rows] + summed[out_rows:]).astype(jnp.bfloat16).T
+    decimated = (summed[:out_rows] + summed[out_rows:]).astype(jnp.bfloat16)
 
     first, second = swap_tm(decimated)
-    paired = jnp.concatenate([first, second], axis=1)
-
-    owner = lax.dynamic_index_in_dim(source_owner, tm, keepdims=False)
-    offset = lax.dynamic_index_in_dim(source_offset, tm, keepdims=False)
-    source_raw = lax.dynamic_slice_in_dim(channel_map, owner * block + offset, SRC)
+    paired = jnp.concatenate([first, second], axis=0).T
+
+    steps = jnp.arange(source_owner.shape[0], dtype=jnp.int32)
+    own_first = jnp.sum(jnp.where(steps == tm, source_owner * block + source_offset, 0))
+    source_raw = lax.dynamic_slice_in_dim(channel_map, own_first, SRC)
     half_raw = lax.dynamic_slice(channel_map.reshape(n_chan, block), (0, tm * half), (n_chan, half))
     index = jnp.concatenate(
         [half_raw, jnp.broadcast_to(source_raw[None], (n_chan, SRC))], axis=1

time: 61.9 us -> 62.3 us (level)
  local copies, waits for them, and re-layouts: 14.4 us -> 11.1 us
  other arithmetic: 11.1 us -> 14.2 us
  between operations: 1.43 us -> 2.18 us
    reduce_sum x1 -> x2, other arithmetic: 0.23 us -> 3.35 us  [the longest x1 2.04 us: decimation_matrix(): jnp.where(cols - STRIDE * rows == tap, fir_taps[None, None, :], 0.0)]
    dynamic_slice x3 -> x1, local copies, waits for them, and re-layouts: 3.21 us -> 0.77 us  [local(): source_raw = lax.dynamic_slice_in_dim(channel_map, own_first, SRC)]
    concatenate x1 -> x0, local copies, waits for them, and re-layouts: 1.5 us -> none  [local(): paired = jnp.concatenate([first, second], axis=1)]
    transpose x0 -> x1, local copies, waits for them, and re-layouts: none -> 1.5 us  [local(): paired = jnp.concatenate([first, second], axis=0).T]
    concatenate x1 -> x0, other arithmetic: 0.95 us -> none  [local(): paired = jnp.concatenate([first, second], axis=1)]
    transpose x1, other arithmetic: 0.07 us -> 0.97 us  [local(): paired = jnp.concatenate([first, second], axis=0).T]
    broadcast_in_dim x1 -> x0, local copies, waits for them, and re-layouts: 0.74 us -> none  [decimation_matrix(): matrix = jnp.where(groups - rows == lead, taps, 0.0).sum(axis=2)]
  transfers between devices with their start and end apart: 4 -> 4, of which waited for: 2 -> 2; matrix products, arithmetic and copies ran while one was open for 29% -> 28% of each run, Pallas kernels for 0% -> 0%
where the time goes in v8:
time: 62.3 us; the launch traced here: 61.8 us
  other arithmetic  14.2 us (23%)
  local copies, waits for them, and re-layouts  11.1 us (18%)
  Pallas kernels  10.5 us (17%)
  starting transfers between devices  9.85 us (16%)
  waiting for transfers between devices  7.25 us (12%)
  matrix products  6.69 us (11%)
  between operations  2.18 us (3%)
    pallas_call x1, Pallas kernels, correlate(): pl.pallas_call(functools.partial(correlate_kernel, factor, bins, group, h...  10.5 us
    all_to_all x1, starting transfers between devices, local(): lax.all_to_all(rows, 'chan', 0, 2, tiled=True).reshape(width, samples)  7.28 us
    all_to_all x1, waiting for transfers between devices, local(): lax.all_to_all(rows, 'chan', 0, 2, tiled=True).reshape(width, samples)  7.03 us
    convert_element_type x4, other arithmetic, split_bf16(): piece = rest.astype(jnp.bfloat16)  5.38 us
    gather x1, local copies, waits for them, and re-layouts, local(): jnp.take(paired, index.reshape(-1), axis=0, mode='clip')  4.6 us
    dot_general x1, matrix products, whiten_series(): jnp.dot(series, jnp.concatenate([hi, lo], axis=1), preferred_element_type...  3.28 us
    dot_general x1, matrix products, local(): jnp.dot(stacked[:, :raw_rows], records, preferred_element_type=jnp.float32)  2.47 us
    reduce_sum x1, other arithmetic, decimation_matrix(): jnp.where(cols - STRIDE * rows == tap, fir_taps[None, None, :], 0.0)  2.04 us
  transfers between devices with their start and end apart: 4, of which 2 were waited for; matrix products, arithmetic and copies ran while one was open for 28% of the time, Pallas kernels for 0%

profile of v8, /device:TPU:0, one launch (start us, length us, event | category | flops | bytes accessed | tf_op | source)
XLA Modules:
  0.0 61.8 jit_solution(1505600274870901650)
XLA Ops:
  0.0 0.9 %slice.34 = bf16[24,3072]{1,0:T(8,128)(2,1)S(1)} slice(bf16[512,3072]{1,0:T(8,128)(2,1)} %param.5), slice={[0:24], [0:3072]} | slice | bytes 294912 | tf_op jit(solution)/shard_map/slice | solution.py:176
  0.9 1.3 %collective-permute-start = (bf16[24,3072]{1,0:T(8,128)(2,1)S(1)}, bf16[24,3072]{1,0:T(8,128)(2,1)S(1)}, u32[]{:S(2)}, u32[]{:S(2)}) collective-permute-start(bf16[24,3072]{1,0:T(8,128)(2,1)S(1)} %slice.34), channel_id=1, source_target_pairs={{1,0},{2,1},{3,2},{4,3},{5,4},{6,5},{7,6},{8,7},{9,8},{10,9},{11,1... | collective-permute-start | bytes 442376 | tf_op jit(solution)/shard_map/ppermute | solution.py:176
  2.3 1.3 %fusion.65 = s32[]{:T(128)} fusion(s32[2]{0:T(128)} %param.9, s32[2]{0:T(128)} %param.8, s32[]{:T(128)S(6)} %axis_index.16), kind=kLoop, calls=%fused_computation.101 | loop fusion | flops 9 | bytes 24 | tf_op jit(solution)/shard_map/reduce_sum | solution.py:189
  4.9 0.7 %reshape.270 = s32[8,384]{1,0:T(8,128)S(1)} reshape(s32[3072]{0:T(1024)} %param.7) | data formatting | bytes 24576 | tf_op jit(solution)/shard_map/reshape | solution.py:191
  6.2 0.8 %dynamic_slice.7 = s32[16]{0:T(128)S(1)} dynamic-slice(s32[3072]{0:T(1024)} %param.7, s32[]{:T(128)S(6)} %select_n.93), dynamic_slice_sizes={16} | dynamic-slice | bytes 132 | tf_op jit(solution)/shard_map/dynamic_slice | solution.py:190
  7.0 0.1 pad.15.clone
  7.1 0.3 fusion.56
  7.4 0.1 iota_subtract_fusion
  7.5 2.0 %select_reduce_fusion = f32[64,536]{1,0:T(8,128)S(1)} fusion(f32[32]{0:T(128)} %param.6, s32[64,536]{1,0:T(8,128)S(1)} %iota_subtract_fusion), kind=kLoop, calls=%fused_computation.1 | loop fusion | flops 3258880 | bytes 274560 | tf_op jit(solution)/shard_map/reduce_sum | solution.py:36
  9.6 0.1 constant_dynamic-slice_fusion
  9.7 2.5 %fusion.30 = f32[128,3072]{1,0:T(8,128)S(1)} fusion(bf16[512,3072]{1,0:T(8,128)(2,1)} %param.5, bf16[64,536]{1,0:T(8,128)(2,1)S(1)} %get-tuple-element.6, bf16[64,536]{1,0:T(8,128)(2,1)S(1)} %get-tuple-element.5), kind=kOutput, calls=%fused_computation.51 | convolution fusion | flops 402915328 | bytes 4855808 | tf_op jit(solution)/shard_map/dot_general | solution.py:180
  12.1 0.1 reshape.279
  12.2 0.3 fusion.53
  12.5 0.0 collective-permute-done
  12.5 0.4 convolution_add_fusion
  12.9 0.0 copy-start.1
  12.9 1.2 %copy-done.1 = f32[128,3072]{1,0:T(8,128)} copy-done((f32[128,3072]{1,0:T(8,128)}, f32[128,3072]{1,0:T(8,128)S(1)}, u32[]{:S(2)}) %copy-start.1) | copy-done | bytes 1572888
  14.0 0.1 fusion.20
  14.1 1.2 %collective-permute-start.1 = (bf16[64,3072]{1,0:T(8,128)(2,1)S(1)}, bf16[64,3072]{1,0:T(8,128)(2,1)S(1)}, u32[]{:S(2)}, u32[]{:S(2)}) collective-permute-start(bf16[64,3072]{1,0:T(8,128)(2,1)S(1)} %fusion.20), channel_id=1, source_target_pairs={{0,1},{1,0},{2,3},{3,2},{4,5},{5,4},{6,7},{7,6},{8,9},{9,8},{10,11... | collective-permute-start | bytes 1179656 | tf_op jit(solution)/shard_map/ppermute | solution.py:156
  15.3 1.9 %multiply_subtract_fusion = (f32[32,32,512]{2,1,0:T(8,128)S(1)}, f32[32,32,512]{2,1,0:T(8,128)}) fusion(f32[32,512]{1,0:T(8,128)S(1)} %get-tuple-element.22, f32[32,512]{1,0:T(8,128)S(1)} %get-tuple-element.21, f32[32,512]{1,0:T(8,128)S(1)} %get-tuple-element.23, f32[32,512]{1,0:T(8,128)S(1)} %get-tuple-element.20), kind=kLoop, calls=%fused_computation.18 | loop fusion | flops 3670016 | bytes 4456448 | tf_op jit(solution)/shard_map/sub | solution.py:50
  17.3 0.0 collective-permute-done.1
  17.3 0.0 copy-done.2
  17.3 0.1 broadcast_select_fusion.1
  17.4 1.0 %maximum_bitcast_fusion = bf16[3072,128]{0,1:T(8,128)(2,1)} fusion(bf16[64,3072]{1,0:T(8,128)(2,1)S(1)} %get-tuple-element.13, bf16[64,3072]{1,0:T(8,128)(2,1)S(1)} %get-tuple-element.12), kind=kLoop, calls=%fused_computation.26 | loop fusion | flops 1572864 | bytes 1572864 | tf_op jit(solution)/shard_map/transpose | solution.py:186
  18.4 1.5 %copy.15 = bf16[3072,128]{1,0:T(8,128)(2,1)S(1)} copy(bf16[3072,128]{0,1:T(8,128)(2,1)} %maximum_bitcast_fusion) | data formatting | bytes 1572864 | tf_op jit(solution)/shard_map/transpose | solution.py:186
  19.9 4.6 %gather_fusion = bf16[1664,128]{1,0:T(8,128)(2,1)} fusion(bf16[3072,128]{1,0:T(8,128)(2,1)S(1)} %copy.15, s32[2048]{0:T(1024)S(1)} %pad_clamp_fusion), kind=kCustom, calls=%fused_computation | custom fusion | bytes 858624 | tf_op jit(solution)/shard_map/jit(_take)/gather | solution.py:196
  24.5 7.3 %all-to-all-start = ((bf16[8,208,128]{2,1,0:T(8,128)(2,1)}), bf16[8,208,128]{2,1,0:T(8,128)(2,1)S(1)}, u32[]{:S(2)}, u32[]{:S(2)}) async-start(bf16[8,208,128]{2,1,0:T(8,128)(2,1)} %bitcast.1), calls=%async_computation | async-start | bytes 851968 | tf_op jit(solution)/shard_map/all_to_all | solution.py:197
  31.8 0.1 abs_compare_fusion
  31.9 0.0 copy-start
  31.9 3.7 %subtract_convert_fusion = bf16[1024,1024]{1,0:T(8,128)(2,1)} fusion(f32[1024,512]{1,0:T(8,128)} %bitcast.22, f32[1024,512]{1,0:T(8,128)S(1)} %bitcast.20), kind=kLoop, calls=%fused_computation.8 | loop fusion | flops 5242880 | bytes 6291456 | tf_op jit(solution)/shard_map/convert_element_type | solution.py:26
  35.6 0.0 copy-done
  35.6 1.6 %fusion.4 = bf16[1024,1024]{1,0:T(8,128)(2,1)} fusion(f32[1024,512]{1,0:T(8,128)S(1)} %bitcast.23, f32[1024,512]{1,0:T(8,128)S(1)} %bitcast.21), kind=kLoop, calls=%fused_computation.10 | loop fusion | flops 4194304 | bytes 6291456 | tf_op jit(solution)/shard_map/convert_element_type | solution.py:26
  37.2 0.2 fusion.64
  37.3 7.0 %all-to-all-done = bf16[8,208,128]{2,1,0:T(8,128)(2,1)S(1)} async-done(((bf16[8,208,128]{2,1,0:T(8,128)(2,1)}), bf16[8,208,128]{2,1,0:T(8,128)(2,1)S(1)}, u32[]{:S(2)}, u32[]{:S(2)}) %all-to-all-start) | async-done | bytes 426016 | tf_op jit(solution)/shard_map/all_to_all | solution.py:197
  44.4 0.1 copy.16
  44.5 3.3 %fusion = f32[208,2048]{1,0:T(8,128)S(1)} fusion(bf16[1024,1024]{1,0:T(8,128)(2,1)} %subtract_convert_fusion, bf16[1024,1024]{1,0:T(8,128)(2,1)} %fusion.4, bf16[26,8,8,128]{3,2,1,0:T(8,128)(2,1)S(1)} %bitcast.27), kind=kOutput, calls=%fused_computation.4 | convolution fusion | flops 880803840 | bytes 6324224 | tf_op jit(solution)/shard_map/dot_general | solution.py:81
  47.8 0.1 slice_add_fusion
  47.9 0.1 fusion.72
  48.0 0.6 multiply_convert_fusion.1
  48.7 0.1 collective-permute-start.2
  48.7 0.3 fusion.51
  49.0 0.1 subtract_convert_fusion.1
  49.2 0.1 copy.17
  49.3 0.1 copy.18
  49.4 0.8 %pad_maximum_fusion.1.lag_ref = bf16[1024,256]{1,0:T(8,128)(2,1)} fusion(bf16[512,256]{1,0:T(8,128)(2,1)S(1)} %copy.18, bf16[512,256]{1,0:T(8,128)(2,1)S(1)} %copy.17), kind=kLoop, calls=%fused_computation.32 | loop fusion | flops 1048576 | bytes 1048576 | tf_op jit(solution)/shard_map/concatenate | solution.py:74
  50.3 0.2 collective-permute-done.2.other_ref
  50.5 0.8 %copy-done.4 = bf16[208,1024]{1,0:T(8,128)(2,1)} copy-done((bf16[208,1024]{1,0:T(8,128)(2,1)}, bf16[208,1024]{1,0:T(8,128)(2,1)S(1)}, u32[]{:S(2)}) %copy-start.4) | copy-done | bytes 426008
  51.3 10.5 %shard_map.55 = f32[32,384,256]{2,1,0:T(8,128)} custom-call(bf16[208,1024]{1,0:T(8,128)(2,1)} %copy-done.3, bf16[208,1024]{1,0:T(8,128)(2,1)} %copy-done.4, bf16[1024,256]{1,0:T(8,128)(2,1)} %pad_maximum_fusion.1.lag_ref), custom_call_target="tpu_custom_call" | custom-call | flops 6480199680 | bytes 13959168 | tf_op jit(solution)/shard_map/pallas_call | solution.py:140
  (11 shorter events, 0.1 us)
Async XLA Ops:
  0.9 11.6 %collective-permute-start = (bf16[24,3072]{1,0:T(8,128)(2,1)S(1)}, bf16[24,3072]{1,0:T(8,128)(2,1)S(1)}, u32[]{:S(2)}, u32[]{:S(2)}) collective-permute-start(bf16[24,3072]{1,0:T(8,128)(2,1)S(1)} %slice.34), channel_id=1, source_target_pairs={{1,0},{2,1},{3,2},{4,3},{5,4},{6,5},{7,6},{8,7},{9,8},{10,9},{11,1... | collective-permute-start | bytes 442376 | tf_op jit(solution)/shard_map/ppermute | solution.py:176
  12.9 1.2 %copy-start.1 = (f32[128,3072]{1,0:T(8,128)}, f32[128,3072]{1,0:T(8,128)S(1)}, u32[]{:S(2)}) copy-start(f32[128,3072]{1,0:T(8,128)S(1)} %convolution_add_fusion) | copy-start | bytes 4718596
  14.1 3.2 %collective-permute-start.1 = (bf16[64,3072]{1,0:T(8,128)(2,1)S(1)}, bf16[64,3072]{1,0:T(8,128)(2,1)S(1)}, u32[]{:S(2)}, u32[]{:S(2)}) collective-permute-start(bf16[64,3072]{1,0:T(8,128)(2,1)S(1)} %fusion.20), channel_id=1, source_target_pairs={{0,1},{1,0},{2,3},{3,2},{4,5},{5,4},{6,7},{7,6},{8,9},{9,8},{10,11... | collective-permute-start | bytes 1179656 | tf_op jit(solution)/shard_map/ppermute | solution.py:156
  15.3 1.9 %copy-start.2 = (f32[128,3072]{1,0:T(8,128)S(1)}, f32[128,3072]{1,0:T(8,128)}, u32[]{:S(2)}) copy-start(f32[128,3072]{1,0:T(8,128)} %copy-done.1) | copy-start | bytes 4718596
  24.5 19.9 %all-to-all-start = ((bf16[8,208,128]{2,1,0:T(8,128)(2,1)}), bf16[8,208,128]{2,1,0:T(8,128)(2,1)S(1)}, u32[]{:S(2)}, u32[]{:S(2)}) async-start(bf16[8,208,128]{2,1,0:T(8,128)(2,1)} %bitcast.1), calls=%async_computation | async-start | bytes 851968 | tf_op jit(solution)/shard_map/all_to_all | solution.py:197
  31.9 3.7 %copy-start = (f32[32,32,512]{2,1,0:T(8,128)S(1)}, f32[32,32,512]{2,1,0:T(8,128)}, u32[]{:S(2)}) copy-start(f32[32,32,512]{2,1,0:T(8,128)} %get-tuple-element.15) | copy-start | bytes 6291460
  48.6 1.8 %copy-start.3 = (bf16[208,1024]{1,0:T(8,128)(2,1)}, bf16[208,1024]{1,0:T(8,128)(2,1)S(1)}, u32[]{:S(2)}) copy-start(bf16[208,1024]{1,0:T(8,128)(2,1)S(1)} %pad_maximum_fusion.2.mine_ref) | copy-start | bytes 1277956
  48.7 1.8 %collective-permute-start.2 = (bf16[208,1024]{1,0:T(8,128)(2,1)S(1)}, bf16[208,1024]{1,0:T(8,128)(2,1)S(1)}, u32[]{:S(2)}, u32[]{:S(2)}) collective-permute-start(bf16[208,1024]{1,0:T(8,128)(2,1)S(1)} %pad_maximum_fusion.2.mine_ref), channel_id=1, source_target_pairs={{0,1},{1,0},{2,3},{3,2},{4,5},{5,4},{6,7},{7,6},{8,9},{9,8},{10,11... | collective-permute-start | bytes 1277960 | tf_op jit(solution)/shard_map/ppermute | solution.py:203
  50.5 0.8 %copy-start.4 = (bf16[208,1024]{1,0:T(8,128)(2,1)}, bf16[208,1024]{1,0:T(8,128)(2,1)S(1)}, u32[]{:S(2)}) copy-start(bf16[208,1024]{1,0:T(8,128)(2,1)S(1)} %collective-permute-done.2.other_ref) | copy-start | bytes 1277956

commit v9 on v8

--- a/solution.py
+++ b/solution.py
@@ -95,7 +95,7 @@
     return jnp.concatenate([real_part * factor, imag_part * factor], axis=1).astype(jnp.bfloat16)
 
 
-def correlate_kernel(factor, bins, group, half, mine_ref, other_ref, lag_ref, out_ref):
+def correlate_kernel(factor, bins, group, half, mine_ref, other_ref, lag_ref, out_ref, cross_ref):
     step = pl.program_id(0)
     first = lax.axis_index("tm") == 0
     lag = lag_ref[...]
@@ -118,13 +118,15 @@
         for part, rcv in enumerate(receivers):
             real_rcv = rcv[:, :bins]
             imag_rcv = rcv[:, bins:]
-            cross = jnp.concatenate(
-                [real_src * real_rcv + imag_src * imag_rcv, imag_src * real_rcv - real_src * imag_rcv],
-                axis=1,
-            ).astype(jnp.bfloat16)
-            out_ref[k, pl.ds(pl.multiple_of(places[part], 8), half), :] = (
-                jnp.dot(cross, lag, preferred_element_type=jnp.float32) * factor
+            at = pl.multiple_of(k * 2 * half + places[part], 8)
+            cross_ref[pl.ds(at, half), :bins] = (real_src * real_rcv + imag_src * imag_rcv).astype(
+                jnp.bfloat16
             )
+            cross_ref[pl.ds(at, half), bins:] = (imag_src * real_rcv - real_src * imag_rcv).astype(
+                jnp.bfloat16
+            )
+    total = jnp.dot(cross_ref[...], lag, preferred_element_type=jnp.float32) * factor
+    out_ref[...] = total.reshape(out_ref.shape)
 
 
 def correlate(low, high, half, lag):
@@ -147,7 +149,10 @@
             pl.BlockSpec((width, lags), lambda s: (0, 0)),
         ],
         out_specs=pl.BlockSpec((group, block, lags), lambda s: (s, 0, 0)),
-        compiler_params=pltpu.CompilerParams(dimension_semantics=("arbitrary",)),
+        scratch_shapes=[pltpu.VMEM((group * block, width), jnp.bfloat16)],
+        compiler_params=pltpu.CompilerParams(
+            dimension_semantics=("arbitrary",), vmem_limit_bytes=48 * 1024 * 1024
+        ),
         cost_estimate=pl.CostEstimate(flops=flops, bytes_accessed=moved, transcendentals=0),
     )(low, high, lag)
 

time: 62.3 us -> 66.3 us (1.064)
  Pallas kernels: 10.5 us -> 14.7 us
  other arithmetic: 14.2 us -> 13.4 us
  local copies, waits for them, and re-layouts: 11.1 us -> 10.3 us
  waiting for transfers between devices: 7.25 us -> 8.04 us
    pallas_call x1, Pallas kernels: 10.5 us -> 14.7 us  [correlate(): pl.pallas_call(functools.partial(correlate_kernel, factor, bins, group, h...]
    concatenate x1, other arithmetic: 0.83 us -> 0.04 us  [lag_kernel(): return jnp.concatenate([cosine, -sine], axis=0).astype(jnp.bfloat16)]
    ppermute x1, waiting for transfers between devices: 0.22 us -> 1 us  [local(): other = lax.ppermute(white, 'tm', perm=[(0, 1), (1, 0)])]
    unnamed x10 -> x6, local copies, waits for them, and re-layouts: 1.94 us -> 1.17 us
  transfers between devices with their start and end apart: 4 -> 4, of which waited for: 2 -> 2; matrix products, arithmetic and copies ran while one was open for 28% -> 25% of each run, Pallas kernels for 0% -> 0%
where the time goes in v9:
time: 66.3 us; the launch traced here: 65.1 us
  Pallas kernels  14.7 us (22%)
  other arithmetic  13.4 us (20%)
  local copies, waits for them, and re-layouts  10.3 us (16%)
  starting transfers between devices  9.84 us (15%)
  waiting for transfers between devices  8.04 us (12%)
  matrix products  6.69 us (10%)
  between operations  2.18 us (3%)
    pallas_call x1, Pallas kernels, correlate(): pl.pallas_call(functools.partial(correlate_kernel, factor, bins, group, h...  14.7 us
    all_to_all x1, starting transfers between devices, local(): lax.all_to_all(rows, 'chan', 0, 2, tiled=True).reshape(width, samples)  7.29 us
    all_to_all x1, waiting for transfers between devices, local(): lax.all_to_all(rows, 'chan', 0, 2, tiled=True).reshape(width, samples)  7.03 us
    convert_element_type x4, other arithmetic, split_bf16(): piece = rest.astype(jnp.bfloat16)  5.37 us
    gather x1, local copies, waits for them, and re-layouts, local(): jnp.take(paired, index.reshape(-1), axis=0, mode='clip')  4.59 us
    dot_general x1, matrix products, whiten_series(): jnp.dot(series, jnp.concatenate([hi, lo], axis=1), preferred_element_type...  3.27 us
    dot_general x1, matrix products, local(): jnp.dot(stacked[:, :raw_rows], records, preferred_element_type=jnp.float32)  2.47 us
    reduce_sum x1, other arithmetic, decimation_matrix(): jnp.where(cols - STRIDE * rows == tap, fir_taps[None, None, :], 0.0)  2.04 us
  transfers between devices with their start and end apart: 4, of which 2 were waited for; matrix products, arithmetic and copies ran while one was open for 25% of the time, Pallas kernels for 0%

profile of v9, /device:TPU:0, one launch (start us, length us, event | category | flops | bytes accessed | tf_op | source)
XLA Modules:
  0.0 65.1 jit_solution(3642719397896177301)
XLA Ops:
  0.0 0.9 %slice.34 = bf16[24,3072]{1,0:T(8,128)(2,1)S(1)} slice(bf16[512,3072]{1,0:T(8,128)(2,1)} %param.5), slice={[0:24], [0:3072]} | slice | bytes 294912 | tf_op jit(solution)/shard_map/slice | solution.py:181
  0.9 1.3 %collective-permute-start = (bf16[24,3072]{1,0:T(8,128)(2,1)S(1)}, bf16[24,3072]{1,0:T(8,128)(2,1)S(1)}, u32[]{:S(2)}, u32[]{:S(2)}) collective-permute-start(bf16[24,3072]{1,0:T(8,128)(2,1)S(1)} %slice.34), channel_id=1, source_target_pairs={{1,0},{2,1},{3,2},{4,3},{5,4},{6,5},{7,6},{8,7},{9,8},{10,9},{11,1... | collective-permute-start | bytes 442376 | tf_op jit(solution)/shard_map/ppermute | solution.py:181
  2.3 1.3 %fusion.65 = s32[]{:T(128)} fusion(s32[2]{0:T(128)} %param.9, s32[2]{0:T(128)} %param.8, s32[]{:T(128)S(6)} %axis_index.16), kind=kLoop, calls=%fused_computation.101 | loop fusion | flops 9 | bytes 24 | tf_op jit(solution)/shard_map/reduce_sum | solution.py:194
  4.9 0.7 %reshape.270 = s32[8,384]{1,0:T(8,128)S(1)} reshape(s32[3072]{0:T(1024)} %param.7) | data formatting | bytes 24576 | tf_op jit(solution)/shard_map/reshape | solution.py:196
  6.2 0.8 %dynamic_slice.7 = s32[16]{0:T(128)S(1)} dynamic-slice(s32[3072]{0:T(1024)} %param.7, s32[]{:T(128)S(6)} %select_n.93), dynamic_slice_sizes={16} | dynamic-slice | bytes 132 | tf_op jit(solution)/shard_map/dynamic_slice | solution.py:195
  7.0 0.1 pad.15.clone
  7.1 0.3 fusion.56
  7.4 0.1 iota_subtract_fusion
  7.5 2.0 %select_reduce_fusion = f32[64,536]{1,0:T(8,128)S(1)} fusion(f32[32]{0:T(128)} %param.6, s32[64,536]{1,0:T(8,128)S(1)} %iota_subtract_fusion), kind=kLoop, calls=%fused_computation.1 | loop fusion | flops 3258880 | bytes 274560 | tf_op jit(solution)/shard_map/reduce_sum | solution.py:36
  9.6 0.1 constant_dynamic-slice_fusion
  9.7 2.5 %fusion.30 = f32[128,3072]{1,0:T(8,128)S(1)} fusion(bf16[512,3072]{1,0:T(8,128)(2,1)} %param.5, bf16[64,536]{1,0:T(8,128)(2,1)S(1)} %get-tuple-element.6, bf16[64,536]{1,0:T(8,128)(2,1)S(1)} %get-tuple-element.5), kind=kOutput, calls=%fused_computation.51 | convolution fusion | flops 402915328 | bytes 4855808 | tf_op jit(solution)/shard_map/dot_general | solution.py:185
  12.1 0.1 reshape.279
  12.2 0.3 fusion.53
  12.5 0.0 collective-permute-done
  12.5 0.4 convolution_add_fusion
  12.9 0.0 copy-start.1
  12.9 1.2 %copy-done.1 = f32[128,3072]{1,0:T(8,128)} copy-done((f32[128,3072]{1,0:T(8,128)}, f32[128,3072]{1,0:T(8,128)S(1)}, u32[]{:S(2)}) %copy-start.1) | copy-done | bytes 1572888
  14.0 0.1 fusion.20
  14.1 1.2 %collective-permute-start.1 = (bf16[64,3072]{1,0:T(8,128)(2,1)S(1)}, bf16[64,3072]{1,0:T(8,128)(2,1)S(1)}, u32[]{:S(2)}, u32[]{:S(2)}) collective-permute-start(bf16[64,3072]{1,0:T(8,128)(2,1)S(1)} %fusion.20), channel_id=1, source_target_pairs={{0,1},{1,0},{2,3},{3,2},{4,5},{5,4},{6,7},{7,6},{8,9},{9,8},{10,11... | collective-permute-start | bytes 1179656 | tf_op jit(solution)/shard_map/ppermute | solution.py:161
  15.3 0.0 copy-start.2
  15.3 1.9 %multiply_subtract_fusion = (f32[32,32,512]{2,1,0:T(8,128)S(1)}, f32[32,32,512]{2,1,0:T(8,128)}) fusion(f32[32,512]{1,0:T(8,128)S(1)} %get-tuple-element.22, f32[32,512]{1,0:T(8,128)S(1)} %get-tuple-element.21, f32[32,512]{1,0:T(8,128)S(1)} %get-tuple-element.23, f32[32,512]{1,0:T(8,128)S(1)} %get-tuple-element.20), kind=kLoop, calls=%fused_computation.18 | loop fusion | flops 3670016 | bytes 4456448 | tf_op jit(solution)/shard_map/sub | solution.py:50
  17.3 0.0 collective-permute-done.1
  17.3 0.0 copy-done.2
  17.3 0.1 broadcast_select_fusion.1
  17.4 0.9 %maximum_bitcast_fusion = bf16[3072,128]{0,1:T(8,128)(2,1)} fusion(bf16[64,3072]{1,0:T(8,128)(2,1)S(1)} %get-tuple-element.13, bf16[64,3072]{1,0:T(8,128)(2,1)S(1)} %get-tuple-element.12), kind=kLoop, calls=%fused_computation.26 | loop fusion | flops 1572864 | bytes 1572864 | tf_op jit(solution)/shard_map/transpose | solution.py:191
  18.3 1.5 %copy.15 = bf16[3072,128]{1,0:T(8,128)(2,1)S(1)} copy(bf16[3072,128]{0,1:T(8,128)(2,1)} %maximum_bitcast_fusion) | data formatting | bytes 1572864 | tf_op jit(solution)/shard_map/transpose | solution.py:191
  19.9 4.6 %gather_fusion = bf16[1664,128]{1,0:T(8,128)(2,1)} fusion(bf16[3072,128]{1,0:T(8,128)(2,1)S(1)} %copy.15, s32[2048]{0:T(1024)S(1)} %pad_clamp_fusion), kind=kCustom, calls=%fused_computation | custom fusion | bytes 858624 | tf_op jit(solution)/shard_map/jit(_take)/gather | solution.py:201
  24.4 7.3 %all-to-all-start = ((bf16[8,208,128]{2,1,0:T(8,128)(2,1)}), bf16[8,208,128]{2,1,0:T(8,128)(2,1)S(1)}, u32[]{:S(2)}, u32[]{:S(2)}) async-start(bf16[8,208,128]{2,1,0:T(8,128)(2,1)} %bitcast.1), calls=%async_computation | async-start | bytes 851968 | tf_op jit(solution)/shard_map/all_to_all | solution.py:202
  31.7 0.1 abs_compare_fusion
  31.9 0.0 copy-start
  31.9 3.6 %subtract_convert_fusion = bf16[1024,1024]{1,0:T(8,128)(2,1)} fusion(f32[1024,512]{1,0:T(8,128)} %bitcast.22, f32[1024,512]{1,0:T(8,128)S(1)} %bitcast.20), kind=kLoop, calls=%fused_computation.8 | loop fusion | flops 5242880 | bytes 6291456 | tf_op jit(solution)/shard_map/convert_element_type | solution.py:26
  35.5 0.0 copy-done
  35.5 1.6 %fusion.4 = bf16[1024,1024]{1,0:T(8,128)(2,1)} fusion(f32[1024,512]{1,0:T(8,128)S(1)} %bitcast.23, f32[1024,512]{1,0:T(8,128)S(1)} %bitcast.21), kind=kLoop, calls=%fused_computation.10 | loop fusion | flops 4194304 | bytes 6291456 | tf_op jit(solution)/shard_map/convert_element_type | solution.py:26
  37.1 0.2 fusion.64
  37.3 7.0 %all-to-all-done = bf16[8,208,128]{2,1,0:T(8,128)(2,1)S(1)} async-done(((bf16[8,208,128]{2,1,0:T(8,128)(2,1)}), bf16[8,208,128]{2,1,0:T(8,128)(2,1)S(1)}, u32[]{:S(2)}, u32[]{:S(2)}) %all-to-all-start) | async-done | bytes 426016 | tf_op jit(solution)/shard_map/all_to_all | solution.py:202
  44.3 0.1 copy.16
  44.4 3.3 %fusion = f32[208,2048]{1,0:T(8,128)S(1)} fusion(bf16[1024,1024]{1,0:T(8,128)(2,1)} %subtract_convert_fusion, bf16[1024,1024]{1,0:T(8,128)(2,1)} %fusion.4, bf16[26,8,8,128]{3,2,1,0:T(8,128)(2,1)S(1)} %bitcast.27), kind=kOutput, calls=%fused_computation.4 | convolution fusion | flops 880803840 | bytes 6324224 | tf_op jit(solution)/shard_map/dot_general | solution.py:81
  47.7 0.1 slice_add_fusion
  47.8 0.1 fusion.72
  47.9 0.6 multiply_convert_fusion.1
  48.6 0.1 collective-permute-start.2
  48.7 0.3 fusion.51
  49.0 0.1 subtract_convert_fusion.1
  49.1 0.1 copy.17
  49.2 0.1 copy.18
  49.4 1.0 %collective-permute-done.2.other_ref = bf16[208,1024]{1,0:T(8,128)(2,1)S(1)} collective-permute-done((bf16[208,1024]{1,0:T(8,128)(2,1)S(1)}, bf16[208,1024]{1,0:T(8,128)(2,1)S(1)}, u32[]{:S(2)}, u32[]{:S(2)}) %collective-permute-start.2) | collective-permute-done | bytes 426016 | tf_op jit(solution)/shard_map/ppermute | solution.py:208
  50.4 14.7 %shard_map.55 = f32[32,384,256]{2,1,0:T(8,128)} custom-call(bf16[208,1024]{1,0:T(8,128)(2,1)S(1)} %pad_maximum_fusion.2.mine_ref, bf16[208,1024]{1,0:T(8,128)(2,1)S(1)} %collective-permute-done.2.other_ref, bf16[1024,256]{1,0:T(8,128)(2,1)S(1)} %pad_maximum_fusion.1.lag_ref), custom_call_target="tpu_custom_call" | custom-call | flops 6480199680 | bytes 13959168 | tf_op jit(solution)/shard_map/pallas_call | solution.py:142
  (8 shorter events, 0.1 us)
Async XLA Ops:
  0.9 11.6 %collective-permute-start = (bf16[24,3072]{1,0:T(8,128)(2,1)S(1)}, bf16[24,3072]{1,0:T(8,128)(2,1)S(1)}, u32[]{:S(2)}, u32[]{:S(2)}) collective-permute-start(bf16[24,3072]{1,0:T(8,128)(2,1)S(1)} %slice.34), channel_id=1, source_target_pairs={{1,0},{2,1},{3,2},{4,3},{5,4},{6,5},{7,6},{8,7},{9,8},{10,9},{11,1... | collective-permute-start | bytes 442376 | tf_op jit(solution)/shard_map/ppermute | solution.py:181
  12.9 1.2 %copy-start.1 = (f32[128,3072]{1,0:T(8,128)}, f32[128,3072]{1,0:T(8,128)S(1)}, u32[]{:S(2)}) copy-start(f32[128,3072]{1,0:T(8,128)S(1)} %convolution_add_fusion) | copy-start | bytes 4718596
  14.1 3.1 %collective-permute-start.1 = (bf16[64,3072]{1,0:T(8,128)(2,1)S(1)}, bf16[64,3072]{1,0:T(8,128)(2,1)S(1)}, u32[]{:S(2)}, u32[]{:S(2)}) collective-permute-start(bf16[64,3072]{1,0:T(8,128)(2,1)S(1)} %fusion.20), channel_id=1, source_target_pairs={{0,1},{1,0},{2,3},{3,2},{4,5},{5,4},{6,7},{7,6},{8,9},{9,8},{10,11... | collective-permute-start | bytes 1179656 | tf_op jit(solution)/shard_map/ppermute | solution.py:161
  15.3 1.9 %copy-start.2 = (f32[128,3072]{1,0:T(8,128)S(1)}, f32[128,3072]{1,0:T(8,128)}, u32[]{:S(2)}) copy-start(f32[128,3072]{1,0:T(8,128)} %copy-done.1) | copy-start | bytes 4718596
  24.4 19.9 %all-to-all-start = ((bf16[8,208,128]{2,1,0:T(8,128)(2,1)}), bf16[8,208,128]{2,1,0:T(8,128)(2,1)S(1)}, u32[]{:S(2)}, u32[]{:S(2)}) async-start(bf16[8,208,128]{2,1,0:T(8,128)(2,1)} %bitcast.1), calls=%async_computation | async-start | bytes 851968 | tf_op jit(solution)/shard_map/all_to_all | solution.py:202
  31.9 3.7 %copy-start = (f32[32,32,512]{2,1,0:T(8,128)S(1)}, f32[32,32,512]{2,1,0:T(8,128)}, u32[]{:S(2)}) copy-start(f32[32,32,512]{2,1,0:T(8,128)} %get-tuple-element.15) | copy-start | bytes 6291460
  48.6 1.8 %collective-permute-start.2 = (bf16[208,1024]{1,0:T(8,128)(2,1)S(1)}, bf16[208,1024]{1,0:T(8,128)(2,1)S(1)}, u32[]{:S(2)}, u32[]{:S(2)}) collective-permute-start(bf16[208,1024]{1,0:T(8,128)(2,1)S(1)} %pad_maximum_fusion.2.mine_ref), channel_id=1, source_target_pairs={{0,1},{1,0},{2,3},{3,2},{4,5},{5,4},{6,7},{7,6},{8,9},{9,8},{10,11... | collective-permute-start | bytes 1277960 | tf_op jit(solution)/shard_map/ppermute | solution.py:208

commit v10 on v8

--- a/solution.py
+++ b/solution.py
@@ -77,9 +77,7 @@
 def whiten_series(series, table):
     samples = series.shape[1]
     bins = samples // 2
-    hi, lo = split_bf16(table, 2)
-    both = jnp.dot(series, jnp.concatenate([hi, lo], axis=1), preferred_element_type=jnp.float32)
-    spectrum = both[:, : 2 * bins] + both[:, 2 * bins :]
+    spectrum = jnp.dot(series, table.astype(jnp.bfloat16), preferred_element_type=jnp.float32)
     real_part = spectrum[:, :bins]
     imag_part = spectrum[:, bins:]
     powers = real_part * real_part + imag_part * imag_part

time: 62.3 us -> 55.2 us (0.89)
  other arithmetic: 14.2 us -> 6.76 us
  waiting for transfers between devices: 7.25 us -> 12.7 us
  matrix products: 6.69 us -> 4.03 us
  local copies, waits for them, and re-layouts: 11.1 us -> 8.77 us
    convert_element_type x4 -> x2, other arithmetic: 5.38 us -> 0.14 us  [split_bf16(): piece = rest.astype(jnp.bfloat16)]
    all_to_all x1, waiting for transfers between devices: 7.03 us -> 11.6 us  [local(): lax.all_to_all(rows, 'chan', 0, 2, tiled=True).reshape(width, samples)]
    dot_general x1, matrix products: 3.28 us -> 0.61 us  [whiten_series(): jnp.dot(series, table.astype(jnp.bfloat16), preferred_element_type=jnp.fl...]
    sub x1 -> x0, other arithmetic: 1.94 us -> none  [dft_table(): cosine = (ch * cl - sh * sl).reshape(samples, bins)]
    unnamed x10 -> x4, local copies, waits for them, and re-layouts: 1.94 us -> 0.79 us
    transpose x1, local copies, waits for them, and re-layouts: 1.5 us -> 0.37 us  [local(): paired = jnp.concatenate([first, second], axis=0).T]
    transpose x1, other arithmetic: 0.97 us -> 0.05 us  [local(): paired = jnp.concatenate([first, second], axis=0).T]
    ppermute x1, waiting for transfers between devices: 0.01 us -> 0.83 us  [swap_tm(): other = lax.ppermute(x, 'tm', perm=[(0, 1), (1, 0)])]
  transfers between devices with their start and end apart: 4 -> 4, of which waited for: 2 -> 3; matrix products, arithmetic and copies ran while one was open for 28% -> 20% of each run, Pallas kernels for 0% -> 0%
where the time goes in v10:
time: 55.2 us; the launch traced here: 54.8 us
  waiting for transfers between devices  12.7 us (23%)
  Pallas kernels  10.5 us (19%)
  starting transfers between devices  9.84 us (18%)
  local copies, waits for them, and re-layouts  8.77 us (16%)
  other arithmetic  6.76 us (12%)
  matrix products  4.03 us (7%)
  between operations  2.18 us (4%)
    all_to_all x1, waiting for transfers between devices, local(): lax.all_to_all(rows, 'chan', 0, 2, tiled=True).reshape(width, samples)  11.6 us
    pallas_call x1, Pallas kernels, correlate(): pl.pallas_call(functools.partial(correlate_kernel, factor, bins, group, h...  10.5 us
    all_to_all x1, starting transfers between devices, local(): lax.all_to_all(rows, 'chan', 0, 2, tiled=True).reshape(width, samples)  7.3 us
    gather x1, local copies, waits for them, and re-layouts, local(): jnp.take(paired, index.reshape(-1), axis=0, mode='clip')  4.59 us
    dot_general x1, matrix products, local(): jnp.dot(stacked[:, :raw_rows], records, preferred_element_type=jnp.float32)  2.46 us
    reduce_sum x1, other arithmetic, decimation_matrix(): jnp.where(cols - STRIDE * rows == tap, fir_taps[None, None, :], 0.0)  2.04 us
    reduce_sum x1, other arithmetic, local(): jnp.sum(jnp.where(steps == tm, source_owner * block + source_offset, 0))  1.31 us
    ppermute x1, starting transfers between devices, local(): halo = lax.ppermute(records[:halo_rows], ('chan', 'tm'), perm=shift)  1.29 us
  transfers between devices with their start and end apart: 4, of which 3 were waited for; matrix products, arithmetic and copies ran while one was open for 20% of the time, Pallas kernels for 0%

profile of v10, /device:TPU:0, one launch (start us, length us, event | category | flops | bytes accessed | tf_op | source)
XLA Modules:
  0.0 54.8 jit_solution(6431369813737736291)
XLA Ops:
  0.0 0.9 %slice.28 = bf16[24,3072]{1,0:T(8,128)(2,1)S(1)} slice(bf16[512,3072]{1,0:T(8,128)(2,1)} %param.5), slice={[0:24], [0:3072]} | slice | bytes 294912 | tf_op jit(solution)/shard_map/slice | solution.py:174
  0.9 1.3 %collective-permute-start = (bf16[24,3072]{1,0:T(8,128)(2,1)S(1)}, bf16[24,3072]{1,0:T(8,128)(2,1)S(1)}, u32[]{:S(2)}, u32[]{:S(2)}) collective-permute-start(bf16[24,3072]{1,0:T(8,128)(2,1)S(1)} %slice.28), channel_id=1, source_target_pairs={{1,0},{2,1},{3,2},{4,3},{5,4},{6,5},{7,6},{8,7},{9,8},{10,9},{11,1... | collective-permute-start | bytes 442376 | tf_op jit(solution)/shard_map/ppermute | solution.py:174
  2.2 1.3 %fusion.64 = s32[]{:T(128)} fusion(s32[2]{0:T(128)} %param.9, s32[2]{0:T(128)} %param.8, s32[]{:T(128)S(6)} %axis_index.16), kind=kLoop, calls=%fused_computation.97 | loop fusion | flops 9 | bytes 24 | tf_op jit(solution)/shard_map/reduce_sum | solution.py:187
  4.9 0.7 %reshape.272 = s32[8,384]{1,0:T(8,128)S(1)} reshape(s32[3072]{0:T(1024)} %param.7) | data formatting | bytes 24576 | tf_op jit(solution)/shard_map/reshape | solution.py:189
  6.2 0.8 %dynamic_slice.7 = s32[16]{0:T(128)S(1)} dynamic-slice(s32[3072]{0:T(1024)} %param.7, s32[]{:T(128)S(6)} %select_n.93), dynamic_slice_sizes={16} | dynamic-slice | bytes 132 | tf_op jit(solution)/shard_map/dynamic_slice | solution.py:188
  7.0 0.1 pad.13.clone
  7.1 0.1 iota_subtract_fusion
  7.2 2.0 %select_reduce_fusion = f32[64,536]{1,0:T(8,128)S(1)} fusion(f32[32]{0:T(128)} %param.6, s32[64,536]{1,0:T(8,128)S(1)} %iota_subtract_fusion), kind=kLoop, calls=%fused_computation.1 | loop fusion | flops 3258880 | bytes 274560 | tf_op jit(solution)/shard_map/reduce_sum | solution.py:36
  9.2 0.1 constant_dynamic-slice_fusion
  9.3 2.5 %fusion.29 = f32[128,3072]{1,0:T(8,128)S(1)} fusion(bf16[512,3072]{1,0:T(8,128)(2,1)} %param.5, bf16[64,536]{1,0:T(8,128)(2,1)S(1)} %get-tuple-element.6, bf16[64,536]{1,0:T(8,128)(2,1)S(1)} %get-tuple-element.5), kind=kOutput, calls=%fused_computation.47 | convolution fusion | flops 402915328 | bytes 4855808 | tf_op jit(solution)/shard_map/dot_general | solution.py:178
  11.8 0.0 collective-permute-done
  11.8 0.4 convolution_add_fusion
  12.2 0.1 fusion.19
  12.2 1.2 %collective-permute-start.1 = (bf16[64,3072]{1,0:T(8,128)(2,1)S(1)}, bf16[64,3072]{1,0:T(8,128)(2,1)S(1)}, u32[]{:S(2)}, u32[]{:S(2)}) collective-permute-start(bf16[64,3072]{1,0:T(8,128)(2,1)S(1)} %fusion.19), channel_id=1, source_target_pairs={{0,1},{1,0},{2,3},{3,2},{4,5},{5,4},{6,7},{7,6},{8,9},{9,8},{10,11... | collective-permute-start | bytes 1179656 | tf_op jit(solution)/shard_map/ppermute | solution.py:154
  13.4 0.1 reshape.281
  13.5 0.3 fusion.52
  13.8 0.1 abs_compare_fusion
  13.9 0.8 %collective-permute-done.1 = bf16[64,3072]{1,0:T(8,128)(2,1)S(1)} collective-permute-done((bf16[64,3072]{1,0:T(8,128)(2,1)S(1)}, bf16[64,3072]{1,0:T(8,128)(2,1)S(1)}, u32[]{:S(2)}, u32[]{:S(2)}) %collective-permute-start.1) | collective-permute-done | bytes 393248 | tf_op jit(solution)/shard_map/ppermute | solution.py:154
  14.8 0.1 broadcast_select_fusion.1
  14.9 0.1 maximum_bitcast_fusion
  14.9 0.4 copy.15
  15.3 4.6 %gather_fusion = bf16[1664,128]{1,0:T(8,128)(2,1)} fusion(bf16[3072,128]{1,0:T(8,128)(2,1)S(1)} %copy.15, s32[2048]{0:T(1024)S(1)} %pad_clamp_fusion), kind=kCustom, calls=%fused_computation | custom fusion | bytes 858624 | tf_op jit(solution)/shard_map/jit(_take)/gather | solution.py:194
  19.9 7.3 %all-to-all-start = ((bf16[8,208,128]{2,1,0:T(8,128)(2,1)}), bf16[8,208,128]{2,1,0:T(8,128)(2,1)S(1)}, u32[]{:S(2)}, u32[]{:S(2)}) async-start(bf16[8,208,128]{2,1,0:T(8,128)(2,1)} %bitcast.1), calls=%async_computation | async-start | bytes 851968 | tf_op jit(solution)/shard_map/all_to_all | solution.py:195
  27.2 0.2 fusion.63
  27.4 0.3 fusion.55
  27.7 0.8 %subtract_convert_fusion = (bf16[32,32,512]{2,1,0:T(8,128)(2,1)S(1)}, bf16[32,32,512]{2,1,0:T(8,128)(2,1)S(1)}) fusion(f32[32,512]{1,0:T(8,128)S(1)} %get-tuple-element.22, f32[32,512]{1,0:T(8,128)S(1)} %get-tuple-element.21, f32[32,512]{1,0:T(8,128)S(1)} %get-tuple-element.23, f32[32,512]{1,0:T(8,128)S(1)} %get-tuple-element.20), kind=kLoop, calls=%fused_computation.15 | loop fusion | flops 4718592 | bytes 2359296 | tf_op jit(solution)/shard_map/convert.10
  28.5 11.6 %all-to-all-done = bf16[8,208,128]{2,1,0:T(8,128)(2,1)S(1)} async-done(((bf16[8,208,128]{2,1,0:T(8,128)(2,1)}), bf16[8,208,128]{2,1,0:T(8,128)(2,1)S(1)}, u32[]{:S(2)}, u32[]{:S(2)}) %all-to-all-start) | async-done | bytes 426016 | tf_op jit(solution)/shard_map/all_to_all | solution.py:195
  40.1 0.1 copy.16
  40.2 0.6 %fusion.6 = f32[208,1024]{1,0:T(8,128)S(1)} fusion(bf16[1024,512]{1,0:T(8,128)(2,1)S(1)} %bitcast.22, bf16[1024,512]{1,0:T(8,128)(2,1)S(1)} %bitcast.21, bf16[26,8,8,128]{3,2,1,0:T(8,128)(2,1)S(1)} %bitcast.25), kind=kOutput, calls=%fused_computation.10 | convolution fusion | flops 440401920 | bytes 3375104 | tf_op jit(solution)/shard_map/dot_general | solution.py:80
  40.9 0.1 fusion.71
  41.0 0.6 %multiply_convert_fusion.1 = (bf16[208,512]{1,0:T(8,128)(2,1)S(1)}, bf16[208,512]{1,0:T(8,128)(2,1)S(1)}) fusion(f32[208,1024]{1,0:T(8,128)S(1)} %fusion.6, pred[512,512]{1,0:T(32,128)(4,1)S(1)} %abs_compare_fusion, bf16[208,512]{1,0:T(8,128)(2,1)S(1)} %get-tuple-element.11, bf16[208,512]{1,0:T(8,128)(2,1)S(1)} %get-tuple-element.10, ...), kind=kOutput, calls=%fused_computation.35 | convolution fusion | flops 331284480 | bytes 2179072 | tf_op jit(solution)/shard_map/dot_general | solution.py:86
  41.6 0.0 copy-start
  41.6 0.1 collective-permute-start.2
  41.7 0.3 fusion.50
  42.0 0.1 subtract_convert_fusion.1
  42.2 0.1 copy.17
  42.3 0.1 copy.18
  42.4 0.8 %pad_maximum_fusion.lag_ref = bf16[1024,256]{1,0:T(8,128)(2,1)} fusion(bf16[512,256]{1,0:T(8,128)(2,1)S(1)} %copy.18, bf16[512,256]{1,0:T(8,128)(2,1)S(1)} %copy.17), kind=kLoop, calls=%fused_computation.28 | loop fusion | flops 1048576 | bytes 1048576 | tf_op jit(solution)/shard_map/concatenate | solution.py:74
  43.3 0.2 collective-permute-done.2.other_ref
  43.5 0.0 copy-done
  43.5 0.0 copy-start.1
  43.5 0.8 %copy-done.1 = bf16[208,1024]{1,0:T(8,128)(2,1)} copy-done((bf16[208,1024]{1,0:T(8,128)(2,1)}, bf16[208,1024]{1,0:T(8,128)(2,1)S(1)}, u32[]{:S(2)}) %copy-start.1) | copy-done | bytes 426008
  44.3 10.5 %shard_map.55 = f32[32,384,256]{2,1,0:T(8,128)} custom-call(bf16[208,1024]{1,0:T(8,128)(2,1)} %copy-done, bf16[208,1024]{1,0:T(8,128)(2,1)} %copy-done.1, bf16[1024,256]{1,0:T(8,128)(2,1)} %pad_maximum_fusion.lag_ref), custom_call_target="tpu_custom_call" | custom-call | flops 6480199680 | bytes 13959168 | tf_op jit(solution)/shard_map/pallas_call | solution.py:138
  (7 shorter events, 0.1 us)
Async XLA Ops:
  0.9 10.9 %collective-permute-start = (bf16[24,3072]{1,0:T(8,128)(2,1)S(1)}, bf16[24,3072]{1,0:T(8,128)(2,1)S(1)}, u32[]{:S(2)}, u32[]{:S(2)}) collective-permute-start(bf16[24,3072]{1,0:T(8,128)(2,1)S(1)} %slice.28), channel_id=1, source_target_pairs={{1,0},{2,1},{3,2},{4,3},{5,4},{6,5},{7,6},{8,7},{9,8},{10,9},{11,1... | collective-permute-start | bytes 442376 | tf_op jit(solution)/shard_map/ppermute | solution.py:174
  12.2 2.5 %collective-permute-start.1 = (bf16[64,3072]{1,0:T(8,128)(2,1)S(1)}, bf16[64,3072]{1,0:T(8,128)(2,1)S(1)}, u32[]{:S(2)}, u32[]{:S(2)}) collective-permute-start(bf16[64,3072]{1,0:T(8,128)(2,1)S(1)} %fusion.19), channel_id=1, source_target_pairs={{0,1},{1,0},{2,3},{3,2},{4,5},{5,4},{6,7},{7,6},{8,9},{9,8},{10,11... | collective-permute-start | bytes 1179656 | tf_op jit(solution)/shard_map/ppermute | solution.py:154
  19.9 20.2 %all-to-all-start = ((bf16[8,208,128]{2,1,0:T(8,128)(2,1)}), bf16[8,208,128]{2,1,0:T(8,128)(2,1)S(1)}, u32[]{:S(2)}, u32[]{:S(2)}) async-start(bf16[8,208,128]{2,1,0:T(8,128)(2,1)} %bitcast.1), calls=%async_computation | async-start | bytes 851968 | tf_op jit(solution)/shard_map/all_to_all | solution.py:195
  41.6 1.8 %copy-start = (bf16[208,1024]{1,0:T(8,128)(2,1)}, bf16[208,1024]{1,0:T(8,128)(2,1)S(1)}, u32[]{:S(2)}) copy-start(bf16[208,1024]{1,0:T(8,128)(2,1)S(1)} %pad_maximum_fusion.1.mine_ref) | copy-start | bytes 1277956
  41.6 1.8 %collective-permute-start.2 = (bf16[208,1024]{1,0:T(8,128)(2,1)S(1)}, bf16[208,1024]{1,0:T(8,128)(2,1)S(1)}, u32[]{:S(2)}, u32[]{:S(2)}) collective-permute-start(bf16[208,1024]{1,0:T(8,128)(2,1)S(1)} %pad_maximum_fusion.1.mine_ref), channel_id=1, source_target_pairs={{0,1},{1,0},{2,3},{3,2},{4,5},{5,4},{6,7},{7,6},{8,9},{9,8},{10,11... | collective-permute-start | bytes 1277960 | tf_op jit(solution)/shard_map/ppermute | solution.py:201
  43.5 0.8 %copy-start.1 = (bf16[208,1024]{1,0:T(8,128)(2,1)}, bf16[208,1024]{1,0:T(8,128)(2,1)S(1)}, u32[]{:S(2)}) copy-start(bf16[208,1024]{1,0:T(8,128)(2,1)S(1)} %collective-permute-done.2.other_ref) | copy-start | bytes 1277956

commit v11 on v10

--- a/solution.py
+++ b/solution.py
@@ -19,21 +19,14 @@
 epsilon = 1e-06
 
 
-def split_bf16(x, parts):
-    pieces = []
-    rest = x
-    for _ in range(parts):
-        piece = rest.astype(jnp.bfloat16)
-        pieces.append(piece)
-        rest = rest - piece.astype(jnp.float32)
-    return pieces
-
-
 def decimation_matrix(fir_taps, out_rows, in_rows):
-    rows = jnp.arange(out_rows, dtype=jnp.int32)[:, None, None]
-    cols = jnp.arange(in_rows, dtype=jnp.int32)[None, :, None]
-    tap = jnp.arange(TAPS, dtype=jnp.int32)[None, None, :]
-    return jnp.where(cols - STRIDE * rows == tap, fir_taps[None, None, :], 0.0).sum(axis=2)
+    leads = TAPS // STRIDE
+    rows = jnp.arange(out_rows, dtype=jnp.int32)[:, None, None, None]
+    groups = jnp.arange(in_rows // STRIDE, dtype=jnp.int32)[None, :, None, None]
+    lead = jnp.arange(leads, dtype=jnp.int32)[None, None, :, None]
+    taps = fir_taps.reshape(1, 1, leads, STRIDE)
+    matrix = jnp.where(groups - rows == lead, taps, 0.0).sum(axis=2)
+    return matrix.reshape(out_rows, in_rows)
 
 
 def dft_table(samples, bins, time_index):
@@ -81,13 +74,7 @@
     real_part = spectrum[:, :bins]
     imag_part = spectrum[:, bins:]
     powers = real_part * real_part + imag_part * imag_part
-    pieces = split_bf16(powers, 3)
-    band = band_matrix(bins)
-    window = jnp.dot(
-        jnp.concatenate(pieces, axis=1),
-        jnp.concatenate([band] * 3, axis=0),
-        preferred_element_type=jnp.float32,
-    )
+    window = jnp.dot(powers.astype(jnp.bfloat16), band_matrix(bins), preferred_element_type=jnp.float32)
     window_span = 2 * HALF_BAND + 1
     factor = 1.0 / jnp.sqrt(window / window_span + epsilon)
     return jnp.concatenate([real_part * factor, imag_part * factor], axis=1).astype(jnp.bfloat16)
@@ -174,11 +161,10 @@
     halo = lax.ppermute(records[:halo_rows], ("chan", "tm"), perm=shift)
 
     taps_matrix = decimation_matrix(fir_taps, out_rows, raw_rows + halo_rows)
-    stacked = jnp.concatenate(split_bf16(taps_matrix, 2), axis=0)
-    main = jnp.dot(stacked[:, :raw_rows], records, preferred_element_type=jnp.float32)
-    tail = jnp.dot(stacked[:, raw_rows:], halo, preferred_element_type=jnp.float32)
-    summed = main + tail
-    decimated = (summed[:out_rows] + summed[out_rows:]).astype(jnp.bfloat16)
+    taps_matrix = taps_matrix.astype(jnp.bfloat16)
+    main = jnp.dot(taps_matrix[:, :raw_rows], records, preferred_element_type=jnp.float32)
+    tail = jnp.dot(taps_matrix[:, raw_rows:], halo, preferred_element_type=jnp.float32)
+    decimated = (main + tail).astype(jnp.bfloat16)
 
     first, second = swap_tm(decimated)
     paired = jnp.concatenate([first, second], axis=0).T

time: 55.2 us -> 51.7 us (0.937)
  other arithmetic: 6.76 us -> 3.88 us
    reduce_sum x1, other arithmetic: 2.04 us -> 0.23 us  [decimation_matrix(): matrix = jnp.where(groups - rows == lead, taps, 0.0).sum(axis=2)]
    broadcast_in_dim x0 -> x1, local copies, waits for them, and re-layouts: none -> 0.74 us  [decimation_matrix(): matrix = jnp.where(groups - rows == lead, taps, 0.0).sum(axis=2)]
    reshape x1, local copies, waits for them, and re-layouts: 0.71 us -> 0.01 us  [local(): channel_map.reshape(n_chan, block)]
    dynamic_slice x1, local copies, waits for them, and re-layouts: 0.78 us -> 0.08 us  [local(): source_raw = lax.dynamic_slice_in_dim(channel_map, own_first, SRC)]
    reduce_sum x1, other arithmetic: 1.31 us -> 0.63 us  [local(): jnp.sum(jnp.where(steps == tm, source_owner * block + source_offset, 0))]
  transfers between devices with their start and end apart: 4 -> 4, of which waited for: 3 -> 3; matrix products, arithmetic and copies ran while one was open for 20% -> 15% of each run, Pallas kernels for 0% -> 0%
where the time goes in v11:
time: 51.7 us; the launch traced here: 51.4 us
  waiting for transfers between devices  12.8 us (25%)
  Pallas kernels  10.5 us (20%)
  starting transfers between devices  9.85 us (19%)
  local copies, waits for them, and re-layouts  8.3 us (16%)
  other arithmetic  3.88 us (8%)
  matrix products  3.84 us (7%)
  between operations  2.18 us (4%)
    all_to_all x1, waiting for transfers between devices, local(): lax.all_to_all(rows, 'chan', 0, 2, tiled=True).reshape(width, samples)  11.6 us
    pallas_call x1, Pallas kernels, correlate(): pl.pallas_call(functools.partial(correlate_kernel, factor, bins, group, h...  10.5 us
    all_to_all x1, starting transfers between devices, local(): lax.all_to_all(rows, 'chan', 0, 2, tiled=True).reshape(width, samples)  7.3 us
    gather x1, local copies, waits for them, and re-layouts, local(): jnp.take(paired, index.reshape(-1), axis=0, mode='clip')  4.59 us
    dot_general x1, matrix products, local(): jnp.dot(taps_matrix[:, :raw_rows], records, preferred_element_type=jnp.fl...  2.6 us
    ppermute x1, starting transfers between devices, local(): halo = lax.ppermute(records[:halo_rows], ('chan', 'tm'), perm=shift)  1.29 us
    ppermute x1, starting transfers between devices, swap_tm(): other = lax.ppermute(x, 'tm', perm=[(0, 1), (1, 0)])  1.19 us
  transfers between devices with their start and end apart: 4, of which 3 were waited for; matrix products, arithmetic and copies ran while one was open for 15% of the time, Pallas kernels for 0%

profile of v11, /device:TPU:0, one launch (start us, length us, event | category | flops | bytes accessed | tf_op | source)
XLA Modules:
  0.0 51.4 jit_solution(4192478482691048512)
XLA Ops:
  0.0 0.9 %slice.22 = bf16[24,3072]{1,0:T(8,128)(2,1)S(1)} slice(bf16[512,3072]{1,0:T(8,128)(2,1)} %param.5), slice={[0:24], [0:3072]} | slice | bytes 294912 | tf_op jit(solution)/shard_map/slice | solution.py:161
  0.9 1.3 %collective-permute-start = (bf16[24,3072]{1,0:T(8,128)(2,1)S(1)}, bf16[24,3072]{1,0:T(8,128)(2,1)S(1)}, u32[]{:S(2)}, u32[]{:S(2)}) collective-permute-start(bf16[24,3072]{1,0:T(8,128)(2,1)S(1)} %slice.22), channel_id=1, source_target_pairs={{1,0},{2,1},{3,2},{4,3},{5,4},{6,5},{7,6},{8,7},{9,8},{10,9},{11,1... | collective-permute-start | bytes 442376 | tf_op jit(solution)/shard_map/ppermute | solution.py:161
  2.2 0.7 %broadcast_in_dim.33 = f32[4,8]{1,0:T(4,128)S(1)} reshape(f32[32]{0:T(128)} %param.6) | data formatting | bytes 256 | tf_op jit(solution)/shard_map/jit(_where)/broadcast_in_dim | solution.py:28
  3.0 0.2 select_reduce_fusion
  3.3 0.2 copy.15
  3.5 0.0 copy-start.2
  3.5 0.0 copy-start.3
  3.5 0.0 copy-start.1
  3.5 2.6 %fusion.10 = f32[64,3072]{1,0:T(8,128)S(1)} fusion(bf16[512,3072]{1,0:T(8,128)(2,1)} %param.5, bf16[64,536]{0,1:T(8,128)(2,1)S(1)} %bitcast.26), kind=kOutput, calls=%fused_computation.27 | convolution fusion | flops 201326592 | bytes 4063232 | tf_op jit(solution)/shard_map/dot_general | solution.py:165
  6.1 0.0 copy-done.2
  6.1 0.0 copy-done.3
  6.1 0.6 %fusion.45 = s32[]{:T(128)} fusion(s32[2]{0:T(128)S(1)} %copy-done.2, s32[2]{0:T(128)S(1)} %copy-done.3, s32[]{:T(128)S(6)} %axis_index.16), kind=kLoop, calls=%fused_computation.79 | loop fusion | flops 9 | bytes 24 | tf_op jit(solution)/shard_map/reduce_sum | solution.py:173
  8.0 0.0 copy-done.1
  8.7 0.1 dynamic_slice.7
  8.8 0.1 pad.7.clone
  8.9 0.1 constant_dynamic-slice_fusion
  8.9 0.0 collective-permute-done
  8.9 0.3 fusion
  9.2 1.2 %collective-permute-start.1 = (bf16[64,3072]{1,0:T(8,128)(2,1)S(1)}, bf16[64,3072]{1,0:T(8,128)(2,1)S(1)}, u32[]{:S(2)}, u32[]{:S(2)}) collective-permute-start(bf16[64,3072]{1,0:T(8,128)(2,1)S(1)} %fusion), channel_id=1, source_target_pairs={{0,1},{1,0},{2,3},{3,2},{4,5},{5,4},{6,7},{7,6},{8,9},{9,8},{10,11... | collective-permute-start | bytes 1179656 | tf_op jit(solution)/shard_map/ppermute | solution.py:141
  10.4 0.1 reshape.277
  10.6 0.3 fusion.32
  10.8 0.9 %collective-permute-done.1 = bf16[64,3072]{1,0:T(8,128)(2,1)S(1)} collective-permute-done((bf16[64,3072]{1,0:T(8,128)(2,1)S(1)}, bf16[64,3072]{1,0:T(8,128)(2,1)S(1)}, u32[]{:S(2)}, u32[]{:S(2)}) %collective-permute-start.1) | collective-permute-done | bytes 393248 | tf_op jit(solution)/shard_map/ppermute | solution.py:141
  11.8 0.1 broadcast_select_fusion.1
  11.8 0.1 maximum_bitcast_fusion
  11.9 0.4 copy.16
  12.3 4.6 %gather_fusion = bf16[1664,128]{1,0:T(8,128)(2,1)} fusion(bf16[3072,128]{1,0:T(8,128)(2,1)S(1)} %copy.16, s32[2048]{0:T(1024)S(1)} %pad_clamp_fusion), kind=kCustom, calls=%fused_computation | custom fusion | bytes 858624 | tf_op jit(solution)/shard_map/jit(_take)/gather | solution.py:180
  16.9 7.3 %all-to-all-start = ((bf16[8,208,128]{2,1,0:T(8,128)(2,1)}), bf16[8,208,128]{2,1,0:T(8,128)(2,1)S(1)}, u32[]{:S(2)}, u32[]{:S(2)}) async-start(bf16[8,208,128]{2,1,0:T(8,128)(2,1)} %bitcast.2), calls=%async_computation | async-start | bytes 851968 | tf_op jit(solution)/shard_map/all_to_all | solution.py:181
  24.2 0.2 fusion.43
  24.3 0.3 fusion.35
  24.7 0.8 %subtract_convert_fusion = (bf16[32,32,512]{2,1,0:T(8,128)(2,1)S(1)}, bf16[32,32,512]{2,1,0:T(8,128)(2,1)S(1)}) fusion(f32[32,512]{1,0:T(8,128)S(1)} %get-tuple-element.17, f32[32,512]{1,0:T(8,128)S(1)} %get-tuple-element.16, f32[32,512]{1,0:T(8,128)S(1)} %get-tuple-element.18, f32[32,512]{1,0:T(8,128)S(1)} %get-tuple-element.15), kind=kLoop, calls=%fused_computation.8 | loop fusion | flops 4718592 | bytes 2359296 | tf_op jit(solution)/shard_map/convert.9
  25.4 11.6 %all-to-all-done = bf16[8,208,128]{2,1,0:T(8,128)(2,1)S(1)} async-done(((bf16[8,208,128]{2,1,0:T(8,128)(2,1)}), bf16[8,208,128]{2,1,0:T(8,128)(2,1)S(1)}, u32[]{:S(2)}, u32[]{:S(2)}) %all-to-all-start) | async-done | bytes 426016 | tf_op jit(solution)/shard_map/all_to_all | solution.py:181
  37.1 0.1 copy.17
  37.2 0.6 %fusion.1 = f32[208,1024]{1,0:T(8,128)S(1)} fusion(bf16[1024,512]{1,0:T(8,128)(2,1)S(1)} %bitcast.23, bf16[1024,512]{1,0:T(8,128)(2,1)S(1)} %bitcast.22, bf16[26,8,8,128]{3,2,1,0:T(8,128)(2,1)S(1)} %bitcast.28), kind=kOutput, calls=%fused_computation.3 | convolution fusion | flops 440401920 | bytes 3375104 | tf_op jit(solution)/shard_map/dot_general | solution.py:73
  37.8 0.3 multiply_convert_fusion.1
  38.2 0.0 copy-start
  38.2 0.1 collective-permute-start.2
  38.3 0.3 fusion.30
  38.6 0.1 subtract_convert_fusion.1
  38.7 0.1 copy.18
  38.9 0.1 copy.19
  39.0 0.8 %pad_maximum_fusion.lag_ref = bf16[1024,256]{1,0:T(8,128)(2,1)} fusion(bf16[512,256]{1,0:T(8,128)(2,1)S(1)} %copy.19, bf16[512,256]{1,0:T(8,128)(2,1)S(1)} %copy.18), kind=kLoop, calls=%fused_computation.15 | loop fusion | flops 1048576 | bytes 1048576 | tf_op jit(solution)/shard_map/concatenate | solution.py:67
  39.9 0.2 collective-permute-done.2.other_ref
  40.1 0.0 copy-done
  40.1 0.0 copy-start.4
  40.1 0.8 %copy-done.4 = bf16[208,1024]{1,0:T(8,128)(2,1)} copy-done((bf16[208,1024]{1,0:T(8,128)(2,1)}, bf16[208,1024]{1,0:T(8,128)(2,1)S(1)}, u32[]{:S(2)}) %copy-start.4) | copy-done | bytes 426008
  40.8 10.5 %shard_map.55 = f32[32,384,256]{2,1,0:T(8,128)} custom-call(bf16[208,1024]{1,0:T(8,128)(2,1)} %copy-done, bf16[208,1024]{1,0:T(8,128)(2,1)} %copy-done.4, bf16[1024,256]{1,0:T(8,128)(2,1)} %pad_maximum_fusion.lag_ref), custom_call_target="tpu_custom_call" | custom-call | flops 6480199680 | bytes 13959168 | tf_op jit(solution)/shard_map/pallas_call | solution.py:125
  (8 shorter events, 0.1 us)
Async XLA Ops:
  0.9 8.0 %collective-permute-start = (bf16[24,3072]{1,0:T(8,128)(2,1)S(1)}, bf16[24,3072]{1,0:T(8,128)(2,1)S(1)}, u32[]{:S(2)}, u32[]{:S(2)}) collective-permute-start(bf16[24,3072]{1,0:T(8,128)(2,1)S(1)} %slice.22), channel_id=1, source_target_pairs={{1,0},{2,1},{3,2},{4,3},{5,4},{6,5},{7,6},{8,7},{9,8},{10,9},{11,1... | collective-permute-start | bytes 442376 | tf_op jit(solution)/shard_map/ppermute | solution.py:161
  3.5 2.6 %copy-start.2 = (s32[2]{0:T(128)S(1)}, s32[2]{0:T(128)}, u32[]{:S(2)}) copy-start(s32[2]{0:T(128)} %param.9) | copy-start | bytes 28
  3.5 2.6 %copy-start.3 = (s32[2]{0:T(128)S(1)}, s32[2]{0:T(128)}, u32[]{:S(2)}) copy-start(s32[2]{0:T(128)} %param.8) | copy-start | bytes 28
  3.5 4.6 %copy-start.1 = (s32[3072]{0:T(1024)S(1)}, s32[3072]{0:T(1024)}, u32[]{:S(2)}) copy-start(s32[3072]{0:T(1024)} %param.7) | copy-start | bytes 36868
  9.2 2.5 %collective-permute-start.1 = (bf16[64,3072]{1,0:T(8,128)(2,1)S(1)}, bf16[64,3072]{1,0:T(8,128)(2,1)S(1)}, u32[]{:S(2)}, u32[]{:S(2)}) collective-permute-start(bf16[64,3072]{1,0:T(8,128)(2,1)S(1)} %fusion), channel_id=1, source_target_pairs={{0,1},{1,0},{2,3},{3,2},{4,5},{5,4},{6,7},{7,6},{8,9},{9,8},{10,11... | collective-permute-start | bytes 1179656 | tf_op jit(solution)/shard_map/ppermute | solution.py:141
  16.9 20.2 %all-to-all-start = ((bf16[8,208,128]{2,1,0:T(8,128)(2,1)}), bf16[8,208,128]{2,1,0:T(8,128)(2,1)S(1)}, u32[]{:S(2)}, u32[]{:S(2)}) async-start(bf16[8,208,128]{2,1,0:T(8,128)(2,1)} %bitcast.2), calls=%async_computation | async-start | bytes 851968 | tf_op jit(solution)/shard_map/all_to_all | solution.py:181
  38.2 1.8 %copy-start = (bf16[208,1024]{1,0:T(8,128)(2,1)}, bf16[208,1024]{1,0:T(8,128)(2,1)S(1)}, u32[]{:S(2)}) copy-start(bf16[208,1024]{1,0:T(8,128)(2,1)S(1)} %pad_maximum_fusion.1.mine_ref) | copy-start | bytes 1277956
  38.2 1.8 %collective-permute-start.2 = (bf16[208,1024]{1,0:T(8,128)(2,1)S(1)}, bf16[208,1024]{1,0:T(8,128)(2,1)S(1)}, u32[]{:S(2)}, u32[]{:S(2)}) collective-permute-start(bf16[208,1024]{1,0:T(8,128)(2,1)S(1)} %pad_maximum_fusion.1.mine_ref), channel_id=1, source_target_pairs={{0,1},{1,0},{2,3},{3,2},{4,5},{5,4},{6,7},{7,6},{8,9},{9,8},{10,11... | collective-permute-start | bytes 1277960 | tf_op jit(solution)/shard_map/ppermute | solution.py:187
  40.1 0.8 %copy-start.4 = (bf16[208,1024]{1,0:T(8,128)(2,1)}, bf16[208,1024]{1,0:T(8,128)(2,1)S(1)}, u32[]{:S(2)}) copy-start(bf16[208,1024]{1,0:T(8,128)(2,1)S(1)} %collective-permute-done.2.other_ref) | copy-start | bytes 1277956

commit v12 on v11

--- a/solution.py
+++ b/solution.py
@@ -51,20 +51,16 @@
     return near.astype(jnp.bfloat16)
 
 
-def lag_kernel(samples, first_lag, lag_count):
+def lag_pieces(samples, first_lag, lag_count):
     bin_count = samples // 2
     inner = 32
-    frequency = jnp.arange(bin_count, dtype=jnp.int32)[:, None]
-    low = jnp.arange(inner, dtype=jnp.int32)[None, :]
-    high = first_lag - LAGS // 2 + jnp.arange(lag_count // inner, dtype=jnp.int32)[None, :] * inner
+    shifts = first_lag - LAGS // 2 + jnp.arange(lag_count, dtype=jnp.int32)[None, :]
+    high = jnp.arange(bin_count // inner, dtype=jnp.int32)[:, None] * inner
+    low = jnp.arange(inner, dtype=jnp.int32)[:, None]
     scale = two_pi / samples
-    low_angle = jnp.mod(frequency * low, samples).astype(jnp.float32) * scale
-    high_angle = jnp.mod(frequency * high, samples).astype(jnp.float32) * scale
-    cl, sl = jnp.cos(low_angle)[:, None, :], jnp.sin(low_angle)[:, None, :]
-    ch, sh = jnp.cos(high_angle)[:, :, None], jnp.sin(high_angle)[:, :, None]
-    cosine = (ch * cl - sh * sl).reshape(bin_count, lag_count)
-    sine = (sh * cl + ch * sl).reshape(bin_count, lag_count)
-    return jnp.concatenate([cosine, -sine], axis=0).astype(jnp.bfloat16)
+    high_angle = jnp.mod(high * shifts, samples).astype(jnp.float32) * scale
+    low_angle = jnp.mod(low * shifts, samples).astype(jnp.float32) * scale
+    return jnp.cos(high_angle), jnp.sin(high_angle), jnp.cos(low_angle), jnp.sin(low_angle)
 
 
 def whiten_series(series, table):
@@ -80,9 +76,25 @@
     return jnp.concatenate([real_part * factor, imag_part * factor], axis=1).astype(jnp.bfloat16)
 
 
-def correlate_kernel(factor, bins, group, half, mine_ref, other_ref, lag_ref, out_ref):
+def correlate_kernel(
+    factor, bins, group, half, mine_ref, other_ref, ch_ref, sh_ref, cl_ref, sl_ref, out_ref, lag_ref
+):
     step = pl.program_id(0)
     first = lax.axis_index("tm") == 0
+
+    @pl.when(step == 0)
+    def _():
+        inner = cl_ref.shape[0]
+        cl = cl_ref[...]
+        sl = sl_ref[...]
+        for h in range(bins // inner):
+            ch = ch_ref[h : h + 1, :]
+            sh = sh_ref[h : h + 1, :]
+            lag_ref[h * inner : (h + 1) * inner, :] = (ch * cl - sh * sl).astype(jnp.bfloat16)
+            lag_ref[bins + h * inner : bins + (h + 1) * inner, :] = (-(sh * cl + ch * sl)).astype(
+                jnp.bfloat16
+            )
+
     lag = lag_ref[...]
     receivers = [mine_ref[:half, :].astype(jnp.float32), other_ref[:half, :].astype(jnp.float32)]
     places = [jnp.where(first, 0, half), jnp.where(first, half, 0)]
@@ -112,16 +124,16 @@
             )
 
 
-def correlate(low, high, half, lag):
+def correlate(low, high, half, pieces):
     rows, width = low.shape
     bins = width // 2
     count = 2 * (rows - half)
     block = 2 * half
-    lags = lag.shape[1]
+    lags = pieces[0].shape[1]
     group = 8
     factor = 1.0 / math.sqrt(bins)
     flops = 2 * count * block * width * lags + 6 * count * block * bins
-    moved = 4 * rows * width + 2 * lags * width + 4 * count * block * lags
+    moved = 4 * rows * width + 4 * lags * (bins // 16 + 64) + 4 * count * block * lags
     return pl.pallas_call(
         functools.partial(correlate_kernel, factor, bins, group, half),
         out_shape=jax.ShapeDtypeStruct((count, block, lags), jnp.float32),
@@ -129,12 +141,13 @@
         in_specs=[
             pl.BlockSpec((rows, width), lambda s: (0, 0)),
             pl.BlockSpec((rows, width), lambda s: (0, 0)),
-            pl.BlockSpec((width, lags), lambda s: (0, 0)),
-        ],
+        ]
+        + [pl.BlockSpec(piece.shape, lambda s: (0, 0)) for piece in pieces],
         out_specs=pl.BlockSpec((group, block, lags), lambda s: (s, 0, 0)),
+        scratch_shapes=[pltpu.VMEM((width, lags), jnp.bfloat16)],
         compiler_params=pltpu.CompilerParams(dimension_semantics=("arbitrary",)),
         cost_estimate=pl.CostEstimate(flops=flops, bytes_accessed=moved, transcendentals=0),
-    )(low, high, lag)
+    )(low, high, *pieces)
 
 
 def swap_tm(x):
@@ -181,11 +194,11 @@
     series = lax.all_to_all(rows, "chan", 0, 2, tiled=True).reshape(width, samples)
     table = dft_table(samples, bins, jnp.arange(samples, dtype=jnp.int32))
     lag_share = LAGS // n_tm
-    lag = lag_kernel(samples, tm * lag_share, lag_share)
+    pieces = lag_pieces(samples, tm * lag_share, lag_share)
 
     white = whiten_series(series, table)
     other = lax.ppermute(white, "tm", perm=[(0, 1), (1, 0)])
-    result = correlate(white, other, half, lag)
+    result = correlate(white, other, half, pieces)
     return result.reshape(STEPS, SRC, block, lag_share)
 
 

time: 51.7 us -> 51.7 us (level)
    sin x1 -> x2, other arithmetic: 0.28 us -> 1.53 us  [the longest x1 0.77 us: lag_pieces(): jnp.sin(high_angle)]
    concatenate x1 -> x0, other arithmetic: 0.84 us -> none  [lag_kernel(): return jnp.concatenate([cosine, -sine], axis=0).astype(jnp.bfloat16)]
where the time goes in v12:
time: 51.7 us; the launch traced here: 51.4 us
  waiting for transfers between devices  13 us (25%)
  Pallas kernels  10.6 us (21%)
  starting transfers between devices  9.85 us (19%)
  local copies, waits for them, and re-layouts  8.01 us (15%)
  other arithmetic  4 us (8%)
  matrix products  3.84 us (7%)
  between operations  2.16 us (4%)
    all_to_all x1, waiting for transfers between devices, local(): lax.all_to_all(rows, 'chan', 0, 2, tiled=True).reshape(width, samples)  11.5 us
    pallas_call x1, Pallas kernels, correlate(): pl.pallas_call(functools.partial(correlate_kernel, factor, bins, group, h...  10.6 us
    all_to_all x1, starting transfers between devices, local(): lax.all_to_all(rows, 'chan', 0, 2, tiled=True).reshape(width, samples)  7.3 us
    gather x1, local copies, waits for them, and re-layouts, local(): jnp.take(paired, index.reshape(-1), axis=0, mode='clip')  4.59 us
    dot_general x1, matrix products, local(): jnp.dot(taps_matrix[:, :raw_rows], records, preferred_element_type=jnp.fl...  2.6 us
    ppermute x1, starting transfers between devices, local(): halo = lax.ppermute(records[:halo_rows], ('chan', 'tm'), perm=shift)  1.29 us
    ppermute x1, waiting for transfers between devices, swap_tm(): other = lax.ppermute(x, 'tm', perm=[(0, 1), (1, 0)])  1.23 us
    ppermute x1, starting transfers between devices, swap_tm(): other = lax.ppermute(x, 'tm', perm=[(0, 1), (1, 0)])  1.19 us
  transfers between devices with their start and end apart: 4, of which 3 were waited for; matrix products, arithmetic and copies ran while one was open for 15% of the time, Pallas kernels for 0%

profile of v12, /device:TPU:0, one launch (start us, length us, event | category | flops | bytes accessed | tf_op | source)
XLA Modules:
  0.0 51.4 jit_solution(3886918470047220935)
XLA Ops:
  0.0 0.9 %slice.22 = bf16[24,3072]{1,0:T(8,128)(2,1)S(1)} slice(bf16[512,3072]{1,0:T(8,128)(2,1)} %param.5), slice={[0:24], [0:3072]} | slice | bytes 294912 | tf_op jit(solution)/shard_map/slice | solution.py:174
  0.9 1.3 %collective-permute-start = (bf16[24,3072]{1,0:T(8,128)(2,1)S(1)}, bf16[24,3072]{1,0:T(8,128)(2,1)S(1)}, u32[]{:S(2)}, u32[]{:S(2)}) collective-permute-start(bf16[24,3072]{1,0:T(8,128)(2,1)S(1)} %slice.22), channel_id=1, source_target_pairs={{1,0},{2,1},{3,2},{4,3},{5,4},{6,5},{7,6},{8,7},{9,8},{10,9},{11,1... | collective-permute-start | bytes 442376 | tf_op jit(solution)/shard_map/ppermute | solution.py:174
  2.2 0.7 %broadcast_in_dim.33 = f32[4,8]{1,0:T(4,128)S(1)} reshape(f32[32]{0:T(128)} %param.6) | data formatting | bytes 256 | tf_op jit(solution)/shard_map/jit(_where)/broadcast_in_dim | solution.py:28
  3.0 0.2 select_reduce_fusion
  3.3 0.2 copy.11
  3.5 0.0 copy-start.2
  3.5 0.0 copy-start.3
  3.5 0.0 copy-start.1
  3.5 2.6 %fusion.10 = f32[64,3072]{1,0:T(8,128)S(1)} fusion(bf16[512,3072]{1,0:T(8,128)(2,1)} %param.5, bf16[64,536]{0,1:T(8,128)(2,1)S(1)} %bitcast.22), kind=kOutput, calls=%fused_computation.24 | convolution fusion | flops 201326592 | bytes 4063232 | tf_op jit(solution)/shard_map/dot_general | solution.py:178
  6.1 0.0 copy-done.2
  6.1 0.0 copy-done.3
  6.1 0.6 %fusion.42 = s32[]{:T(128)} fusion(s32[2]{0:T(128)S(1)} %copy-done.2, s32[2]{0:T(128)S(1)} %copy-done.3, s32[]{:T(128)S(6)} %axis_index.16), kind=kLoop, calls=%fused_computation.76 | loop fusion | flops 9 | bytes 24 | tf_op jit(solution)/shard_map/reduce_sum | solution.py:186
  8.0 0.0 copy-done.1
  8.7 0.1 dynamic_slice.7
  8.8 0.1 pad.5.clone
  8.9 0.1 constant_dynamic-slice_fusion
  8.9 0.0 collective-permute-done
  8.9 0.3 fusion
  9.2 1.2 %collective-permute-start.1 = (bf16[64,3072]{1,0:T(8,128)(2,1)S(1)}, bf16[64,3072]{1,0:T(8,128)(2,1)S(1)}, u32[]{:S(2)}, u32[]{:S(2)}) collective-permute-start(bf16[64,3072]{1,0:T(8,128)(2,1)S(1)} %fusion), channel_id=1, source_target_pairs={{0,1},{1,0},{2,3},{3,2},{4,5},{5,4},{6,7},{7,6},{8,9},{9,8},{10,11... | collective-permute-start | bytes 1179656 | tf_op jit(solution)/shard_map/ppermute | solution.py:154
  10.4 0.1 reshape.176
  10.6 1.2 %collective-permute-done.1 = bf16[64,3072]{1,0:T(8,128)(2,1)S(1)} collective-permute-done((bf16[64,3072]{1,0:T(8,128)(2,1)S(1)}, bf16[64,3072]{1,0:T(8,128)(2,1)S(1)}, u32[]{:S(2)}, u32[]{:S(2)}) %collective-permute-start.1) | collective-permute-done | bytes 393248 | tf_op jit(solution)/shard_map/ppermute | solution.py:154
  11.8 0.1 broadcast_select_fusion.1
  11.8 0.1 maximum_bitcast_fusion
  11.9 0.4 copy.12
  12.3 4.6 %gather_fusion = bf16[1664,128]{1,0:T(8,128)(2,1)} fusion(bf16[3072,128]{1,0:T(8,128)(2,1)S(1)} %copy.12, s32[2048]{0:T(1024)S(1)} %pad_clamp_fusion), kind=kCustom, calls=%fused_computation | custom fusion | bytes 858624 | tf_op jit(solution)/shard_map/jit(_take)/gather | solution.py:193
  16.9 7.3 %all-to-all-start = ((bf16[8,208,128]{2,1,0:T(8,128)(2,1)}), bf16[8,208,128]{2,1,0:T(8,128)(2,1)S(1)}, u32[]{:S(2)}, u32[]{:S(2)}) async-start(bf16[8,208,128]{2,1,0:T(8,128)(2,1)} %bitcast.2), calls=%async_computation | async-start | bytes 851968 | tf_op jit(solution)/shard_map/all_to_all | solution.py:194
  24.2 0.3 fusion.29
  24.5 0.3 fusion.32
  24.8 0.8 %subtract_convert_fusion = (bf16[32,32,512]{2,1,0:T(8,128)(2,1)S(1)}, bf16[32,32,512]{2,1,0:T(8,128)(2,1)S(1)}) fusion(f32[32,512]{1,0:T(8,128)S(1)} %get-tuple-element.17, f32[32,512]{1,0:T(8,128)S(1)} %get-tuple-element.16, f32[32,512]{1,0:T(8,128)S(1)} %get-tuple-element.18, f32[32,512]{1,0:T(8,128)S(1)} %get-tuple-element.15), kind=kLoop, calls=%fused_computation.8 | loop fusion | flops 4718592 | bytes 2359296 | tf_op jit(solution)/shard_map/convert.5
  25.6 11.5 %all-to-all-done = bf16[8,208,128]{2,1,0:T(8,128)(2,1)S(1)} async-done(((bf16[8,208,128]{2,1,0:T(8,128)(2,1)}), bf16[8,208,128]{2,1,0:T(8,128)(2,1)S(1)}, u32[]{:S(2)}, u32[]{:S(2)}) %all-to-all-start) | async-done | bytes 426016 | tf_op jit(solution)/shard_map/all_to_all | solution.py:194
  37.1 0.1 copy.13
  37.2 0.6 %fusion.1 = f32[208,1024]{1,0:T(8,128)S(1)} fusion(bf16[1024,512]{1,0:T(8,128)(2,1)S(1)} %bitcast.21, bf16[1024,512]{1,0:T(8,128)(2,1)S(1)} %bitcast.20, bf16[26,8,8,128]{3,2,1,0:T(8,128)(2,1)S(1)} %bitcast.24), kind=kOutput, calls=%fused_computation.3 | convolution fusion | flops 440401920 | bytes 3375104 | tf_op jit(solution)/shard_map/dot_general | solution.py:69
  37.8 0.3 multiply_convert_fusion.1
  38.2 0.0 copy-start
  38.2 0.1 collective-permute-start.2
  38.3 0.8 %fusion.39 = (f32[16,256]{1,0:T(8,128)}, f32[16,256]{1,0:T(8,128)}) fusion(s32[256]{0:T(256)S(1)} %iota_add_fusion, s32[16]{0:T(128)S(1)} %iota_multiply_fusion.1), kind=kLoop, calls=%fused_computation.71 | loop fusion | flops 57344 | bytes 33856 | tf_op jit(solution)/shard_map/sin | solution.py:63
  39.1 0.8 %fusion.37 = (f32[32,256]{1,0:T(8,128)}, f32[32,256]{1,0:T(8,128)}) fusion(s32[256]{0:T(256)S(1)} %iota_add_fusion), kind=kLoop, calls=%fused_computation.67 | loop fusion | flops 114688 | bytes 66560 | tf_op jit(solution)/shard_map/sin | solution.py:63
  39.8 0.2 collective-permute-done.2.other_ref
  40.1 0.0 copy-start.4
  40.1 0.0 copy-done
  40.1 0.8 %copy-done.4 = bf16[208,1024]{1,0:T(8,128)(2,1)} copy-done((bf16[208,1024]{1,0:T(8,128)(2,1)}, bf16[208,1024]{1,0:T(8,128)(2,1)S(1)}, u32[]{:S(2)}) %copy-start.4) | copy-done | bytes 426008
  40.8 10.6 %shard_map.55 = f32[32,384,256]{2,1,0:T(8,128)} custom-call(bf16[208,1024]{1,0:T(8,128)(2,1)} %copy-done, bf16[208,1024]{1,0:T(8,128)(2,1)} %copy-done.4, f32[16,256]{1,0:T(8,128)} %get-tuple-element.12.ch_ref, f32[16,256]{1,0:T(8,128)} %get-tuple-element.11.sh_ref, f32[32,256]{1,0:T(8,128)} %get-tuple-element.14.cl_ref, f32[32,256]{1,0:T(8,128)} %get-tuple-element.13.sl_ref), custom_call_target="tpu_custom_call" | custom-call | flops 6480199680 | bytes 13533184 | tf_op jit(solution)/shard_map/pallas_call | solution.py:137
  (9 shorter events, 0.1 us)
Async XLA Ops:
  0.9 8.0 %collective-permute-start = (bf16[24,3072]{1,0:T(8,128)(2,1)S(1)}, bf16[24,3072]{1,0:T(8,128)(2,1)S(1)}, u32[]{:S(2)}, u32[]{:S(2)}) collective-permute-start(bf16[24,3072]{1,0:T(8,128)(2,1)S(1)} %slice.22), channel_id=1, source_target_pairs={{1,0},{2,1},{3,2},{4,3},{5,4},{6,5},{7,6},{8,7},{9,8},{10,9},{11,1... | collective-permute-start | bytes 442376 | tf_op jit(solution)/shard_map/ppermute | solution.py:174
  3.5 2.6 %copy-start.2 = (s32[2]{0:T(128)S(1)}, s32[2]{0:T(128)}, u32[]{:S(2)}) copy-start(s32[2]{0:T(128)} %param.9) | copy-start | bytes 28
  3.5 2.6 %copy-start.3 = (s32[2]{0:T(128)S(1)}, s32[2]{0:T(128)}, u32[]{:S(2)}) copy-start(s32[2]{0:T(128)} %param.8) | copy-start | bytes 28
  3.5 4.6 %copy-start.1 = (s32[3072]{0:T(1024)S(1)}, s32[3072]{0:T(1024)}, u32[]{:S(2)}) copy-start(s32[3072]{0:T(1024)} %param.7) | copy-start | bytes 36868
  9.2 2.5 %collective-permute-start.1 = (bf16[64,3072]{1,0:T(8,128)(2,1)S(1)}, bf16[64,3072]{1,0:T(8,128)(2,1)S(1)}, u32[]{:S(2)}, u32[]{:S(2)}) collective-permute-start(bf16[64,3072]{1,0:T(8,128)(2,1)S(1)} %fusion), channel_id=1, source_target_pairs={{0,1},{1,0},{2,3},{3,2},{4,5},{5,4},{6,7},{7,6},{8,9},{9,8},{10,11... | collective-permute-start | bytes 1179656 | tf_op jit(solution)/shard_map/ppermute | solution.py:154
  16.9 20.2 %all-to-all-start = ((bf16[8,208,128]{2,1,0:T(8,128)(2,1)}), bf16[8,208,128]{2,1,0:T(8,128)(2,1)S(1)}, u32[]{:S(2)}, u32[]{:S(2)}) async-start(bf16[8,208,128]{2,1,0:T(8,128)(2,1)} %bitcast.2), calls=%async_computation | async-start | bytes 851968 | tf_op jit(solution)/shard_map/all_to_all | solution.py:194
  38.2 1.9 %copy-start = (bf16[208,1024]{1,0:T(8,128)(2,1)}, bf16[208,1024]{1,0:T(8,128)(2,1)S(1)}, u32[]{:S(2)}) copy-start(bf16[208,1024]{1,0:T(8,128)(2,1)S(1)} %pad_maximum_fusion.mine_ref) | copy-start | bytes 1277956
  38.2 1.8 %collective-permute-start.2 = (bf16[208,1024]{1,0:T(8,128)(2,1)S(1)}, bf16[208,1024]{1,0:T(8,128)(2,1)S(1)}, u32[]{:S(2)}, u32[]{:S(2)}) collective-permute-start(bf16[208,1024]{1,0:T(8,128)(2,1)S(1)} %pad_maximum_fusion.mine_ref), channel_id=1, source_target_pairs={{0,1},{1,0},{2,3},{3,2},{4,5},{5,4},{6,7},{7,6},{8,9},{9,8},{10,11... | collective-permute-start | bytes 1277960 | tf_op jit(solution)/shard_map/ppermute | solution.py:200
  40.1 0.8 %copy-start.4 = (bf16[208,1024]{1,0:T(8,128)(2,1)}, bf16[208,1024]{1,0:T(8,128)(2,1)S(1)}, u32[]{:S(2)}) copy-start(bf16[208,1024]{1,0:T(8,128)(2,1)S(1)} %collective-permute-done.2.other_ref) | copy-start | bytes 1277956

commit v13 on v12

--- a/solution.py
+++ b/solution.py
@@ -63,14 +63,14 @@
     return jnp.cos(high_angle), jnp.sin(high_angle), jnp.cos(low_angle), jnp.sin(low_angle)
 
 
-def whiten_series(series, table):
+def whiten_series(series, table, band):
     samples = series.shape[1]
     bins = samples // 2
     spectrum = jnp.dot(series, table.astype(jnp.bfloat16), preferred_element_type=jnp.float32)
     real_part = spectrum[:, :bins]
     imag_part = spectrum[:, bins:]
     powers = real_part * real_part + imag_part * imag_part
-    window = jnp.dot(powers.astype(jnp.bfloat16), band_matrix(bins), preferred_element_type=jnp.float32)
+    window = jnp.dot(powers.astype(jnp.bfloat16), band, preferred_element_type=jnp.float32)
     window_span = 2 * HALF_BAND + 1
     factor = 1.0 / jnp.sqrt(window / window_span + epsilon)
     return jnp.concatenate([real_part * factor, imag_part * factor], axis=1).astype(jnp.bfloat16)
@@ -196,7 +196,10 @@
     lag_share = LAGS // n_tm
     pieces = lag_pieces(samples, tm * lag_share, lag_share)
 
-    white = whiten_series(series, table)
+    series, table, band, pieces = lax.optimization_barrier(
+        (series, table, band_matrix(bins), pieces)
+    )
+    white = whiten_series(series, table, band)
     other = lax.ppermute(white, "tm", perm=[(0, 1), (1, 0)])
     result = correlate(white, other, half, pieces)
     return result.reshape(STEPS, SRC, block, lag_share)

time: 51.7 us -> 56.2 us (1.087)
  other arithmetic: 4 us -> 7.97 us
  local copies, waits for them, and re-layouts: 8.01 us -> 10.8 us
  waiting for transfers between devices: 13 us -> 10.5 us
    all_to_all x1, waiting for transfers between devices: 11.5 us -> 8.77 us  [local(): lax.all_to_all(rows, 'chan', 0, 2, tiled=True).reshape(width, samples)]
    sub x0 -> x1, other arithmetic: none -> 1.69 us  [dft_table(): cosine = (ch * cl - sh * sl).reshape(samples, bins)]
    ppermute x1, waiting for transfers between devices: 0.22 us -> 1.76 us  [local(): other = lax.ppermute(white, 'tm', perm=[(0, 1), (1, 0)])]
    concatenate x0 -> x1, other arithmetic: none -> 1.48 us  [dft_table(): return jnp.concatenate([cosine, -sine], axis=1)]
    ppermute x1, waiting for transfers between devices: 1.23 us -> 0.01 us  [swap_tm(): other = lax.ppermute(x, 'tm', perm=[(0, 1), (1, 0)])]
    all_to_all x1, local copies, waits for them, and re-layouts: 0.11 us -> 1.12 us  [local(): lax.all_to_all(rows, 'chan', 0, 2, tiled=True).reshape(width, samples)]
    convert_element_type x0 -> x1, other arithmetic: none -> 0.88 us  [band_matrix(): return near.astype(jnp.bfloat16)]
    another operation x1 -> x0, other arithmetic: 0.76 us -> none
  transfers between devices with their start and end apart: 4 -> 4, of which waited for: 3 -> 2; matrix products, arithmetic and copies ran while one was open for 15% -> 23% of each run, Pallas kernels for 0% -> 0%
where the time goes in v13:
time: 56.2 us; the launch traced here: 55.6 us
  local copies, waits for them, and re-layouts  10.8 us (19%)
  Pallas kernels  10.6 us (19%)
  waiting for transfers between devices  10.5 us (19%)
  starting transfers between devices  9.84 us (18%)
  other arithmetic  7.97 us (14%)
  matrix products  3.8 us (7%)
  between operations  2.15 us (4%)
    pallas_call x1, Pallas kernels, correlate(): pl.pallas_call(functools.partial(correlate_kernel, factor, bins, group, h...  10.6 us
    all_to_all x1, waiting for transfers between devices, local(): lax.all_to_all(rows, 'chan', 0, 2, tiled=True).reshape(width, samples)  8.77 us
    all_to_all x1, starting transfers between devices, local(): lax.all_to_all(rows, 'chan', 0, 2, tiled=True).reshape(width, samples)  7.28 us
    gather x1, local copies, waits for them, and re-layouts, local(): jnp.take(paired, index.reshape(-1), axis=0, mode='clip')  4.55 us
    dot_general x1, matrix products, local(): jnp.dot(taps_matrix[:, :raw_rows], records, preferred_element_type=jnp.fl...  2.58 us
    ppermute x1, waiting for transfers between devices, local(): other = lax.ppermute(white, 'tm', perm=[(0, 1), (1, 0)])  1.76 us
    sub x1, other arithmetic, dft_table(): cosine = (ch * cl - sh * sl).reshape(samples, bins)  1.69 us
    concatenate x1, other arithmetic, dft_table(): return jnp.concatenate([cosine, -sine], axis=1)  1.48 us
  transfers between devices with their start and end apart: 4, of which 2 were waited for; matrix products, arithmetic and copies ran while one was open for 23% of the time, Pallas kernels for 0%

profile of v13, /device:TPU:0, one launch (start us, length us, event | category | flops | bytes accessed | tf_op | source)
XLA Modules:
  0.0 55.6 jit_solution(4875740309982256338)
XLA Ops:
  0.0 0.9 %slice.22 = bf16[24,3072]{1,0:T(8,128)(2,1)S(1)} slice(bf16[512,3072]{1,0:T(8,128)(2,1)} %param.5), slice={[0:24], [0:3072]} | slice | bytes 294912 | tf_op jit(solution)/shard_map/slice | solution.py:174
  0.9 1.3 %collective-permute-start = (bf16[24,3072]{1,0:T(8,128)(2,1)S(1)}, bf16[24,3072]{1,0:T(8,128)(2,1)S(1)}, u32[]{:S(2)}, u32[]{:S(2)}) collective-permute-start(bf16[24,3072]{1,0:T(8,128)(2,1)S(1)} %slice.22), channel_id=1, source_target_pairs={{1,0},{2,1},{3,2},{4,3},{5,4},{6,5},{7,6},{8,7},{9,8},{10,9},{11,1... | collective-permute-start | bytes 442376 | tf_op jit(solution)/shard_map/ppermute | solution.py:174
  2.3 1.3 %fusion.38 = s32[]{:T(128)} fusion(s32[2]{0:T(128)} %param.9, s32[2]{0:T(128)} %param.8, s32[]{:T(128)S(6)} %axis_index.16), kind=kLoop, calls=%fused_computation.74 | loop fusion | flops 9 | bytes 24 | tf_op jit(solution)/shard_map/reduce_sum | solution.py:186
  4.9 0.7 %reshape.165 = s32[8,384]{1,0:T(8,128)S(1)} reshape(s32[3072]{0:T(1024)} %param.7) | data formatting | bytes 24576 | tf_op jit(solution)/shard_map/reshape | solution.py:188
  6.2 0.8 %dynamic_slice.7 = s32[16]{0:T(128)S(1)} dynamic-slice(s32[3072]{0:T(1024)} %param.7, s32[]{:T(128)S(6)} %select_n.73), dynamic_slice_sizes={16} | dynamic-slice | bytes 132 | tf_op jit(solution)/shard_map/dynamic_slice | solution.py:187
  7.0 0.1 pad.5.clone
  7.1 0.7 %broadcast_in_dim.33 = f32[4,8]{1,0:T(4,128)S(1)} reshape(f32[32]{0:T(128)} %param.6) | data formatting | bytes 256 | tf_op jit(solution)/shard_map/jit(_where)/broadcast_in_dim | solution.py:28
  7.8 0.1 constant_dynamic-slice_fusion
  7.9 0.1 reshape.174
  8.0 0.2 select_reduce_fusion
  8.3 0.2 copy.11
  8.5 0.3 fusion.28
  8.8 2.6 %fusion.6 = f32[64,3072]{1,0:T(8,128)S(1)} fusion(bf16[512,3072]{1,0:T(8,128)(2,1)} %param.5, bf16[64,536]{0,1:T(8,128)(2,1)S(1)} %bitcast.26), kind=kOutput, calls=%fused_computation.22 | convolution fusion | flops 201326592 | bytes 4063232 | tf_op jit(solution)/shard_map/dot_general | solution.py:178
  11.4 0.3 fusion.25
  11.7 0.0 collective-permute-done
  11.7 0.3 fusion
  12.0 1.2 %collective-permute-start.1 = (bf16[64,3072]{1,0:T(8,128)(2,1)S(1)}, bf16[64,3072]{1,0:T(8,128)(2,1)S(1)}, u32[]{:S(2)}, u32[]{:S(2)}) collective-permute-start(bf16[64,3072]{1,0:T(8,128)(2,1)S(1)} %fusion), channel_id=1, source_target_pairs={{0,1},{1,0},{2,3},{3,2},{4,5},{5,4},{6,7},{7,6},{8,9},{9,8},{10,11... | collective-permute-start | bytes 1179656 | tf_op jit(solution)/shard_map/ppermute | solution.py:154
  13.2 1.7 %multiply_subtract_fusion = (bf16[32,32,512]{2,1,0:T(8,128)(2,1)S(1)}, bf16[32,32,512]{2,1,0:T(8,128)(2,1)}) fusion(f32[32,512]{1,0:T(8,128)S(1)} %get-tuple-element.31, f32[32,512]{1,0:T(8,128)S(1)} %get-tuple-element.30, f32[32,512]{1,0:T(8,128)S(1)} %get-tuple-element.32, f32[32,512]{1,0:T(8,128)S(1)} %get-tuple-element.29), kind=kLoop, calls=%fused_computation.7 | loop fusion | flops 4718592 | bytes 2359296 | tf_op jit(solution)/shard_map/sub | solution.py:43
  14.9 0.0 collective-permute-done.1
  14.9 0.1 broadcast_select_fusion.1
  15.0 0.1 maximum_bitcast_fusion
  15.0 0.4 copy.12
  15.4 4.5 %gather_fusion = bf16[1664,128]{1,0:T(8,128)(2,1)} fusion(bf16[3072,128]{1,0:T(8,128)(2,1)S(1)} %copy.12, s32[2048]{0:T(1024)S(1)} %pad_clamp_fusion), kind=kCustom, calls=%fused_computation | custom fusion | bytes 858624 | tf_op jit(solution)/shard_map/jit(_take)/gather | solution.py:193
  19.9 7.3 %all-to-all-start = ((bf16[8,208,128]{2,1,0:T(8,128)(2,1)}), bf16[8,208,128]{2,1,0:T(8,128)(2,1)}, u32[]{:S(2)}, u32[]{:S(2)}) async-start(bf16[8,208,128]{2,1,0:T(8,128)(2,1)} %bitcast.2), calls=%async_computation | async-start | bytes 851968 | tf_op jit(solution)/shard_map/all_to_all | solution.py:194
  27.2 0.9 %fusion.5 = bf16[512,512]{1,0:T(8,128)(2,1)} fusion(), kind=kLoop, calls=%fused_computation.13 | loop fusion | flops 1048576 | bytes 524288 | tf_op jit(solution)/shard_map/convert_element_type | solution.py:51
  28.1 1.5 %pad_maximum_fusion = bf16[1024,1024]{1,0:T(8,128)(2,1)S(1)} fusion(bf16[1024,512]{1,0:T(8,128)(2,1)} %bitcast.23, bf16[1024,512]{1,0:T(8,128)(2,1)S(1)} %bitcast.22), kind=kLoop, calls=%fused_computation.1 | loop fusion | flops 4194304 | bytes 4194304 | tf_op jit(solution)/shard_map/concatenate | solution.py:45
  29.6 0.8 %fusion.35 = (f32[16,256]{1,0:T(8,128)}, f32[16,256]{1,0:T(8,128)}) fusion(s32[256]{0:T(256)S(1)} %iota_add_fusion, s32[16]{0:T(128)S(1)} %iota_multiply_fusion.1), kind=kLoop, calls=%fused_computation.69 | loop fusion | flops 57344 | bytes 33856 | tf_op jit(solution)/shard_map/sin | solution.py:63
  30.4 0.8 %fusion.33 = (f32[32,256]{1,0:T(8,128)}, f32[32,256]{1,0:T(8,128)}) fusion(s32[256]{0:T(256)S(1)} %iota_add_fusion), kind=kLoop, calls=%fused_computation.65 | loop fusion | flops 114688 | bytes 66560 | tf_op jit(solution)/shard_map/sin | solution.py:63
  31.1 8.8 %all-to-all-done = bf16[8,208,128]{2,1,0:T(8,128)(2,1)} async-done(((bf16[8,208,128]{2,1,0:T(8,128)(2,1)}), bf16[8,208,128]{2,1,0:T(8,128)(2,1)}, u32[]{:S(2)}, u32[]{:S(2)}) %all-to-all-start) | async-done | bytes 426016 | tf_op jit(solution)/shard_map/all_to_all | solution.py:194
  39.9 1.1 %copy.13 = bf16[1,208,8,128]{3,2,1,0:T(8,128)(2,1)S(1)} copy(bf16[1,208,8,128]{3,1,2,0:T(8,128)(2,1)} %bitcast.4) | data formatting | bytes 851968 | tf_op jit(solution)/shard_map/all_to_all | solution.py:194
  41.0 0.0 copy-start
  41.0 0.1 copy.16
  41.1 0.6 %fusion.40 = f32[208,1024]{1,0:T(8,128)S(1)} fusion(bf16[208,1024]{1,0:T(8,128)(2,1)S(1)} %bitcast.24, bf16[1024,1024]{1,0:T(8,128)(2,1)S(1)} %pad_maximum_fusion), kind=kOutput, calls=%fused_computation.80 | convolution fusion | flops 436207616 | bytes 3375104 | tf_op jit(solution)/shard_map/dot_general | solution.py:69
  41.7 0.3 copy-done
  42.1 0.3 multiply_convert_fusion.1
  42.4 0.0 copy-start.1
  42.5 0.1 collective-permute-start.2
  42.5 1.8 %collective-permute-done.2.other_ref = bf16[208,1024]{1,0:T(8,128)(2,1)S(1)} collective-permute-done((bf16[208,1024]{1,0:T(8,128)(2,1)S(1)}, bf16[208,1024]{1,0:T(8,128)(2,1)S(1)}, u32[]{:S(2)}, u32[]{:S(2)}) %collective-permute-start.2) | collective-permute-done | bytes 426016 | tf_op jit(solution)/shard_map/ppermute | solution.py:203
  44.3 0.0 copy-done.1
  44.3 0.0 copy-start.2
  44.3 0.8 %copy-done.2 = bf16[208,1024]{1,0:T(8,128)(2,1)} copy-done((bf16[208,1024]{1,0:T(8,128)(2,1)}, bf16[208,1024]{1,0:T(8,128)(2,1)S(1)}, u32[]{:S(2)}) %copy-start.2) | copy-done | bytes 426008
  45.1 10.6 %shard_map.55 = f32[32,384,256]{2,1,0:T(8,128)} custom-call(bf16[208,1024]{1,0:T(8,128)(2,1)} %copy-done.1, bf16[208,1024]{1,0:T(8,128)(2,1)} %copy-done.2, f32[16,256]{1,0:T(8,128)} %get-tuple-element.15.ch_ref, f32[16,256]{1,0:T(8,128)} %get-tuple-element.16.sh_ref, f32[32,256]{1,0:T(8,128)} %get-tuple-element.17.cl_ref, f32[32,256]{1,0:T(8,128)} %get-tuple-element.18.sl_ref), custom_call_target="tpu_custom_call" | custom-call | flops 6480199680 | bytes 13533184 | tf_op jit(solution)/shard_map/pallas_call | solution.py:137
  (8 shorter events, 0.1 us)
Async XLA Ops:
  0.9 10.8 %collective-permute-start = (bf16[24,3072]{1,0:T(8,128)(2,1)S(1)}, bf16[24,3072]{1,0:T(8,128)(2,1)S(1)}, u32[]{:S(2)}, u32[]{:S(2)}) collective-permute-start(bf16[24,3072]{1,0:T(8,128)(2,1)S(1)} %slice.22), channel_id=1, source_target_pairs={{1,0},{2,1},{3,2},{4,3},{5,4},{6,5},{7,6},{8,7},{9,8},{10,9},{11,1... | collective-permute-start | bytes 442376 | tf_op jit(solution)/shard_map/ppermute | solution.py:174
  12.0 2.9 %collective-permute-start.1 = (bf16[64,3072]{1,0:T(8,128)(2,1)S(1)}, bf16[64,3072]{1,0:T(8,128)(2,1)S(1)}, u32[]{:S(2)}, u32[]{:S(2)}) collective-permute-start(bf16[64,3072]{1,0:T(8,128)(2,1)S(1)} %fusion), channel_id=1, source_target_pairs={{0,1},{1,0},{2,3},{3,2},{4,5},{5,4},{6,7},{7,6},{8,9},{9,8},{10,11... | collective-permute-start | bytes 1179656 | tf_op jit(solution)/shard_map/ppermute | solution.py:154
  19.9 20.0 %all-to-all-start = ((bf16[8,208,128]{2,1,0:T(8,128)(2,1)}), bf16[8,208,128]{2,1,0:T(8,128)(2,1)}, u32[]{:S(2)}, u32[]{:S(2)}) async-start(bf16[8,208,128]{2,1,0:T(8,128)(2,1)} %bitcast.2), calls=%async_computation | async-start | bytes 851968 | tf_op jit(solution)/shard_map/all_to_all | solution.py:194
  41.0 1.0 %copy-start = (bf16[512,512]{1,0:T(8,128)(2,1)S(1)}, bf16[512,512]{1,0:T(8,128)(2,1)}, u32[]{:S(2)}) copy-start(bf16[512,512]{1,0:T(8,128)(2,1)} %fusion.5) | copy-start | bytes 1572868
  42.4 1.8 %copy-start.1 = (bf16[208,1024]{1,0:T(8,128)(2,1)}, bf16[208,1024]{1,0:T(8,128)(2,1)S(1)}, u32[]{:S(2)}) copy-start(bf16[208,1024]{1,0:T(8,128)(2,1)S(1)} %pad_maximum_fusion.1.mine_ref) | copy-start | bytes 1277956
  42.5 1.8 %collective-permute-start.2 = (bf16[208,1024]{1,0:T(8,128)(2,1)S(1)}, bf16[208,1024]{1,0:T(8,128)(2,1)S(1)}, u32[]{:S(2)}, u32[]{:S(2)}) collective-permute-start(bf16[208,1024]{1,0:T(8,128)(2,1)S(1)} %pad_maximum_fusion.1.mine_ref), channel_id=1, source_target_pairs={{0,1},{1,0},{2,3},{3,2},{4,5},{5,4},{6,7},{7,6},{8,9},{9,8},{10,11... | collective-permute-start | bytes 1277960 | tf_op jit(solution)/shard_map/ppermute | solution.py:203
  44.3 0.8 %copy-start.2 = (bf16[208,1024]{1,0:T(8,128)(2,1)}, bf16[208,1024]{1,0:T(8,128)(2,1)S(1)}, u32[]{:S(2)}) copy-start(bf16[208,1024]{1,0:T(8,128)(2,1)S(1)} %collective-permute-done.2.other_ref) | copy-start | bytes 1277956

commit v14 on v11

--- a/solution.py
+++ b/solution.py
@@ -118,7 +118,7 @@
     count = 2 * (rows - half)
     block = 2 * half
     lags = lag.shape[1]
-    group = 8
+    group = 4
     factor = 1.0 / math.sqrt(bins)
     flops = 2 * count * block * width * lags + 6 * count * block * bins
     moved = 4 * rows * width + 2 * lags * width + 4 * count * block * lags

time: 51.7 us -> 52.4 us (1.014)
  Pallas kernels: 10.5 us -> 11.2 us
    pallas_call x1, Pallas kernels: 10.5 us -> 11.2 us  [correlate(): pl.pallas_call(functools.partial(correlate_kernel, factor, bins, group, h...]
where the time goes in v14:
time: 52.4 us; the launch traced here: 52.1 us
  waiting for transfers between devices  12.8 us (24%)
  Pallas kernels  11.2 us (21%)
  starting transfers between devices  9.85 us (19%)
  local copies, waits for them, and re-layouts  8.3 us (16%)
  other arithmetic  3.88 us (7%)
  matrix products  3.84 us (7%)
  between operations  2.18 us (4%)
    all_to_all x1, waiting for transfers between devices, local(): lax.all_to_all(rows, 'chan', 0, 2, tiled=True).reshape(width, samples)  11.6 us
    pallas_call x1, Pallas kernels, correlate(): pl.pallas_call(functools.partial(correlate_kernel, factor, bins, group, h...  11.2 us
    all_to_all x1, starting transfers between devices, local(): lax.all_to_all(rows, 'chan', 0, 2, tiled=True).reshape(width, samples)  7.3 us
    gather x1, local copies, waits for them, and re-layouts, local(): jnp.take(paired, index.reshape(-1), axis=0, mode='clip')  4.59 us
    dot_general x1, matrix products, local(): jnp.dot(taps_matrix[:, :raw_rows], records, preferred_element_type=jnp.fl...  2.6 us
    ppermute x1, starting transfers between devices, local(): halo = lax.ppermute(records[:halo_rows], ('chan', 'tm'), perm=shift)  1.29 us
    ppermute x1, starting transfers between devices, swap_tm(): other = lax.ppermute(x, 'tm', perm=[(0, 1), (1, 0)])  1.19 us
  transfers between devices with their start and end apart: 4, of which 3 were waited for; matrix products, arithmetic and copies ran while one was open for 15% of the time, Pallas kernels for 0%

profile of v14, /device:TPU:0, one launch (start us, length us, event | category | flops | bytes accessed | tf_op | source)
XLA Modules:
  0.0 52.1 jit_solution(13464236648871364261)
XLA Ops:
  0.0 0.9 %slice.22 = bf16[24,3072]{1,0:T(8,128)(2,1)S(1)} slice(bf16[512,3072]{1,0:T(8,128)(2,1)} %param.5), slice={[0:24], [0:3072]} | slice | bytes 294912 | tf_op jit(solution)/shard_map/slice | solution.py:161
  0.9 1.3 %collective-permute-start = (bf16[24,3072]{1,0:T(8,128)(2,1)S(1)}, bf16[24,3072]{1,0:T(8,128)(2,1)S(1)}, u32[]{:S(2)}, u32[]{:S(2)}) collective-permute-start(bf16[24,3072]{1,0:T(8,128)(2,1)S(1)} %slice.22), channel_id=1, source_target_pairs={{1,0},{2,1},{3,2},{4,3},{5,4},{6,5},{7,6},{8,7},{9,8},{10,9},{11,1... | collective-permute-start | bytes 442376 | tf_op jit(solution)/shard_map/ppermute | solution.py:161
  2.2 0.7 %broadcast_in_dim.33 = f32[4,8]{1,0:T(4,128)S(1)} reshape(f32[32]{0:T(128)} %param.6) | data formatting | bytes 256 | tf_op jit(solution)/shard_map/jit(_where)/broadcast_in_dim | solution.py:28
  3.0 0.2 select_reduce_fusion
  3.3 0.2 copy.15
  3.5 0.0 copy-start.2
  3.5 0.0 copy-start.3
  3.5 0.0 copy-start.1
  3.5 2.6 %fusion.10 = f32[64,3072]{1,0:T(8,128)S(1)} fusion(bf16[512,3072]{1,0:T(8,128)(2,1)} %param.5, bf16[64,536]{0,1:T(8,128)(2,1)S(1)} %bitcast.26), kind=kOutput, calls=%fused_computation.27 | convolution fusion | flops 201326592 | bytes 4063232 | tf_op jit(solution)/shard_map/dot_general | solution.py:165
  6.1 0.0 copy-done.2
  6.1 0.0 copy-done.3
  6.1 0.6 %fusion.45 = s32[]{:T(128)} fusion(s32[2]{0:T(128)S(1)} %copy-done.2, s32[2]{0:T(128)S(1)} %copy-done.3, s32[]{:T(128)S(6)} %axis_index.16), kind=kLoop, calls=%fused_computation.79 | loop fusion | flops 9 | bytes 24 | tf_op jit(solution)/shard_map/reduce_sum | solution.py:173
  8.0 0.0 copy-done.1
  8.7 0.1 dynamic_slice.7
  8.8 0.1 pad.7.clone
  8.9 0.1 constant_dynamic-slice_fusion
  8.9 0.0 collective-permute-done
  8.9 0.3 fusion
  9.2 1.2 %collective-permute-start.1 = (bf16[64,3072]{1,0:T(8,128)(2,1)S(1)}, bf16[64,3072]{1,0:T(8,128)(2,1)S(1)}, u32[]{:S(2)}, u32[]{:S(2)}) collective-permute-start(bf16[64,3072]{1,0:T(8,128)(2,1)S(1)} %fusion), channel_id=1, source_target_pairs={{0,1},{1,0},{2,3},{3,2},{4,5},{5,4},{6,7},{7,6},{8,9},{9,8},{10,11... | collective-permute-start | bytes 1179656 | tf_op jit(solution)/shard_map/ppermute | solution.py:141
  10.4 0.1 reshape.277
  10.6 0.3 fusion.32
  10.8 0.9 %collective-permute-done.1 = bf16[64,3072]{1,0:T(8,128)(2,1)S(1)} collective-permute-done((bf16[64,3072]{1,0:T(8,128)(2,1)S(1)}, bf16[64,3072]{1,0:T(8,128)(2,1)S(1)}, u32[]{:S(2)}, u32[]{:S(2)}) %collective-permute-start.1) | collective-permute-done | bytes 393248 | tf_op jit(solution)/shard_map/ppermute | solution.py:141
  11.8 0.1 broadcast_select_fusion.1
  11.8 0.1 maximum_bitcast_fusion
  11.9 0.4 copy.16
  12.3 4.6 %gather_fusion = bf16[1664,128]{1,0:T(8,128)(2,1)} fusion(bf16[3072,128]{1,0:T(8,128)(2,1)S(1)} %copy.16, s32[2048]{0:T(1024)S(1)} %pad_clamp_fusion), kind=kCustom, calls=%fused_computation | custom fusion | bytes 858624 | tf_op jit(solution)/shard_map/jit(_take)/gather | solution.py:180
  16.9 7.3 %all-to-all-start = ((bf16[8,208,128]{2,1,0:T(8,128)(2,1)}), bf16[8,208,128]{2,1,0:T(8,128)(2,1)S(1)}, u32[]{:S(2)}, u32[]{:S(2)}) async-start(bf16[8,208,128]{2,1,0:T(8,128)(2,1)} %bitcast.2), calls=%async_computation | async-start | bytes 851968 | tf_op jit(solution)/shard_map/all_to_all | solution.py:181
  24.2 0.2 fusion.43
  24.3 0.3 fusion.35
  24.7 0.8 %subtract_convert_fusion = (bf16[32,32,512]{2,1,0:T(8,128)(2,1)S(1)}, bf16[32,32,512]{2,1,0:T(8,128)(2,1)S(1)}) fusion(f32[32,512]{1,0:T(8,128)S(1)} %get-tuple-element.17, f32[32,512]{1,0:T(8,128)S(1)} %get-tuple-element.16, f32[32,512]{1,0:T(8,128)S(1)} %get-tuple-element.18, f32[32,512]{1,0:T(8,128)S(1)} %get-tuple-element.15), kind=kLoop, calls=%fused_computation.8 | loop fusion | flops 4718592 | bytes 2359296 | tf_op jit(solution)/shard_map/convert.9
  25.4 11.6 %all-to-all-done = bf16[8,208,128]{2,1,0:T(8,128)(2,1)S(1)} async-done(((bf16[8,208,128]{2,1,0:T(8,128)(2,1)}), bf16[8,208,128]{2,1,0:T(8,128)(2,1)S(1)}, u32[]{:S(2)}, u32[]{:S(2)}) %all-to-all-start) | async-done | bytes 426016 | tf_op jit(solution)/shard_map/all_to_all | solution.py:181
  37.1 0.1 copy.17
  37.2 0.6 %fusion.1 = f32[208,1024]{1,0:T(8,128)S(1)} fusion(bf16[1024,512]{1,0:T(8,128)(2,1)S(1)} %bitcast.23, bf16[1024,512]{1,0:T(8,128)(2,1)S(1)} %bitcast.22, bf16[26,8,8,128]{3,2,1,0:T(8,128)(2,1)S(1)} %bitcast.28), kind=kOutput, calls=%fused_computation.3 | convolution fusion | flops 440401920 | bytes 3375104 | tf_op jit(solution)/shard_map/dot_general | solution.py:73
  37.8 0.3 multiply_convert_fusion.1
  38.2 0.0 copy-start
  38.2 0.1 collective-permute-start.2
  38.3 0.3 fusion.30
  38.6 0.1 subtract_convert_fusion.1
  38.7 0.1 copy.18
  38.9 0.1 copy.19
  39.0 0.8 %pad_maximum_fusion.lag_ref = bf16[1024,256]{1,0:T(8,128)(2,1)} fusion(bf16[512,256]{1,0:T(8,128)(2,1)S(1)} %copy.19, bf16[512,256]{1,0:T(8,128)(2,1)S(1)} %copy.18), kind=kLoop, calls=%fused_computation.15 | loop fusion | flops 1048576 | bytes 1048576 | tf_op jit(solution)/shard_map/concatenate | solution.py:67
  39.9 0.2 collective-permute-done.2.other_ref
  40.1 0.0 copy-done
  40.1 0.0 copy-start.4
  40.1 0.8 %copy-done.4 = bf16[208,1024]{1,0:T(8,128)(2,1)} copy-done((bf16[208,1024]{1,0:T(8,128)(2,1)}, bf16[208,1024]{1,0:T(8,128)(2,1)S(1)}, u32[]{:S(2)}) %copy-start.4) | copy-done | bytes 426008
  40.8 11.2 %shard_map.55 = f32[32,384,256]{2,1,0:T(8,128)} custom-call(bf16[208,1024]{1,0:T(8,128)(2,1)} %copy-done, bf16[208,1024]{1,0:T(8,128)(2,1)} %copy-done.4, bf16[1024,256]{1,0:T(8,128)(2,1)} %pad_maximum_fusion.lag_ref), custom_call_target="tpu_custom_call" | custom-call | flops 6480199680 | bytes 13959168 | tf_op jit(solution)/shard_map/pallas_call | solution.py:125
  (8 shorter events, 0.1 us)
Async XLA Ops:
  0.9 8.0 %collective-permute-start = (bf16[24,3072]{1,0:T(8,128)(2,1)S(1)}, bf16[24,3072]{1,0:T(8,128)(2,1)S(1)}, u32[]{:S(2)}, u32[]{:S(2)}) collective-permute-start(bf16[24,3072]{1,0:T(8,128)(2,1)S(1)} %slice.22), channel_id=1, source_target_pairs={{1,0},{2,1},{3,2},{4,3},{5,4},{6,5},{7,6},{8,7},{9,8},{10,9},{11,1... | collective-permute-start | bytes 442376 | tf_op jit(solution)/shard_map/ppermute | solution.py:161
  3.5 2.6 %copy-start.2 = (s32[2]{0:T(128)S(1)}, s32[2]{0:T(128)}, u32[]{:S(2)}) copy-start(s32[2]{0:T(128)} %param.9) | copy-start | bytes 28
  3.5 2.6 %copy-start.3 = (s32[2]{0:T(128)S(1)}, s32[2]{0:T(128)}, u32[]{:S(2)}) copy-start(s32[2]{0:T(128)} %param.8) | copy-start | bytes 28
  3.5 4.6 %copy-start.1 = (s32[3072]{0:T(1024)S(1)}, s32[3072]{0:T(1024)}, u32[]{:S(2)}) copy-start(s32[3072]{0:T(1024)} %param.7) | copy-start | bytes 36868
  9.2 2.5 %collective-permute-start.1 = (bf16[64,3072]{1,0:T(8,128)(2,1)S(1)}, bf16[64,3072]{1,0:T(8,128)(2,1)S(1)}, u32[]{:S(2)}, u32[]{:S(2)}) collective-permute-start(bf16[64,3072]{1,0:T(8,128)(2,1)S(1)} %fusion), channel_id=1, source_target_pairs={{0,1},{1,0},{2,3},{3,2},{4,5},{5,4},{6,7},{7,6},{8,9},{9,8},{10,11... | collective-permute-start | bytes 1179656 | tf_op jit(solution)/shard_map/ppermute | solution.py:141
  16.9 20.2 %all-to-all-start = ((bf16[8,208,128]{2,1,0:T(8,128)(2,1)}), bf16[8,208,128]{2,1,0:T(8,128)(2,1)S(1)}, u32[]{:S(2)}, u32[]{:S(2)}) async-start(bf16[8,208,128]{2,1,0:T(8,128)(2,1)} %bitcast.2), calls=%async_computation | async-start | bytes 851968 | tf_op jit(solution)/shard_map/all_to_all | solution.py:181
  38.2 1.8 %copy-start = (bf16[208,1024]{1,0:T(8,128)(2,1)}, bf16[208,1024]{1,0:T(8,128)(2,1)S(1)}, u32[]{:S(2)}) copy-start(bf16[208,1024]{1,0:T(8,128)(2,1)S(1)} %pad_maximum_fusion.1.mine_ref) | copy-start | bytes 1277956
  38.2 1.8 %collective-permute-start.2 = (bf16[208,1024]{1,0:T(8,128)(2,1)S(1)}, bf16[208,1024]{1,0:T(8,128)(2,1)S(1)}, u32[]{:S(2)}, u32[]{:S(2)}) collective-permute-start(bf16[208,1024]{1,0:T(8,128)(2,1)S(1)} %pad_maximum_fusion.1.mine_ref), channel_id=1, source_target_pairs={{0,1},{1,0},{2,3},{3,2},{4,5},{5,4},{6,7},{7,6},{8,9},{9,8},{10,11... | collective-permute-start | bytes 1277960 | tf_op jit(solution)/shard_map/ppermute | solution.py:187
  40.1 0.8 %copy-start.4 = (bf16[208,1024]{1,0:T(8,128)(2,1)}, bf16[208,1024]{1,0:T(8,128)(2,1)S(1)}, u32[]{:S(2)}) copy-start(bf16[208,1024]{1,0:T(8,128)(2,1)S(1)} %collective-permute-done.2.other_ref) | copy-start | bytes 1277956

commit v15 on v14

--- a/solution.py
+++ b/solution.py
@@ -118,7 +118,7 @@
     count = 2 * (rows - half)
     block = 2 * half
     lags = lag.shape[1]
-    group = 4
+    group = 16
     factor = 1.0 / math.sqrt(bins)
     flops = 2 * count * block * width * lags + 6 * count * block * bins
     moved = 4 * rows * width + 2 * lags * width + 4 * count * block * lags

time: 52.4 us -> 52.3 us (level)
  no operation moved by 1% of the time
where the time goes in v15:
time: 52.3 us; the launch traced here: 52 us
  waiting for transfers between devices  12.8 us (24%)
  Pallas kernels  11.2 us (21%)
  starting transfers between devices  9.85 us (19%)
  local copies, waits for them, and re-layouts  8.3 us (16%)
  other arithmetic  3.88 us (7%)
  matrix products  3.84 us (7%)
  between operations  2.18 us (4%)
    all_to_all x1, waiting for transfers between devices, local(): lax.all_to_all(rows, 'chan', 0, 2, tiled=True).reshape(width, samples)  11.6 us
    pallas_call x1, Pallas kernels, correlate(): pl.pallas_call(functools.partial(correlate_kernel, factor, bins, group, h...  11.2 us
    all_to_all x1, starting transfers between devices, local(): lax.all_to_all(rows, 'chan', 0, 2, tiled=True).reshape(width, samples)  7.3 us
    gather x1, local copies, waits for them, and re-layouts, local(): jnp.take(paired, index.reshape(-1), axis=0, mode='clip')  4.59 us
    dot_general x1, matrix products, local(): jnp.dot(taps_matrix[:, :raw_rows], records, preferred_element_type=jnp.fl...  2.6 us
    ppermute x1, starting transfers between devices, local(): halo = lax.ppermute(records[:halo_rows], ('chan', 'tm'), perm=shift)  1.29 us
    ppermute x1, starting transfers between devices, swap_tm(): other = lax.ppermute(x, 'tm', perm=[(0, 1), (1, 0)])  1.19 us
  transfers between devices with their start and end apart: 4, of which 3 were waited for; matrix products, arithmetic and copies ran while one was open for 15% of the time, Pallas kernels for 0%

profile of v15, /device:TPU:0, one launch (start us, length us, event | category | flops | bytes accessed | tf_op | source)
XLA Modules:
  0.0 52.0 jit_solution(15300782389454290721)
XLA Ops:
  0.0 0.9 %slice.22 = bf16[24,3072]{1,0:T(8,128)(2,1)S(1)} slice(bf16[512,3072]{1,0:T(8,128)(2,1)} %param.5), slice={[0:24], [0:3072]} | slice | bytes 294912 | tf_op jit(solution)/shard_map/slice | solution.py:161
  0.9 1.3 %collective-permute-start = (bf16[24,3072]{1,0:T(8,128)(2,1)S(1)}, bf16[24,3072]{1,0:T(8,128)(2,1)S(1)}, u32[]{:S(2)}, u32[]{:S(2)}) collective-permute-start(bf16[24,3072]{1,0:T(8,128)(2,1)S(1)} %slice.22), channel_id=1, source_target_pairs={{1,0},{2,1},{3,2},{4,3},{5,4},{6,5},{7,6},{8,7},{9,8},{10,9},{11,1... | collective-permute-start | bytes 442376 | tf_op jit(solution)/shard_map/ppermute | solution.py:161
  2.2 0.7 %broadcast_in_dim.33 = f32[4,8]{1,0:T(4,128)S(1)} reshape(f32[32]{0:T(128)} %param.6) | data formatting | bytes 256 | tf_op jit(solution)/shard_map/jit(_where)/broadcast_in_dim | solution.py:28
  3.0 0.2 select_reduce_fusion
  3.3 0.2 copy.15
  3.5 0.0 copy-start.2
  3.5 0.0 copy-start.3
  3.5 0.0 copy-start.1
  3.5 2.6 %fusion.10 = f32[64,3072]{1,0:T(8,128)S(1)} fusion(bf16[512,3072]{1,0:T(8,128)(2,1)} %param.5, bf16[64,536]{0,1:T(8,128)(2,1)S(1)} %bitcast.26), kind=kOutput, calls=%fused_computation.27 | convolution fusion | flops 201326592 | bytes 4063232 | tf_op jit(solution)/shard_map/dot_general | solution.py:165
  6.1 0.0 copy-done.2
  6.1 0.0 copy-done.3
  6.1 0.6 %fusion.45 = s32[]{:T(128)} fusion(s32[2]{0:T(128)S(1)} %copy-done.2, s32[2]{0:T(128)S(1)} %copy-done.3, s32[]{:T(128)S(6)} %axis_index.16), kind=kLoop, calls=%fused_computation.79 | loop fusion | flops 9 | bytes 24 | tf_op jit(solution)/shard_map/reduce_sum | solution.py:173
  8.0 0.0 copy-done.1
  8.7 0.1 dynamic_slice.7
  8.8 0.1 pad.7.clone
  8.9 0.1 constant_dynamic-slice_fusion
  8.9 0.0 collective-permute-done
  8.9 0.3 fusion
  9.2 1.2 %collective-permute-start.1 = (bf16[64,3072]{1,0:T(8,128)(2,1)S(1)}, bf16[64,3072]{1,0:T(8,128)(2,1)S(1)}, u32[]{:S(2)}, u32[]{:S(2)}) collective-permute-start(bf16[64,3072]{1,0:T(8,128)(2,1)S(1)} %fusion), channel_id=1, source_target_pairs={{0,1},{1,0},{2,3},{3,2},{4,5},{5,4},{6,7},{7,6},{8,9},{9,8},{10,11... | collective-permute-start | bytes 1179656 | tf_op jit(solution)/shard_map/ppermute | solution.py:141
  10.4 0.1 reshape.277
  10.6 0.3 fusion.32
  10.8 0.9 %collective-permute-done.1 = bf16[64,3072]{1,0:T(8,128)(2,1)S(1)} collective-permute-done((bf16[64,3072]{1,0:T(8,128)(2,1)S(1)}, bf16[64,3072]{1,0:T(8,128)(2,1)S(1)}, u32[]{:S(2)}, u32[]{:S(2)}) %collective-permute-start.1) | collective-permute-done | bytes 393248 | tf_op jit(solution)/shard_map/ppermute | solution.py:141
  11.8 0.1 broadcast_select_fusion.1
  11.8 0.1 maximum_bitcast_fusion
  11.9 0.4 copy.16
  12.3 4.6 %gather_fusion = bf16[1664,128]{1,0:T(8,128)(2,1)} fusion(bf16[3072,128]{1,0:T(8,128)(2,1)S(1)} %copy.16, s32[2048]{0:T(1024)S(1)} %pad_clamp_fusion), kind=kCustom, calls=%fused_computation | custom fusion | bytes 858624 | tf_op jit(solution)/shard_map/jit(_take)/gather | solution.py:180
  16.9 7.3 %all-to-all-start = ((bf16[8,208,128]{2,1,0:T(8,128)(2,1)}), bf16[8,208,128]{2,1,0:T(8,128)(2,1)S(1)}, u32[]{:S(2)}, u32[]{:S(2)}) async-start(bf16[8,208,128]{2,1,0:T(8,128)(2,1)} %bitcast.2), calls=%async_computation | async-start | bytes 851968 | tf_op jit(solution)/shard_map/all_to_all | solution.py:181
  24.2 0.2 fusion.43
  24.3 0.3 fusion.35
  24.7 0.8 %subtract_convert_fusion = (bf16[32,32,512]{2,1,0:T(8,128)(2,1)S(1)}, bf16[32,32,512]{2,1,0:T(8,128)(2,1)S(1)}) fusion(f32[32,512]{1,0:T(8,128)S(1)} %get-tuple-element.17, f32[32,512]{1,0:T(8,128)S(1)} %get-tuple-element.16, f32[32,512]{1,0:T(8,128)S(1)} %get-tuple-element.18, f32[32,512]{1,0:T(8,128)S(1)} %get-tuple-element.15), kind=kLoop, calls=%fused_computation.8 | loop fusion | flops 4718592 | bytes 2359296 | tf_op jit(solution)/shard_map/convert.9
  25.4 11.6 %all-to-all-done = bf16[8,208,128]{2,1,0:T(8,128)(2,1)S(1)} async-done(((bf16[8,208,128]{2,1,0:T(8,128)(2,1)}), bf16[8,208,128]{2,1,0:T(8,128)(2,1)S(1)}, u32[]{:S(2)}, u32[]{:S(2)}) %all-to-all-start) | async-done | bytes 426016 | tf_op jit(solution)/shard_map/all_to_all | solution.py:181
  37.1 0.1 copy.17
  37.2 0.6 %fusion.1 = f32[208,1024]{1,0:T(8,128)S(1)} fusion(bf16[1024,512]{1,0:T(8,128)(2,1)S(1)} %bitcast.23, bf16[1024,512]{1,0:T(8,128)(2,1)S(1)} %bitcast.22, bf16[26,8,8,128]{3,2,1,0:T(8,128)(2,1)S(1)} %bitcast.28), kind=kOutput, calls=%fused_computation.3 | convolution fusion | flops 440401920 | bytes 3375104 | tf_op jit(solution)/shard_map/dot_general | solution.py:73
  37.8 0.3 multiply_convert_fusion.1
  38.2 0.0 copy-start
  38.2 0.1 collective-permute-start.2
  38.3 0.3 fusion.30
  38.6 0.1 subtract_convert_fusion.1
  38.7 0.1 copy.18
  38.9 0.1 copy.19
  39.0 0.8 %pad_maximum_fusion.lag_ref = bf16[1024,256]{1,0:T(8,128)(2,1)} fusion(bf16[512,256]{1,0:T(8,128)(2,1)S(1)} %copy.19, bf16[512,256]{1,0:T(8,128)(2,1)S(1)} %copy.18), kind=kLoop, calls=%fused_computation.15 | loop fusion | flops 1048576 | bytes 1048576 | tf_op jit(solution)/shard_map/concatenate | solution.py:67
  39.9 0.2 collective-permute-done.2.other_ref
  40.1 0.0 copy-done
  40.1 0.0 copy-start.4
  40.1 0.8 %copy-done.4 = bf16[208,1024]{1,0:T(8,128)(2,1)} copy-done((bf16[208,1024]{1,0:T(8,128)(2,1)}, bf16[208,1024]{1,0:T(8,128)(2,1)S(1)}, u32[]{:S(2)}) %copy-start.4) | copy-done | bytes 426008
  40.8 11.2 %shard_map.55 = f32[32,384,256]{2,1,0:T(8,128)} custom-call(bf16[208,1024]{1,0:T(8,128)(2,1)} %copy-done, bf16[208,1024]{1,0:T(8,128)(2,1)} %copy-done.4, bf16[1024,256]{1,0:T(8,128)(2,1)} %pad_maximum_fusion.lag_ref), custom_call_target="tpu_custom_call" | custom-call | flops 6480199680 | bytes 13959168 | tf_op jit(solution)/shard_map/pallas_call | solution.py:125
  (8 shorter events, 0.1 us)
Async XLA Ops:
  0.9 8.0 %collective-permute-start = (bf16[24,3072]{1,0:T(8,128)(2,1)S(1)}, bf16[24,3072]{1,0:T(8,128)(2,1)S(1)}, u32[]{:S(2)}, u32[]{:S(2)}) collective-permute-start(bf16[24,3072]{1,0:T(8,128)(2,1)S(1)} %slice.22), channel_id=1, source_target_pairs={{1,0},{2,1},{3,2},{4,3},{5,4},{6,5},{7,6},{8,7},{9,8},{10,9},{11,1... | collective-permute-start | bytes 442376 | tf_op jit(solution)/shard_map/ppermute | solution.py:161
  3.5 2.6 %copy-start.2 = (s32[2]{0:T(128)S(1)}, s32[2]{0:T(128)}, u32[]{:S(2)}) copy-start(s32[2]{0:T(128)} %param.9) | copy-start | bytes 28
  3.5 2.6 %copy-start.3 = (s32[2]{0:T(128)S(1)}, s32[2]{0:T(128)}, u32[]{:S(2)}) copy-start(s32[2]{0:T(128)} %param.8) | copy-start | bytes 28
  3.5 4.6 %copy-start.1 = (s32[3072]{0:T(1024)S(1)}, s32[3072]{0:T(1024)}, u32[]{:S(2)}) copy-start(s32[3072]{0:T(1024)} %param.7) | copy-start | bytes 36868
  9.2 2.5 %collective-permute-start.1 = (bf16[64,3072]{1,0:T(8,128)(2,1)S(1)}, bf16[64,3072]{1,0:T(8,128)(2,1)S(1)}, u32[]{:S(2)}, u32[]{:S(2)}) collective-permute-start(bf16[64,3072]{1,0:T(8,128)(2,1)S(1)} %fusion), channel_id=1, source_target_pairs={{0,1},{1,0},{2,3},{3,2},{4,5},{5,4},{6,7},{7,6},{8,9},{9,8},{10,11... | collective-permute-start | bytes 1179656 | tf_op jit(solution)/shard_map/ppermute | solution.py:141
  16.9 20.2 %all-to-all-start = ((bf16[8,208,128]{2,1,0:T(8,128)(2,1)}), bf16[8,208,128]{2,1,0:T(8,128)(2,1)S(1)}, u32[]{:S(2)}, u32[]{:S(2)}) async-start(bf16[8,208,128]{2,1,0:T(8,128)(2,1)} %bitcast.2), calls=%async_computation | async-start | bytes 851968 | tf_op jit(solution)/shard_map/all_to_all | solution.py:181
  38.2 1.8 %copy-start = (bf16[208,1024]{1,0:T(8,128)(2,1)}, bf16[208,1024]{1,0:T(8,128)(2,1)S(1)}, u32[]{:S(2)}) copy-start(bf16[208,1024]{1,0:T(8,128)(2,1)S(1)} %pad_maximum_fusion.1.mine_ref) | copy-start | bytes 1277956
  38.2 1.8 %collective-permute-start.2 = (bf16[208,1024]{1,0:T(8,128)(2,1)S(1)}, bf16[208,1024]{1,0:T(8,128)(2,1)S(1)}, u32[]{:S(2)}, u32[]{:S(2)}) collective-permute-start(bf16[208,1024]{1,0:T(8,128)(2,1)S(1)} %pad_maximum_fusion.1.mine_ref), channel_id=1, source_target_pairs={{0,1},{1,0},{2,3},{3,2},{4,5},{5,4},{6,7},{7,6},{8,9},{9,8},{10,11... | collective-permute-start | bytes 1277960 | tf_op jit(solution)/shard_map/ppermute | solution.py:187
  40.1 0.8 %copy-start.4 = (bf16[208,1024]{1,0:T(8,128)(2,1)}, bf16[208,1024]{1,0:T(8,128)(2,1)S(1)}, u32[]{:S(2)}) copy-start(bf16[208,1024]{1,0:T(8,128)(2,1)S(1)} %collective-permute-done.2.other_ref) | copy-start | bytes 1277956

commit v16 on v11

--- a/solution.py
+++ b/solution.py
@@ -80,8 +80,13 @@
     return jnp.concatenate([real_part * factor, imag_part * factor], axis=1).astype(jnp.bfloat16)
 
 
-def correlate_kernel(factor, bins, group, half, mine_ref, other_ref, lag_ref, out_ref):
+def correlate_kernel(factor, bins, group, half, mine_ref, other_ref, lag_ref, out_ref, buf, sems):
     step = pl.program_id(0)
+    last = pl.num_programs(0) - 1
+
+    def copy(slot, index):
+        return pltpu.make_async_copy(buf.at[slot], out_ref.at[index], sems.at[slot])
+
     first = lax.axis_index("tm") == 0
     lag = lag_ref[...]
     receivers = [mine_ref[:half, :].astype(jnp.float32), other_ref[:half, :].astype(jnp.float32)]
@@ -97,6 +102,15 @@
     for g in range(1, every.shape[0] // group):
         picked = jnp.where(step == g, every[g * group : (g + 1) * group], picked)
     for k in range(group):
+        slot = k % 2
+        if k >= 2:
+            copy(slot, 0).wait()
+        else:
+
+            @pl.when(step > 0)
+            def _():
+                copy(slot, 0).wait()
+
         row = picked[k : k + 1]
         real_src = row[:, :bins]
         imag_src = row[:, bins:]
@@ -107,9 +121,15 @@
                 [real_src * real_rcv + imag_src * imag_rcv, imag_src * real_rcv - real_src * imag_rcv],
                 axis=1,
             ).astype(jnp.bfloat16)
-            out_ref[k, pl.ds(pl.multiple_of(places[part], 8), half), :] = (
+            buf[slot, pl.ds(pl.multiple_of(places[part], 8), half), :] = (
                 jnp.dot(cross, lag, preferred_element_type=jnp.float32) * factor
             )
+        copy(slot, step * group + k).start()
+
+    @pl.when(step == last)
+    def _():
+        for slot in range(2):
+            copy(slot, 0).wait()
 
 
 def correlate(low, high, half, lag):
@@ -131,7 +151,8 @@
             pl.BlockSpec((rows, width), lambda s: (0, 0)),
             pl.BlockSpec((width, lags), lambda s: (0, 0)),
         ],
-        out_specs=pl.BlockSpec((group, block, lags), lambda s: (s, 0, 0)),
+        out_specs=pl.BlockSpec(memory_space=pl.ANY),
+        scratch_shapes=[pltpu.VMEM((2, block, lags), jnp.float32), pltpu.SemaphoreType.DMA((2,))],
         compiler_params=pltpu.CompilerParams(dimension_semantics=("arbitrary",)),
         cost_estimate=pl.CostEstimate(flops=flops, bytes_accessed=moved, transcendentals=0),
     )(low, high, lag)

time: 51.7 us -> 61.4 us (1.19)
  Pallas kernels: 10.5 us -> 20.2 us
    pallas_call x1, Pallas kernels: 10.5 us -> 20.2 us  [correlate(): pl.pallas_call(functools.partial(correlate_kernel, factor, bins, group, h...]
  transfers between devices with their start and end apart: 4 -> 4, of which waited for: 3 -> 3; matrix products, arithmetic and copies ran while one was open for 15% -> 13% of each run, Pallas kernels for 0% -> 0%
where the time goes in v16:
time: 61.4 us; the launch traced here: 61.1 us
  Pallas kernels  20.2 us (33%)
  waiting for transfers between devices  12.8 us (21%)
  starting transfers between devices  9.85 us (16%)
  local copies, waits for them, and re-layouts  8.3 us (14%)
  other arithmetic  3.88 us (6%)
  matrix products  3.84 us (6%)
  between operations  2.18 us (4%)
    pallas_call x1, Pallas kernels, correlate(): pl.pallas_call(functools.partial(correlate_kernel, factor, bins, group, h...  20.2 us
    all_to_all x1, waiting for transfers between devices, local(): lax.all_to_all(rows, 'chan', 0, 2, tiled=True).reshape(width, samples)  11.6 us
    all_to_all x1, starting transfers between devices, local(): lax.all_to_all(rows, 'chan', 0, 2, tiled=True).reshape(width, samples)  7.3 us
    gather x1, local copies, waits for them, and re-layouts, local(): jnp.take(paired, index.reshape(-1), axis=0, mode='clip')  4.59 us
    dot_general x1, matrix products, local(): jnp.dot(taps_matrix[:, :raw_rows], records, preferred_element_type=jnp.fl...  2.6 us
    ppermute x1, starting transfers between devices, local(): halo = lax.ppermute(records[:halo_rows], ('chan', 'tm'), perm=shift)  1.29 us
  transfers between devices with their start and end apart: 4, of which 3 were waited for; matrix products, arithmetic and copies ran while one was open for 13% of the time, Pallas kernels for 0%

profile of v16, /device:TPU:0, one launch (start us, length us, event | category | flops | bytes accessed | tf_op | source)
XLA Modules:
  0.0 61.1 jit_solution(1099953027083549241)
XLA Ops:
  0.0 0.9 %slice.22 = bf16[24,3072]{1,0:T(8,128)(2,1)S(1)} slice(bf16[512,3072]{1,0:T(8,128)(2,1)} %param.5), slice={[0:24], [0:3072]} | slice | bytes 294912 | tf_op jit(solution)/shard_map/slice | solution.py:182
  0.9 1.3 %collective-permute-start = (bf16[24,3072]{1,0:T(8,128)(2,1)S(1)}, bf16[24,3072]{1,0:T(8,128)(2,1)S(1)}, u32[]{:S(2)}, u32[]{:S(2)}) collective-permute-start(bf16[24,3072]{1,0:T(8,128)(2,1)S(1)} %slice.22), channel_id=1, source_target_pairs={{1,0},{2,1},{3,2},{4,3},{5,4},{6,5},{7,6},{8,7},{9,8},{10,9},{11,1... | collective-permute-start | bytes 442376 | tf_op jit(solution)/shard_map/ppermute | solution.py:182
  2.2 0.7 %broadcast_in_dim.33 = f32[4,8]{1,0:T(4,128)S(1)} reshape(f32[32]{0:T(128)} %param.6) | data formatting | bytes 256 | tf_op jit(solution)/shard_map/jit(_where)/broadcast_in_dim | solution.py:28
  3.0 0.2 select_reduce_fusion
  3.3 0.2 copy.15
  3.5 0.0 copy-start.2
  3.5 0.0 copy-start.3
  3.5 0.0 copy-start.1
  3.5 2.6 %fusion.10 = f32[64,3072]{1,0:T(8,128)S(1)} fusion(bf16[512,3072]{1,0:T(8,128)(2,1)} %param.5, bf16[64,536]{0,1:T(8,128)(2,1)S(1)} %bitcast.26), kind=kOutput, calls=%fused_computation.27 | convolution fusion | flops 201326592 | bytes 4063232 | tf_op jit(solution)/shard_map/dot_general | solution.py:186
  6.1 0.0 copy-done.2
  6.1 0.0 copy-done.3
  6.1 0.6 %fusion.45 = s32[]{:T(128)} fusion(s32[2]{0:T(128)S(1)} %copy-done.2, s32[2]{0:T(128)S(1)} %copy-done.3, s32[]{:T(128)S(6)} %axis_index.16), kind=kLoop, calls=%fused_computation.79 | loop fusion | flops 9 | bytes 24 | tf_op jit(solution)/shard_map/reduce_sum | solution.py:194
  8.0 0.0 copy-done.1
  8.7 0.1 dynamic_slice.7
  8.8 0.1 pad.7.clone
  8.9 0.1 constant_dynamic-slice_fusion
  8.9 0.0 collective-permute-done
  8.9 0.3 fusion
  9.2 1.2 %collective-permute-start.1 = (bf16[64,3072]{1,0:T(8,128)(2,1)S(1)}, bf16[64,3072]{1,0:T(8,128)(2,1)S(1)}, u32[]{:S(2)}, u32[]{:S(2)}) collective-permute-start(bf16[64,3072]{1,0:T(8,128)(2,1)S(1)} %fusion), channel_id=1, source_target_pairs={{0,1},{1,0},{2,3},{3,2},{4,5},{5,4},{6,7},{7,6},{8,9},{9,8},{10,11... | collective-permute-start | bytes 1179656 | tf_op jit(solution)/shard_map/ppermute | solution.py:162
  10.4 0.1 reshape.277
  10.6 0.3 fusion.32
  10.8 0.9 %collective-permute-done.1 = bf16[64,3072]{1,0:T(8,128)(2,1)S(1)} collective-permute-done((bf16[64,3072]{1,0:T(8,128)(2,1)S(1)}, bf16[64,3072]{1,0:T(8,128)(2,1)S(1)}, u32[]{:S(2)}, u32[]{:S(2)}) %collective-permute-start.1) | collective-permute-done | bytes 393248 | tf_op jit(solution)/shard_map/ppermute | solution.py:162
  11.8 0.1 broadcast_select_fusion.1
  11.8 0.1 maximum_bitcast_fusion
  11.9 0.4 copy.16
  12.3 4.6 %gather_fusion = bf16[1664,128]{1,0:T(8,128)(2,1)} fusion(bf16[3072,128]{1,0:T(8,128)(2,1)S(1)} %copy.16, s32[2048]{0:T(1024)S(1)} %pad_clamp_fusion), kind=kCustom, calls=%fused_computation | custom fusion | bytes 858624 | tf_op jit(solution)/shard_map/jit(_take)/gather | solution.py:201
  16.9 7.3 %all-to-all-start = ((bf16[8,208,128]{2,1,0:T(8,128)(2,1)}), bf16[8,208,128]{2,1,0:T(8,128)(2,1)S(1)}, u32[]{:S(2)}, u32[]{:S(2)}) async-start(bf16[8,208,128]{2,1,0:T(8,128)(2,1)} %bitcast.2), calls=%async_computation | async-start | bytes 851968 | tf_op jit(solution)/shard_map/all_to_all | solution.py:202
  24.2 0.2 fusion.43
  24.3 0.3 fusion.35
  24.7 0.8 %subtract_convert_fusion = (bf16[32,32,512]{2,1,0:T(8,128)(2,1)S(1)}, bf16[32,32,512]{2,1,0:T(8,128)(2,1)S(1)}) fusion(f32[32,512]{1,0:T(8,128)S(1)} %get-tuple-element.17, f32[32,512]{1,0:T(8,128)S(1)} %get-tuple-element.16, f32[32,512]{1,0:T(8,128)S(1)} %get-tuple-element.18, f32[32,512]{1,0:T(8,128)S(1)} %get-tuple-element.15), kind=kLoop, calls=%fused_computation.8 | loop fusion | flops 4718592 | bytes 2359296 | tf_op jit(solution)/shard_map/convert.9
  25.4 11.6 %all-to-all-done = bf16[8,208,128]{2,1,0:T(8,128)(2,1)S(1)} async-done(((bf16[8,208,128]{2,1,0:T(8,128)(2,1)}), bf16[8,208,128]{2,1,0:T(8,128)(2,1)S(1)}, u32[]{:S(2)}, u32[]{:S(2)}) %all-to-all-start) | async-done | bytes 426016 | tf_op jit(solution)/shard_map/all_to_all | solution.py:202
  37.1 0.1 copy.17
  37.2 0.6 %fusion.1 = f32[208,1024]{1,0:T(8,128)S(1)} fusion(bf16[1024,512]{1,0:T(8,128)(2,1)S(1)} %bitcast.23, bf16[1024,512]{1,0:T(8,128)(2,1)S(1)} %bitcast.22, bf16[26,8,8,128]{3,2,1,0:T(8,128)(2,1)S(1)} %bitcast.28), kind=kOutput, calls=%fused_computation.3 | convolution fusion | flops 440401920 | bytes 3375104 | tf_op jit(solution)/shard_map/dot_general | solution.py:73
  37.8 0.3 multiply_convert_fusion.1
  38.2 0.0 copy-start
  38.2 0.1 collective-permute-start.2
  38.3 0.3 fusion.30
  38.6 0.1 subtract_convert_fusion.1
  38.7 0.1 copy.18
  38.9 0.1 copy.19
  39.0 0.8 %pad_maximum_fusion.lag_ref = bf16[1024,256]{1,0:T(8,128)(2,1)} fusion(bf16[512,256]{1,0:T(8,128)(2,1)S(1)} %copy.19, bf16[512,256]{1,0:T(8,128)(2,1)S(1)} %copy.18), kind=kLoop, calls=%fused_computation.15 | loop fusion | flops 1048576 | bytes 1048576 | tf_op jit(solution)/shard_map/concatenate | solution.py:67
  39.9 0.2 collective-permute-done.2.other_ref
  40.1 0.0 copy-done
  40.1 0.0 copy-start.4
  40.1 0.8 %copy-done.4 = bf16[208,1024]{1,0:T(8,128)(2,1)} copy-done((bf16[208,1024]{1,0:T(8,128)(2,1)}, bf16[208,1024]{1,0:T(8,128)(2,1)S(1)}, u32[]{:S(2)}) %copy-start.4) | copy-done | bytes 426008
  40.8 20.2 %shard_map.55 = f32[32,384,256]{2,1,0:T(8,128)} custom-call(bf16[208,1024]{1,0:T(8,128)(2,1)} %copy-done, bf16[208,1024]{1,0:T(8,128)(2,1)} %copy-done.4, bf16[1024,256]{1,0:T(8,128)(2,1)} %pad_maximum_fusion.lag_ref), custom_call_target="tpu_custom_call" | custom-call | flops 6480199680 | bytes 13959168 | tf_op jit(solution)/shard_map/pallas_call | solution.py:145
  (8 shorter events, 0.1 us)
Async XLA Ops:
  0.9 8.0 %collective-permute-start = (bf16[24,3072]{1,0:T(8,128)(2,1)S(1)}, bf16[24,3072]{1,0:T(8,128)(2,1)S(1)}, u32[]{:S(2)}, u32[]{:S(2)}) collective-permute-start(bf16[24,3072]{1,0:T(8,128)(2,1)S(1)} %slice.22), channel_id=1, source_target_pairs={{1,0},{2,1},{3,2},{4,3},{5,4},{6,5},{7,6},{8,7},{9,8},{10,9},{11,1... | collective-permute-start | bytes 442376 | tf_op jit(solution)/shard_map/ppermute | solution.py:182
  3.5 2.6 %copy-start.2 = (s32[2]{0:T(128)S(1)}, s32[2]{0:T(128)}, u32[]{:S(2)}) copy-start(s32[2]{0:T(128)} %param.9) | copy-start | bytes 28
  3.5 2.6 %copy-start.3 = (s32[2]{0:T(128)S(1)}, s32[2]{0:T(128)}, u32[]{:S(2)}) copy-start(s32[2]{0:T(128)} %param.8) | copy-start | bytes 28
  3.5 4.6 %copy-start.1 = (s32[3072]{0:T(1024)S(1)}, s32[3072]{0:T(1024)}, u32[]{:S(2)}) copy-start(s32[3072]{0:T(1024)} %param.7) | copy-start | bytes 36868
  9.2 2.5 %collective-permute-start.1 = (bf16[64,3072]{1,0:T(8,128)(2,1)S(1)}, bf16[64,3072]{1,0:T(8,128)(2,1)S(1)}, u32[]{:S(2)}, u32[]{:S(2)}) collective-permute-start(bf16[64,3072]{1,0:T(8,128)(2,1)S(1)} %fusion), channel_id=1, source_target_pairs={{0,1},{1,0},{2,3},{3,2},{4,5},{5,4},{6,7},{7,6},{8,9},{9,8},{10,11... | collective-permute-start | bytes 1179656 | tf_op jit(solution)/shard_map/ppermute | solution.py:162
  16.9 20.2 %all-to-all-start = ((bf16[8,208,128]{2,1,0:T(8,128)(2,1)}), bf16[8,208,128]{2,1,0:T(8,128)(2,1)S(1)}, u32[]{:S(2)}, u32[]{:S(2)}) async-start(bf16[8,208,128]{2,1,0:T(8,128)(2,1)} %bitcast.2), calls=%async_computation | async-start | bytes 851968 | tf_op jit(solution)/shard_map/all_to_all | solution.py:202
  38.2 1.8 %copy-start = (bf16[208,1024]{1,0:T(8,128)(2,1)}, bf16[208,1024]{1,0:T(8,128)(2,1)S(1)}, u32[]{:S(2)}) copy-start(bf16[208,1024]{1,0:T(8,128)(2,1)S(1)} %pad_maximum_fusion.1.mine_ref) | copy-start | bytes 1277956
  38.2 1.8 %collective-permute-start.2 = (bf16[208,1024]{1,0:T(8,128)(2,1)S(1)}, bf16[208,1024]{1,0:T(8,128)(2,1)S(1)}, u32[]{:S(2)}, u32[]{:S(2)}) collective-permute-start(bf16[208,1024]{1,0:T(8,128)(2,1)S(1)} %pad_maximum_fusion.1.mine_ref), channel_id=1, source_target_pairs={{0,1},{1,0},{2,3},{3,2},{4,5},{5,4},{6,7},{7,6},{8,9},{9,8},{10,11... | collective-permute-start | bytes 1277960 | tf_op jit(solution)/shard_map/ppermute | solution.py:208
  40.1 0.8 %copy-start.4 = (bf16[208,1024]{1,0:T(8,128)(2,1)}, bf16[208,1024]{1,0:T(8,128)(2,1)S(1)}, u32[]{:S(2)}) copy-start(bf16[208,1024]{1,0:T(8,128)(2,1)S(1)} %collective-permute-done.2.other_ref) | copy-start | bytes 1277956

commit v17 on v11

--- a/solution.py
+++ b/solution.py
@@ -157,14 +157,18 @@
     bins = samples // 2
     tm = lax.axis_index("tm")
 
-    shift = [(b, b - 1) for b in range(1, n_dev)]
-    halo = lax.ppermute(records[:halo_rows], ("chan", "tm"), perm=shift)
-
     taps_matrix = decimation_matrix(fir_taps, out_rows, raw_rows + halo_rows)
     taps_matrix = taps_matrix.astype(jnp.bfloat16)
+    reach = halo_rows // STRIDE
+    partial = jnp.dot(
+        taps_matrix[out_rows - reach :, raw_rows:],
+        records[:halo_rows],
+        preferred_element_type=jnp.float32,
+    )
+    shift = [(b, b - 1) for b in range(1, n_dev)]
+    tail = lax.ppermute(partial, ("chan", "tm"), perm=shift)
     main = jnp.dot(taps_matrix[:, :raw_rows], records, preferred_element_type=jnp.float32)
-    tail = jnp.dot(taps_matrix[:, raw_rows:], halo, preferred_element_type=jnp.float32)
-    decimated = (main + tail).astype(jnp.bfloat16)
+    decimated = (main + jnp.pad(tail, ((out_rows - reach, 0), (0, 0)))).astype(jnp.bfloat16)
 
     first, second = swap_tm(decimated)
     paired = jnp.concatenate([first, second], axis=0).T

time: 51.7 us -> 53.7 us (1.039)
  matrix products: 3.84 us -> 4.71 us
  other arithmetic: 3.88 us -> 4.55 us
    slice x1 -> x0, local copies, waits for them, and re-layouts: 0.92 us -> none  [local(): halo = lax.ppermute(records[:halo_rows], ('chan', 'tm'), perm=shift)]
    dot_general x1, matrix products: 0.29 us -> 1.18 us  [local(): jnp.dot(taps_matrix[out_rows - reach:, raw_rows:], records[:halo_rows], p...]
    reshape x1, local copies, waits for them, and re-layouts: 0.01 us -> 0.71 us  [local(): channel_map.reshape(n_chan, block)]
    dynamic_slice x1, local copies, waits for them, and re-layouts: 0.08 us -> 0.77 us  [local(): source_raw = lax.dynamic_slice_in_dim(channel_map, own_first, SRC)]
    reduce_sum x1, other arithmetic: 0.63 us -> 1.31 us  [local(): jnp.sum(jnp.where(steps == tm, source_owner * block + source_offset, 0))]
  transfers between devices with their start and end apart: 4 -> 4, of which waited for: 3 -> 3; matrix products, arithmetic and copies ran while one was open for 15% -> 11% of each run, Pallas kernels for 0% -> 0%
where the time goes in v17:
time: 53.7 us; the launch traced here: 53.3 us
  waiting for transfers between devices  12.8 us (24%)
  Pallas kernels  10.5 us (20%)
  starting transfers between devices  9.86 us (18%)
  local copies, waits for them, and re-layouts  8.75 us (16%)
  matrix products  4.71 us (9%)
  other arithmetic  4.55 us (8%)
  between operations  2.11 us (4%)
    all_to_all x1, waiting for transfers between devices, local(): lax.all_to_all(rows, 'chan', 0, 2, tiled=True).reshape(width, samples)  11.6 us
    pallas_call x1, Pallas kernels, correlate(): pl.pallas_call(functools.partial(correlate_kernel, factor, bins, group, h...  10.5 us
    all_to_all x1, starting transfers between devices, local(): lax.all_to_all(rows, 'chan', 0, 2, tiled=True).reshape(width, samples)  7.3 us
    gather x1, local copies, waits for them, and re-layouts, local(): jnp.take(paired, index.reshape(-1), axis=0, mode='clip')  4.59 us
    dot_general x1, matrix products, local(): jnp.dot(taps_matrix[:, :raw_rows], records, preferred_element_type=jnp.fl...  2.58 us
    reduce_sum x1, other arithmetic, local(): jnp.sum(jnp.where(steps == tm, source_owner * block + source_offset, 0))  1.31 us
    ppermute x1, starting transfers between devices, local(): tail = lax.ppermute(partial, ('chan', 'tm'), perm=shift)  1.29 us
    ppermute x1, starting transfers between devices, swap_tm(): other = lax.ppermute(x, 'tm', perm=[(0, 1), (1, 0)])  1.2 us
  transfers between devices with their start and end apart: 4, of which 3 were waited for; matrix products, arithmetic and copies ran while one was open for 11% of the time, Pallas kernels for 0%

profile of v17, /device:TPU:0, one launch (start us, length us, event | category | flops | bytes accessed | tf_op | source)
XLA Modules:
  0.0 53.3 jit_solution(7470100929968272414)
XLA Ops:
  0.0 0.7 %broadcast_in_dim.33 = f32[4,8]{1,0:T(4,128)S(1)} reshape(f32[32]{0:T(128)} %param.6) | data formatting | bytes 256 | tf_op jit(solution)/shard_map/jit(_where)/broadcast_in_dim | solution.py:28
  0.8 0.2 select_reduce_fusion
  1.0 0.2 copy.15
  1.2 1.2 %fusion.9 = f32[3,3072]{1,0:T(4,128)S(1)} fusion(bf16[512,3072]{1,0:T(8,128)(2,1)} %param.5, bf16[64,536]{0,1:T(8,128)(2,1)S(1)} %bitcast.25), kind=kOutput, calls=%fused_computation.26 | convolution fusion | flops 442368 | bytes 190464 | tf_op jit(solution)/shard_map/dot_general | solution.py:163
  2.4 1.3 %collective-permute-start = (f32[3,3072]{1,0:T(4,128)S(1)}, f32[3,3072]{1,0:T(4,128)S(1)}, u32[]{:S(2)}, u32[]{:S(2)}) collective-permute-start(f32[3,3072]{1,0:T(4,128)S(1)} %fusion.9), channel_id=1, source_target_pairs={{1,0},{2,1},{3,2},{4,3},{5,4},{6,5},{7,6},{8,7},{9,8},{10,9},{11,1... | collective-permute-start | bytes 110600 | tf_op jit(solution)/shard_map/ppermute | solution.py:169
  3.7 0.7 %reshape.268 = s32[8,384]{1,0:T(8,128)S(1)} reshape(s32[3072]{0:T(1024)} %param.7) | data formatting | bytes 24576 | tf_op jit(solution)/shard_map/reshape | solution.py:179
  4.4 0.1 constant_dynamic-slice_fusion
  4.5 1.3 %fusion.48 = s32[]{:T(128)} fusion(s32[2]{0:T(128)} %param.9, s32[2]{0:T(128)} %param.8, s32[]{:T(128)S(6)} %axis_index.16), kind=kLoop, calls=%fused_computation.80 | loop fusion | flops 9 | bytes 24 | tf_op jit(solution)/shard_map/reduce_sum | solution.py:177
  7.7 0.8 %dynamic_slice.7 = s32[16]{0:T(128)S(1)} dynamic-slice(s32[3072]{0:T(1024)} %param.7, s32[]{:T(128)S(6)} %select_n.93), dynamic_slice_sizes={16} | dynamic-slice | bytes 132 | tf_op jit(solution)/shard_map/dynamic_slice | solution.py:178
  8.5 0.1 pad.12.clone
  8.6 0.0 collective-permute-done
  8.6 2.6 %add_convert_fusion = bf16[64,3072]{1,0:T(8,128)(2,1)S(1)} fusion(f32[3,3072]{1,0:T(4,128)S(1)} %collective-permute-done, bf16[512,3072]{1,0:T(8,128)(2,1)} %param.5, bf16[64,536]{0,1:T(8,128)(2,1)S(1)} %bitcast.26), kind=kOutput, calls=%fused_computation.13 | convolution fusion | flops 201719808 | bytes 3719168 | tf_op jit(solution)/shard_map/dot_general | solution.py:170
  11.2 1.2 %collective-permute-start.1 = (bf16[64,3072]{1,0:T(8,128)(2,1)S(1)}, bf16[64,3072]{1,0:T(8,128)(2,1)S(1)}, u32[]{:S(2)}, u32[]{:S(2)}) collective-permute-start(bf16[64,3072]{1,0:T(8,128)(2,1)S(1)} %add_convert_fusion), channel_id=1, source_target_pairs={{0,1},{1,0},{2,3},{3,2},{4,5},{5,4},{6,7},{7,6},{8,9},{9,8},{10,11... | collective-permute-start | bytes 1179656 | tf_op jit(solution)/shard_map/ppermute | solution.py:141
  12.4 0.1 reshape.277
  12.5 0.3 fusion.35
  12.8 0.9 %collective-permute-done.1 = bf16[64,3072]{1,0:T(8,128)(2,1)S(1)} collective-permute-done((bf16[64,3072]{1,0:T(8,128)(2,1)S(1)}, bf16[64,3072]{1,0:T(8,128)(2,1)S(1)}, u32[]{:S(2)}, u32[]{:S(2)}) %collective-permute-start.1) | collective-permute-done | bytes 393248 | tf_op jit(solution)/shard_map/ppermute | solution.py:141
  13.7 0.1 broadcast_select_fusion.1
  13.8 0.1 maximum_bitcast_fusion
  13.8 0.4 copy.16
  14.2 4.6 %gather_fusion = bf16[1664,128]{1,0:T(8,128)(2,1)} fusion(bf16[3072,128]{1,0:T(8,128)(2,1)S(1)} %copy.16, s32[2048]{0:T(1024)S(1)} %pad_clamp_fusion), kind=kCustom, calls=%fused_computation | custom fusion | bytes 858624 | tf_op jit(solution)/shard_map/jit(_take)/gather | solution.py:184
  18.8 7.3 %all-to-all-start = ((bf16[8,208,128]{2,1,0:T(8,128)(2,1)}), bf16[8,208,128]{2,1,0:T(8,128)(2,1)S(1)}, u32[]{:S(2)}, u32[]{:S(2)}) async-start(bf16[8,208,128]{2,1,0:T(8,128)(2,1)} %bitcast.2), calls=%async_computation | async-start | bytes 851968 | tf_op jit(solution)/shard_map/all_to_all | solution.py:185
  26.1 0.2 fusion.46
  26.3 0.3 fusion.38
  26.6 0.8 %subtract_convert_fusion = (bf16[32,32,512]{2,1,0:T(8,128)(2,1)S(1)}, bf16[32,32,512]{2,1,0:T(8,128)(2,1)S(1)}) fusion(f32[32,512]{1,0:T(8,128)S(1)} %get-tuple-element.17, f32[32,512]{1,0:T(8,128)S(1)} %get-tuple-element.16, f32[32,512]{1,0:T(8,128)S(1)} %get-tuple-element.18, f32[32,512]{1,0:T(8,128)S(1)} %get-tuple-element.15), kind=kLoop, calls=%fused_computation.6 | loop fusion | flops 4718592 | bytes 2359296 | tf_op jit(solution)/shard_map/convert.9
  27.4 11.6 %all-to-all-done = bf16[8,208,128]{2,1,0:T(8,128)(2,1)S(1)} async-done(((bf16[8,208,128]{2,1,0:T(8,128)(2,1)}), bf16[8,208,128]{2,1,0:T(8,128)(2,1)S(1)}, u32[]{:S(2)}, u32[]{:S(2)}) %all-to-all-start) | async-done | bytes 426016 | tf_op jit(solution)/shard_map/all_to_all | solution.py:185
  39.0 0.1 copy.17
  39.1 0.6 %fusion = f32[208,1024]{1,0:T(8,128)S(1)} fusion(bf16[1024,512]{1,0:T(8,128)(2,1)S(1)} %bitcast.22, bf16[1024,512]{1,0:T(8,128)(2,1)S(1)} %bitcast.21, bf16[26,8,8,128]{3,2,1,0:T(8,128)(2,1)S(1)} %bitcast.27), kind=kOutput, calls=%fused_computation.1 | convolution fusion | flops 440401920 | bytes 3375104 | tf_op jit(solution)/shard_map/dot_general | solution.py:73
  39.8 0.3 multiply_convert_fusion.1
  40.2 0.0 copy-start
  40.2 0.1 collective-permute-start.2
  40.2 0.3 fusion.33
  40.5 0.1 subtract_convert_fusion.1
  40.7 0.1 copy.18
  40.8 0.1 copy.19
  41.0 0.8 %pad_maximum_fusion.lag_ref = bf16[1024,256]{1,0:T(8,128)(2,1)} fusion(bf16[512,256]{1,0:T(8,128)(2,1)S(1)} %copy.19, bf16[512,256]{1,0:T(8,128)(2,1)S(1)} %copy.18), kind=kLoop, calls=%fused_computation.14 | loop fusion | flops 1048576 | bytes 1048576 | tf_op jit(solution)/shard_map/concatenate | solution.py:67
  41.8 0.2 collective-permute-done.2.other_ref
  42.0 0.0 copy-done
  42.0 0.0 copy-start.1
  42.0 0.8 %copy-done.1 = bf16[208,1024]{1,0:T(8,128)(2,1)} copy-done((bf16[208,1024]{1,0:T(8,128)(2,1)}, bf16[208,1024]{1,0:T(8,128)(2,1)S(1)}, u32[]{:S(2)}) %copy-start.1) | copy-done | bytes 426008
  42.8 10.5 %shard_map.55 = f32[32,384,256]{2,1,0:T(8,128)} custom-call(bf16[208,1024]{1,0:T(8,128)(2,1)} %copy-done, bf16[208,1024]{1,0:T(8,128)(2,1)} %copy-done.1, bf16[1024,256]{1,0:T(8,128)(2,1)} %pad_maximum_fusion.lag_ref), custom_call_target="tpu_custom_call" | custom-call | flops 6480199680 | bytes 13959168 | tf_op jit(solution)/shard_map/pallas_call | solution.py:125
  (7 shorter events, 0.1 us)
Async XLA Ops:
  2.4 6.2 %collective-permute-start = (f32[3,3072]{1,0:T(4,128)S(1)}, f32[3,3072]{1,0:T(4,128)S(1)}, u32[]{:S(2)}, u32[]{:S(2)}) collective-permute-start(f32[3,3072]{1,0:T(4,128)S(1)} %fusion.9), channel_id=1, source_target_pairs={{1,0},{2,1},{3,2},{4,3},{5,4},{6,5},{7,6},{8,7},{9,8},{10,9},{11,1... | collective-permute-start | bytes 110600 | tf_op jit(solution)/shard_map/ppermute | solution.py:169
  11.2 2.5 %collective-permute-start.1 = (bf16[64,3072]{1,0:T(8,128)(2,1)S(1)}, bf16[64,3072]{1,0:T(8,128)(2,1)S(1)}, u32[]{:S(2)}, u32[]{:S(2)}) collective-permute-start(bf16[64,3072]{1,0:T(8,128)(2,1)S(1)} %add_convert_fusion), channel_id=1, source_target_pairs={{0,1},{1,0},{2,3},{3,2},{4,5},{5,4},{6,7},{7,6},{8,9},{9,8},{10,11... | collective-permute-start | bytes 1179656 | tf_op jit(solution)/shard_map/ppermute | solution.py:141
  18.8 20.2 %all-to-all-start = ((bf16[8,208,128]{2,1,0:T(8,128)(2,1)}), bf16[8,208,128]{2,1,0:T(8,128)(2,1)S(1)}, u32[]{:S(2)}, u32[]{:S(2)}) async-start(bf16[8,208,128]{2,1,0:T(8,128)(2,1)} %bitcast.2), calls=%async_computation | async-start | bytes 851968 | tf_op jit(solution)/shard_map/all_to_all | solution.py:185
  40.2 1.8 %copy-start = (bf16[208,1024]{1,0:T(8,128)(2,1)}, bf16[208,1024]{1,0:T(8,128)(2,1)S(1)}, u32[]{:S(2)}) copy-start(bf16[208,1024]{1,0:T(8,128)(2,1)S(1)} %pad_maximum_fusion.1.mine_ref) | copy-start | bytes 1277956
  40.2 1.8 %collective-permute-start.2 = (bf16[208,1024]{1,0:T(8,128)(2,1)S(1)}, bf16[208,1024]{1,0:T(8,128)(2,1)S(1)}, u32[]{:S(2)}, u32[]{:S(2)}) collective-permute-start(bf16[208,1024]{1,0:T(8,128)(2,1)S(1)} %pad_maximum_fusion.1.mine_ref), channel_id=1, source_target_pairs={{0,1},{1,0},{2,3},{3,2},{4,5},{5,4},{6,7},{7,6},{8,9},{9,8},{10,11... | collective-permute-start | bytes 1277960 | tf_op jit(solution)/shard_map/ppermute | solution.py:191
  42.0 0.8 %copy-start.1 = (bf16[208,1024]{1,0:T(8,128)(2,1)}, bf16[208,1024]{1,0:T(8,128)(2,1)S(1)}, u32[]{:S(2)}) copy-start(bf16[208,1024]{1,0:T(8,128)(2,1)S(1)} %collective-permute-done.2.other_ref) | copy-start | bytes 1277956

commit v18 on v11

--- a/solution.py
+++ b/solution.py
@@ -126,11 +126,7 @@
         functools.partial(correlate_kernel, factor, bins, group, half),
         out_shape=jax.ShapeDtypeStruct((count, block, lags), jnp.float32),
         grid=(count // group,),
-        in_specs=[
-            pl.BlockSpec((rows, width), lambda s: (0, 0)),
-            pl.BlockSpec((rows, width), lambda s: (0, 0)),
-            pl.BlockSpec((width, lags), lambda s: (0, 0)),
-        ],
+        in_specs=[pl.BlockSpec(memory_space=pltpu.VMEM)] * 3,
         out_specs=pl.BlockSpec((group, block, lags), lambda s: (s, 0, 0)),
         compiler_params=pltpu.CompilerParams(dimension_semantics=("arbitrary",)),
         cost_estimate=pl.CostEstimate(flops=flops, bytes_accessed=moved, transcendentals=0),

time: 51.7 us -> 51.7 us (level)
  no operation moved by 1% of the time
where the time goes in v18:
time: 51.7 us; the launch traced here: 51.4 us
  waiting for transfers between devices  12.8 us (25%)
  Pallas kernels  10.5 us (20%)
  starting transfers between devices  9.85 us (19%)
  local copies, waits for them, and re-layouts  8.3 us (16%)
  other arithmetic  3.88 us (8%)
  matrix products  3.84 us (7%)
  between operations  2.18 us (4%)
    all_to_all x1, waiting for transfers between devices, local(): lax.all_to_all(rows, 'chan', 0, 2, tiled=True).reshape(width, samples)  11.6 us
    pallas_call x1, Pallas kernels, correlate(): pl.pallas_call(functools.partial(correlate_kernel, factor, bins, group, h...  10.5 us
    all_to_all x1, starting transfers between devices, local(): lax.all_to_all(rows, 'chan', 0, 2, tiled=True).reshape(width, samples)  7.3 us
    gather x1, local copies, waits for them, and re-layouts, local(): jnp.take(paired, index.reshape(-1), axis=0, mode='clip')  4.59 us
    dot_general x1, matrix products, local(): jnp.dot(taps_matrix[:, :raw_rows], records, preferred_element_type=jnp.fl...  2.6 us
    ppermute x1, starting transfers between devices, local(): halo = lax.ppermute(records[:halo_rows], ('chan', 'tm'), perm=shift)  1.29 us
    ppermute x1, starting transfers between devices, swap_tm(): other = lax.ppermute(x, 'tm', perm=[(0, 1), (1, 0)])  1.19 us
  transfers between devices with their start and end apart: 4, of which 3 were waited for; matrix products, arithmetic and copies ran while one was open for 15% of the time, Pallas kernels for 0%

profile of v18, /device:TPU:0, one launch (start us, length us, event | category | flops | bytes accessed | tf_op | source)
XLA Modules:
  0.0 51.4 jit_solution(4192478482691048512)
XLA Ops:
  0.0 0.9 %slice.22 = bf16[24,3072]{1,0:T(8,128)(2,1)S(1)} slice(bf16[512,3072]{1,0:T(8,128)(2,1)} %param.5), slice={[0:24], [0:3072]} | slice | bytes 294912 | tf_op jit(solution)/shard_map/slice | solution.py:157
  0.9 1.3 %collective-permute-start = (bf16[24,3072]{1,0:T(8,128)(2,1)S(1)}, bf16[24,3072]{1,0:T(8,128)(2,1)S(1)}, u32[]{:S(2)}, u32[]{:S(2)}) collective-permute-start(bf16[24,3072]{1,0:T(8,128)(2,1)S(1)} %slice.22), channel_id=1, source_target_pairs={{1,0},{2,1},{3,2},{4,3},{5,4},{6,5},{7,6},{8,7},{9,8},{10,9},{11,1... | collective-permute-start | bytes 442376 | tf_op jit(solution)/shard_map/ppermute | solution.py:157
  2.2 0.7 %broadcast_in_dim.33 = f32[4,8]{1,0:T(4,128)S(1)} reshape(f32[32]{0:T(128)} %param.6) | data formatting | bytes 256 | tf_op jit(solution)/shard_map/jit(_where)/broadcast_in_dim | solution.py:28
  3.0 0.2 select_reduce_fusion
  3.3 0.2 copy.15
  3.5 0.0 copy-start.2
  3.5 0.0 copy-start.3
  3.5 0.0 copy-start.1
  3.5 2.6 %fusion.10 = f32[64,3072]{1,0:T(8,128)S(1)} fusion(bf16[512,3072]{1,0:T(8,128)(2,1)} %param.5, bf16[64,536]{0,1:T(8,128)(2,1)S(1)} %bitcast.26), kind=kOutput, calls=%fused_computation.27 | convolution fusion | flops 201326592 | bytes 4063232 | tf_op jit(solution)/shard_map/dot_general | solution.py:161
  6.1 0.0 copy-done.2
  6.1 0.0 copy-done.3
  6.1 0.6 %fusion.45 = s32[]{:T(128)} fusion(s32[2]{0:T(128)S(1)} %copy-done.2, s32[2]{0:T(128)S(1)} %copy-done.3, s32[]{:T(128)S(6)} %axis_index.16), kind=kLoop, calls=%fused_computation.79 | loop fusion | flops 9 | bytes 24 | tf_op jit(solution)/shard_map/reduce_sum | solution.py:169
  8.0 0.0 copy-done.1
  8.7 0.1 dynamic_slice.7
  8.8 0.1 pad.7.clone
  8.9 0.1 constant_dynamic-slice_fusion
  8.9 0.0 collective-permute-done
  8.9 0.3 fusion
  9.2 1.2 %collective-permute-start.1 = (bf16[64,3072]{1,0:T(8,128)(2,1)S(1)}, bf16[64,3072]{1,0:T(8,128)(2,1)S(1)}, u32[]{:S(2)}, u32[]{:S(2)}) collective-permute-start(bf16[64,3072]{1,0:T(8,128)(2,1)S(1)} %fusion), channel_id=1, source_target_pairs={{0,1},{1,0},{2,3},{3,2},{4,5},{5,4},{6,7},{7,6},{8,9},{9,8},{10,11... | collective-permute-start | bytes 1179656 | tf_op jit(solution)/shard_map/ppermute | solution.py:137
  10.4 0.1 reshape.277
  10.6 0.3 fusion.32
  10.8 0.9 %collective-permute-done.1 = bf16[64,3072]{1,0:T(8,128)(2,1)S(1)} collective-permute-done((bf16[64,3072]{1,0:T(8,128)(2,1)S(1)}, bf16[64,3072]{1,0:T(8,128)(2,1)S(1)}, u32[]{:S(2)}, u32[]{:S(2)}) %collective-permute-start.1) | collective-permute-done | bytes 393248 | tf_op jit(solution)/shard_map/ppermute | solution.py:137
  11.8 0.1 broadcast_select_fusion.1
  11.8 0.1 maximum_bitcast_fusion
  11.9 0.4 copy.16
  12.3 4.6 %gather_fusion = bf16[1664,128]{1,0:T(8,128)(2,1)} fusion(bf16[3072,128]{1,0:T(8,128)(2,1)S(1)} %copy.16, s32[2048]{0:T(1024)S(1)} %pad_clamp_fusion), kind=kCustom, calls=%fused_computation | custom fusion | bytes 858624 | tf_op jit(solution)/shard_map/jit(_take)/gather | solution.py:176
  16.9 7.3 %all-to-all-start = ((bf16[8,208,128]{2,1,0:T(8,128)(2,1)}), bf16[8,208,128]{2,1,0:T(8,128)(2,1)S(1)}, u32[]{:S(2)}, u32[]{:S(2)}) async-start(bf16[8,208,128]{2,1,0:T(8,128)(2,1)} %bitcast.2), calls=%async_computation | async-start | bytes 851968 | tf_op jit(solution)/shard_map/all_to_all | solution.py:177
  24.2 0.2 fusion.43
  24.3 0.3 fusion.35
  24.7 0.8 %subtract_convert_fusion = (bf16[32,32,512]{2,1,0:T(8,128)(2,1)S(1)}, bf16[32,32,512]{2,1,0:T(8,128)(2,1)S(1)}) fusion(f32[32,512]{1,0:T(8,128)S(1)} %get-tuple-element.17, f32[32,512]{1,0:T(8,128)S(1)} %get-tuple-element.16, f32[32,512]{1,0:T(8,128)S(1)} %get-tuple-element.18, f32[32,512]{1,0:T(8,128)S(1)} %get-tuple-element.15), kind=kLoop, calls=%fused_computation.8 | loop fusion | flops 4718592 | bytes 2359296 | tf_op jit(solution)/shard_map/convert.9
  25.4 11.6 %all-to-all-done = bf16[8,208,128]{2,1,0:T(8,128)(2,1)S(1)} async-done(((bf16[8,208,128]{2,1,0:T(8,128)(2,1)}), bf16[8,208,128]{2,1,0:T(8,128)(2,1)S(1)}, u32[]{:S(2)}, u32[]{:S(2)}) %all-to-all-start) | async-done | bytes 426016 | tf_op jit(solution)/shard_map/all_to_all | solution.py:177
  37.1 0.1 copy.17
  37.2 0.6 %fusion.1 = f32[208,1024]{1,0:T(8,128)S(1)} fusion(bf16[1024,512]{1,0:T(8,128)(2,1)S(1)} %bitcast.23, bf16[1024,512]{1,0:T(8,128)(2,1)S(1)} %bitcast.22, bf16[26,8,8,128]{3,2,1,0:T(8,128)(2,1)S(1)} %bitcast.28), kind=kOutput, calls=%fused_computation.3 | convolution fusion | flops 440401920 | bytes 3375104 | tf_op jit(solution)/shard_map/dot_general | solution.py:73
  37.8 0.3 multiply_convert_fusion.1
  38.2 0.0 copy-start
  38.2 0.1 collective-permute-start.2
  38.3 0.3 fusion.30
  38.6 0.1 subtract_convert_fusion.1
  38.7 0.1 copy.18
  38.9 0.1 copy.19
  39.0 0.8 %pad_maximum_fusion.lag_ref = bf16[1024,256]{1,0:T(8,128)(2,1)} fusion(bf16[512,256]{1,0:T(8,128)(2,1)S(1)} %copy.19, bf16[512,256]{1,0:T(8,128)(2,1)S(1)} %copy.18), kind=kLoop, calls=%fused_computation.15 | loop fusion | flops 1048576 | bytes 1048576 | tf_op jit(solution)/shard_map/concatenate | solution.py:67
  39.9 0.2 collective-permute-done.2.other_ref
  40.1 0.0 copy-done
  40.1 0.0 copy-start.4
  40.1 0.8 %copy-done.4 = bf16[208,1024]{1,0:T(8,128)(2,1)} copy-done((bf16[208,1024]{1,0:T(8,128)(2,1)}, bf16[208,1024]{1,0:T(8,128)(2,1)S(1)}, u32[]{:S(2)}) %copy-start.4) | copy-done | bytes 426008
  40.8 10.5 %shard_map.55 = f32[32,384,256]{2,1,0:T(8,128)} custom-call(bf16[208,1024]{1,0:T(8,128)(2,1)} %copy-done, bf16[208,1024]{1,0:T(8,128)(2,1)} %copy-done.4, bf16[1024,256]{1,0:T(8,128)(2,1)} %pad_maximum_fusion.lag_ref), custom_call_target="tpu_custom_call" | custom-call | flops 6480199680 | bytes 13959168 | tf_op jit(solution)/shard_map/pallas_call | solution.py:125
  (8 shorter events, 0.1 us)
Async XLA Ops:
  0.9 8.0 %collective-permute-start = (bf16[24,3072]{1,0:T(8,128)(2,1)S(1)}, bf16[24,3072]{1,0:T(8,128)(2,1)S(1)}, u32[]{:S(2)}, u32[]{:S(2)}) collective-permute-start(bf16[24,3072]{1,0:T(8,128)(2,1)S(1)} %slice.22), channel_id=1, source_target_pairs={{1,0},{2,1},{3,2},{4,3},{5,4},{6,5},{7,6},{8,7},{9,8},{10,9},{11,1... | collective-permute-start | bytes 442376 | tf_op jit(solution)/shard_map/ppermute | solution.py:157
  3.5 2.6 %copy-start.2 = (s32[2]{0:T(128)S(1)}, s32[2]{0:T(128)}, u32[]{:S(2)}) copy-start(s32[2]{0:T(128)} %param.9) | copy-start | bytes 28
  3.5 2.6 %copy-start.3 = (s32[2]{0:T(128)S(1)}, s32[2]{0:T(128)}, u32[]{:S(2)}) copy-start(s32[2]{0:T(128)} %param.8) | copy-start | bytes 28
  3.5 4.6 %copy-start.1 = (s32[3072]{0:T(1024)S(1)}, s32[3072]{0:T(1024)}, u32[]{:S(2)}) copy-start(s32[3072]{0:T(1024)} %param.7) | copy-start | bytes 36868
  9.2 2.5 %collective-permute-start.1 = (bf16[64,3072]{1,0:T(8,128)(2,1)S(1)}, bf16[64,3072]{1,0:T(8,128)(2,1)S(1)}, u32[]{:S(2)}, u32[]{:S(2)}) collective-permute-start(bf16[64,3072]{1,0:T(8,128)(2,1)S(1)} %fusion), channel_id=1, source_target_pairs={{0,1},{1,0},{2,3},{3,2},{4,5},{5,4},{6,7},{7,6},{8,9},{9,8},{10,11... | collective-permute-start | bytes 1179656 | tf_op jit(solution)/shard_map/ppermute | solution.py:137
  16.9 20.2 %all-to-all-start = ((bf16[8,208,128]{2,1,0:T(8,128)(2,1)}), bf16[8,208,128]{2,1,0:T(8,128)(2,1)S(1)}, u32[]{:S(2)}, u32[]{:S(2)}) async-start(bf16[8,208,128]{2,1,0:T(8,128)(2,1)} %bitcast.2), calls=%async_computation | async-start | bytes 851968 | tf_op jit(solution)/shard_map/all_to_all | solution.py:177
  38.2 1.8 %copy-start = (bf16[208,1024]{1,0:T(8,128)(2,1)}, bf16[208,1024]{1,0:T(8,128)(2,1)S(1)}, u32[]{:S(2)}) copy-start(bf16[208,1024]{1,0:T(8,128)(2,1)S(1)} %pad_maximum_fusion.1.mine_ref) | copy-start | bytes 1277956
  38.2 1.8 %collective-permute-start.2 = (bf16[208,1024]{1,0:T(8,128)(2,1)S(1)}, bf16[208,1024]{1,0:T(8,128)(2,1)S(1)}, u32[]{:S(2)}, u32[]{:S(2)}) collective-permute-start(bf16[208,1024]{1,0:T(8,128)(2,1)S(1)} %pad_maximum_fusion.1.mine_ref), channel_id=1, source_target_pairs={{0,1},{1,0},{2,3},{3,2},{4,5},{5,4},{6,7},{7,6},{8,9},{9,8},{10,11... | collective-permute-start | bytes 1277960 | tf_op jit(solution)/shard_map/ppermute | solution.py:183
  40.1 0.8 %copy-start.4 = (bf16[208,1024]{1,0:T(8,128)(2,1)}, bf16[208,1024]{1,0:T(8,128)(2,1)S(1)}, u32[]{:S(2)}) copy-start(bf16[208,1024]{1,0:T(8,128)(2,1)S(1)} %collective-permute-done.2.other_ref) | copy-start | bytes 1277956

commit v19 on v11

--- a/solution.py
+++ b/solution.py
@@ -178,7 +178,8 @@
     )
     width = index.shape[1]
     rows = jnp.take(paired, index.reshape(-1), axis=0, mode="clip").reshape(n_chan, width, -1)
-    series = lax.all_to_all(rows, "chan", 0, 2, tiled=True).reshape(width, samples)
+    arrived = lax.all_to_all(rows, "chan", 0, 0, tiled=True)
+    series = arrived.transpose(1, 0, 2).reshape(width, samples)
     table = dft_table(samples, bins, jnp.arange(samples, dtype=jnp.int32))
     lag_share = LAGS // n_tm
     lag = lag_kernel(samples, tm * lag_share, lag_share)

time: 51.7 us -> 51.6 us (level)
  no operation moved by 1% of the time
where the time goes in v19:
time: 51.6 us; the launch traced here: 51.3 us
  waiting for transfers between devices  12.8 us (25%)
  Pallas kernels  10.5 us (20%)
  starting transfers between devices  9.85 us (19%)
  local copies, waits for them, and re-layouts  8.19 us (16%)
  other arithmetic  3.88 us (8%)
  matrix products  3.83 us (7%)
  between operations  2.18 us (4%)
    all_to_all x1, waiting for transfers between devices, local(): arrived = lax.all_to_all(rows, 'chan', 0, 0, tiled=True)  11.6 us
    pallas_call x1, Pallas kernels, correlate(): pl.pallas_call(functools.partial(correlate_kernel, factor, bins, group, h...  10.5 us
    all_to_all x1, starting transfers between devices, local(): arrived = lax.all_to_all(rows, 'chan', 0, 0, tiled=True)  7.3 us
    gather x1, local copies, waits for them, and re-layouts, local(): jnp.take(paired, index.reshape(-1), axis=0, mode='clip')  4.59 us
    dot_general x1, matrix products, local(): jnp.dot(taps_matrix[:, :raw_rows], records, preferred_element_type=jnp.fl...  2.6 us
    ppermute x1, starting transfers between devices, local(): halo = lax.ppermute(records[:halo_rows], ('chan', 'tm'), perm=shift)  1.29 us
    ppermute x1, starting transfers between devices, swap_tm(): other = lax.ppermute(x, 'tm', perm=[(0, 1), (1, 0)])  1.19 us
  transfers between devices with their start and end apart: 4, of which 3 were waited for; matrix products, arithmetic and copies ran while one was open for 15% of the time, Pallas kernels for 0%

profile of v19, /device:TPU:0, one launch (start us, length us, event | category | flops | bytes accessed | tf_op | source)
XLA Modules:
  0.0 51.3 jit_solution(17030422580372844510)
XLA Ops:
  0.0 0.9 %slice.22 = bf16[24,3072]{1,0:T(8,128)(2,1)S(1)} slice(bf16[512,3072]{1,0:T(8,128)(2,1)} %param.5), slice={[0:24], [0:3072]} | slice | bytes 294912 | tf_op jit(solution)/shard_map/slice | solution.py:161
  0.9 1.3 %collective-permute-start = (bf16[24,3072]{1,0:T(8,128)(2,1)S(1)}, bf16[24,3072]{1,0:T(8,128)(2,1)S(1)}, u32[]{:S(2)}, u32[]{:S(2)}) collective-permute-start(bf16[24,3072]{1,0:T(8,128)(2,1)S(1)} %slice.22), channel_id=1, source_target_pairs={{1,0},{2,1},{3,2},{4,3},{5,4},{6,5},{7,6},{8,7},{9,8},{10,9},{11,1... | collective-permute-start | bytes 442376 | tf_op jit(solution)/shard_map/ppermute | solution.py:161
  2.2 0.7 %broadcast_in_dim.33 = f32[4,8]{1,0:T(4,128)S(1)} reshape(f32[32]{0:T(128)} %param.6) | data formatting | bytes 256 | tf_op jit(solution)/shard_map/jit(_where)/broadcast_in_dim | solution.py:28
  3.0 0.2 select_reduce_fusion
  3.3 0.2 copy.15
  3.5 0.0 copy-start.2
  3.5 0.0 copy-start.3
  3.5 0.0 copy-start.1
  3.5 2.6 %fusion.10 = f32[64,3072]{1,0:T(8,128)S(1)} fusion(bf16[512,3072]{1,0:T(8,128)(2,1)} %param.5, bf16[64,536]{0,1:T(8,128)(2,1)S(1)} %bitcast.25), kind=kOutput, calls=%fused_computation.27 | convolution fusion | flops 201326592 | bytes 4063232 | tf_op jit(solution)/shard_map/dot_general | solution.py:165
  6.1 0.0 copy-done.2
  6.1 0.0 copy-done.3
  6.1 0.6 %fusion.45 = s32[]{:T(128)} fusion(s32[2]{0:T(128)S(1)} %copy-done.2, s32[2]{0:T(128)S(1)} %copy-done.3, s32[]{:T(128)S(6)} %axis_index.16), kind=kLoop, calls=%fused_computation.79 | loop fusion | flops 9 | bytes 24 | tf_op jit(solution)/shard_map/reduce_sum | solution.py:173
  8.0 0.0 copy-done.1
  8.7 0.1 dynamic_slice.7
  8.8 0.1 pad.7.clone
  8.9 0.1 constant_dynamic-slice_fusion
  8.9 0.0 collective-permute-done
  8.9 0.3 fusion
  9.2 1.2 %collective-permute-start.1 = (bf16[64,3072]{1,0:T(8,128)(2,1)S(1)}, bf16[64,3072]{1,0:T(8,128)(2,1)S(1)}, u32[]{:S(2)}, u32[]{:S(2)}) collective-permute-start(bf16[64,3072]{1,0:T(8,128)(2,1)S(1)} %fusion), channel_id=1, source_target_pairs={{0,1},{1,0},{2,3},{3,2},{4,5},{5,4},{6,7},{7,6},{8,9},{9,8},{10,11... | collective-permute-start | bytes 1179656 | tf_op jit(solution)/shard_map/ppermute | solution.py:141
  10.4 0.1 reshape.276
  10.6 0.3 fusion.32
  10.8 0.9 %collective-permute-done.1 = bf16[64,3072]{1,0:T(8,128)(2,1)S(1)} collective-permute-done((bf16[64,3072]{1,0:T(8,128)(2,1)S(1)}, bf16[64,3072]{1,0:T(8,128)(2,1)S(1)}, u32[]{:S(2)}, u32[]{:S(2)}) %collective-permute-start.1) | collective-permute-done | bytes 393248 | tf_op jit(solution)/shard_map/ppermute | solution.py:141
  11.8 0.1 broadcast_select_fusion.1
  11.8 0.1 maximum_bitcast_fusion
  11.9 0.4 copy.16
  12.3 4.6 %gather_fusion = bf16[1664,128]{1,0:T(8,128)(2,1)} fusion(bf16[3072,128]{1,0:T(8,128)(2,1)S(1)} %copy.16, s32[2048]{0:T(1024)S(1)} %pad_clamp_fusion), kind=kCustom, calls=%fused_computation | custom fusion | bytes 858624 | tf_op jit(solution)/shard_map/jit(_take)/gather | solution.py:180
  16.9 7.3 %all-to-all-start = ((bf16[8,208,128]{2,1,0:T(8,128)(2,1)}), bf16[8,208,128]{2,1,0:T(8,128)(2,1)S(1)}, u32[]{:S(2)}, u32[]{:S(2)}) async-start(bf16[8,208,128]{2,1,0:T(8,128)(2,1)} %bitcast.2), calls=%async_computation | async-start | bytes 851968 | tf_op jit(solution)/shard_map/all_to_all | solution.py:181
  24.2 0.2 fusion.43
  24.3 0.3 fusion.35
  24.7 0.8 %subtract_convert_fusion = (bf16[32,32,512]{2,1,0:T(8,128)(2,1)S(1)}, bf16[32,32,512]{2,1,0:T(8,128)(2,1)S(1)}) fusion(f32[32,512]{1,0:T(8,128)S(1)} %get-tuple-element.17, f32[32,512]{1,0:T(8,128)S(1)} %get-tuple-element.16, f32[32,512]{1,0:T(8,128)S(1)} %get-tuple-element.18, f32[32,512]{1,0:T(8,128)S(1)} %get-tuple-element.15), kind=kLoop, calls=%fused_computation.8 | loop fusion | flops 4718592 | bytes 2359296 | tf_op jit(solution)/shard_map/convert.9
  25.4 11.6 %all-to-all-done = bf16[8,208,128]{2,1,0:T(8,128)(2,1)S(1)} async-done(((bf16[8,208,128]{2,1,0:T(8,128)(2,1)}), bf16[8,208,128]{2,1,0:T(8,128)(2,1)S(1)}, u32[]{:S(2)}, u32[]{:S(2)}) %all-to-all-start) | async-done | bytes 426016 | tf_op jit(solution)/shard_map/all_to_all | solution.py:181
  37.1 0.6 %fusion.1 = f32[208,1024]{1,0:T(8,128)S(1)} fusion(bf16[1024,512]{1,0:T(8,128)(2,1)S(1)} %bitcast.22, bf16[1024,512]{1,0:T(8,128)(2,1)S(1)} %bitcast.21, bf16[8,208,128]{2,1,0:T(8,128)(2,1)S(1)} %all-to-all-done), kind=kOutput, calls=%fused_computation.3 | convolution fusion | flops 440401920 | bytes 3375104 | tf_op jit(solution)/shard_map/dot_general | solution.py:73
  37.7 0.3 multiply_convert_fusion.1
  38.1 0.0 copy-start
  38.1 0.1 collective-permute-start.2
  38.2 0.3 fusion.30
  38.5 0.1 subtract_convert_fusion.1
  38.6 0.1 copy.18
  38.8 0.1 copy.19
  38.9 0.8 %pad_maximum_fusion.lag_ref = bf16[1024,256]{1,0:T(8,128)(2,1)} fusion(bf16[512,256]{1,0:T(8,128)(2,1)S(1)} %copy.19, bf16[512,256]{1,0:T(8,128)(2,1)S(1)} %copy.18), kind=kLoop, calls=%fused_computation.15 | loop fusion | flops 1048576 | bytes 1048576 | tf_op jit(solution)/shard_map/concatenate | solution.py:67
  39.7 0.2 collective-permute-done.2.other_ref
  39.9 0.0 copy-done
  39.9 0.0 copy-start.4
  39.9 0.8 %copy-done.4 = bf16[208,1024]{1,0:T(8,128)(2,1)} copy-done((bf16[208,1024]{1,0:T(8,128)(2,1)}, bf16[208,1024]{1,0:T(8,128)(2,1)S(1)}, u32[]{:S(2)}) %copy-start.4) | copy-done | bytes 426008
  40.7 10.5 %shard_map.55 = f32[32,384,256]{2,1,0:T(8,128)} custom-call(bf16[208,1024]{1,0:T(8,128)(2,1)} %copy-done, bf16[208,1024]{1,0:T(8,128)(2,1)} %copy-done.4, bf16[1024,256]{1,0:T(8,128)(2,1)} %pad_maximum_fusion.lag_ref), custom_call_target="tpu_custom_call" | custom-call | flops 6480199680 | bytes 13959168 | tf_op jit(solution)/shard_map/pallas_call | solution.py:125
  (8 shorter events, 0.1 us)
Async XLA Ops:
  0.9 8.0 %collective-permute-start = (bf16[24,3072]{1,0:T(8,128)(2,1)S(1)}, bf16[24,3072]{1,0:T(8,128)(2,1)S(1)}, u32[]{:S(2)}, u32[]{:S(2)}) collective-permute-start(bf16[24,3072]{1,0:T(8,128)(2,1)S(1)} %slice.22), channel_id=1, source_target_pairs={{1,0},{2,1},{3,2},{4,3},{5,4},{6,5},{7,6},{8,7},{9,8},{10,9},{11,1... | collective-permute-start | bytes 442376 | tf_op jit(solution)/shard_map/ppermute | solution.py:161
  3.5 2.6 %copy-start.2 = (s32[2]{0:T(128)S(1)}, s32[2]{0:T(128)}, u32[]{:S(2)}) copy-start(s32[2]{0:T(128)} %param.9) | copy-start | bytes 28
  3.5 2.6 %copy-start.3 = (s32[2]{0:T(128)S(1)}, s32[2]{0:T(128)}, u32[]{:S(2)}) copy-start(s32[2]{0:T(128)} %param.8) | copy-start | bytes 28
  3.5 4.6 %copy-start.1 = (s32[3072]{0:T(1024)S(1)}, s32[3072]{0:T(1024)}, u32[]{:S(2)}) copy-start(s32[3072]{0:T(1024)} %param.7) | copy-start | bytes 36868
  9.2 2.5 %collective-permute-start.1 = (bf16[64,3072]{1,0:T(8,128)(2,1)S(1)}, bf16[64,3072]{1,0:T(8,128)(2,1)S(1)}, u32[]{:S(2)}, u32[]{:S(2)}) collective-permute-start(bf16[64,3072]{1,0:T(8,128)(2,1)S(1)} %fusion), channel_id=1, source_target_pairs={{0,1},{1,0},{2,3},{3,2},{4,5},{5,4},{6,7},{7,6},{8,9},{9,8},{10,11... | collective-permute-start | bytes 1179656 | tf_op jit(solution)/shard_map/ppermute | solution.py:141
  16.9 20.2 %all-to-all-start = ((bf16[8,208,128]{2,1,0:T(8,128)(2,1)}), bf16[8,208,128]{2,1,0:T(8,128)(2,1)S(1)}, u32[]{:S(2)}, u32[]{:S(2)}) async-start(bf16[8,208,128]{2,1,0:T(8,128)(2,1)} %bitcast.2), calls=%async_computation | async-start | bytes 851968 | tf_op jit(solution)/shard_map/all_to_all | solution.py:181
  38.1 1.8 %copy-start = (bf16[208,1024]{1,0:T(8,128)(2,1)}, bf16[208,1024]{1,0:T(8,128)(2,1)S(1)}, u32[]{:S(2)}) copy-start(bf16[208,1024]{1,0:T(8,128)(2,1)S(1)} %pad_maximum_fusion.1.mine_ref) | copy-start | bytes 1277956
  38.1 1.8 %collective-permute-start.2 = (bf16[208,1024]{1,0:T(8,128)(2,1)S(1)}, bf16[208,1024]{1,0:T(8,128)(2,1)S(1)}, u32[]{:S(2)}, u32[]{:S(2)}) collective-permute-start(bf16[208,1024]{1,0:T(8,128)(2,1)S(1)} %pad_maximum_fusion.1.mine_ref), channel_id=1, source_target_pairs={{0,1},{1,0},{2,3},{3,2},{4,5},{5,4},{6,7},{7,6},{8,9},{9,8},{10,11... | collective-permute-start | bytes 1277960 | tf_op jit(solution)/shard_map/ppermute | solution.py:188
  39.9 0.8 %copy-start.4 = (bf16[208,1024]{1,0:T(8,128)(2,1)}, bf16[208,1024]{1,0:T(8,128)(2,1)S(1)}, u32[]{:S(2)}) copy-start(bf16[208,1024]{1,0:T(8,128)(2,1)S(1)} %collective-permute-done.2.other_ref) | copy-start | bytes 1277956

commit v20 on v18

--- a/solution.py
+++ b/solution.py
@@ -3,6 +3,8 @@
 
 import jax
 import jax.numpy as jnp
+import ml_dtypes
+import numpy as np
 from jax import lax
 from jax.experimental import pallas as pl
 from jax.experimental.pallas import tpu as pltpu
@@ -51,20 +53,17 @@
     return near.astype(jnp.bfloat16)
 
 
-def lag_kernel(samples, first_lag, lag_count):
+def lag_tables(samples, cores):
     bin_count = samples // 2
-    inner = 32
-    frequency = jnp.arange(bin_count, dtype=jnp.int32)[:, None]
-    low = jnp.arange(inner, dtype=jnp.int32)[None, :]
-    high = first_lag - LAGS // 2 + jnp.arange(lag_count // inner, dtype=jnp.int32)[None, :] * inner
-    scale = two_pi / samples
-    low_angle = jnp.mod(frequency * low, samples).astype(jnp.float32) * scale
-    high_angle = jnp.mod(frequency * high, samples).astype(jnp.float32) * scale
-    cl, sl = jnp.cos(low_angle)[:, None, :], jnp.sin(low_angle)[:, None, :]
-    ch, sh = jnp.cos(high_angle)[:, :, None], jnp.sin(high_angle)[:, :, None]
-    cosine = (ch * cl - sh * sl).reshape(bin_count, lag_count)
-    sine = (sh * cl + ch * sl).reshape(bin_count, lag_count)
-    return jnp.concatenate([cosine, -sine], axis=0).astype(jnp.bfloat16)
+    share = LAGS // cores
+    frequency = np.arange(bin_count, dtype=np.int64)[:, None]
+    tables = []
+    for core in range(cores):
+        shifts = core * share + np.arange(share, dtype=np.int64)[None, :] - LAGS // 2
+        phases = np.mod(frequency * shifts, samples).astype(np.float32)
+        angles = phases * np.float32(two_pi / samples)
+        tables.append(np.concatenate([np.cos(angles), -np.sin(angles)], axis=0))
+    return np.stack(tables).astype(ml_dtypes.bfloat16)
 
 
 def whiten_series(series, table):
@@ -80,10 +79,10 @@
     return jnp.concatenate([real_part * factor, imag_part * factor], axis=1).astype(jnp.bfloat16)
 
 
-def correlate_kernel(factor, bins, group, half, mine_ref, other_ref, lag_ref, out_ref):
+def correlate_kernel(factor, bins, group, half, tm_ref, mine_ref, other_ref, lag_ref, out_ref):
     step = pl.program_id(0)
-    first = lax.axis_index("tm") == 0
-    lag = lag_ref[...]
+    first = tm_ref[0] == 0
+    lag = lag_ref[0]
     receivers = [mine_ref[:half, :].astype(jnp.float32), other_ref[:half, :].astype(jnp.float32)]
     places = [jnp.where(first, 0, half), jnp.where(first, half, 0)]
     mine_src = mine_ref[half:, :]
@@ -112,12 +111,12 @@
             )
 
 
-def correlate(low, high, half, lag):
+def correlate(tm, low, high, half, lag):
     rows, width = low.shape
     bins = width // 2
     count = 2 * (rows - half)
     block = 2 * half
-    lags = lag.shape[1]
+    lags = lag.shape[2]
     group = 8
     factor = 1.0 / math.sqrt(bins)
     flops = 2 * count * block * width * lags + 6 * count * block * bins
@@ -125,12 +124,19 @@
     return pl.pallas_call(
         functools.partial(correlate_kernel, factor, bins, group, half),
         out_shape=jax.ShapeDtypeStruct((count, block, lags), jnp.float32),
-        grid=(count // group,),
-        in_specs=[pl.BlockSpec(memory_space=pltpu.VMEM)] * 3,
-        out_specs=pl.BlockSpec((group, block, lags), lambda s: (s, 0, 0)),
+        grid_spec=pltpu.PrefetchScalarGridSpec(
+            num_scalar_prefetch=1,
+            grid=(count // group,),
+            in_specs=[
+                pl.BlockSpec((rows, width), lambda s, tm_ref: (0, 0)),
+                pl.BlockSpec((rows, width), lambda s, tm_ref: (0, 0)),
+                pl.BlockSpec((1, width, lags), lambda s, tm_ref: (tm_ref[0], 0, 0)),
+            ],
+            out_specs=pl.BlockSpec((group, block, lags), lambda s, tm_ref: (s, 0, 0)),
+        ),
         compiler_params=pltpu.CompilerParams(dimension_semantics=("arbitrary",)),
         cost_estimate=pl.CostEstimate(flops=flops, bytes_accessed=moved, transcendentals=0),
-    )(low, high, lag)
+    )(tm, low, high, lag)
 
 
 def swap_tm(x):
@@ -177,11 +183,11 @@
     series = lax.all_to_all(rows, "chan", 0, 2, tiled=True).reshape(width, samples)
     table = dft_table(samples, bins, jnp.arange(samples, dtype=jnp.int32))
     lag_share = LAGS // n_tm
-    lag = lag_kernel(samples, tm * lag_share, lag_share)
+    lag = jnp.asarray(lag_tables(samples, n_tm))
 
     white = whiten_series(series, table)
     other = lax.ppermute(white, "tm", perm=[(0, 1), (1, 0)])
-    result = correlate(white, other, half, lag)
+    result = correlate(jnp.reshape(tm, (1,)).astype(jnp.int32), white, other, half, lag)
     return result.reshape(STEPS, SRC, block, lag_share)
 
 

time: 51.7 us -> 51.6 us (level)
  waiting for transfers between devices: 12.8 us -> 14.4 us
  other arithmetic: 3.88 us -> 2.46 us
    ppermute x1, waiting for transfers between devices: 0.2 us -> 1.76 us  [local(): other = lax.ppermute(white, 'tm', perm=[(0, 1), (1, 0)])]
    concatenate x1 -> x0, other arithmetic: 0.84 us -> none  [lag_kernel(): return jnp.concatenate([cosine, -sine], axis=0).astype(jnp.bfloat16)]
  transfers between devices with their start and end apart: 4 -> 4, of which waited for: 3 -> 3; matrix products, arithmetic and copies ran while one was open for 15% -> 12% of each run, Pallas kernels for 0% -> 0%
where the time goes in v20:
time: 51.6 us; the launch traced here: 51.3 us
  waiting for transfers between devices  14.4 us (28%)
  Pallas kernels  10.6 us (21%)
  starting transfers between devices  9.85 us (19%)
  local copies, waits for them, and re-layouts  8.01 us (16%)
  matrix products  3.84 us (7%)
  other arithmetic  2.46 us (5%)
  between operations  2.14 us (4%)
    all_to_all x1, waiting for transfers between devices, local(): lax.all_to_all(rows, 'chan', 0, 2, tiled=True).reshape(width, samples)  11.5 us
    pallas_call x1, Pallas kernels, correlate(): pl.pallas_call(functools.partial(correlate_kernel, factor, bins, group, h...  10.6 us
    all_to_all x1, starting transfers between devices, local(): lax.all_to_all(rows, 'chan', 0, 2, tiled=True).reshape(width, samples)  7.3 us
    gather x1, local copies, waits for them, and re-layouts, local(): jnp.take(paired, index.reshape(-1), axis=0, mode='clip')  4.59 us
    dot_general x1, matrix products, local(): jnp.dot(taps_matrix[:, :raw_rows], records, preferred_element_type=jnp.fl...  2.6 us
    ppermute x1, waiting for transfers between devices, local(): other = lax.ppermute(white, 'tm', perm=[(0, 1), (1, 0)])  1.76 us
    ppermute x1, starting transfers between devices, local(): halo = lax.ppermute(records[:halo_rows], ('chan', 'tm'), perm=shift)  1.29 us
    ppermute x1, starting transfers between devices, swap_tm(): other = lax.ppermute(x, 'tm', perm=[(0, 1), (1, 0)])  1.19 us
  transfers between devices with their start and end apart: 4, of which 3 were waited for; matrix products, arithmetic and copies ran while one was open for 12% of the time, Pallas kernels for 0%

profile of v20, /device:TPU:0, one launch (start us, length us, event | category | flops | bytes accessed | tf_op | source)
XLA Modules:
  0.0 51.3 jit_solution(8698693929948430048)
XLA Ops:
  0.0 0.9 %slice.22 = bf16[24,3072]{1,0:T(8,128)(2,1)S(1)} slice(bf16[512,3072]{1,0:T(8,128)(2,1)} %param.6), slice={[0:24], [0:3072]} | slice | bytes 294912 | tf_op jit(solution)/shard_map/slice | solution.py:163
  0.9 1.3 %collective-permute-start = (bf16[24,3072]{1,0:T(8,128)(2,1)S(1)}, bf16[24,3072]{1,0:T(8,128)(2,1)S(1)}, u32[]{:S(2)}, u32[]{:S(2)}) collective-permute-start(bf16[24,3072]{1,0:T(8,128)(2,1)S(1)} %slice.22), channel_id=1, source_target_pairs={{1,0},{2,1},{3,2},{4,3},{5,4},{6,5},{7,6},{8,7},{9,8},{10,9},{11,1... | collective-permute-start | bytes 442376 | tf_op jit(solution)/shard_map/ppermute | solution.py:163
  2.2 0.7 %broadcast_in_dim.48 = f32[4,8]{1,0:T(4,128)S(1)} reshape(f32[32]{0:T(128)} %param.7) | data formatting | bytes 256 | tf_op jit(solution)/shard_map/jit(_where)/broadcast_in_dim | solution.py:30
  3.0 0.2 select_reduce_fusion
  3.3 0.2 copy.12
  3.4 0.0 copy-start.2
  3.5 0.0 copy-start.3
  3.5 0.0 copy-start.1
  3.5 2.6 %fusion.10 = f32[64,3072]{1,0:T(8,128)S(1)} fusion(bf16[512,3072]{1,0:T(8,128)(2,1)} %param.6, bf16[64,536]{0,1:T(8,128)(2,1)S(1)} %bitcast.23), kind=kOutput, calls=%fused_computation.24 | convolution fusion | flops 201326592 | bytes 4063232 | tf_op jit(solution)/shard_map/dot_general | solution.py:167
  6.1 0.0 copy-done.2
  6.1 0.0 copy-done.3
  6.1 0.6 %fusion.29 = s32[]{:T(128)} fusion(s32[2]{0:T(128)S(1)} %copy-done.2, s32[2]{0:T(128)S(1)} %copy-done.3, s32[]{:T(128)} %axis_index.16), kind=kLoop, calls=%fused_computation.54 | loop fusion | flops 9 | bytes 24 | tf_op jit(solution)/shard_map/reduce_sum | solution.py:175
  8.0 0.0 copy-done.1
  8.7 0.1 dynamic_slice.7
  8.8 0.1 pad.5.clone
  8.9 0.0 collective-permute-done
  8.9 0.3 fusion
  9.2 1.2 %collective-permute-start.1 = (bf16[64,3072]{1,0:T(8,128)(2,1)S(1)}, bf16[64,3072]{1,0:T(8,128)(2,1)S(1)}, u32[]{:S(2)}, u32[]{:S(2)}) collective-permute-start(bf16[64,3072]{1,0:T(8,128)(2,1)S(1)} %fusion), channel_id=1, source_target_pairs={{0,1},{1,0},{2,3},{3,2},{4,5},{5,4},{6,7},{7,6},{8,9},{9,8},{10,11... | collective-permute-start | bytes 1179656 | tf_op jit(solution)/shard_map/ppermute | solution.py:143
  10.4 0.1 constant_dynamic-slice_fusion
  10.4 0.1 reshape.170
  10.5 1.2 %collective-permute-done.1 = bf16[64,3072]{1,0:T(8,128)(2,1)S(1)} collective-permute-done((bf16[64,3072]{1,0:T(8,128)(2,1)S(1)}, bf16[64,3072]{1,0:T(8,128)(2,1)S(1)}, u32[]{:S(2)}, u32[]{:S(2)}) %collective-permute-start.1) | collective-permute-done | bytes 393248 | tf_op jit(solution)/shard_map/ppermute | solution.py:143
  11.7 0.1 broadcast_select_fusion.1
  11.8 0.1 maximum_bitcast_fusion
  11.8 0.4 copy.13
  12.2 4.6 %gather_fusion = bf16[1664,128]{1,0:T(8,128)(2,1)} fusion(bf16[3072,128]{1,0:T(8,128)(2,1)S(1)} %copy.13, s32[2048]{0:T(1024)S(1)} %pad_clamp_fusion), kind=kCustom, calls=%fused_computation | custom fusion | bytes 858624 | tf_op jit(solution)/shard_map/jit(_take)/gather | solution.py:182
  16.8 7.3 %all-to-all-start = ((bf16[8,208,128]{2,1,0:T(8,128)(2,1)}), bf16[8,208,128]{2,1,0:T(8,128)(2,1)S(1)}, u32[]{:S(2)}, u32[]{:S(2)}) async-start(bf16[8,208,128]{2,1,0:T(8,128)(2,1)} %bitcast.3), calls=%async_computation | async-start | bytes 851968 | tf_op jit(solution)/shard_map/all_to_all | solution.py:183
  24.1 0.3 fusion.24
  24.4 0.3 fusion.27
  24.7 0.8 %subtract_convert_fusion = (bf16[32,32,512]{2,1,0:T(8,128)(2,1)S(1)}, bf16[32,32,512]{2,1,0:T(8,128)(2,1)S(1)}) fusion(f32[32,512]{1,0:T(8,128)S(1)} %get-tuple-element.13, f32[32,512]{1,0:T(8,128)S(1)} %get-tuple-element.12, f32[32,512]{1,0:T(8,128)S(1)} %get-tuple-element.14, f32[32,512]{1,0:T(8,128)S(1)} %get-tuple-element.11), kind=kLoop, calls=%fused_computation.8 | loop fusion | flops 4718592 | bytes 2359296 | tf_op jit(solution)/shard_map/convert.5
  25.5 11.5 %all-to-all-done = bf16[8,208,128]{2,1,0:T(8,128)(2,1)S(1)} async-done(((bf16[8,208,128]{2,1,0:T(8,128)(2,1)}), bf16[8,208,128]{2,1,0:T(8,128)(2,1)S(1)}, u32[]{:S(2)}, u32[]{:S(2)}) %all-to-all-start) | async-done | bytes 426016 | tf_op jit(solution)/shard_map/all_to_all | solution.py:183
  37.0 0.1 copy.14
  37.1 0.6 %fusion.1 = f32[208,1024]{1,0:T(8,128)S(1)} fusion(bf16[1024,512]{1,0:T(8,128)(2,1)S(1)} %bitcast.22, bf16[1024,512]{1,0:T(8,128)(2,1)S(1)} %bitcast.21, bf16[26,8,8,128]{3,2,1,0:T(8,128)(2,1)S(1)} %bitcast.25), kind=kOutput, calls=%fused_computation.3 | convolution fusion | flops 440401920 | bytes 3375104 | tf_op jit(solution)/shard_map/dot_general | solution.py:72
  37.7 0.3 multiply_convert_fusion.1
  38.1 0.0 copy-start
  38.1 0.1 collective-permute-start.2
  38.2 1.8 %collective-permute-done.2.other_ref = bf16[208,1024]{1,0:T(8,128)(2,1)S(1)} collective-permute-done((bf16[208,1024]{1,0:T(8,128)(2,1)S(1)}, bf16[208,1024]{1,0:T(8,128)(2,1)S(1)}, u32[]{:S(2)}, u32[]{:S(2)}) %collective-permute-start.2) | collective-permute-done | bytes 426016 | tf_op jit(solution)/shard_map/ppermute | solution.py:189
  40.0 0.0 copy-start.4
  40.0 0.0 copy-done
  40.0 0.8 %copy-done.4 = bf16[208,1024]{1,0:T(8,128)(2,1)} copy-done((bf16[208,1024]{1,0:T(8,128)(2,1)}, bf16[208,1024]{1,0:T(8,128)(2,1)S(1)}, u32[]{:S(2)}) %copy-start.4) | copy-done | bytes 426008
  40.7 10.6 %shard_map.64 = f32[32,384,256]{2,1,0:T(8,128)} custom-call(s32[1]{0:T(128)} %bitcast.tm_ref, bf16[208,1024]{1,0:T(8,128)(2,1)} %copy-done, bf16[208,1024]{1,0:T(8,128)(2,1)} %copy-done.4, bf16[2,1024,256]{2,1,0:T(8,128)(2,1)} %constant.47.clone.lag_ref), custom_call_target="tpu_custom_call" | custom-call | flops 6480199680 | bytes 13959168 | tf_op jit(solution)/shard_map/pallas_call | solution.py:124
  (7 shorter events, 0.1 us)
Async XLA Ops:
  0.9 7.9 %collective-permute-start = (bf16[24,3072]{1,0:T(8,128)(2,1)S(1)}, bf16[24,3072]{1,0:T(8,128)(2,1)S(1)}, u32[]{:S(2)}, u32[]{:S(2)}) collective-permute-start(bf16[24,3072]{1,0:T(8,128)(2,1)S(1)} %slice.22), channel_id=1, source_target_pairs={{1,0},{2,1},{3,2},{4,3},{5,4},{6,5},{7,6},{8,7},{9,8},{10,9},{11,1... | collective-permute-start | bytes 442376 | tf_op jit(solution)/shard_map/ppermute | solution.py:163
  3.4 2.6 %copy-start.2 = (s32[2]{0:T(128)S(1)}, s32[2]{0:T(128)}, u32[]{:S(2)}) copy-start(s32[2]{0:T(128)} %param.10) | copy-start | bytes 28
  3.5 2.6 %copy-start.3 = (s32[2]{0:T(128)S(1)}, s32[2]{0:T(128)}, u32[]{:S(2)}) copy-start(s32[2]{0:T(128)} %param.9) | copy-start | bytes 28
  3.5 4.6 %copy-start.1 = (s32[3072]{0:T(1024)S(1)}, s32[3072]{0:T(1024)}, u32[]{:S(2)}) copy-start(s32[3072]{0:T(1024)} %param.8) | copy-start | bytes 36868
  9.2 2.5 %collective-permute-start.1 = (bf16[64,3072]{1,0:T(8,128)(2,1)S(1)}, bf16[64,3072]{1,0:T(8,128)(2,1)S(1)}, u32[]{:S(2)}, u32[]{:S(2)}) collective-permute-start(bf16[64,3072]{1,0:T(8,128)(2,1)S(1)} %fusion), channel_id=1, source_target_pairs={{0,1},{1,0},{2,3},{3,2},{4,5},{5,4},{6,7},{7,6},{8,9},{9,8},{10,11... | collective-permute-start | bytes 1179656 | tf_op jit(solution)/shard_map/ppermute | solution.py:143
  16.8 20.2 %all-to-all-start = ((bf16[8,208,128]{2,1,0:T(8,128)(2,1)}), bf16[8,208,128]{2,1,0:T(8,128)(2,1)S(1)}, u32[]{:S(2)}, u32[]{:S(2)}) async-start(bf16[8,208,128]{2,1,0:T(8,128)(2,1)} %bitcast.3), calls=%async_computation | async-start | bytes 851968 | tf_op jit(solution)/shard_map/all_to_all | solution.py:183
  38.1 1.9 %copy-start = (bf16[208,1024]{1,0:T(8,128)(2,1)}, bf16[208,1024]{1,0:T(8,128)(2,1)S(1)}, u32[]{:S(2)}) copy-start(bf16[208,1024]{1,0:T(8,128)(2,1)S(1)} %pad_maximum_fusion.mine_ref) | copy-start | bytes 1277956
  38.1 1.8 %collective-permute-start.2 = (bf16[208,1024]{1,0:T(8,128)(2,1)S(1)}, bf16[208,1024]{1,0:T(8,128)(2,1)S(1)}, u32[]{:S(2)}, u32[]{:S(2)}) collective-permute-start(bf16[208,1024]{1,0:T(8,128)(2,1)S(1)} %pad_maximum_fusion.mine_ref), channel_id=1, source_target_pairs={{0,1},{1,0},{2,3},{3,2},{4,5},{5,4},{6,7},{7,6},{8,9},{9,8},{10,11... | collective-permute-start | bytes 1277960 | tf_op jit(solution)/shard_map/ppermute | solution.py:189
  40.0 0.8 %copy-start.4 = (bf16[208,1024]{1,0:T(8,128)(2,1)}, bf16[208,1024]{1,0:T(8,128)(2,1)S(1)}, u32[]{:S(2)}) copy-start(bf16[208,1024]{1,0:T(8,128)(2,1)S(1)} %collective-permute-done.2.other_ref) | copy-start | bytes 1277956

commit v21 on v20

--- a/solution.py
+++ b/solution.py
@@ -79,14 +79,16 @@
     return jnp.concatenate([real_part * factor, imag_part * factor], axis=1).astype(jnp.bfloat16)
 
 
-def correlate_kernel(factor, bins, group, half, tm_ref, mine_ref, other_ref, lag_ref, out_ref):
+def correlate_kernel(factor, bins, group, tm_ref, rcv_ref, mine_ref, other_ref, lag_ref, *rest):
+    out_ref = rest[-1]
     step = pl.program_id(0)
     first = tm_ref[0] == 0
     lag = lag_ref[0]
-    receivers = [mine_ref[:half, :].astype(jnp.float32), other_ref[:half, :].astype(jnp.float32)]
-    places = [jnp.where(first, 0, half), jnp.where(first, half, 0)]
-    mine_src = mine_ref[half:, :]
-    other_src = other_ref[half:, :]
+    rcv = rcv_ref[...].astype(jnp.float32)
+    real_rcv = rcv[:, :bins]
+    imag_rcv = rcv[:, bins:]
+    mine_src = mine_ref[...]
+    other_src = other_ref[...]
     every = jnp.where(
         first,
         jnp.concatenate([mine_src, other_src], axis=0),
@@ -99,44 +101,53 @@
         row = picked[k : k + 1]
         real_src = row[:, :bins]
         imag_src = row[:, bins:]
-        for part, rcv in enumerate(receivers):
-            real_rcv = rcv[:, :bins]
-            imag_rcv = rcv[:, bins:]
-            cross = jnp.concatenate(
-                [real_src * real_rcv + imag_src * imag_rcv, imag_src * real_rcv - real_src * imag_rcv],
-                axis=1,
-            ).astype(jnp.bfloat16)
-            out_ref[k, pl.ds(pl.multiple_of(places[part], 8), half), :] = (
-                jnp.dot(cross, lag, preferred_element_type=jnp.float32) * factor
-            )
-
-
-def correlate(tm, low, high, half, lag):
-    rows, width = low.shape
+        cross = jnp.concatenate(
+            [real_src * real_rcv + imag_src * imag_rcv, imag_src * real_rcv - real_src * imag_rcv],
+            axis=1,
+        ).astype(jnp.bfloat16)
+        out_ref[k] = jnp.dot(cross, lag, preferred_element_type=jnp.float32) * factor
+
+
+def correlate(tm, receivers, mine_src, other_src, lag, own, previous):
+    half, width = receivers.shape
     bins = width // 2
-    count = 2 * (rows - half)
+    count = 2 * mine_src.shape[0]
     block = 2 * half
     lags = lag.shape[2]
     group = 8
     factor = 1.0 / math.sqrt(bins)
-    flops = 2 * count * block * width * lags + 6 * count * block * bins
-    moved = 4 * rows * width + 2 * lags * width + 4 * count * block * lags
+    flops = 2 * count * half * width * lags + 6 * count * half * bins
+    moved = 2 * half * width + 2 * lags * width + 4 * count * half * lags
+
+    def out_index(s, tm_ref):
+        core = tm_ref[0] if own else 1 - tm_ref[0]
+        return (s, core, 0)
+
+    operands = [tm, receivers, mine_src, other_src, lag]
+    in_specs = [
+        pl.BlockSpec(receivers.shape, lambda s, tm_ref: (0, 0)),
+        pl.BlockSpec(mine_src.shape, lambda s, tm_ref: (0, 0)),
+        pl.BlockSpec(other_src.shape, lambda s, tm_ref: (0, 0)),
+        pl.BlockSpec((1, width, lags), lambda s, tm_ref: (tm_ref[0], 0, 0)),
+    ]
+    aliases = {}
+    if previous is not None:
+        operands.append(previous)
+        in_specs.append(pl.BlockSpec(memory_space=pl.ANY))
+        aliases = {len(operands) - 1: 0}
     return pl.pallas_call(
-        functools.partial(correlate_kernel, factor, bins, group, half),
+        functools.partial(correlate_kernel, factor, bins, group),
         out_shape=jax.ShapeDtypeStruct((count, block, lags), jnp.float32),
         grid_spec=pltpu.PrefetchScalarGridSpec(
             num_scalar_prefetch=1,
             grid=(count // group,),
-            in_specs=[
-                pl.BlockSpec((rows, width), lambda s, tm_ref: (0, 0)),
-                pl.BlockSpec((rows, width), lambda s, tm_ref: (0, 0)),
-                pl.BlockSpec((1, width, lags), lambda s, tm_ref: (tm_ref[0], 0, 0)),
-            ],
-            out_specs=pl.BlockSpec((group, block, lags), lambda s, tm_ref: (s, 0, 0)),
+            in_specs=in_specs,
+            out_specs=pl.BlockSpec((group, half, lags), out_index),
         ),
+        input_output_aliases=aliases,
         compiler_params=pltpu.CompilerParams(dimension_semantics=("arbitrary",)),
         cost_estimate=pl.CostEstimate(flops=flops, bytes_accessed=moved, transcendentals=0),
-    )(tm, low, high, lag)
+    )(*operands)
 
 
 def swap_tm(x):
@@ -186,8 +197,12 @@
     lag = jnp.asarray(lag_tables(samples, n_tm))
 
     white = whiten_series(series, table)
-    other = lax.ppermute(white, "tm", perm=[(0, 1), (1, 0)])
-    result = correlate(jnp.reshape(tm, (1,)).astype(jnp.int32), white, other, half, lag)
+    swap = [(0, 1), (1, 0)]
+    other_src = lax.ppermute(white[half:], "tm", perm=swap)
+    other_rcv = lax.ppermute(white[:half], "tm", perm=swap)
+    core = jnp.reshape(tm, (1,)).astype(jnp.int32)
+    result = correlate(core, white[:half], white[half:], other_src, lag, True, None)
+    result = correlate(core, other_rcv, white[half:], other_src, lag, False, result)
     return result.reshape(STEPS, SRC, block, lag_share)
 
 

time: 51.6 us -> 54.8 us (1.062)
  Pallas kernels: 10.6 us -> 13.2 us
  local copies, waits for them, and re-layouts: 8.01 us -> 8.61 us
    pallas_call x1 -> x2, Pallas kernels: 10.6 us -> 13.2 us  [correlate(): pl.pallas_call(functools.partial(correlate_kernel, factor, bins, group),...]
    unnamed x10 -> x14, local copies, waits for them, and re-layouts: 0.77 us -> 1.37 us
    ppermute x1 -> x2, waiting for transfers between devices: 1.76 us -> 1.26 us  [the longest x1 1.25 us: local(): other_src = lax.ppermute(white[half:], 'tm', perm=swap)]
  transfers between devices with their start and end apart: 4 -> 5, of which waited for: 3 -> 3; matrix products, arithmetic and copies ran while one was open for 12% -> 11% of each run, Pallas kernels for 0% -> 12%
where the time goes in v21:
time: 54.8 us; the launch traced here: 54.5 us
  waiting for transfers between devices  13.9 us (25%)
  Pallas kernels  13.2 us (24%)
  starting transfers between devices  10.3 us (19%)
  local copies, waits for them, and re-layouts  8.61 us (16%)
  matrix products  3.84 us (7%)
  other arithmetic  2.46 us (4%)
  between operations  2.16 us (4%)
    pallas_call x2, Pallas kernels, correlate(): pl.pallas_call(functools.partial(correlate_kernel, factor, bins, group),...  13.2 us
    all_to_all x1, waiting for transfers between devices, local(): lax.all_to_all(rows, 'chan', 0, 2, tiled=True).reshape(width, samples)  11.5 us
    all_to_all x1, starting transfers between devices, local(): lax.all_to_all(rows, 'chan', 0, 2, tiled=True).reshape(width, samples)  7.3 us
    gather x1, local copies, waits for them, and re-layouts, local(): jnp.take(paired, index.reshape(-1), axis=0, mode='clip')  4.59 us
    dot_general x1, matrix products, local(): jnp.dot(taps_matrix[:, :raw_rows], records, preferred_element_type=jnp.fl...  2.6 us
    unnamed x14, local copies, waits for them, and re-layouts  1.37 us
    ppermute x1, starting transfers between devices, local(): halo = lax.ppermute(records[:halo_rows], ('chan', 'tm'), perm=shift)  1.29 us
    ppermute x1, waiting for transfers between devices, local(): other_src = lax.ppermute(white[half:], 'tm', perm=swap)  1.25 us
  transfers between devices with their start and end apart: 5, of which 3 were waited for; matrix products, arithmetic and copies ran while one was open for 11% of the time, Pallas kernels for 12%

profile of v21, /device:TPU:0, one launch (start us, length us, event | category | flops | bytes accessed | tf_op | source)
XLA Modules:
  0.0 54.5 jit_solution(234361894898709540)
XLA Ops:
  0.0 0.9 %slice.31 = bf16[24,3072]{1,0:T(8,128)(2,1)S(1)} slice(bf16[512,3072]{1,0:T(8,128)(2,1)} %param.6), slice={[0:24], [0:3072]} | slice | bytes 294912 | tf_op jit(solution)/shard_map/slice | solution.py:174
  0.9 1.3 %collective-permute-start = (bf16[24,3072]{1,0:T(8,128)(2,1)S(1)}, bf16[24,3072]{1,0:T(8,128)(2,1)S(1)}, u32[]{:S(2)}, u32[]{:S(2)}) collective-permute-start(bf16[24,3072]{1,0:T(8,128)(2,1)S(1)} %slice.31), channel_id=1, source_target_pairs={{1,0},{2,1},{3,2},{4,3},{5,4},{6,5},{7,6},{8,7},{9,8},{10,9},{11,1... | collective-permute-start | bytes 442376 | tf_op jit(solution)/shard_map/ppermute | solution.py:174
  2.2 0.7 %broadcast_in_dim.48 = f32[4,8]{1,0:T(4,128)S(1)} reshape(f32[32]{0:T(128)} %param.7) | data formatting | bytes 256 | tf_op jit(solution)/shard_map/jit(_where)/broadcast_in_dim | solution.py:30
  3.0 0.2 select_reduce_fusion
  3.3 0.2 copy.13
  3.4 0.0 copy-start.5
  3.5 0.0 copy-start.6
  3.5 0.0 copy-start.4
  3.5 2.6 %fusion.11 = f32[64,3072]{1,0:T(8,128)S(1)} fusion(bf16[512,3072]{1,0:T(8,128)(2,1)} %param.6, bf16[64,536]{0,1:T(8,128)(2,1)S(1)} %bitcast.23), kind=kOutput, calls=%fused_computation.26 | convolution fusion | flops 201326592 | bytes 4063232 | tf_op jit(solution)/shard_map/dot_general | solution.py:178
  6.1 0.0 copy-done.5
  6.1 0.0 copy-done.6
  6.1 0.6 %fusion.30 = s32[]{:T(128)} fusion(s32[2]{0:T(128)S(1)} %copy-done.5, s32[2]{0:T(128)S(1)} %copy-done.6, s32[]{:T(128)} %axis_index.16), kind=kLoop, calls=%fused_computation.57 | loop fusion | flops 9 | bytes 24 | tf_op jit(solution)/shard_map/reduce_sum | solution.py:186
  8.0 0.0 copy-done.4
  8.7 0.1 dynamic_slice.7
  8.8 0.1 pad.5.clone
  8.9 0.0 collective-permute-done
  8.9 0.3 fusion
  9.2 1.2 %collective-permute-start.1 = (bf16[64,3072]{1,0:T(8,128)(2,1)S(1)}, bf16[64,3072]{1,0:T(8,128)(2,1)S(1)}, u32[]{:S(2)}, u32[]{:S(2)}) collective-permute-start(bf16[64,3072]{1,0:T(8,128)(2,1)S(1)} %fusion), channel_id=1, source_target_pairs={{0,1},{1,0},{2,3},{3,2},{4,5},{5,4},{6,7},{7,6},{8,9},{9,8},{10,11... | collective-permute-start | bytes 1179656 | tf_op jit(solution)/shard_map/ppermute | solution.py:154
  10.4 0.1 constant_dynamic-slice_fusion
  10.4 0.1 reshape.170
  10.5 1.2 %collective-permute-done.1 = bf16[64,3072]{1,0:T(8,128)(2,1)S(1)} collective-permute-done((bf16[64,3072]{1,0:T(8,128)(2,1)S(1)}, bf16[64,3072]{1,0:T(8,128)(2,1)S(1)}, u32[]{:S(2)}, u32[]{:S(2)}) %collective-permute-start.1) | collective-permute-done | bytes 393248 | tf_op jit(solution)/shard_map/ppermute | solution.py:154
  11.7 0.1 broadcast_select_fusion.1
  11.8 0.1 maximum_bitcast_fusion
  11.8 0.4 copy.14
  12.2 4.6 %gather_fusion = bf16[1664,128]{1,0:T(8,128)(2,1)} fusion(bf16[3072,128]{1,0:T(8,128)(2,1)S(1)} %copy.14, s32[2048]{0:T(1024)S(1)} %pad_clamp_fusion), kind=kCustom, calls=%fused_computation | custom fusion | bytes 858624 | tf_op jit(solution)/shard_map/jit(_take)/gather | solution.py:193
  16.8 7.3 %all-to-all-start = ((bf16[8,208,128]{2,1,0:T(8,128)(2,1)}), bf16[8,208,128]{2,1,0:T(8,128)(2,1)S(1)}, u32[]{:S(2)}, u32[]{:S(2)}) async-start(bf16[8,208,128]{2,1,0:T(8,128)(2,1)} %bitcast.3), calls=%async_computation | async-start | bytes 851968 | tf_op jit(solution)/shard_map/all_to_all | solution.py:194
  24.1 0.3 fusion.25
  24.4 0.3 fusion.28
  24.7 0.8 %subtract_convert_fusion = (bf16[32,32,512]{2,1,0:T(8,128)(2,1)S(1)}, bf16[32,32,512]{2,1,0:T(8,128)(2,1)S(1)}) fusion(f32[32,512]{1,0:T(8,128)S(1)} %get-tuple-element.13, f32[32,512]{1,0:T(8,128)S(1)} %get-tuple-element.12, f32[32,512]{1,0:T(8,128)S(1)} %get-tuple-element.14, f32[32,512]{1,0:T(8,128)S(1)} %get-tuple-element.11), kind=kLoop, calls=%fused_computation.8 | loop fusion | flops 4718592 | bytes 2359296 | tf_op jit(solution)/shard_map/convert.5
  25.5 11.5 %all-to-all-done = bf16[8,208,128]{2,1,0:T(8,128)(2,1)S(1)} async-done(((bf16[8,208,128]{2,1,0:T(8,128)(2,1)}), bf16[8,208,128]{2,1,0:T(8,128)(2,1)S(1)}, u32[]{:S(2)}, u32[]{:S(2)}) %all-to-all-start) | async-done | bytes 426016 | tf_op jit(solution)/shard_map/all_to_all | solution.py:194
  37.0 0.1 copy.15
  37.1 0.6 %fusion.1 = f32[208,1024]{1,0:T(8,128)S(1)} fusion(bf16[1024,512]{1,0:T(8,128)(2,1)S(1)} %bitcast.22, bf16[1024,512]{1,0:T(8,128)(2,1)S(1)} %bitcast.21, bf16[26,8,8,128]{3,2,1,0:T(8,128)(2,1)S(1)} %bitcast.25), kind=kOutput, calls=%fused_computation.3 | convolution fusion | flops 440401920 | bytes 3375104 | tf_op jit(solution)/shard_map/dot_general | solution.py:72
  37.7 0.3 multiply_convert_fusion
  38.1 0.0 copy-start
  38.1 0.1 collective-permute-start.2
  38.2 0.0 copy-start.2
  38.2 0.5 collective-permute-start.3
  38.7 1.3 %collective-permute-done.3.other_ref = bf16[16,1024]{1,0:T(8,128)(2,1)S(1)} collective-permute-done((bf16[16,1024]{1,0:T(8,128)(2,1)S(1)}, bf16[16,1024]{1,0:T(8,128)(2,1)S(1)}, u32[]{:S(2)}, u32[]{:S(2)}) %collective-permute-start.3) | collective-permute-done | bytes 32800 | tf_op jit(solution)/shard_map/ppermute | solution.py:201
  40.0 0.0 copy-start.3
  40.0 0.0 copy-done
  40.0 0.0 copy-done.2
  40.0 0.6 %copy-done.3 = bf16[16,1024]{1,0:T(8,128)(2,1)} copy-done((bf16[16,1024]{1,0:T(8,128)(2,1)}, bf16[16,1024]{1,0:T(8,128)(2,1)S(1)}, u32[]{:S(2)}) %copy-start.3) | copy-done | bytes 32792
  40.6 6.6 %shard_map.64.rest_0_ = f32[32,384,256]{2,1,0:T(8,128)} custom-call(s32[1]{0:T(128)} %bitcast.tm_ref, bf16[192,1024]{1,0:T(8,128)(2,1)} %copy-done, bf16[16,1024]{1,0:T(8,128)(2,1)} %copy-done.2, bf16[16,1024]{1,0:T(8,128)(2,1)} %copy-done.3, bf16[2,1024,256]{2,1,0:T(8,128)(2,1)} %constant.47.clone.lag_ref), custom_call_target="tpu_custom_call" | custom-call | flops 3240099840 | bytes 7208960 | tf_op jit(solution)/shard_map/pallas_call | solution.py:138
  47.2 0.0 collective-permute-done.2.rcv_ref
  47.2 0.0 copy-start.1
  47.2 0.7 %copy-done.1 = bf16[192,1024]{1,0:T(8,128)(2,1)} copy-done((bf16[192,1024]{1,0:T(8,128)(2,1)}, bf16[192,1024]{1,0:T(8,128)(2,1)S(1)}, u32[]{:S(2)}) %copy-start.1) | copy-done | bytes 393240
  47.9 6.6 %shard_map.65 = f32[32,384,256]{2,1,0:T(8,128)} custom-call(s32[1]{0:T(128)} %bitcast.tm_ref, bf16[192,1024]{1,0:T(8,128)(2,1)} %copy-done.1, bf16[16,1024]{1,0:T(8,128)(2,1)} %copy-done.2, bf16[16,1024]{1,0:T(8,128)(2,1)} %copy-done.3, bf16[2,1024,256]{2,1,0:T(8,128)(2,1)} %constant.47.clone.lag_ref, ...), custom_call_target="tpu_custom_call", output_to_operand_aliasing={{}: (5, {})} | custom-call | flops 3240099840 | bytes 7208960 | tf_op jit(solution)/shard_map/pallas_call | solution.py:138
  (8 shorter events, 0.1 us)
Async XLA Ops:
  0.9 7.9 %collective-permute-start = (bf16[24,3072]{1,0:T(8,128)(2,1)S(1)}, bf16[24,3072]{1,0:T(8,128)(2,1)S(1)}, u32[]{:S(2)}, u32[]{:S(2)}) collective-permute-start(bf16[24,3072]{1,0:T(8,128)(2,1)S(1)} %slice.31), channel_id=1, source_target_pairs={{1,0},{2,1},{3,2},{4,3},{5,4},{6,5},{7,6},{8,7},{9,8},{10,9},{11,1... | collective-permute-start | bytes 442376 | tf_op jit(solution)/shard_map/ppermute | solution.py:174
  3.4 2.6 %copy-start.5 = (s32[2]{0:T(128)S(1)}, s32[2]{0:T(128)}, u32[]{:S(2)}) copy-start(s32[2]{0:T(128)} %param.10) | copy-start | bytes 28
  3.5 2.6 %copy-start.6 = (s32[2]{0:T(128)S(1)}, s32[2]{0:T(128)}, u32[]{:S(2)}) copy-start(s32[2]{0:T(128)} %param.9) | copy-start | bytes 28
  3.5 4.6 %copy-start.4 = (s32[3072]{0:T(1024)S(1)}, s32[3072]{0:T(1024)}, u32[]{:S(2)}) copy-start(s32[3072]{0:T(1024)} %param.8) | copy-start | bytes 36868
  9.2 2.5 %collective-permute-start.1 = (bf16[64,3072]{1,0:T(8,128)(2,1)S(1)}, bf16[64,3072]{1,0:T(8,128)(2,1)S(1)}, u32[]{:S(2)}, u32[]{:S(2)}) collective-permute-start(bf16[64,3072]{1,0:T(8,128)(2,1)S(1)} %fusion), channel_id=1, source_target_pairs={{0,1},{1,0},{2,3},{3,2},{4,5},{5,4},{6,7},{7,6},{8,9},{9,8},{10,11... | collective-permute-start | bytes 1179656 | tf_op jit(solution)/shard_map/ppermute | solution.py:154
  16.8 20.2 %all-to-all-start = ((bf16[8,208,128]{2,1,0:T(8,128)(2,1)}), bf16[8,208,128]{2,1,0:T(8,128)(2,1)S(1)}, u32[]{:S(2)}, u32[]{:S(2)}) async-start(bf16[8,208,128]{2,1,0:T(8,128)(2,1)} %bitcast.3), calls=%async_computation | async-start | bytes 851968 | tf_op jit(solution)/shard_map/all_to_all | solution.py:194
  38.1 1.9 %copy-start = (bf16[192,1024]{1,0:T(8,128)(2,1)}, bf16[192,1024]{1,0:T(8,128)(2,1)S(1)}, u32[]{:S(2)}) copy-start(bf16[192,1024]{1,0:T(8,128)(2,1)S(1)} %fusion.10.rcv_ref) | copy-start | bytes 1179652
  38.1 9.0 %collective-permute-start.2 = (bf16[192,1024]{1,0:T(8,128)(2,1)S(1)}, bf16[192,1024]{1,0:T(8,128)(2,1)S(1)}, u32[]{:S(2)}, u32[]{:S(2)}) collective-permute-start(bf16[192,1024]{1,0:T(8,128)(2,1)S(1)} %fusion.10.rcv_ref), channel_id=1, source_target_pairs={{0,1},{1,0},{2,3},{3,2},{4,5},{5,4},{6,7},{7,6},{8,9},{9,8},{10,11... | collective-permute-start | bytes 1179656 | tf_op jit(solution)/shard_map/ppermute | solution.py:202
  38.2 1.8 %copy-start.2 = (bf16[16,1024]{1,0:T(8,128)(2,1)}, bf16[16,1024]{1,0:T(8,128)(2,1)S(1)}, u32[]{:S(2)}) copy-start(bf16[16,1024]{1,0:T(8,128)(2,1)S(1)} %pad_maximum_fusion.mine_ref) | copy-start | bytes 98308
  38.2 1.7 %collective-permute-start.3 = (bf16[16,1024]{1,0:T(8,128)(2,1)S(1)}, bf16[16,1024]{1,0:T(8,128)(2,1)S(1)}, u32[]{:S(2)}, u32[]{:S(2)}) collective-permute-start(bf16[16,1024]{1,0:T(8,128)(2,1)S(1)} %pad_maximum_fusion.mine_ref), channel_id=1, source_target_pairs={{0,1},{1,0},{2,3},{3,2},{4,5},{5,4},{6,7},{7,6},{8,9},{9,8},{10,11... | collective-permute-start | bytes 98312 | tf_op jit(solution)/shard_map/ppermute | solution.py:201
  40.0 0.6 %copy-start.3 = (bf16[16,1024]{1,0:T(8,128)(2,1)}, bf16[16,1024]{1,0:T(8,128)(2,1)S(1)}, u32[]{:S(2)}) copy-start(bf16[16,1024]{1,0:T(8,128)(2,1)S(1)} %collective-permute-done.3.other_ref) | copy-start | bytes 98308
  47.2 0.7 %copy-start.1 = (bf16[192,1024]{1,0:T(8,128)(2,1)}, bf16[192,1024]{1,0:T(8,128)(2,1)S(1)}, u32[]{:S(2)}) copy-start(bf16[192,1024]{1,0:T(8,128)(2,1)S(1)} %collective-permute-done.2.rcv_ref) | copy-start | bytes 1179652

commit v22 on v11

--- a/solution.py
+++ b/solution.py
@@ -152,7 +152,7 @@
     block = channels // n_chan
     half = block // n_tm
     out_rows = raw_rows // STRIDE
-    halo_rows = TAPS - STRIDE
+    halo_rows = TAPS
     samples = out_rows * n_dev
     bins = samples // 2
     tm = lax.axis_index("tm")

time: 51.7 us -> 51.7 us (level)
  no operation moved by 1% of the time
where the time goes in v22:
time: 51.7 us; the launch traced here: 51.4 us
  waiting for transfers between devices  12.8 us (25%)
  Pallas kernels  10.5 us (20%)
  starting transfers between devices  9.86 us (19%)
  local copies, waits for them, and re-layouts  8.32 us (16%)
  other arithmetic  3.88 us (8%)
  matrix products  3.83 us (7%)
  between operations  2.19 us (4%)
    all_to_all x1, waiting for transfers between devices, local(): lax.all_to_all(rows, 'chan', 0, 2, tiled=True).reshape(width, samples)  11.6 us
    pallas_call x1, Pallas kernels, correlate(): pl.pallas_call(functools.partial(correlate_kernel, factor, bins, group, h...  10.5 us
    all_to_all x1, starting transfers between devices, local(): lax.all_to_all(rows, 'chan', 0, 2, tiled=True).reshape(width, samples)  7.3 us
    gather x1, local copies, waits for them, and re-layouts, local(): jnp.take(paired, index.reshape(-1), axis=0, mode='clip')  4.59 us
    dot_general x1, matrix products, local(): jnp.dot(taps_matrix[:, :raw_rows], records, preferred_element_type=jnp.fl...  2.59 us
    ppermute x1, starting transfers between devices, local(): halo = lax.ppermute(records[:halo_rows], ('chan', 'tm'), perm=shift)  1.29 us
    ppermute x1, starting transfers between devices, swap_tm(): other = lax.ppermute(x, 'tm', perm=[(0, 1), (1, 0)])  1.19 us
  transfers between devices with their start and end apart: 4, of which 3 were waited for; matrix products, arithmetic and copies ran while one was open for 15% of the time, Pallas kernels for 0%

profile of v22, /device:TPU:0, one launch (start us, length us, event | category | flops | bytes accessed | tf_op | source)
XLA Modules:
  0.0 51.4 jit_solution(10013568192466810118)
XLA Ops:
  0.0 0.9 %slice.22 = bf16[32,3072]{1,0:T(8,128)(2,1)S(1)} slice(bf16[512,3072]{1,0:T(8,128)(2,1)} %param.5), slice={[0:32], [0:3072]} | slice | bytes 393216 | tf_op jit(solution)/shard_map/slice | solution.py:161
  0.9 1.3 %collective-permute-start = (bf16[32,3072]{1,0:T(8,128)(2,1)S(1)}, bf16[32,3072]{1,0:T(8,128)(2,1)S(1)}, u32[]{:S(2)}, u32[]{:S(2)}) collective-permute-start(bf16[32,3072]{1,0:T(8,128)(2,1)S(1)} %slice.22), channel_id=1, source_target_pairs={{1,0},{2,1},{3,2},{4,3},{5,4},{6,5},{7,6},{8,7},{9,8},{10,9},{11,1... | collective-permute-start | bytes 589832 | tf_op jit(solution)/shard_map/ppermute | solution.py:161
  2.3 0.7 %broadcast_in_dim.33 = f32[4,8]{1,0:T(4,128)S(1)} reshape(f32[32]{0:T(128)} %param.6) | data formatting | bytes 256 | tf_op jit(solution)/shard_map/jit(_where)/broadcast_in_dim | solution.py:28
  3.0 0.2 select_reduce_fusion
  3.3 0.2 copy.15
  3.5 0.0 copy-start.2
  3.5 0.0 copy-start.3
  3.5 0.0 copy-start.1
  3.5 2.6 %fusion.10 = f32[64,3072]{1,0:T(8,128)S(1)} fusion(bf16[512,3072]{1,0:T(8,128)(2,1)} %param.5, bf16[64,544]{0,1:T(8,128)(2,1)S(1)} %bitcast.26), kind=kOutput, calls=%fused_computation.27 | convolution fusion | flops 201326592 | bytes 4063232 | tf_op jit(solution)/shard_map/dot_general | solution.py:165
  6.1 0.0 copy-done.2
  6.1 0.0 copy-done.3
  6.1 0.6 %fusion.45 = s32[]{:T(128)} fusion(s32[2]{0:T(128)S(1)} %copy-done.2, s32[2]{0:T(128)S(1)} %copy-done.3, s32[]{:T(128)S(6)} %axis_index.16), kind=kLoop, calls=%fused_computation.79 | loop fusion | flops 9 | bytes 24 | tf_op jit(solution)/shard_map/reduce_sum | solution.py:173
  8.1 0.0 copy-done.1
  8.7 0.1 dynamic_slice.7
  8.8 0.1 pad.7.clone
  8.9 0.1 constant_dynamic-slice_fusion
  9.0 0.0 collective-permute-done
  9.0 0.3 fusion
  9.2 1.2 %collective-permute-start.1 = (bf16[64,3072]{1,0:T(8,128)(2,1)S(1)}, bf16[64,3072]{1,0:T(8,128)(2,1)S(1)}, u32[]{:S(2)}, u32[]{:S(2)}) collective-permute-start(bf16[64,3072]{1,0:T(8,128)(2,1)S(1)} %fusion), channel_id=1, source_target_pairs={{0,1},{1,0},{2,3},{3,2},{4,5},{5,4},{6,7},{7,6},{8,9},{9,8},{10,11... | collective-permute-start | bytes 1179656 | tf_op jit(solution)/shard_map/ppermute | solution.py:141
  10.4 0.1 reshape.277
  10.6 0.3 fusion.32
  10.8 0.9 %collective-permute-done.1 = bf16[64,3072]{1,0:T(8,128)(2,1)S(1)} collective-permute-done((bf16[64,3072]{1,0:T(8,128)(2,1)S(1)}, bf16[64,3072]{1,0:T(8,128)(2,1)S(1)}, u32[]{:S(2)}, u32[]{:S(2)}) %collective-permute-start.1) | collective-permute-done | bytes 393248 | tf_op jit(solution)/shard_map/ppermute | solution.py:141
  11.8 0.1 broadcast_select_fusion.1
  11.8 0.1 maximum_bitcast_fusion
  11.9 0.4 copy.16
  12.3 4.6 %gather_fusion = bf16[1664,128]{1,0:T(8,128)(2,1)} fusion(bf16[3072,128]{1,0:T(8,128)(2,1)S(1)} %copy.16, s32[2048]{0:T(1024)S(1)} %pad_clamp_fusion), kind=kCustom, calls=%fused_computation | custom fusion | bytes 858624 | tf_op jit(solution)/shard_map/jit(_take)/gather | solution.py:180
  16.9 7.3 %all-to-all-start = ((bf16[8,208,128]{2,1,0:T(8,128)(2,1)}), bf16[8,208,128]{2,1,0:T(8,128)(2,1)S(1)}, u32[]{:S(2)}, u32[]{:S(2)}) async-start(bf16[8,208,128]{2,1,0:T(8,128)(2,1)} %bitcast.2), calls=%async_computation | async-start | bytes 851968 | tf_op jit(solution)/shard_map/all_to_all | solution.py:181
  24.2 0.2 fusion.44
  24.3 0.3 fusion.35
  24.7 0.8 %subtract_convert_fusion = (bf16[32,32,512]{2,1,0:T(8,128)(2,1)S(1)}, bf16[32,32,512]{2,1,0:T(8,128)(2,1)S(1)}) fusion(f32[32,512]{1,0:T(8,128)S(1)} %get-tuple-element.17, f32[32,512]{1,0:T(8,128)S(1)} %get-tuple-element.16, f32[32,512]{1,0:T(8,128)S(1)} %get-tuple-element.18, f32[32,512]{1,0:T(8,128)S(1)} %get-tuple-element.15), kind=kLoop, calls=%fused_computation.8 | loop fusion | flops 4718592 | bytes 2359296 | tf_op jit(solution)/shard_map/convert.9
  25.4 11.6 %all-to-all-done = bf16[8,208,128]{2,1,0:T(8,128)(2,1)S(1)} async-done(((bf16[8,208,128]{2,1,0:T(8,128)(2,1)}), bf16[8,208,128]{2,1,0:T(8,128)(2,1)S(1)}, u32[]{:S(2)}, u32[]{:S(2)}) %all-to-all-start) | async-done | bytes 426016 | tf_op jit(solution)/shard_map/all_to_all | solution.py:181
  37.1 0.1 copy.17
  37.2 0.6 %fusion.1 = f32[208,1024]{1,0:T(8,128)S(1)} fusion(bf16[1024,512]{1,0:T(8,128)(2,1)S(1)} %bitcast.23, bf16[1024,512]{1,0:T(8,128)(2,1)S(1)} %bitcast.22, bf16[26,8,8,128]{3,2,1,0:T(8,128)(2,1)S(1)} %bitcast.28), kind=kOutput, calls=%fused_computation.3 | convolution fusion | flops 440401920 | bytes 3375104 | tf_op jit(solution)/shard_map/dot_general | solution.py:73
  37.8 0.3 multiply_convert_fusion.1
  38.2 0.0 copy-start
  38.2 0.1 collective-permute-start.2
  38.3 0.3 fusion.30
  38.6 0.1 subtract_convert_fusion.1
  38.7 0.1 copy.18
  38.9 0.1 copy.19
  39.0 0.8 %pad_maximum_fusion.lag_ref = bf16[1024,256]{1,0:T(8,128)(2,1)} fusion(bf16[512,256]{1,0:T(8,128)(2,1)S(1)} %copy.19, bf16[512,256]{1,0:T(8,128)(2,1)S(1)} %copy.18), kind=kLoop, calls=%fused_computation.15 | loop fusion | flops 1048576 | bytes 1048576 | tf_op jit(solution)/shard_map/concatenate | solution.py:67
  39.9 0.2 collective-permute-done.2.other_ref
  40.1 0.0 copy-done
  40.1 0.0 copy-start.4
  40.1 0.8 %copy-done.4 = bf16[208,1024]{1,0:T(8,128)(2,1)} copy-done((bf16[208,1024]{1,0:T(8,128)(2,1)}, bf16[208,1024]{1,0:T(8,128)(2,1)S(1)}, u32[]{:S(2)}) %copy-start.4) | copy-done | bytes 426008
  40.9 10.5 %shard_map.55 = f32[32,384,256]{2,1,0:T(8,128)} custom-call(bf16[208,1024]{1,0:T(8,128)(2,1)} %copy-done, bf16[208,1024]{1,0:T(8,128)(2,1)} %copy-done.4, bf16[1024,256]{1,0:T(8,128)(2,1)} %pad_maximum_fusion.lag_ref), custom_call_target="tpu_custom_call" | custom-call | flops 6480199680 | bytes 13959168 | tf_op jit(solution)/shard_map/pallas_call | solution.py:125
  (8 shorter events, 0.1 us)
Async XLA Ops:
  0.9 8.0 %collective-permute-start = (bf16[32,3072]{1,0:T(8,128)(2,1)S(1)}, bf16[32,3072]{1,0:T(8,128)(2,1)S(1)}, u32[]{:S(2)}, u32[]{:S(2)}) collective-permute-start(bf16[32,3072]{1,0:T(8,128)(2,1)S(1)} %slice.22), channel_id=1, source_target_pairs={{1,0},{2,1},{3,2},{4,3},{5,4},{6,5},{7,6},{8,7},{9,8},{10,9},{11,1... | collective-permute-start | bytes 589832 | tf_op jit(solution)/shard_map/ppermute | solution.py:161
  3.5 2.6 %copy-start.2 = (s32[2]{0:T(128)S(1)}, s32[2]{0:T(128)}, u32[]{:S(2)}) copy-start(s32[2]{0:T(128)} %param.9) | copy-start | bytes 28
  3.5 2.6 %copy-start.3 = (s32[2]{0:T(128)S(1)}, s32[2]{0:T(128)}, u32[]{:S(2)}) copy-start(s32[2]{0:T(128)} %param.8) | copy-start | bytes 28
  3.5 4.6 %copy-start.1 = (s32[3072]{0:T(1024)S(1)}, s32[3072]{0:T(1024)}, u32[]{:S(2)}) copy-start(s32[3072]{0:T(1024)} %param.7) | copy-start | bytes 36868
  9.2 2.5 %collective-permute-start.1 = (bf16[64,3072]{1,0:T(8,128)(2,1)S(1)}, bf16[64,3072]{1,0:T(8,128)(2,1)S(1)}, u32[]{:S(2)}, u32[]{:S(2)}) collective-permute-start(bf16[64,3072]{1,0:T(8,128)(2,1)S(1)} %fusion), channel_id=1, source_target_pairs={{0,1},{1,0},{2,3},{3,2},{4,5},{5,4},{6,7},{7,6},{8,9},{9,8},{10,11... | collective-permute-start | bytes 1179656 | tf_op jit(solution)/shard_map/ppermute | solution.py:141
  16.9 20.2 %all-to-all-start = ((bf16[8,208,128]{2,1,0:T(8,128)(2,1)}), bf16[8,208,128]{2,1,0:T(8,128)(2,1)S(1)}, u32[]{:S(2)}, u32[]{:S(2)}) async-start(bf16[8,208,128]{2,1,0:T(8,128)(2,1)} %bitcast.2), calls=%async_computation | async-start | bytes 851968 | tf_op jit(solution)/shard_map/all_to_all | solution.py:181
  38.2 1.8 %copy-start = (bf16[208,1024]{1,0:T(8,128)(2,1)}, bf16[208,1024]{1,0:T(8,128)(2,1)S(1)}, u32[]{:S(2)}) copy-start(bf16[208,1024]{1,0:T(8,128)(2,1)S(1)} %pad_maximum_fusion.1.mine_ref) | copy-start | bytes 1277956
  38.2 1.8 %collective-permute-start.2 = (bf16[208,1024]{1,0:T(8,128)(2,1)S(1)}, bf16[208,1024]{1,0:T(8,128)(2,1)S(1)}, u32[]{:S(2)}, u32[]{:S(2)}) collective-permute-start(bf16[208,1024]{1,0:T(8,128)(2,1)S(1)} %pad_maximum_fusion.1.mine_ref), channel_id=1, source_target_pairs={{0,1},{1,0},{2,3},{3,2},{4,5},{5,4},{6,7},{7,6},{8,9},{9,8},{10,11... | collective-permute-start | bytes 1277960 | tf_op jit(solution)/shard_map/ppermute | solution.py:187
  40.1 0.8 %copy-start.4 = (bf16[208,1024]{1,0:T(8,128)(2,1)}, bf16[208,1024]{1,0:T(8,128)(2,1)S(1)}, u32[]{:S(2)}) copy-start(bf16[208,1024]{1,0:T(8,128)(2,1)S(1)} %collective-permute-done.2.other_ref) | copy-start | bytes 1277956

commit v23 on v11

--- a/solution.py
+++ b/solution.py
@@ -20,13 +20,12 @@
 
 
 def decimation_matrix(fir_taps, out_rows, in_rows):
-    leads = TAPS // STRIDE
-    rows = jnp.arange(out_rows, dtype=jnp.int32)[:, None, None, None]
-    groups = jnp.arange(in_rows // STRIDE, dtype=jnp.int32)[None, :, None, None]
-    lead = jnp.arange(leads, dtype=jnp.int32)[None, None, :, None]
-    taps = fir_taps.reshape(1, 1, leads, STRIDE)
-    matrix = jnp.where(groups - rows == lead, taps, 0.0).sum(axis=2)
-    return matrix.reshape(out_rows, in_rows)
+    rows = jnp.arange(out_rows, dtype=jnp.int32)[:, None, None]
+    cols = jnp.arange(in_rows, dtype=jnp.int32)[None, :, None]
+    tap = jnp.arange(TAPS, dtype=jnp.int32)[None, None, :]
+    onehot = (cols - STRIDE * rows == tap).astype(jnp.bfloat16)
+    matrix = jnp.dot(onehot, fir_taps.astype(jnp.bfloat16), preferred_element_type=jnp.float32)
+    return matrix.astype(jnp.bfloat16)
 
 
 def dft_table(samples, bins, time_index):
@@ -161,7 +160,6 @@
     halo = lax.ppermute(records[:halo_rows], ("chan", "tm"), perm=shift)
 
     taps_matrix = decimation_matrix(fir_taps, out_rows, raw_rows + halo_rows)
-    taps_matrix = taps_matrix.astype(jnp.bfloat16)
     main = jnp.dot(taps_matrix[:, :raw_rows], records, preferred_element_type=jnp.float32)
     tail = jnp.dot(taps_matrix[:, raw_rows:], halo, preferred_element_type=jnp.float32)
     decimated = (main + tail).astype(jnp.bfloat16)

time: 51.7 us -> 52.1 us (level)
  matrix products: 3.84 us -> 5.33 us
  local copies, waits for them, and re-layouts: 8.3 us -> 7.39 us
    dot_general x0 -> x1, matrix products: none -> 1.58 us  [decimation_matrix(): jnp.dot(onehot, fir_taps.astype(jnp.bfloat16), preferred_element_type=jnp...]
    broadcast_in_dim x1 -> x0, local copies, waits for them, and re-layouts: 0.74 us -> none  [decimation_matrix(): matrix = jnp.where(groups - rows == lead, taps, 0.0).sum(axis=2)]
  transfers between devices with their start and end apart: 4 -> 4, of which waited for: 3 -> 3; matrix products, arithmetic and copies ran while one was open for 15% -> 16% of each run, Pallas kernels for 0% -> 0%
where the time goes in v23:
time: 52.1 us; the launch traced here: 51.7 us
  waiting for transfers between devices  12.8 us (25%)
  Pallas kernels  10.5 us (20%)
  starting transfers between devices  9.85 us (19%)
  local copies, waits for them, and re-layouts  7.39 us (14%)
  matrix products  5.33 us (10%)
  other arithmetic  3.66 us (7%)
  between operations  2.18 us (4%)
    all_to_all x1, waiting for transfers between devices, local(): lax.all_to_all(rows, 'chan', 0, 2, tiled=True).reshape(width, samples)  11.6 us
    pallas_call x1, Pallas kernels, correlate(): pl.pallas_call(functools.partial(correlate_kernel, factor, bins, group, h...  10.5 us
    all_to_all x1, starting transfers between devices, local(): lax.all_to_all(rows, 'chan', 0, 2, tiled=True).reshape(width, samples)  7.3 us
    gather x1, local copies, waits for them, and re-layouts, local(): jnp.take(paired, index.reshape(-1), axis=0, mode='clip')  4.59 us
    dot_general x1, matrix products, local(): jnp.dot(taps_matrix[:, :raw_rows], records, preferred_element_type=jnp.fl...  2.55 us
    dot_general x1, matrix products, decimation_matrix(): jnp.dot(onehot, fir_taps.astype(jnp.bfloat16), preferred_element_type=jnp...  1.58 us
    ppermute x1, starting transfers between devices, local(): halo = lax.ppermute(records[:halo_rows], ('chan', 'tm'), perm=shift)  1.29 us
    ppermute x1, starting transfers between devices, swap_tm(): other = lax.ppermute(x, 'tm', perm=[(0, 1), (1, 0)])  1.19 us
  transfers between devices with their start and end apart: 4, of which 3 were waited for; matrix products, arithmetic and copies ran while one was open for 16% of the time, Pallas kernels for 0%

profile of v23, /device:TPU:0, one launch (start us, length us, event | category | flops | bytes accessed | tf_op | source)
XLA Modules:
  0.0 51.7 jit_solution(11048205251091220736)
XLA Ops:
  0.0 0.9 %slice.22 = bf16[24,3072]{1,0:T(8,128)(2,1)S(1)} slice(bf16[512,3072]{1,0:T(8,128)(2,1)} %param.5), slice={[0:24], [0:3072]} | slice | bytes 294912 | tf_op jit(solution)/shard_map/slice | solution.py:160
  0.9 1.3 %collective-permute-start = (bf16[24,3072]{1,0:T(8,128)(2,1)S(1)}, bf16[24,3072]{1,0:T(8,128)(2,1)S(1)}, u32[]{:S(2)}, u32[]{:S(2)}) collective-permute-start(bf16[24,3072]{1,0:T(8,128)(2,1)S(1)} %slice.22), channel_id=1, source_target_pairs={{1,0},{2,1},{3,2},{4,3},{5,4},{6,5},{7,6},{8,7},{9,8},{10,9},{11,1... | collective-permute-start | bytes 442376 | tf_op jit(solution)/shard_map/ppermute | solution.py:160
  2.2 0.1 iota_subtract_fusion
  2.3 1.6 %fusion = bf16[1,64,536]{2,0,1:T(2,128)(2,1)S(1)} fusion(s32[64,536]{1,0:T(8,128)S(1)} %iota_subtract_fusion, f32[32]{0:T(128)} %param.6), kind=kOutput, calls=%fused_computation.2 | convolution fusion | flops 3293216 | bytes 205952 | tf_op jit(solution)/shard_map/dot_general | solution.py:27
  3.9 0.0 copy-start.2
  3.9 0.0 copy-start.3
  3.9 0.0 copy-start.1
  3.9 2.5 %fusion.21 = f32[64,3072]{1,0:T(8,128)S(1)} fusion(bf16[512,3072]{1,0:T(8,128)(2,1)} %param.5, bf16[64,536]{1,0:T(8,128)(2,1)S(1)} %bitcast.32), kind=kOutput, calls=%fused_computation.49 | convolution fusion | flops 201326592 | bytes 3997696 | tf_op jit(solution)/shard_map/dot_general | solution.py:163
  6.5 0.0 copy-done.2
  6.5 0.0 copy-done.3
  6.5 0.6 %fusion.47 = s32[]{:T(128)} fusion(s32[2]{0:T(128)S(1)} %copy-done.2, s32[2]{0:T(128)S(1)} %copy-done.3, s32[]{:T(128)S(6)} %axis_index.16), kind=kLoop, calls=%fused_computation.81 | loop fusion | flops 9 | bytes 24 | tf_op jit(solution)/shard_map/reduce_sum | solution.py:171
  8.5 0.0 copy-done.1
  9.1 0.1 dynamic_slice.7
  9.2 0.1 pad.7.clone
  9.3 0.1 constant_dynamic-slice_fusion
  9.4 0.0 collective-permute-done
  9.4 0.2 fusion.1
  9.6 1.2 %collective-permute-start.1 = (bf16[64,3072]{1,0:T(8,128)(2,1)S(1)}, bf16[64,3072]{1,0:T(8,128)(2,1)S(1)}, u32[]{:S(2)}, u32[]{:S(2)}) collective-permute-start(bf16[64,3072]{1,0:T(8,128)(2,1)S(1)} %fusion.1), channel_id=1, source_target_pairs={{0,1},{1,0},{2,3},{3,2},{4,5},{5,4},{6,7},{7,6},{8,9},{9,8},{10,11... | collective-permute-start | bytes 1179656 | tf_op jit(solution)/shard_map/ppermute | solution.py:140
  10.8 0.1 reshape.280
  10.9 0.3 fusion.34
  11.2 0.9 %collective-permute-done.1 = bf16[64,3072]{1,0:T(8,128)(2,1)S(1)} collective-permute-done((bf16[64,3072]{1,0:T(8,128)(2,1)S(1)}, bf16[64,3072]{1,0:T(8,128)(2,1)S(1)}, u32[]{:S(2)}, u32[]{:S(2)}) %collective-permute-start.1) | collective-permute-done | bytes 393248 | tf_op jit(solution)/shard_map/ppermute | solution.py:140
  12.2 0.1 broadcast_select_fusion.1
  12.2 0.1 maximum_bitcast_fusion
  12.3 0.4 copy.15
  12.7 4.6 %gather_fusion = bf16[1664,128]{1,0:T(8,128)(2,1)} fusion(bf16[3072,128]{1,0:T(8,128)(2,1)S(1)} %copy.15, s32[2048]{0:T(1024)S(1)} %pad_clamp_fusion), kind=kCustom, calls=%fused_computation | custom fusion | bytes 858624 | tf_op jit(solution)/shard_map/jit(_take)/gather | solution.py:178
  17.2 7.3 %all-to-all-start = ((bf16[8,208,128]{2,1,0:T(8,128)(2,1)}), bf16[8,208,128]{2,1,0:T(8,128)(2,1)S(1)}, u32[]{:S(2)}, u32[]{:S(2)}) async-start(bf16[8,208,128]{2,1,0:T(8,128)(2,1)} %bitcast.3), calls=%async_computation | async-start | bytes 851968 | tf_op jit(solution)/shard_map/all_to_all | solution.py:179
  24.6 0.2 fusion.46
  24.7 0.3 fusion.37
  25.1 0.8 %subtract_convert_fusion = (bf16[32,32,512]{2,1,0:T(8,128)(2,1)S(1)}, bf16[32,32,512]{2,1,0:T(8,128)(2,1)S(1)}) fusion(f32[32,512]{1,0:T(8,128)S(1)} %get-tuple-element.17, f32[32,512]{1,0:T(8,128)S(1)} %get-tuple-element.16, f32[32,512]{1,0:T(8,128)S(1)} %get-tuple-element.18, f32[32,512]{1,0:T(8,128)S(1)} %get-tuple-element.15), kind=kLoop, calls=%fused_computation.11 | loop fusion | flops 4718592 | bytes 2359296 | tf_op jit(solution)/shard_map/convert.9
  25.8 11.6 %all-to-all-done = bf16[8,208,128]{2,1,0:T(8,128)(2,1)S(1)} async-done(((bf16[8,208,128]{2,1,0:T(8,128)(2,1)}), bf16[8,208,128]{2,1,0:T(8,128)(2,1)S(1)}, u32[]{:S(2)}, u32[]{:S(2)}) %all-to-all-start) | async-done | bytes 426016 | tf_op jit(solution)/shard_map/all_to_all | solution.py:179
  37.5 0.1 copy.16
  37.6 0.6 %fusion.3 = f32[208,1024]{1,0:T(8,128)S(1)} fusion(bf16[1024,512]{1,0:T(8,128)(2,1)S(1)} %bitcast.28, bf16[1024,512]{1,0:T(8,128)(2,1)S(1)} %bitcast.27, bf16[26,8,8,128]{3,2,1,0:T(8,128)(2,1)S(1)} %bitcast.31), kind=kOutput, calls=%fused_computation.6 | convolution fusion | flops 440401920 | bytes 3375104 | tf_op jit(solution)/shard_map/dot_general | solution.py:72
  38.2 0.3 multiply_convert_fusion.1
  38.6 0.0 copy-start
  38.6 0.1 collective-permute-start.2
  38.7 0.3 fusion.32
  39.0 0.1 subtract_convert_fusion.1
  39.1 0.1 copy.17
  39.2 0.1 copy.18
  39.4 0.8 %pad_maximum_fusion.lag_ref = bf16[1024,256]{1,0:T(8,128)(2,1)} fusion(bf16[512,256]{1,0:T(8,128)(2,1)S(1)} %copy.18, bf16[512,256]{1,0:T(8,128)(2,1)S(1)} %copy.17), kind=kLoop, calls=%fused_computation.17 | loop fusion | flops 1048576 | bytes 1048576 | tf_op jit(solution)/shard_map/concatenate | solution.py:66
  40.2 0.2 collective-permute-done.2.other_ref
  40.4 0.0 copy-done
  40.4 0.0 copy-start.4
  40.4 0.8 %copy-done.4 = bf16[208,1024]{1,0:T(8,128)(2,1)} copy-done((bf16[208,1024]{1,0:T(8,128)(2,1)}, bf16[208,1024]{1,0:T(8,128)(2,1)S(1)}, u32[]{:S(2)}) %copy-start.4) | copy-done | bytes 426008
  41.2 10.5 %shard_map.55 = f32[32,384,256]{2,1,0:T(8,128)} custom-call(bf16[208,1024]{1,0:T(8,128)(2,1)} %copy-done, bf16[208,1024]{1,0:T(8,128)(2,1)} %copy-done.4, bf16[1024,256]{1,0:T(8,128)(2,1)} %pad_maximum_fusion.lag_ref), custom_call_target="tpu_custom_call" | custom-call | flops 6480199680 | bytes 13959168 | tf_op jit(solution)/shard_map/pallas_call | solution.py:124
  (8 shorter events, 0.1 us)
Async XLA Ops:
  0.9 8.4 %collective-permute-start = (bf16[24,3072]{1,0:T(8,128)(2,1)S(1)}, bf16[24,3072]{1,0:T(8,128)(2,1)S(1)}, u32[]{:S(2)}, u32[]{:S(2)}) collective-permute-start(bf16[24,3072]{1,0:T(8,128)(2,1)S(1)} %slice.22), channel_id=1, source_target_pairs={{1,0},{2,1},{3,2},{4,3},{5,4},{6,5},{7,6},{8,7},{9,8},{10,9},{11,1... | collective-permute-start | bytes 442376 | tf_op jit(solution)/shard_map/ppermute | solution.py:160
  3.9 2.6 %copy-start.2 = (s32[2]{0:T(128)S(1)}, s32[2]{0:T(128)}, u32[]{:S(2)}) copy-start(s32[2]{0:T(128)} %param.9) | copy-start | bytes 28
  3.9 2.6 %copy-start.3 = (s32[2]{0:T(128)S(1)}, s32[2]{0:T(128)}, u32[]{:S(2)}) copy-start(s32[2]{0:T(128)} %param.8) | copy-start | bytes 28
  3.9 4.5 %copy-start.1 = (s32[3072]{0:T(1024)S(1)}, s32[3072]{0:T(1024)}, u32[]{:S(2)}) copy-start(s32[3072]{0:T(1024)} %param.7) | copy-start | bytes 36868
  9.6 2.5 %collective-permute-start.1 = (bf16[64,3072]{1,0:T(8,128)(2,1)S(1)}, bf16[64,3072]{1,0:T(8,128)(2,1)S(1)}, u32[]{:S(2)}, u32[]{:S(2)}) collective-permute-start(bf16[64,3072]{1,0:T(8,128)(2,1)S(1)} %fusion.1), channel_id=1, source_target_pairs={{0,1},{1,0},{2,3},{3,2},{4,5},{5,4},{6,7},{7,6},{8,9},{9,8},{10,11... | collective-permute-start | bytes 1179656 | tf_op jit(solution)/shard_map/ppermute | solution.py:140
  17.2 20.2 %all-to-all-start = ((bf16[8,208,128]{2,1,0:T(8,128)(2,1)}), bf16[8,208,128]{2,1,0:T(8,128)(2,1)S(1)}, u32[]{:S(2)}, u32[]{:S(2)}) async-start(bf16[8,208,128]{2,1,0:T(8,128)(2,1)} %bitcast.3), calls=%async_computation | async-start | bytes 851968 | tf_op jit(solution)/shard_map/all_to_all | solution.py:179
  38.6 1.8 %copy-start = (bf16[208,1024]{1,0:T(8,128)(2,1)}, bf16[208,1024]{1,0:T(8,128)(2,1)S(1)}, u32[]{:S(2)}) copy-start(bf16[208,1024]{1,0:T(8,128)(2,1)S(1)} %pad_maximum_fusion.1.mine_ref) | copy-start | bytes 1277956
  38.6 1.8 %collective-permute-start.2 = (bf16[208,1024]{1,0:T(8,128)(2,1)S(1)}, bf16[208,1024]{1,0:T(8,128)(2,1)S(1)}, u32[]{:S(2)}, u32[]{:S(2)}) collective-permute-start(bf16[208,1024]{1,0:T(8,128)(2,1)S(1)} %pad_maximum_fusion.1.mine_ref), channel_id=1, source_target_pairs={{0,1},{1,0},{2,3},{3,2},{4,5},{5,4},{6,7},{7,6},{8,9},{9,8},{10,11... | collective-permute-start | bytes 1277960 | tf_op jit(solution)/shard_map/ppermute | solution.py:185
  40.4 0.8 %copy-start.4 = (bf16[208,1024]{1,0:T(8,128)(2,1)}, bf16[208,1024]{1,0:T(8,128)(2,1)S(1)}, u32[]{:S(2)}) copy-start(bf16[208,1024]{1,0:T(8,128)(2,1)S(1)} %collective-permute-done.2.other_ref) | copy-start | bytes 1277956

commit v24 on v11

--- a/solution.py
+++ b/solution.py
@@ -162,12 +162,13 @@
 
     taps_matrix = decimation_matrix(fir_taps, out_rows, raw_rows + halo_rows)
     taps_matrix = taps_matrix.astype(jnp.bfloat16)
-    main = jnp.dot(taps_matrix[:, :raw_rows], records, preferred_element_type=jnp.float32)
-    tail = jnp.dot(taps_matrix[:, raw_rows:], halo, preferred_element_type=jnp.float32)
+    dims = (((0,), (1,)), ((), ()))
+    main = lax.dot_general(records, taps_matrix[:, :raw_rows], dims, preferred_element_type=jnp.float32)
+    tail = lax.dot_general(halo, taps_matrix[:, raw_rows:], dims, preferred_element_type=jnp.float32)
     decimated = (main + tail).astype(jnp.bfloat16)
 
     first, second = swap_tm(decimated)
-    paired = jnp.concatenate([first, second], axis=0).T
+    paired = jnp.concatenate([first, second], axis=1)
 
     steps = jnp.arange(source_owner.shape[0], dtype=jnp.int32)
     own_first = jnp.sum(jnp.where(steps == tm, source_owner * block + source_offset, 0))

time: 51.7 us -> 51.7 us (level)
  no operation moved by 1% of the time
where the time goes in v24:
time: 51.7 us; the launch traced here: 51.4 us
  waiting for transfers between devices  12.8 us (25%)
  Pallas kernels  10.5 us (20%)
  starting transfers between devices  9.85 us (19%)
  local copies, waits for them, and re-layouts  8.3 us (16%)
  other arithmetic  3.88 us (8%)
  matrix products  3.84 us (7%)
  between operations  2.18 us (4%)
    all_to_all x1, waiting for transfers between devices, local(): lax.all_to_all(rows, 'chan', 0, 2, tiled=True).reshape(width, samples)  11.6 us
    pallas_call x1, Pallas kernels, correlate(): pl.pallas_call(functools.partial(correlate_kernel, factor, bins, group, h...  10.5 us
    all_to_all x1, starting transfers between devices, local(): lax.all_to_all(rows, 'chan', 0, 2, tiled=True).reshape(width, samples)  7.3 us
    gather x1, local copies, waits for them, and re-layouts, local(): jnp.take(paired, index.reshape(-1), axis=0, mode='clip')  4.59 us
    dot_general x1, matrix products, local(): lax.dot_general(records, taps_matrix[:, :raw_rows], dims, preferred_eleme...  2.6 us
    ppermute x1, starting transfers between devices, local(): halo = lax.ppermute(records[:halo_rows], ('chan', 'tm'), perm=shift)  1.29 us
    ppermute x1, starting transfers between devices, swap_tm(): other = lax.ppermute(x, 'tm', perm=[(0, 1), (1, 0)])  1.19 us
  transfers between devices with their start and end apart: 4, of which 3 were waited for; matrix products, arithmetic and copies ran while one was open for 15% of the time, Pallas kernels for 0%

profile of v24, /device:TPU:0, one launch (start us, length us, event | category | flops | bytes accessed | tf_op | source)
XLA Modules:
  0.0 51.4 jit_solution(4192478482691048512)
XLA Ops:
  0.0 0.9 %slice.22 = bf16[24,3072]{1,0:T(8,128)(2,1)S(1)} slice(bf16[512,3072]{1,0:T(8,128)(2,1)} %param.5), slice={[0:24], [0:3072]} | slice | bytes 294912 | tf_op jit(solution)/shard_map/slice | solution.py:161
  0.9 1.3 %collective-permute-start = (bf16[24,3072]{1,0:T(8,128)(2,1)S(1)}, bf16[24,3072]{1,0:T(8,128)(2,1)S(1)}, u32[]{:S(2)}, u32[]{:S(2)}) collective-permute-start(bf16[24,3072]{1,0:T(8,128)(2,1)S(1)} %slice.22), channel_id=1, source_target_pairs={{1,0},{2,1},{3,2},{4,3},{5,4},{6,5},{7,6},{8,7},{9,8},{10,9},{11,1... | collective-permute-start | bytes 442376 | tf_op jit(solution)/shard_map/ppermute | solution.py:161
  2.2 0.7 %broadcast_in_dim.33 = f32[4,8]{1,0:T(4,128)S(1)} reshape(f32[32]{0:T(128)} %param.6) | data formatting | bytes 256 | tf_op jit(solution)/shard_map/jit(_where)/broadcast_in_dim | solution.py:28
  3.0 0.2 select_reduce_fusion
  3.3 0.2 copy.15
  3.5 0.0 copy-start.2
  3.5 0.0 copy-start.3
  3.5 0.0 copy-start.1
  3.5 2.6 %fusion.11 = f32[64,3072]{1,0:T(8,128)S(1)} fusion(bf16[512,3072]{1,0:T(8,128)(2,1)} %param.5, bf16[64,536]{0,1:T(8,128)(2,1)S(1)} %bitcast.26), kind=kOutput, calls=%fused_computation.28 | convolution fusion | flops 201326592 | bytes 4063232 | tf_op jit(solution)/shard_map/dot_general | solution.py:166
  6.1 0.0 copy-done.2
  6.1 0.0 copy-done.3
  6.1 0.6 %fusion.46 = s32[]{:T(128)} fusion(s32[2]{0:T(128)S(1)} %copy-done.2, s32[2]{0:T(128)S(1)} %copy-done.3, s32[]{:T(128)S(6)} %axis_index.16), kind=kLoop, calls=%fused_computation.80 | loop fusion | flops 9 | bytes 24 | tf_op jit(solution)/shard_map/reduce_sum | solution.py:174
  8.0 0.0 copy-done.1
  8.7 0.1 dynamic_slice.7
  8.8 0.1 pad.7.clone
  8.9 0.1 constant_dynamic-slice_fusion
  8.9 0.0 collective-permute-done
  8.9 0.3 fusion.1
  9.2 1.2 %collective-permute-start.1 = (bf16[3072,64]{0,1:T(8,128)(2,1)S(1)}, bf16[3072,64]{0,1:T(8,128)(2,1)S(1)}, u32[]{:S(2)}, u32[]{:S(2)}) collective-permute-start(bf16[3072,64]{0,1:T(8,128)(2,1)S(1)} %fusion.1), channel_id=1, source_target_pairs={{0,1},{1,0},{2,3},{3,2},{4,5},{5,4},{6,7},{7,6},{8,9},{9,8},{10,11... | collective-permute-start | bytes 1179656 | tf_op jit(solution)/shard_map/ppermute | solution.py:141
  10.4 0.1 reshape.277
  10.6 0.3 fusion.33
  10.8 0.9 %collective-permute-done.1 = bf16[3072,64]{0,1:T(8,128)(2,1)S(1)} collective-permute-done((bf16[3072,64]{0,1:T(8,128)(2,1)S(1)}, bf16[3072,64]{0,1:T(8,128)(2,1)S(1)}, u32[]{:S(2)}, u32[]{:S(2)}) %collective-permute-start.1) | collective-permute-done | bytes 393248 | tf_op jit(solution)/shard_map/ppermute | solution.py:141
  11.8 0.1 broadcast_select_fusion.1
  11.8 0.1 pad_maximum_fusion
  11.9 0.4 copy.16
  12.3 4.6 %gather_fusion = bf16[1664,128]{1,0:T(8,128)(2,1)} fusion(bf16[3072,128]{1,0:T(8,128)(2,1)S(1)} %copy.16, s32[2048]{0:T(1024)S(1)} %pad_clamp_fusion), kind=kCustom, calls=%fused_computation | custom fusion | bytes 858624 | tf_op jit(solution)/shard_map/jit(_take)/gather | solution.py:181
  16.9 7.3 %all-to-all-start = ((bf16[8,208,128]{2,1,0:T(8,128)(2,1)}), bf16[8,208,128]{2,1,0:T(8,128)(2,1)S(1)}, u32[]{:S(2)}, u32[]{:S(2)}) async-start(bf16[8,208,128]{2,1,0:T(8,128)(2,1)} %bitcast.2), calls=%async_computation | async-start | bytes 851968 | tf_op jit(solution)/shard_map/all_to_all | solution.py:182
  24.2 0.2 fusion.44
  24.3 0.3 fusion.36
  24.7 0.8 %subtract_convert_fusion = (bf16[32,32,512]{2,1,0:T(8,128)(2,1)S(1)}, bf16[32,32,512]{2,1,0:T(8,128)(2,1)S(1)}) fusion(f32[32,512]{1,0:T(8,128)S(1)} %get-tuple-element.17, f32[32,512]{1,0:T(8,128)S(1)} %get-tuple-element.16, f32[32,512]{1,0:T(8,128)S(1)} %get-tuple-element.18, f32[32,512]{1,0:T(8,128)S(1)} %get-tuple-element.15), kind=kLoop, calls=%fused_computation.9 | loop fusion | flops 4718592 | bytes 2359296 | tf_op jit(solution)/shard_map/convert.9
  25.4 11.6 %all-to-all-done = bf16[8,208,128]{2,1,0:T(8,128)(2,1)S(1)} async-done(((bf16[8,208,128]{2,1,0:T(8,128)(2,1)}), bf16[8,208,128]{2,1,0:T(8,128)(2,1)S(1)}, u32[]{:S(2)}, u32[]{:S(2)}) %all-to-all-start) | async-done | bytes 426016 | tf_op jit(solution)/shard_map/all_to_all | solution.py:182
  37.1 0.1 copy.17
  37.2 0.6 %fusion.2 = f32[208,1024]{1,0:T(8,128)S(1)} fusion(bf16[1024,512]{1,0:T(8,128)(2,1)S(1)} %bitcast.23, bf16[1024,512]{1,0:T(8,128)(2,1)S(1)} %bitcast.22, bf16[26,8,8,128]{3,2,1,0:T(8,128)(2,1)S(1)} %bitcast.28), kind=kOutput, calls=%fused_computation.4 | convolution fusion | flops 440401920 | bytes 3375104 | tf_op jit(solution)/shard_map/dot_general | solution.py:73
  37.8 0.3 multiply_convert_fusion.1
  38.2 0.0 copy-start
  38.2 0.1 collective-permute-start.2
  38.3 0.3 fusion.31
  38.6 0.1 subtract_convert_fusion.1
  38.7 0.1 copy.18
  38.9 0.1 copy.19
  39.0 0.8 %pad_maximum_fusion.1.lag_ref = bf16[1024,256]{1,0:T(8,128)(2,1)} fusion(bf16[512,256]{1,0:T(8,128)(2,1)S(1)} %copy.19, bf16[512,256]{1,0:T(8,128)(2,1)S(1)} %copy.18), kind=kLoop, calls=%fused_computation.16 | loop fusion | flops 1048576 | bytes 1048576 | tf_op jit(solution)/shard_map/concatenate | solution.py:67
  39.9 0.2 collective-permute-done.2.other_ref
  40.1 0.0 copy-done
  40.1 0.0 copy-start.4
  40.1 0.8 %copy-done.4 = bf16[208,1024]{1,0:T(8,128)(2,1)} copy-done((bf16[208,1024]{1,0:T(8,128)(2,1)}, bf16[208,1024]{1,0:T(8,128)(2,1)S(1)}, u32[]{:S(2)}) %copy-start.4) | copy-done | bytes 426008
  40.8 10.5 %shard_map.55 = f32[32,384,256]{2,1,0:T(8,128)} custom-call(bf16[208,1024]{1,0:T(8,128)(2,1)} %copy-done, bf16[208,1024]{1,0:T(8,128)(2,1)} %copy-done.4, bf16[1024,256]{1,0:T(8,128)(2,1)} %pad_maximum_fusion.1.lag_ref), custom_call_target="tpu_custom_call" | custom-call | flops 6480199680 | bytes 13959168 | tf_op jit(solution)/shard_map/pallas_call | solution.py:125
  (8 shorter events, 0.1 us)
Async XLA Ops:
  0.9 8.0 %collective-permute-start = (bf16[24,3072]{1,0:T(8,128)(2,1)S(1)}, bf16[24,3072]{1,0:T(8,128)(2,1)S(1)}, u32[]{:S(2)}, u32[]{:S(2)}) collective-permute-start(bf16[24,3072]{1,0:T(8,128)(2,1)S(1)} %slice.22), channel_id=1, source_target_pairs={{1,0},{2,1},{3,2},{4,3},{5,4},{6,5},{7,6},{8,7},{9,8},{10,9},{11,1... | collective-permute-start | bytes 442376 | tf_op jit(solution)/shard_map/ppermute | solution.py:161
  3.5 2.6 %copy-start.2 = (s32[2]{0:T(128)S(1)}, s32[2]{0:T(128)}, u32[]{:S(2)}) copy-start(s32[2]{0:T(128)} %param.9) | copy-start | bytes 28
  3.5 2.6 %copy-start.3 = (s32[2]{0:T(128)S(1)}, s32[2]{0:T(128)}, u32[]{:S(2)}) copy-start(s32[2]{0:T(128)} %param.8) | copy-start | bytes 28
  3.5 4.6 %copy-start.1 = (s32[3072]{0:T(1024)S(1)}, s32[3072]{0:T(1024)}, u32[]{:S(2)}) copy-start(s32[3072]{0:T(1024)} %param.7) | copy-start | bytes 36868
  9.2 2.5 %collective-permute-start.1 = (bf16[3072,64]{0,1:T(8,128)(2,1)S(1)}, bf16[3072,64]{0,1:T(8,128)(2,1)S(1)}, u32[]{:S(2)}, u32[]{:S(2)}) collective-permute-start(bf16[3072,64]{0,1:T(8,128)(2,1)S(1)} %fusion.1), channel_id=1, source_target_pairs={{0,1},{1,0},{2,3},{3,2},{4,5},{5,4},{6,7},{7,6},{8,9},{9,8},{10,11... | collective-permute-start | bytes 1179656 | tf_op jit(solution)/shard_map/ppermute | solution.py:141
  16.9 20.2 %all-to-all-start = ((bf16[8,208,128]{2,1,0:T(8,128)(2,1)}), bf16[8,208,128]{2,1,0:T(8,128)(2,1)S(1)}, u32[]{:S(2)}, u32[]{:S(2)}) async-start(bf16[8,208,128]{2,1,0:T(8,128)(2,1)} %bitcast.2), calls=%async_computation | async-start | bytes 851968 | tf_op jit(solution)/shard_map/all_to_all | solution.py:182
  38.2 1.8 %copy-start = (bf16[208,1024]{1,0:T(8,128)(2,1)}, bf16[208,1024]{1,0:T(8,128)(2,1)S(1)}, u32[]{:S(2)}) copy-start(bf16[208,1024]{1,0:T(8,128)(2,1)S(1)} %pad_maximum_fusion.2.mine_ref) | copy-start | bytes 1277956
  38.2 1.8 %collective-permute-start.2 = (bf16[208,1024]{1,0:T(8,128)(2,1)S(1)}, bf16[208,1024]{1,0:T(8,128)(2,1)S(1)}, u32[]{:S(2)}, u32[]{:S(2)}) collective-permute-start(bf16[208,1024]{1,0:T(8,128)(2,1)S(1)} %pad_maximum_fusion.2.mine_ref), channel_id=1, source_target_pairs={{0,1},{1,0},{2,3},{3,2},{4,5},{5,4},{6,7},{7,6},{8,9},{9,8},{10,11... | collective-permute-start | bytes 1277960 | tf_op jit(solution)/shard_map/ppermute | solution.py:188
  40.1 0.8 %copy-start.4 = (bf16[208,1024]{1,0:T(8,128)(2,1)}, bf16[208,1024]{1,0:T(8,128)(2,1)S(1)}, u32[]{:S(2)}) copy-start(bf16[208,1024]{1,0:T(8,128)(2,1)S(1)} %collective-permute-done.2.other_ref) | copy-start | bytes 1277956

commit v25 on v11

--- a/solution.py
+++ b/solution.py
@@ -166,8 +166,8 @@
     tail = jnp.dot(taps_matrix[:, raw_rows:], halo, preferred_element_type=jnp.float32)
     decimated = (main + tail).astype(jnp.bfloat16)
 
-    first, second = swap_tm(decimated)
-    paired = jnp.concatenate([first, second], axis=0).T
+    other = lax.ppermute(decimated, "tm", perm=[(0, 1), (1, 0)])
+    paired = jnp.concatenate([decimated, other], axis=0).T
 
     steps = jnp.arange(source_owner.shape[0], dtype=jnp.int32)
     own_first = jnp.sum(jnp.where(steps == tm, source_owner * block + source_offset, 0))
@@ -179,7 +179,10 @@
     width = index.shape[1]
     rows = jnp.take(paired, index.reshape(-1), axis=0, mode="clip").reshape(n_chan, width, -1)
     series = lax.all_to_all(rows, "chan", 0, 2, tiled=True).reshape(width, samples)
-    table = dft_table(samples, bins, jnp.arange(samples, dtype=jnp.int32))
+    chunk = 2 * out_rows
+    column = jnp.arange(samples, dtype=jnp.int32)
+    time_index = column - column % chunk + (column % chunk + tm * out_rows) % chunk
+    table = dft_table(samples, bins, time_index)
     lag_share = LAGS // n_tm
     lag = lag_kernel(samples, tm * lag_share, lag_share)
 

time: 51.7 us -> 53.9 us (1.043)
  local copies, waits for them, and re-layouts: 8.3 us -> 9.68 us
  other arithmetic: 3.88 us -> 4.54 us
    reshape x1, local copies, waits for them, and re-layouts: 0.01 us -> 0.71 us  [local(): channel_map.reshape(n_chan, block)]
    dynamic_slice x1, local copies, waits for them, and re-layouts: 0.08 us -> 0.78 us  [local(): source_raw = lax.dynamic_slice_in_dim(channel_map, own_first, SRC)]
    reduce_sum x1, other arithmetic: 0.63 us -> 1.31 us  [local(): jnp.sum(jnp.where(steps == tm, source_owner * block + source_offset, 0))]
  transfers between devices with their start and end apart: 4 -> 4, of which waited for: 3 -> 3; matrix products, arithmetic and copies ran while one was open for 15% -> 19% of each run, Pallas kernels for 0% -> 0%
where the time goes in v25:
time: 53.9 us; the launch traced here: 53.5 us
  waiting for transfers between devices  12.9 us (24%)
  Pallas kernels  10.5 us (19%)
  starting transfers between devices  9.85 us (18%)
  local copies, waits for them, and re-layouts  9.68 us (18%)
  other arithmetic  4.54 us (8%)
  matrix products  3.82 us (7%)
  between operations  2.16 us (4%)
    all_to_all x1, waiting for transfers between devices, local(): lax.all_to_all(rows, 'chan', 0, 2, tiled=True).reshape(width, samples)  11.6 us
    pallas_call x1, Pallas kernels, correlate(): pl.pallas_call(functools.partial(correlate_kernel, factor, bins, group, h...  10.5 us
    all_to_all x1, starting transfers between devices, local(): lax.all_to_all(rows, 'chan', 0, 2, tiled=True).reshape(width, samples)  7.3 us
    gather x1, local copies, waits for them, and re-layouts, local(): jnp.take(paired, index.reshape(-1), axis=0, mode='clip')  4.59 us
    dot_general x1, matrix products, local(): jnp.dot(taps_matrix[:, :raw_rows], records, preferred_element_type=jnp.fl...  2.58 us
    reduce_sum x1, other arithmetic, local(): jnp.sum(jnp.where(steps == tm, source_owner * block + source_offset, 0))  1.31 us
    ppermute x1, starting transfers between devices, local(): halo = lax.ppermute(records[:halo_rows], ('chan', 'tm'), perm=shift)  1.29 us
    ppermute x1, starting transfers between devices, local(): other = lax.ppermute(decimated, 'tm', perm=[(0, 1), (1, 0)])  1.19 us
  transfers between devices with their start and end apart: 4, of which 3 were waited for; matrix products, arithmetic and copies ran while one was open for 19% of the time, Pallas kernels for 0%

profile of v25, /device:TPU:0, one launch (start us, length us, event | category | flops | bytes accessed | tf_op | source)
XLA Modules:
  0.0 53.5 jit_solution(560343156249459512)
XLA Ops:
  0.0 0.9 %slice.20 = bf16[24,3072]{1,0:T(8,128)(2,1)S(1)} slice(bf16[512,3072]{1,0:T(8,128)(2,1)} %param.5), slice={[0:24], [0:3072]} | slice | bytes 294912 | tf_op jit(solution)/shard_map/slice | solution.py:161
  0.9 1.3 %collective-permute-start = (bf16[24,3072]{1,0:T(8,128)(2,1)S(1)}, bf16[24,3072]{1,0:T(8,128)(2,1)S(1)}, u32[]{:S(2)}, u32[]{:S(2)}) collective-permute-start(bf16[24,3072]{1,0:T(8,128)(2,1)S(1)} %slice.20), channel_id=1, source_target_pairs={{1,0},{2,1},{3,2},{4,3},{5,4},{6,5},{7,6},{8,7},{9,8},{10,9},{11,1... | collective-permute-start | bytes 442376 | tf_op jit(solution)/shard_map/ppermute | solution.py:161
  2.3 1.3 %fusion.48 = s32[]{:T(128)} fusion(s32[2]{0:T(128)} %param.9, s32[2]{0:T(128)} %param.8, s32[]{:T(128)S(6)} %axis_index.12), kind=kLoop, calls=%fused_computation.88 | loop fusion | flops 9 | bytes 24 | tf_op jit(solution)/shard_map/reduce_sum | solution.py:173
  4.9 0.7 %reshape.260 = s32[8,384]{1,0:T(8,128)S(1)} reshape(s32[3072]{0:T(1024)} %param.7) | data formatting | bytes 24576 | tf_op jit(solution)/shard_map/reshape | solution.py:175
  6.2 0.8 %dynamic_slice.7 = s32[16]{0:T(128)S(1)} dynamic-slice(s32[3072]{0:T(1024)} %param.7, s32[]{:T(128)S(6)} %select_n.96), dynamic_slice_sizes={16} | dynamic-slice | bytes 132 | tf_op jit(solution)/shard_map/dynamic_slice | solution.py:174
  7.0 0.1 pad.7.clone
  7.1 0.7 %broadcast_in_dim.33 = f32[4,8]{1,0:T(4,128)S(1)} reshape(f32[32]{0:T(128)} %param.6) | data formatting | bytes 256 | tf_op jit(solution)/shard_map/jit(_where)/broadcast_in_dim | solution.py:28
  7.8 0.1 constant_dynamic-slice_fusion
  7.9 0.1 reshape.266
  8.0 0.2 select_reduce_fusion
  8.3 0.2 copy.15
  8.5 2.6 %fusion.10 = f32[64,3072]{1,0:T(8,128)S(1)} fusion(bf16[512,3072]{1,0:T(8,128)(2,1)} %param.5, bf16[64,536]{0,1:T(8,128)(2,1)S(1)} %bitcast.26), kind=kOutput, calls=%fused_computation.25 | convolution fusion | flops 201326592 | bytes 4063232 | tf_op jit(solution)/shard_map/dot_general | solution.py:165
  11.1 0.0 collective-permute-done
  11.1 0.3 fusion
  11.4 1.2 %collective-permute-start.1 = (bf16[64,3072]{1,0:T(8,128)(2,1)S(1)}, bf16[64,3072]{1,0:T(8,128)(2,1)S(1)}, u32[]{:S(2)}, u32[]{:S(2)}) collective-permute-start(bf16[64,3072]{1,0:T(8,128)(2,1)S(1)} %fusion), channel_id=1, source_target_pairs={{0,1},{1,0},{2,3},{3,2},{4,5},{5,4},{6,7},{7,6},{8,9},{9,8},{10,11... | collective-permute-start | bytes 1179656 | tf_op jit(solution)/shard_map/ppermute | solution.py:169
  12.6 0.3 fusion.32
  12.9 1.0 %collective-permute-done.1 = bf16[64,3072]{1,0:T(8,128)(2,1)S(1)} collective-permute-done((bf16[64,3072]{1,0:T(8,128)(2,1)S(1)}, bf16[64,3072]{1,0:T(8,128)(2,1)S(1)}, u32[]{:S(2)}, u32[]{:S(2)}) %collective-permute-start.1) | collective-permute-done | bytes 393248 | tf_op jit(solution)/shard_map/ppermute | solution.py:169
  13.9 0.1 maximum_bitcast_fusion
  14.0 0.4 copy.16
  14.4 4.6 %gather_fusion = bf16[1664,128]{1,0:T(8,128)(2,1)} fusion(bf16[3072,128]{1,0:T(8,128)(2,1)S(1)} %copy.16, s32[2048]{0:T(1024)S(1)} %pad_clamp_fusion), kind=kCustom, calls=%fused_computation | custom fusion | bytes 858624 | tf_op jit(solution)/shard_map/jit(_take)/gather | solution.py:180
  19.0 7.3 %all-to-all-start = ((bf16[8,208,128]{2,1,0:T(8,128)(2,1)}), bf16[8,208,128]{2,1,0:T(8,128)(2,1)S(1)}, u32[]{:S(2)}, u32[]{:S(2)}) async-start(bf16[8,208,128]{2,1,0:T(8,128)(2,1)} %bitcast.2), calls=%async_computation | async-start | bytes 851968 | tf_op jit(solution)/shard_map/all_to_all | solution.py:181
  26.3 0.2 fusion.45
  26.4 0.3 fusion.35
  26.8 0.8 %subtract_convert_fusion = (bf16[32,32,512]{2,1,0:T(8,128)(2,1)S(1)}, bf16[32,32,512]{2,1,0:T(8,128)(2,1)S(1)}) fusion(f32[32,512]{1,0:T(8,128)S(1)} %get-tuple-element.17, f32[32,512]{1,0:T(8,128)S(1)} %get-tuple-element.14, f32[32,512]{1,0:T(8,128)S(1)} %get-tuple-element.18, f32[32,512]{1,0:T(8,128)S(1)} %get-tuple-element.13), kind=kLoop, calls=%fused_computation.8 | loop fusion | flops 4718592 | bytes 2359296 | tf_op jit(solution)/shard_map/convert.9
  27.5 11.6 %all-to-all-done = bf16[8,208,128]{2,1,0:T(8,128)(2,1)S(1)} async-done(((bf16[8,208,128]{2,1,0:T(8,128)(2,1)}), bf16[8,208,128]{2,1,0:T(8,128)(2,1)S(1)}, u32[]{:S(2)}, u32[]{:S(2)}) %all-to-all-start) | async-done | bytes 426016 | tf_op jit(solution)/shard_map/all_to_all | solution.py:181
  39.2 0.1 copy.17
  39.3 0.6 %fusion.1 = f32[208,1024]{1,0:T(8,128)S(1)} fusion(bf16[1024,512]{1,0:T(8,128)(2,1)S(1)} %bitcast.23, bf16[1024,512]{1,0:T(8,128)(2,1)S(1)} %bitcast.22, bf16[26,8,8,128]{3,2,1,0:T(8,128)(2,1)S(1)} %bitcast.28), kind=kOutput, calls=%fused_computation.3 | convolution fusion | flops 440401920 | bytes 3375104 | tf_op jit(solution)/shard_map/dot_general | solution.py:73
  39.9 0.3 multiply_convert_fusion.1
  40.3 0.0 copy-start
  40.3 0.1 collective-permute-start.2
  40.4 0.3 fusion.30
  40.7 0.1 subtract_convert_fusion.1
  40.8 0.1 copy.18
  41.0 0.1 copy.19
  41.1 0.8 %pad_maximum_fusion.lag_ref = bf16[1024,256]{1,0:T(8,128)(2,1)} fusion(bf16[512,256]{1,0:T(8,128)(2,1)S(1)} %copy.19, bf16[512,256]{1,0:T(8,128)(2,1)S(1)} %copy.18), kind=kLoop, calls=%fused_computation.15 | loop fusion | flops 1048576 | bytes 1048576 | tf_op jit(solution)/shard_map/concatenate | solution.py:67
  41.9 0.2 collective-permute-done.2.other_ref
  42.2 0.0 copy-done
  42.2 0.0 copy-start.1
  42.2 0.8 %copy-done.1 = bf16[208,1024]{1,0:T(8,128)(2,1)} copy-done((bf16[208,1024]{1,0:T(8,128)(2,1)}, bf16[208,1024]{1,0:T(8,128)(2,1)S(1)}, u32[]{:S(2)}) %copy-start.1) | copy-done | bytes 426008
  42.9 10.5 %shard_map.55 = f32[32,384,256]{2,1,0:T(8,128)} custom-call(bf16[208,1024]{1,0:T(8,128)(2,1)} %copy-done, bf16[208,1024]{1,0:T(8,128)(2,1)} %copy-done.1, bf16[1024,256]{1,0:T(8,128)(2,1)} %pad_maximum_fusion.lag_ref), custom_call_target="tpu_custom_call" | custom-call | flops 6480199680 | bytes 13959168 | tf_op jit(solution)/shard_map/pallas_call | solution.py:125
  (10 shorter events, 0.2 us)
Async XLA Ops:
  0.9 10.2 %collective-permute-start = (bf16[24,3072]{1,0:T(8,128)(2,1)S(1)}, bf16[24,3072]{1,0:T(8,128)(2,1)S(1)}, u32[]{:S(2)}, u32[]{:S(2)}) collective-permute-start(bf16[24,3072]{1,0:T(8,128)(2,1)S(1)} %slice.20), channel_id=1, source_target_pairs={{1,0},{2,1},{3,2},{4,3},{5,4},{6,5},{7,6},{8,7},{9,8},{10,9},{11,1... | collective-permute-start | bytes 442376 | tf_op jit(solution)/shard_map/ppermute | solution.py:161
  11.4 2.5 %collective-permute-start.1 = (bf16[64,3072]{1,0:T(8,128)(2,1)S(1)}, bf16[64,3072]{1,0:T(8,128)(2,1)S(1)}, u32[]{:S(2)}, u32[]{:S(2)}) collective-permute-start(bf16[64,3072]{1,0:T(8,128)(2,1)S(1)} %fusion), channel_id=1, source_target_pairs={{0,1},{1,0},{2,3},{3,2},{4,5},{5,4},{6,7},{7,6},{8,9},{9,8},{10,11... | collective-permute-start | bytes 1179656 | tf_op jit(solution)/shard_map/ppermute | solution.py:169
  19.0 20.2 %all-to-all-start = ((bf16[8,208,128]{2,1,0:T(8,128)(2,1)}), bf16[8,208,128]{2,1,0:T(8,128)(2,1)S(1)}, u32[]{:S(2)}, u32[]{:S(2)}) async-start(bf16[8,208,128]{2,1,0:T(8,128)(2,1)} %bitcast.2), calls=%async_computation | async-start | bytes 851968 | tf_op jit(solution)/shard_map/all_to_all | solution.py:181
  40.3 1.8 %copy-start = (bf16[208,1024]{1,0:T(8,128)(2,1)}, bf16[208,1024]{1,0:T(8,128)(2,1)S(1)}, u32[]{:S(2)}) copy-start(bf16[208,1024]{1,0:T(8,128)(2,1)S(1)} %pad_maximum_fusion.1.mine_ref) | copy-start | bytes 1277956
  40.3 1.8 %collective-permute-start.2 = (bf16[208,1024]{1,0:T(8,128)(2,1)S(1)}, bf16[208,1024]{1,0:T(8,128)(2,1)S(1)}, u32[]{:S(2)}, u32[]{:S(2)}) collective-permute-start(bf16[208,1024]{1,0:T(8,128)(2,1)S(1)} %pad_maximum_fusion.1.mine_ref), channel_id=1, source_target_pairs={{0,1},{1,0},{2,3},{3,2},{4,5},{5,4},{6,7},{7,6},{8,9},{9,8},{10,11... | collective-permute-start | bytes 1277960 | tf_op jit(solution)/shard_map/ppermute | solution.py:190
  42.2 0.8 %copy-start.1 = (bf16[208,1024]{1,0:T(8,128)(2,1)}, bf16[208,1024]{1,0:T(8,128)(2,1)S(1)}, u32[]{:S(2)}) copy-start(bf16[208,1024]{1,0:T(8,128)(2,1)S(1)} %collective-permute-done.2.other_ref) | copy-start | bytes 1277956

commit v26 on v11

--- a/solution.py
+++ b/solution.py
@@ -177,7 +177,7 @@
         [half_raw, jnp.broadcast_to(source_raw[None], (n_chan, SRC))], axis=1
     )
     width = index.shape[1]
-    rows = jnp.take(paired, index.reshape(-1), axis=0, mode="clip").reshape(n_chan, width, -1)
+    rows = paired.at[index.reshape(-1)].get(mode="promise_in_bounds").reshape(n_chan, width, -1)
     series = lax.all_to_all(rows, "chan", 0, 2, tiled=True).reshape(width, samples)
     table = dft_table(samples, bins, jnp.arange(samples, dtype=jnp.int32))
     lag_share = LAGS // n_tm

time: 51.7 us -> 53.8 us (1.041)
  local copies, waits for them, and re-layouts: 8.3 us -> 9.68 us
  other arithmetic: 3.88 us -> 4.57 us
    reshape x1, local copies, waits for them, and re-layouts: 0.01 us -> 0.71 us  [local(): channel_map.reshape(n_chan, block)]
    dynamic_slice x1, local copies, waits for them, and re-layouts: 0.08 us -> 0.77 us  [local(): source_raw = lax.dynamic_slice_in_dim(channel_map, own_first, SRC)]
    reduce_sum x1, other arithmetic: 0.63 us -> 1.31 us  [local(): jnp.sum(jnp.where(steps == tm, source_owner * block + source_offset, 0))]
  transfers between devices with their start and end apart: 4 -> 4, of which waited for: 3 -> 3; matrix products, arithmetic and copies ran while one was open for 15% -> 19% of each run, Pallas kernels for 0% -> 0%
where the time goes in v26:
time: 53.8 us; the launch traced here: 53.4 us
  waiting for transfers between devices  12.8 us (24%)
  Pallas kernels  10.5 us (20%)
  starting transfers between devices  9.84 us (18%)
  local copies, waits for them, and re-layouts  9.68 us (18%)
  other arithmetic  4.57 us (8%)
  matrix products  3.82 us (7%)
  between operations  2.14 us (4%)
    all_to_all x1, waiting for transfers between devices, local(): lax.all_to_all(rows, 'chan', 0, 2, tiled=True).reshape(width, samples)  11.6 us
    pallas_call x1, Pallas kernels, correlate(): pl.pallas_call(functools.partial(correlate_kernel, factor, bins, group, h...  10.5 us
    all_to_all x1, starting transfers between devices, local(): lax.all_to_all(rows, 'chan', 0, 2, tiled=True).reshape(width, samples)  7.29 us
    gather x1, local copies, waits for them, and re-layouts, local(): paired.at[index.reshape(-1)].get(mode='promise_in_bounds')  4.59 us
    dot_general x1, matrix products, local(): jnp.dot(taps_matrix[:, :raw_rows], records, preferred_element_type=jnp.fl...  2.58 us
    reduce_sum x1, other arithmetic, local(): jnp.sum(jnp.where(steps == tm, source_owner * block + source_offset, 0))  1.31 us
    ppermute x1, starting transfers between devices, local(): halo = lax.ppermute(records[:halo_rows], ('chan', 'tm'), perm=shift)  1.29 us
    ppermute x1, starting transfers between devices, swap_tm(): other = lax.ppermute(x, 'tm', perm=[(0, 1), (1, 0)])  1.19 us
  transfers between devices with their start and end apart: 4, of which 3 were waited for; matrix products, arithmetic and copies ran while one was open for 19% of the time, Pallas kernels for 0%

profile of v26, /device:TPU:0, one launch (start us, length us, event | category | flops | bytes accessed | tf_op | source)
XLA Modules:
  0.0 53.4 jit_solution(322223779687255739)
XLA Ops:
  0.0 0.9 %slice.22 = bf16[24,3072]{1,0:T(8,128)(2,1)S(1)} slice(bf16[512,3072]{1,0:T(8,128)(2,1)} %param.5), slice={[0:24], [0:3072]} | slice | bytes 294912 | tf_op jit(solution)/shard_map/slice | solution.py:161
  0.9 1.3 %collective-permute-start = (bf16[24,3072]{1,0:T(8,128)(2,1)S(1)}, bf16[24,3072]{1,0:T(8,128)(2,1)S(1)}, u32[]{:S(2)}, u32[]{:S(2)}) collective-permute-start(bf16[24,3072]{1,0:T(8,128)(2,1)S(1)} %slice.22), channel_id=1, source_target_pairs={{1,0},{2,1},{3,2},{4,3},{5,4},{6,5},{7,6},{8,7},{9,8},{10,9},{11,1... | collective-permute-start | bytes 442376 | tf_op jit(solution)/shard_map/ppermute | solution.py:161
  2.2 1.3 %fusion.46 = s32[]{:T(128)} fusion(s32[2]{0:T(128)} %param.9, s32[2]{0:T(128)} %param.8, s32[]{:T(128)S(6)} %axis_index.16), kind=kLoop, calls=%fused_computation.81 | loop fusion | flops 9 | bytes 24 | tf_op jit(solution)/shard_map/reduce_sum | solution.py:173
  4.9 0.7 %reshape.297 = s32[8,384]{1,0:T(8,128)S(1)} reshape(s32[3072]{0:T(1024)} %param.7) | data formatting | bytes 24576 | tf_op jit(solution)/shard_map/reshape | solution.py:175
  6.2 0.8 %dynamic_slice.7 = s32[16]{0:T(128)S(1)} dynamic-slice(s32[3072]{0:T(1024)} %param.7, s32[]{:T(128)S(6)} %select_n.103), dynamic_slice_sizes={16} | dynamic-slice | bytes 132 | tf_op jit(solution)/shard_map/dynamic_slice | solution.py:174
  7.0 0.1 pad.7.clone
  7.1 0.7 %broadcast_in_dim.29 = f32[4,8]{1,0:T(4,128)S(1)} reshape(f32[32]{0:T(128)} %param.6) | data formatting | bytes 256 | tf_op jit(solution)/shard_map/jit(_where)/broadcast_in_dim | solution.py:28
  7.8 0.2 select_reduce_fusion
  8.1 0.2 copy.15
  8.3 2.6 %fusion.10 = f32[64,3072]{1,0:T(8,128)S(1)} fusion(bf16[512,3072]{1,0:T(8,128)(2,1)} %param.5, bf16[64,536]{0,1:T(8,128)(2,1)S(1)} %bitcast.26), kind=kOutput, calls=%fused_computation.27 | convolution fusion | flops 201326592 | bytes 4063232 | tf_op jit(solution)/shard_map/dot_general | solution.py:165
  10.9 0.1 constant_dynamic-slice_fusion
  10.9 0.0 collective-permute-done
  10.9 0.3 fusion
  11.2 1.2 %collective-permute-start.1 = (bf16[64,3072]{1,0:T(8,128)(2,1)S(1)}, bf16[64,3072]{1,0:T(8,128)(2,1)S(1)}, u32[]{:S(2)}, u32[]{:S(2)}) collective-permute-start(bf16[64,3072]{1,0:T(8,128)(2,1)S(1)} %fusion), channel_id=1, source_target_pairs={{0,1},{1,0},{2,3},{3,2},{4,5},{5,4},{6,7},{7,6},{8,9},{9,8},{10,11... | collective-permute-start | bytes 1179656 | tf_op jit(solution)/shard_map/ppermute | solution.py:141
  12.4 0.1 reshape.298
  12.6 0.3 fusion.32
  12.9 0.9 %collective-permute-done.1 = bf16[64,3072]{1,0:T(8,128)(2,1)S(1)} collective-permute-done((bf16[64,3072]{1,0:T(8,128)(2,1)S(1)}, bf16[64,3072]{1,0:T(8,128)(2,1)S(1)}, u32[]{:S(2)}, u32[]{:S(2)}) %collective-permute-start.1) | collective-permute-done | bytes 393248 | tf_op jit(solution)/shard_map/ppermute | solution.py:141
  13.8 0.1 broadcast_select_fusion.1
  13.8 0.1 maximum_bitcast_fusion
  13.9 0.4 copy.16
  14.3 4.6 %gather_fusion = bf16[1664,128]{1,0:T(8,128)(2,1)} fusion(bf16[3072,128]{1,0:T(8,128)(2,1)S(1)} %copy.16, s32[2048]{0:T(1024)S(1)} %pad_clamp_fusion), kind=kCustom, calls=%fused_computation | custom fusion | bytes 858624 | tf_op jit(solution)/shard_map/gather | solution.py:180
  18.9 7.3 %all-to-all-start = ((bf16[8,208,128]{2,1,0:T(8,128)(2,1)}), bf16[8,208,128]{2,1,0:T(8,128)(2,1)S(1)}, u32[]{:S(2)}, u32[]{:S(2)}) async-start(bf16[8,208,128]{2,1,0:T(8,128)(2,1)} %bitcast.2), calls=%async_computation | async-start | bytes 851968 | tf_op jit(solution)/shard_map/all_to_all | solution.py:181
  26.2 0.2 fusion.43
  26.3 0.3 fusion.35
  26.7 0.8 %subtract_convert_fusion = (bf16[32,32,512]{2,1,0:T(8,128)(2,1)S(1)}, bf16[32,32,512]{2,1,0:T(8,128)(2,1)S(1)}) fusion(f32[32,512]{1,0:T(8,128)S(1)} %get-tuple-element.17, f32[32,512]{1,0:T(8,128)S(1)} %get-tuple-element.16, f32[32,512]{1,0:T(8,128)S(1)} %get-tuple-element.18, f32[32,512]{1,0:T(8,128)S(1)} %get-tuple-element.15), kind=kLoop, calls=%fused_computation.8 | loop fusion | flops 4718592 | bytes 2359296 | tf_op jit(solution)/shard_map/convert.9
  27.4 11.6 %all-to-all-done = bf16[8,208,128]{2,1,0:T(8,128)(2,1)S(1)} async-done(((bf16[8,208,128]{2,1,0:T(8,128)(2,1)}), bf16[8,208,128]{2,1,0:T(8,128)(2,1)S(1)}, u32[]{:S(2)}, u32[]{:S(2)}) %all-to-all-start) | async-done | bytes 426016 | tf_op jit(solution)/shard_map/all_to_all | solution.py:181
  39.1 0.1 copy.17
  39.2 0.6 %fusion.1 = f32[208,1024]{1,0:T(8,128)S(1)} fusion(bf16[1024,512]{1,0:T(8,128)(2,1)S(1)} %bitcast.23, bf16[1024,512]{1,0:T(8,128)(2,1)S(1)} %bitcast.22, bf16[26,8,8,128]{3,2,1,0:T(8,128)(2,1)S(1)} %bitcast.28), kind=kOutput, calls=%fused_computation.3 | convolution fusion | flops 440401920 | bytes 3375104 | tf_op jit(solution)/shard_map/dot_general | solution.py:73
  39.8 0.3 multiply_convert_fusion.1
  40.2 0.0 copy-start
  40.2 0.1 collective-permute-start.2
  40.3 0.3 fusion.30
  40.6 0.1 subtract_convert_fusion.1
  40.7 0.1 copy.18
  40.9 0.1 copy.19
  41.0 0.8 %pad_maximum_fusion.lag_ref = bf16[1024,256]{1,0:T(8,128)(2,1)} fusion(bf16[512,256]{1,0:T(8,128)(2,1)S(1)} %copy.19, bf16[512,256]{1,0:T(8,128)(2,1)S(1)} %copy.18), kind=kLoop, calls=%fused_computation.15 | loop fusion | flops 1048576 | bytes 1048576 | tf_op jit(solution)/shard_map/concatenate | solution.py:67
  41.8 0.2 collective-permute-done.2.other_ref
  42.1 0.0 copy-done
  42.1 0.0 copy-start.1
  42.1 0.8 %copy-done.1 = bf16[208,1024]{1,0:T(8,128)(2,1)} copy-done((bf16[208,1024]{1,0:T(8,128)(2,1)}, bf16[208,1024]{1,0:T(8,128)(2,1)S(1)}, u32[]{:S(2)}) %copy-start.1) | copy-done | bytes 426008
  42.8 10.5 %shard_map.55 = f32[32,384,256]{2,1,0:T(8,128)} custom-call(bf16[208,1024]{1,0:T(8,128)(2,1)} %copy-done, bf16[208,1024]{1,0:T(8,128)(2,1)} %copy-done.1, bf16[1024,256]{1,0:T(8,128)(2,1)} %pad_maximum_fusion.lag_ref), custom_call_target="tpu_custom_call" | custom-call | flops 6480199680 | bytes 13959168 | tf_op jit(solution)/shard_map/pallas_call | solution.py:125
  (8 shorter events, 0.1 us)
Async XLA Ops:
  0.9 10.0 %collective-permute-start = (bf16[24,3072]{1,0:T(8,128)(2,1)S(1)}, bf16[24,3072]{1,0:T(8,128)(2,1)S(1)}, u32[]{:S(2)}, u32[]{:S(2)}) collective-permute-start(bf16[24,3072]{1,0:T(8,128)(2,1)S(1)} %slice.22), channel_id=1, source_target_pairs={{1,0},{2,1},{3,2},{4,3},{5,4},{6,5},{7,6},{8,7},{9,8},{10,9},{11,1... | collective-permute-start | bytes 442376 | tf_op jit(solution)/shard_map/ppermute | solution.py:161
  11.2 2.5 %collective-permute-start.1 = (bf16[64,3072]{1,0:T(8,128)(2,1)S(1)}, bf16[64,3072]{1,0:T(8,128)(2,1)S(1)}, u32[]{:S(2)}, u32[]{:S(2)}) collective-permute-start(bf16[64,3072]{1,0:T(8,128)(2,1)S(1)} %fusion), channel_id=1, source_target_pairs={{0,1},{1,0},{2,3},{3,2},{4,5},{5,4},{6,7},{7,6},{8,9},{9,8},{10,11... | collective-permute-start | bytes 1179656 | tf_op jit(solution)/shard_map/ppermute | solution.py:141
  18.9 20.2 %all-to-all-start = ((bf16[8,208,128]{2,1,0:T(8,128)(2,1)}), bf16[8,208,128]{2,1,0:T(8,128)(2,1)S(1)}, u32[]{:S(2)}, u32[]{:S(2)}) async-start(bf16[8,208,128]{2,1,0:T(8,128)(2,1)} %bitcast.2), calls=%async_computation | async-start | bytes 851968 | tf_op jit(solution)/shard_map/all_to_all | solution.py:181
  40.2 1.8 %copy-start = (bf16[208,1024]{1,0:T(8,128)(2,1)}, bf16[208,1024]{1,0:T(8,128)(2,1)S(1)}, u32[]{:S(2)}) copy-start(bf16[208,1024]{1,0:T(8,128)(2,1)S(1)} %pad_maximum_fusion.1.mine_ref) | copy-start | bytes 1277956
  40.2 1.8 %collective-permute-start.2 = (bf16[208,1024]{1,0:T(8,128)(2,1)S(1)}, bf16[208,1024]{1,0:T(8,128)(2,1)S(1)}, u32[]{:S(2)}, u32[]{:S(2)}) collective-permute-start(bf16[208,1024]{1,0:T(8,128)(2,1)S(1)} %pad_maximum_fusion.1.mine_ref), channel_id=1, source_target_pairs={{0,1},{1,0},{2,3},{3,2},{4,5},{5,4},{6,7},{7,6},{8,9},{9,8},{10,11... | collective-permute-start | bytes 1277960 | tf_op jit(solution)/shard_map/ppermute | solution.py:187
  42.1 0.8 %copy-start.1 = (bf16[208,1024]{1,0:T(8,128)(2,1)}, bf16[208,1024]{1,0:T(8,128)(2,1)S(1)}, u32[]{:S(2)}) copy-start(bf16[208,1024]{1,0:T(8,128)(2,1)S(1)} %collective-permute-done.2.other_ref) | copy-start | bytes 1277956
